TPU v7x, 32 devices: a whole 2x2x4 slice. The times are simulated.
32 devices in a mesh: groups: 2 (over y), seq: 4 (over z), head: 2 (over x), rep: 2 (over core).
Axes of the slice: x: 2, y: 2, z: 4, core: 2. Of those that a mesh axis runs over, the one named last changes fastest.
Arguments:
- queries: bfloat16 [4, 3072, 1536], P(('groups', 'rep'), 'seq', 'head'), parts along dimension 0, may hold values from -320 to 320
- key_matrix: bfloat16 [4, 3072, 1536], P(('groups', 'rep'), 'seq', 'head'), parts along dimension 0, may hold values from -8 to 8
- values: bfloat16 [4, 3072, 1536], P(('groups', 'rep'), 'seq', 'head'), parts along dimension 0, may hold values from -6 to 6
- output_gradient: bfloat16 [4, 3072, 1536], P(('groups', 'rep'), 'seq', 'head'), parts along dimension 0, may hold values from -288 to 288
- normed: bfloat16 [4, 3072, 1536], P(('groups', 'rep'), 'seq', 'head'), parts along dimension 0, may hold values from -6 to 6
- adapter_down_weight: bfloat16 [1536, 64], P('head'), may hold values from -0.15625 to 0.15625
- adapter_up_weight: bfloat16 [64, 1536], P(None, 'head'), may hold values from -0.1796875 to 0.1796875
- listed_key_tiles: int32 [16, 3], P('groups'), parts along dimension 0, may hold values from 0 to 7, as said below
- listed_tile_count: int32 [16], P('groups'), parts along dimension 0, may hold values from 1 to 3
Outputs:
- query_grad: bfloat16 [4, 3072, 1536], P(('groups', 'rep'), 'seq', 'head'), parts along dimension 0
- key_grad: bfloat16 [4, 3072, 1536], P(('groups', 'rep'), 'seq', 'head'), parts along dimension 0
- value_gradient: bfloat16 [4, 3072, 1536], P(('groups', 'rep'), 'seq', 'head'), parts along dimension 0
- down_projection_grad: float32 [3072, 64], P(('groups', 'head')), parts along dimension 0
- up_projection_grad: float32 [128, 1536], P('groups', 'head'), parts along dimension 0
There are 2 independent parts, one for each index of `groups`. A program takes and returns all parts, laid end to end along the dimension named above; an argument that names none is the same for every part. Nothing has to cross between parts.
Inputs may be any that keep to these rules, and one draw needn't show every extreme that they name: `listed_key_tiles`: for query tile i the first listed_tile_count[i] entries are distinct tiles within 1 tiles of i, one of them i itself; the remaining entries equal i.
All inputs are finite; a program needn't handle non-finite values.
Results may differ from a plain program's by a relative error of at most 0.0078.
Values may be sent and summed in bfloat16 or wider, within the bound.
No kernel may reach another device: no remote copies, remote signals or barrier semaphores. Data moves between devices by JAX's collectives and lax.ppermute only.
A program may use at most 64 MiB of HBM per device.

v0:
```python
import jax
import jax.numpy as jnp
from jax import lax
from jax.sharding import PartitionSpec as P

TILE = 384
TILES_DEV = 2
REACH = 1
HEAD_SIZE = 128


adapter_scale = 0.0078125
masked_score = -1e30


def shifted(shard, axis, by):
    peers = lax.axis_size(axis)
    pairs = [(i, i + by) for i in range(peers) if 0 <= i + by < peers]
    return lax.ppermute(shard, axis, pairs)


def butterfly_sum(tree, axis):
    peers = lax.axis_size(axis)
    if peers & (peers - 1):
        return lax.psum(tree, axis)
    step = 1
    while step < peers:
        pairs = [(i, i ^ step) for i in range(peers)]
        other = lax.ppermute(tree, axis, pairs)
        tree = jax.tree.map(lambda a, b: a + b, tree, other)
        step *= 2
    return tree


def chosen_pairs(listed_key_tiles, listed_tile_count, query_tiles, key_tiles):
    total_tiles = listed_key_tiles.shape[0]
    clipped = jnp.clip(query_tiles, 0, total_tiles - 1)
    one_hot = (clipped[:, None] == jnp.arange(total_tiles, dtype=jnp.int32)[None, :]).astype(
        jnp.int32
    )
    key_lists = jnp.sum(one_hot[:, :, None] * listed_key_tiles[None, :, :], axis=1)
    counts = jnp.sum(one_hot * listed_tile_count[None, :], axis=1)
    slot_ids = jnp.arange(listed_key_tiles.shape[1], dtype=jnp.int32)
    matched = (key_lists == key_tiles[:, None]) & (slot_ids[None, :] < counts[:, None])
    inside = (query_tiles >= 0) & (query_tiles < total_tiles)
    return jnp.any(matched, axis=1) & inside


def block_scores(tile_query, keys, bias):
    score_scale = HEAD_SIZE ** (-0.5)
    raw = jnp.einsum("cqhd,ckhd->chqk", tile_query, keys, preferred_element_type=jnp.float32)
    return score_scale * raw + bias


def tile_backward(tile_query, tile_grad, keys, values, biases):
    scores = [block_scores(tile_query, k, b) for k, b in zip(keys, biases)]
    row_max = scores[0].max(axis=-1, keepdims=True)
    for s in scores[1:]:
        row_max = jnp.maximum(row_max, s.max(axis=-1, keepdims=True))
    total = sum(jnp.sum(jnp.exp(s - row_max), axis=-1, keepdims=True) for s in scores)
    log_total = row_max + jnp.log(total)
    weights = [jnp.exp(s - log_total).astype(jnp.bfloat16) for s in scores]
    grad_weights = [
        jnp.einsum("cqhd,ckhd->chqk", tile_grad, v, preferred_element_type=jnp.float32)
        for v in values
    ]
    row_dot = sum(
        jnp.sum(w.astype(jnp.float32) * g, axis=-1, keepdims=True)
        for w, g in zip(weights, grad_weights)
    )
    grad_scores = [
        (w.astype(jnp.float32) * (g - row_dot)).astype(jnp.bfloat16)
        for w, g in zip(weights, grad_weights)
    ]
    return weights, grad_scores


def key_terms(grad_scores, weights, tile_query, tile_grad):
    score_scale = HEAD_SIZE ** (-0.5)
    key_term = score_scale * jnp.einsum(
        "chqk,cqhd->ckhd", grad_scores, tile_query, preferred_element_type=jnp.float32
    )
    value_term = jnp.einsum(
        "chqk,cqhd->ckhd", weights, tile_grad, preferred_element_type=jnp.float32
    )
    return key_term, value_term


def on_device(
    queries,
    key_matrix,
    values,
    output_gradient,
    normed,
    adapter_down_weight,
    adapter_up_weight,
    listed_key_tiles,
    listed_tile_count,
):
    score_scale = HEAD_SIZE ** (-0.5)
    clip_count, block_len, width = queries.shape
    local_heads = width // HEAD_SIZE
    position = lax.axis_index("seq")
    first_tile = position * TILES_DEV

    def heads(x, t):
        return x[:, t * TILE:(t + 1) * TILE].reshape(clip_count, TILE, local_heads, HEAD_SIZE)

    down_piece = jnp.einsum(
        "pqg,gv->pqv", normed, adapter_down_weight, preferred_element_type=jnp.float32
    )
    lowered_rows = butterfly_sum(down_piece, "head").astype(jnp.bfloat16)

    left_kv = shifted(
        jnp.stack((key_matrix[:, block_len - TILE:], values[:, block_len - TILE:]), 0), "seq", 1
    )
    right_kv = shifted(jnp.stack((key_matrix[:, :TILE], values[:, :TILE]), 0), "seq", -1)

    q_a, q_b = heads(queries, 0), heads(queries, 1)
    g_a, g_b = heads(output_gradient, 0), heads(output_gradient, 1)
    k_a, k_b = heads(key_matrix, 0), heads(key_matrix, 1)
    v_a, v_b = heads(values, 0), heads(values, 1)
    k_l = left_kv[0].reshape(clip_count, TILE, local_heads, HEAD_SIZE)
    v_l = left_kv[1].reshape(clip_count, TILE, local_heads, HEAD_SIZE)
    k_r = right_kv[0].reshape(clip_count, TILE, local_heads, HEAD_SIZE)
    v_r = right_kv[1].reshape(clip_count, TILE, local_heads, HEAD_SIZE)

    tile_a, tile_b = first_tile, first_tile + 1
    allowed = chosen_pairs(
        listed_key_tiles,
        listed_tile_count,
        jnp.stack([tile_a, tile_a, tile_a, tile_b, tile_b, tile_b]).astype(jnp.int32),
        jnp.stack([tile_a - 1, tile_a, tile_b, tile_a, tile_b, tile_b + 1]).astype(jnp.int32),
    )
    bias = jnp.where(allowed, 0.0, masked_score).astype(jnp.float32)

    w_a, ds_a = tile_backward(q_a, g_a, (k_l, k_a, k_b), (v_l, v_a, v_b), bias[0:3])
    w_b, ds_b = tile_backward(q_b, g_b, (k_a, k_b, k_r), (v_a, v_b, v_r), bias[3:6])

    dk_l, dv_l = key_terms(ds_a[0], w_a[0], q_a, g_a)
    dk_r, dv_r = key_terms(ds_b[2], w_b[2], q_b, g_b)
    to_left = jnp.stack((dk_l, dv_l), 0).astype(jnp.bfloat16)
    to_right = jnp.stack((dk_r, dv_r), 0).astype(jnp.bfloat16)
    from_right = shifted(to_left, "seq", -1)
    from_left = shifted(to_right, "seq", 1)

    def query_term(ds, keys):
        return sum(
            jnp.einsum("chqk,ckhd->cqhd", d, k, preferred_element_type=jnp.float32)
            for d, k in zip(ds, keys)
        )

    dq_a = score_scale * query_term(ds_a, (k_l, k_a, k_b))
    dq_b = score_scale * query_term(ds_b, (k_a, k_b, k_r))
    query_grad = jnp.concatenate((dq_a, dq_b), 1).reshape(clip_count, block_len, width)
    query_grad = query_grad.astype(jnp.bfloat16)

    dk_aa, dv_aa = key_terms(ds_a[1], w_a[1], q_a, g_a)
    dk_ba, dv_ba = key_terms(ds_b[0], w_b[0], q_b, g_b)
    dk_ab, dv_ab = key_terms(ds_a[2], w_a[2], q_a, g_a)
    dk_bb, dv_bb = key_terms(ds_b[1], w_b[1], q_b, g_b)

    def finish(own, arrived):
        own = own.reshape(clip_count, TILE, width).astype(jnp.bfloat16).astype(jnp.float32)
        return own + arrived.reshape(clip_count, TILE, width).astype(jnp.float32)

    key_grad = jnp.concatenate(
        (finish(dk_aa + dk_ba, from_left[0]), finish(dk_ab + dk_bb, from_right[0])), 1
    ).astype(jnp.bfloat16)
    value_gradient = jnp.concatenate(
        (finish(dv_aa + dv_ba, from_left[1]), finish(dv_ab + dv_bb, from_right[1])), 1
    ).astype(jnp.bfloat16)

    backward_piece = jnp.einsum(
        "dsi,ji->dsj", value_gradient, adapter_up_weight, preferred_element_type=jnp.float32
    )
    backward_rows = butterfly_sum(backward_piece, "head").astype(jnp.bfloat16)
    gradient_down_local = adapter_scale * jnp.einsum(
        "yhm,yhz->mz", normed, backward_rows, preferred_element_type=jnp.float32
    )
    gradient_up_local = adapter_scale * jnp.einsum(
        "igb,igu->bu", lowered_rows, value_gradient, preferred_element_type=jnp.float32
    )
    down_projection_grad, up_projection_grad = butterfly_sum(
        butterfly_sum((gradient_down_local, gradient_up_local), "rep"), "seq"
    )
    return (query_grad, key_grad, value_gradient, down_projection_grad, up_projection_grad)


def solution(mesh):
    in_specs = (
        P(("groups", "rep"), "seq", "head"),
        P(("groups", "rep"), "seq", "head"),
        P(("groups", "rep"), "seq", "head"),
        P(("groups", "rep"), "seq", "head"),
        P(("groups", "rep"), "seq", "head"),
        P("head", None),
        P(None, "head"),
        P("groups", None),
        P("groups"),
    )
    out_specs = (
        P(("groups", "rep"), "seq", "head"),
        P(("groups", "rep"), "seq", "head"),
        P(("groups", "rep"), "seq", "head"),
        P(("groups", "head"), None),
        P("groups", "head"),
    )
    return jax.shard_map(
        on_device, mesh=mesh, in_specs=in_specs, out_specs=out_specs, check_vma=False
    )
```

profile of v0, /device:TPU:0, one launch (start us, length us, event | category | flops | bytes accessed | tf_op | source)
XLA Modules:
  0.0 208.7 jit_solution(14908118889696249043)
XLA Ops:
  10.4 6.6 %collective-permute-start = (bf16[2,1,384,768]{2,3,1,0:T(8,128)(2,1)}, bf16[2,1,384,768]{2,3,1,0:T(8,128)(2,1)}, u32[]{:S(2)}, u32[]{:S(2)}) collective-permute-start(bf16[2,1,384,768]{2,3,1,0:T(8,128)(2,1)} %pad_maximum_fusion), channel_id=1, source_target_pairs={{0,4},{4,8},{8,12},{1,5},{5,9},{9,13},{2,6},{6,10},{10,14},{3,7},{... | collective-permute-start | bytes 3538952 | tf_op jit(solution)/shard_map/ppermute | solution.py:19
  25.5 3.0 %fusion.22 = (f32[6,384]{1,0:T(8,128)S(1)}, f32[6,384,384]{2,1,0:T(8,128)}) fusion(f32[]{:T(128)} %bitcast.24, bf16[384,6,128]{0,2,1:T(8,128)(2,1)S(1)} %bitcast.252, bf16[384,6,128]{0,2,1:T(8,128)(2,1)S(1)} %bitcast.270), kind=kOutput, calls=%fused_computation.56 | convolution fusion | flops 229144320 | bytes 4727812 | tf_op jit(solution)/shard_map/cqhd,ckhd->chqk/dot_general | solution.py:51
  28.5 3.1 %fusion.23 = (f32[6,384]{1,0:T(8,128)S(1)}, f32[6,384,384]{2,1,0:T(8,128)}) fusion(f32[]{:T(128)} %bitcast.25, bf16[384,6,128]{0,2,1:T(8,128)(2,1)S(1)} %bitcast.253, bf16[384,6,128]{0,2,1:T(8,128)(2,1)S(1)} %bitcast.265), kind=kOutput, calls=%fused_computation.57 | convolution fusion | flops 229144320 | bytes 4727812 | tf_op jit(solution)/shard_map/cqhd,ckhd->chqk/dot_general | solution.py:51
  31.6 3.3 %fusion.21 = (f32[6,384]{1,0:T(8,128)S(1)}, f32[6,384,384]{1,2,0:T(8,128)}) fusion(f32[]{:T(128)} %bitcast.13, bf16[384,6,128]{0,2,1:T(8,128)(2,1)S(1)} %bitcast.258, bf16[384,6,128]{0,2,1:T(8,128)(2,1)S(1)} %bitcast.266), kind=kOutput, calls=%fused_computation.55 | convolution fusion | flops 229144320 | bytes 4727812 | tf_op jit(solution)/shard_map/cqhd,ckhd->chqk/dot_general | solution.py:51
  47.1 4.2 %exponential_reduce_fusion.3 = (f32[6,384]{1,0:T(8,128)S(1)}, f32[6,384]{1,0:T(8,128)S(1)}, f32[6,384]{1,0:T(8,128)S(1)}) fusion(f32[6,384,384]{1,2,0:T(8,128)S(1)} %get-tuple-element.86, f32[6,384]{1,0:T(8,128)S(1)} %maximum_maximum_fusion.1, f32[]{:T(128)} %bitcast.11, f32[]{:T(128)} %bitcast.13, f32[6,384,384]{1,2,0:T(8,128)S(1)} %copy-done.3, ...), kind=kLoop, calls=%fused_computation.50 | loop fusion | flops 10609920 | bytes 10653708 | tf_op jit(solution)/shard_map/reduce_sum | solution.py:60
  51.4 7.0 %fusion.2 = (f32[6,384]{1,0:T(8,128)S(1)}, bf16[6,384,384]{1,2,0:T(8,128)(2,1)}, f32[6,384]{1,0:T(8,128)S(1)}, bf16[6,384,384]{1,2,0:T(8,128)(2,1)}, f32[6,384]{...) fusion(f32[6,384]{1,0:T(8,128)S(1)} %log_add_fusion.1, f32[]{:T(128)} %bitcast.11, ...), kind=kOutput, calls=%fused_computation.14 | convolution fusion | flops 245064960 | bytes 27758604 | tf_op jit(solution)/shard_map/cqhd,ckhd->chqk/dot_general | solution.py:64
  58.4 7.9 %fusion.1 = (bf16[6,384,384]{1,2,0:T(8,128)(2,1)}, bf16[6,384,384]{1,2,0:T(8,128)(2,1)}, bf16[6,384,384]{1,2,0:T(8,128)(2,1)}) fusion(bf16[6,384,384]{1,2,0:T(8,128)(2,1)} %get-tuple-element.60, f32[6,384,384]{2,1,0:T(8,128)} %copy-done.4, f32[6,384]{1,0:T(8,128)S(1)} %add_add_fusion.1, f32[6,384,384]{1,2,0:T(8,128)} %get-tuple-element.87, ...), kind=kLoop, calls=%fused_computation.13 | loop fusion | flops 10616832 | bytes 21242880 | tf_op jit(solution)/shard_map/convert_element_type | solution.py:72
  66.3 3.3 %convolution_bitcast_fusion = f32[6,128,384]{2,1,0:T(8,128)} fusion(bf16[384,6,128]{0,2,1:T(8,128)(2,1)} %bitcast.267, bf16[6,384,384]{1,2,0:T(8,128)(2,1)} %get-tuple-element.56), kind=kOutput, calls=%fused_computation.73 | convolution fusion | flops 226492416 | bytes 3538944 | tf_op jit(solution)/shard_map/chqk,ckhd->cqhd/dot_general | solution.py:149
  81.4 4.2 %exponential_reduce_fusion = (f32[6,384]{1,0:T(8,128)S(1)}, f32[6,384]{1,0:T(8,128)S(1)}, f32[6,384]{1,0:T(8,128)S(1)}) fusion(f32[6,384,384]{2,1,0:T(8,128)S(1)} %copy-done.2, f32[6,384]{1,0:T(8,128)S(1)} %maximum_maximum_fusion, f32[]{:T(128)} %bitcast.25, f32[]{:T(128)} %bitcast.29, f32[6,384,384]{1,2,0:T(8,128)S(1)} %get-tuple-element.75, f32[]{:T(128)} %bitcast.24, ...), kind=kLoop, calls=%fused_computation.42 | loop fusion | flops 10609920 | bytes 10653708 | tf_op jit(solution)/shard_map/reduce_sum | solution.py:60
  85.6 8.5 %fusion.8 = (f32[6,384]{1,0:T(8,128)S(1)}, bf16[6,384,384]{2,1,0:T(8,128)(2,1)}, f32[6,384]{1,0:T(8,128)S(1)}, bf16[6,384,384]{2,1,0:T(8,128)(2,1)}, f32[6,384]{...) fusion(f32[6,384]{1,0:T(8,128)S(1)} %log_add_fusion, f32[]{:T(128)} %bitcast.25, ...), kind=kOutput, calls=%fused_computation.20 | convolution fusion | flops 245064960 | bytes 27758604 | tf_op jit(solution)/shard_map/cqhd,ckhd->chqk/dot_general | solution.py:64
  94.1 3.0 %fusion.44 = bf16[1,1,384,6,128]{2,4,3,1,0:T(8,128)(2,1)} fusion(bf16[384,6,128]{0,2,1:T(8,128)(2,1)S(1)} %bitcast.243, bf16[6,384,384]{2,1,0:T(8,128)(2,1)} %get-tuple-element.65), kind=kOutput, calls=%fused_computation.91 | convolution fusion | flops 226787328 | bytes 2949120 | tf_op jit(solution)/shard_map/chqk,cqhd->ckhd/dot_general | solution.py:83
  97.1 4.1 %fusion.11 = (bf16[6,384,384]{2,1,0:T(8,128)(2,1)S(1)}, bf16[6,384,384]{2,1,0:T(8,128)(2,1)S(1)}, bf16[6,384,384]{2,1,0:T(8,128)(2,1)S(1)}) fusion(bf16[6,384,384]{2,1,0:T(8,128)(2,1)} %get-tuple-element.65, f32[6,384,384]{1,2,0:T(8,128)S(1)} %fusion.86, f32[6,384]{1,0:T(8,128)S(1)} %add_add_fusion, f32[6,384,384]{2,1,0:T(8,128)} %get-tuple-element.80, ...), kind=kLoop, calls=%fused_computation.23 | loop fusion | flops 10616832 | bytes 21242880 | tf_op jit(solution)/shard_map/convert_element_type | solution.py:72
  112.0 3.4 %fusion.37 = f32[6,384,128]{1,2,0:T(8,128)} fusion(f32[6,384,128]{1,2,0:T(8,128)} %fusion.89, bf16[384,6,128]{0,2,1:T(8,128)(2,1)S(1)} %bitcast.256, bf16[6,384,384]{2,1,0:T(8,128)(2,1)} %copy-done.18), kind=kOutput, calls=%fused_computation.82 | convolution fusion | flops 227672064 | bytes 4718592 | tf_op jit(solution)/shard_map/chqk,cqhd->ckhd/dot_general | solution.py:80
  121.9 2.9 %fusion.34 = f32[6,384,128]{1,2,0:T(8,128)} fusion(f32[6,384,128]{1,2,0:T(8,128)} %fusion.88, bf16[384,6,128]{0,2,1:T(8,128)(2,1)S(1)} %bitcast.257, bf16[6,384,384]{2,1,0:T(8,128)(2,1)S(1)} %copy-done.17), kind=kOutput, calls=%fused_computation.79 | convolution fusion | flops 227672064 | bytes 4718592 | tf_op jit(solution)/shard_map/chqk,cqhd->ckhd/dot_general | solution.py:80
  124.7 2.7 %copy.201 = f32[384,768]{1,0:T(8,128)} copy(f32[384,768]{0,1:T(8,128)} %bitcast.285) | data formatting | bytes 2359296 | tf_op jit(solution)/shard_map/convert_element_type | solution.py:164
  129.9 6.0 %collective-permute-start.2 = (bf16[2,1,384,6,128]{2,4,3,1,0:T(8,128)(2,1)}, bf16[2,1,384,6,128]{2,4,3,1,0:T(8,128)(2,1)}, u32[]{:S(2)}, u32[]{:S(2)}) collective-permute-start(bf16[2,1,384,6,128]{2,4,3,1,0:T(8,128)(2,1)} %pad_maximum_fusion.3), channel_id=1, source_target_pairs={{0,4},{4,8},{8,12},{1,5},{5,9},{9,13},{2,6},{6,10},{10,14},{3,7},{... | collective-permute-start | bytes 3538952 | tf_op jit(solution)/shard_map/ppermute | solution.py:19
  138.1 2.7 %copy.214 = f32[384,768]{1,0:T(8,128)} copy(f32[384,768]{0,1:T(8,128)} %bitcast.288) | data formatting | bytes 2359296 | tf_op jit(solution)/shard_map/convert_element_type | solution.py:164
  153.1 6.2 %collective-permute-done.2 = bf16[2,1,384,6,128]{2,4,3,1,0:T(8,128)(2,1)} collective-permute-done((bf16[2,1,384,6,128]{2,4,3,1,0:T(8,128)(2,1)}, bf16[2,1,384,6,128]{2,4,3,1,0:T(8,128)(2,1)}, u32[]{:S(2)}, u32[]{:S(2)}) %collective-permute-start.2) | collective-permute-done | bytes 1179680 | tf_op jit(solution)/shard_map/ppermute | solution.py:19
  164.7 2.7 %add_convert_fusion = bf16[384,768]{1,0:T(8,128)(2,1)} fusion(f32[384,768]{1,0:T(8,128)} %copy.214, f32[384,768]{1,0:T(8,128)} %copy.215), kind=kLoop, calls=%fused_computation.107 | loop fusion | flops 589824 | bytes 2949120 | tf_op jit(solution)/shard_map/convert.18
  174.8 2.9 %collective-permute-done.4 = f32[1,768,64]{1,2,0:T(8,128)S(1)} collective-permute-done((f32[1,768,64]{1,2,0:T(8,128)S(1)}, f32[1,768,64]{1,2,0:T(8,128)S(1)}, u32[]{:S(2)}, u32[]{:S(2)}) %collective-permute-start.4) | collective-permute-done | bytes 196640 | tf_op jit(solution)/shard_map/ppermute | solution.py:29
  182.3 4.4 %collective-permute-done.10 = f32[64,768]{1,0:T(8,128)S(1)} collective-permute-done((f32[64,768]{1,0:T(8,128)S(1)}, f32[64,768]{1,0:T(8,128)S(1)}, u32[]{:S(2)}, u32[]{:S(2)}) %collective-permute-start.10) | collective-permute-done | bytes 196640 | tf_op jit(solution)/shard_map/ppermute | solution.py:29
  186.7 4.0 %collective-permute-start.11 = (f32[64,768]{1,0:T(8,128)S(1)}, f32[64,768]{1,0:T(8,128)S(1)}, u32[]{:S(2)}, u32[]{:S(2)}) collective-permute-start(f32[64,768]{1,0:T(8,128)S(1)} %add.307), channel_id=1, source_target_pairs={{0,8},{4,12},{8,0},{12,4},{1,9},{5,13},{9,1},{13,5},{2,10},{6,14},... | collective-permute-start | bytes 589832 | tf_op jit(solution)/shard_map/ppermute | solution.py:29
  190.7 4.2 %collective-permute-start.7 = (f32[768,64]{0,1:T(8,128)S(1)}, f32[768,64]{0,1:T(8,128)S(1)}, u32[]{:S(2)}, u32[]{:S(2)}) collective-permute-start(f32[768,64]{0,1:T(8,128)S(1)} %add.303), channel_id=1, source_target_pairs={{0,8},{4,12},{8,0},{12,4},{1,9},{5,13},{9,1},{13,5},{2,10},{6,14},... | collective-permute-start | bytes 589832 | tf_op jit(solution)/shard_map/ppermute | solution.py:29
  197.0 7.8 %collective-permute-done.11 = f32[64,768]{1,0:T(8,128)S(1)} collective-permute-done((f32[64,768]{1,0:T(8,128)S(1)}, f32[64,768]{1,0:T(8,128)S(1)}, u32[]{:S(2)}, u32[]{:S(2)}) %collective-permute-start.11) | collective-permute-done | bytes 196640 | tf_op jit(solution)/shard_map/ppermute | solution.py:29
  (195 shorter events, 99.4 us)
Async XLA Ops:
  0.6 16.4 %copy-start = (bf16[1,768,768]{2,1,0:T(8,128)(2,1)S(1)}, bf16[1,768,768]{2,1,0:T(8,128)(2,1)}, u32[]{:S(2)}) copy-start(bf16[1,768,768]{2,1,0:T(8,128)(2,1)} %param.13) | copy-start | bytes 3538948
  5.0 20.5 %copy-start.14 = (bf16[1,384,768]{1,2,0:T(8,128)(2,1)}, bf16[1,384,768]{1,2,0:T(8,128)(2,1)S(1)}, u32[]{:S(2)}) copy-start(bf16[1,384,768]{1,2,0:T(8,128)(2,1)S(1)} %copy.275) | copy-start | bytes 1769476
  6.2 70.0 %collective-permute-start.1 = (bf16[2,1,384,768]{2,3,1,0:T(8,128)(2,1)}, bf16[2,1,384,768]{2,3,1,0:T(8,128)(2,1)}, u32[]{:S(2)}, u32[]{:S(2)}) collective-permute-start(bf16[2,1,384,768]{2,3,1,0:T(8,128)(2,1)} %pad_maximum_fusion.1), channel_id=1, source_target_pairs={{4,0},{8,4},{12,8},{5,1},{9,5},{13,9},{6,2},{10,6},{14,10},{7,3},{... | collective-permute-start | bytes 3538952 | tf_op jit(solution)/shard_map/ppermute | solution.py:19
  8.9 22.7 %copy-start.12 = (bf16[1,384,768]{1,2,0:T(8,128)(2,1)}, bf16[1,384,768]{1,2,0:T(8,128)(2,1)S(1)}, u32[]{:S(2)}) copy-start(bf16[1,384,768]{1,2,0:T(8,128)(2,1)S(1)} %copy.272) | copy-start | bytes 1769476
  9.2 9.0 %copy-start.27 = (bf16[1,384,768]{1,2,0:T(8,128)(2,1)}, bf16[1,384,768]{1,2,0:T(8,128)(2,1)S(1)}, u32[]{:S(2)}) copy-start(bf16[1,384,768]{1,2,0:T(8,128)(2,1)S(1)} %copy.273) | copy-start | bytes 1769476
  9.2 7.8 %copy-start.46 = (bf16[768,64]{0,1:T(8,128)(2,1)S(1)}, bf16[768,64]{0,1:T(8,128)(2,1)}, u32[]{:S(2)}) copy-start(bf16[768,64]{0,1:T(8,128)(2,1)} %param.14) | copy-start | bytes 294916
  9.2 11.1 %copy-start.48 = (s32[8]{0:T(128)S(1)}, s32[8]{0:T(128)}, u32[]{:S(2)}) copy-start(s32[8]{0:T(128)} %param.17) | copy-start | bytes 100
  9.3 11.2 %copy-start.47 = (s32[8,3]{0,1:T(4,128)S(1)}, s32[8,3]{0,1:T(4,128)}, u32[]{:S(2)}) copy-start(s32[8,3]{0,1:T(4,128)} %param.16) | copy-start | bytes 292
  10.4 31.4 %collective-permute-start = (bf16[2,1,384,768]{2,3,1,0:T(8,128)(2,1)}, bf16[2,1,384,768]{2,3,1,0:T(8,128)(2,1)}, u32[]{:S(2)}, u32[]{:S(2)}) collective-permute-start(bf16[2,1,384,768]{2,3,1,0:T(8,128)(2,1)} %pad_maximum_fusion), channel_id=1, source_target_pairs={{0,4},{4,8},{8,12},{1,5},{5,9},{9,13},{2,6},{6,10},{10,14},{3,7},{... | collective-permute-start | bytes 3538952 | tf_op jit(solution)/shard_map/ppermute | solution.py:19
  18.2 155.1 %collective-permute-start.8 = (f32[1,768,64]{1,2,0:T(8,128)}, f32[1,768,64]{1,2,0:T(8,128)}, u32[]{:S(2)}, u32[]{:S(2)}) collective-permute-start(f32[1,768,64]{1,2,0:T(8,128)} %fusion.52), channel_id=1, source_target_pairs={{0,2},{2,0},{1,3},{3,1},{4,6},{6,4},{5,7},{7,5},{8,10},{10,8},{9,1... | collective-permute-start | bytes 589832 | tf_op jit(solution)/shard_map/ppermute | solution.py:29
  43.8 7.5 %copy-start.4 = (f32[6,384,384]{2,1,0:T(8,128)}, f32[6,384,384]{2,1,0:T(8,128)S(1)}, u32[]{:S(2)}) copy-start(f32[6,384,384]{2,1,0:T(8,128)S(1)} %fusion.83) | copy-start | bytes 10616836
  120.6 29.5 %collective-permute-start.3 = (bf16[2,1,384,6,128]{2,4,3,1,0:T(8,128)(2,1)}, bf16[2,1,384,6,128]{2,4,3,1,0:T(8,128)(2,1)}, u32[]{:S(2)}, u32[]{:S(2)}) collective-permute-start(bf16[2,1,384,6,128]{2,4,3,1,0:T(8,128)(2,1)} %pad_maximum_fusion.4), channel_id=1, source_target_pairs={{4,0},{8,4},{12,8},{5,1},{9,5},{13,9},{6,2},{10,6},{14,10},{7,3},{... | collective-permute-start | bytes 3538952 | tf_op jit(solution)/shard_map/ppermute | solution.py:19
  127.5 8.3 %copy-start.21 = (bf16[6,384,384]{1,2,0:T(8,128)(2,1)S(1)}, bf16[6,384,384]{1,2,0:T(8,128)(2,1)}, u32[]{:S(2)}) copy-start(bf16[6,384,384]{1,2,0:T(8,128)(2,1)} %get-tuple-element.58) | copy-start | bytes 5308420
  129.9 6.6 %copy-start.25 = (bf16[6,384,384]{2,1,0:T(8,128)(2,1)S(1)}, bf16[6,384,384]{2,1,0:T(8,128)(2,1)}, u32[]{:S(2)}) copy-start(bf16[6,384,384]{2,1,0:T(8,128)(2,1)} %get-tuple-element.33) | copy-start | bytes 5308420
  129.9 29.5 %collective-permute-start.2 = (bf16[2,1,384,6,128]{2,4,3,1,0:T(8,128)(2,1)}, bf16[2,1,384,6,128]{2,4,3,1,0:T(8,128)(2,1)}, u32[]{:S(2)}, u32[]{:S(2)}) collective-permute-start(bf16[2,1,384,6,128]{2,4,3,1,0:T(8,128)(2,1)} %pad_maximum_fusion.3), channel_id=1, source_target_pairs={{0,4},{4,8},{8,12},{1,5},{5,9},{9,13},{2,6},{6,10},{10,14},{3,7},{... | collective-permute-start | bytes 3538952 | tf_op jit(solution)/shard_map/ppermute | solution.py:19
  171.9 6.2 %copy-start.38 = (f32[384,768]{1,0:T(8,128)S(1)}, f32[384,768]{1,0:T(8,128)}, u32[]{:S(2)}) copy-start(f32[384,768]{1,0:T(8,128)} %copy.208) | copy-start | bytes 3538948
  171.9 6.2 %copy-start.40 = (f32[384,768]{1,0:T(8,128)S(1)}, f32[384,768]{1,0:T(8,128)}, u32[]{:S(2)}) copy-start(f32[384,768]{1,0:T(8,128)} %copy.209) | copy-start | bytes 3538948
  172.0 5.7 %collective-permute-start.4 = (f32[1,768,64]{1,2,0:T(8,128)S(1)}, f32[1,768,64]{1,2,0:T(8,128)S(1)}, u32[]{:S(2)}, u32[]{:S(2)}) collective-permute-start(f32[1,768,64]{1,2,0:T(8,128)S(1)} %convolution_bitcast_fusion.2), channel_id=1, source_target_pairs={{0,2},{2,0},{1,3},{3,1},{4,6},{6,4},{5,7},{7,5},{8,10},{10,8},{9,1... | collective-permute-start | bytes 589832 | tf_op jit(solution)/shard_map/ppermute | solution.py:29
  174.7 3.6 %collective-permute-start.9 = (f32[64,768]{1,0:T(8,128)S(1)}, f32[64,768]{1,0:T(8,128)S(1)}, u32[]{:S(2)}, u32[]{:S(2)}) collective-permute-start(f32[64,768]{1,0:T(8,128)S(1)} %convolution_multiply_fusion.2), channel_id=1, source_target_pairs={{0,1},{1,0},{2,3},{3,2},{4,5},{5,4},{6,7},{7,6},{8,9},{9,8},{10,11... | collective-permute-start | bytes 589832 | tf_op jit(solution)/shard_map/ppermute | solution.py:29
  178.0 2.8 %collective-permute-start.5 = (f32[768,64]{0,1:T(8,128)S(1)}, f32[768,64]{0,1:T(8,128)S(1)}, u32[]{:S(2)}, u32[]{:S(2)}) collective-permute-start(f32[768,64]{0,1:T(8,128)S(1)} %fusion.58), channel_id=1, source_target_pairs={{0,1},{1,0},{2,3},{3,2},{4,5},{5,4},{6,7},{7,6},{8,9},{9,8},{10,11... | collective-permute-start | bytes 589832 | tf_op jit(solution)/shard_map/ppermute | solution.py:29
  178.3 8.3 %collective-permute-start.10 = (f32[64,768]{1,0:T(8,128)S(1)}, f32[64,768]{1,0:T(8,128)S(1)}, u32[]{:S(2)}, u32[]{:S(2)}) collective-permute-start(f32[64,768]{1,0:T(8,128)S(1)} %add.306), channel_id=1, source_target_pairs={{0,4},{4,0},{8,12},{12,8},{1,5},{5,1},{9,13},{13,9},{2,6},{6,2},{1... | collective-permute-start | bytes 589832 | tf_op jit(solution)/shard_map/ppermute | solution.py:29
  180.9 9.7 %collective-permute-start.6 = (f32[768,64]{0,1:T(8,128)S(1)}, f32[768,64]{0,1:T(8,128)S(1)}, u32[]{:S(2)}, u32[]{:S(2)}) collective-permute-start(f32[768,64]{0,1:T(8,128)S(1)} %add.302), channel_id=1, source_target_pairs={{0,4},{4,0},{8,12},{12,8},{1,5},{5,1},{9,13},{13,9},{2,6},{6,2},{1... | collective-permute-start | bytes 589832 | tf_op jit(solution)/shard_map/ppermute | solution.py:29
  186.7 18.2 %collective-permute-start.11 = (f32[64,768]{1,0:T(8,128)S(1)}, f32[64,768]{1,0:T(8,128)S(1)}, u32[]{:S(2)}, u32[]{:S(2)}) collective-permute-start(f32[64,768]{1,0:T(8,128)S(1)} %add.307), channel_id=1, source_target_pairs={{0,8},{4,12},{8,0},{12,4},{1,9},{5,13},{9,1},{13,5},{2,10},{6,14},... | collective-permute-start | bytes 589832 | tf_op jit(solution)/shard_map/ppermute | solution.py:29
  190.7 17.4 %collective-permute-start.7 = (f32[768,64]{0,1:T(8,128)S(1)}, f32[768,64]{0,1:T(8,128)S(1)}, u32[]{:S(2)}, u32[]{:S(2)}) collective-permute-start(f32[768,64]{0,1:T(8,128)S(1)} %add.303), channel_id=1, source_target_pairs={{0,8},{4,12},{8,0},{12,4},{1,9},{5,13},{9,1},{13,5},{2,10},{6,14},... | collective-permute-start | bytes 589832 | tf_op jit(solution)/shard_map/ppermute | solution.py:29
  (37 other events, 89.1 us)
where the time goes:
time: 210 us; the launch traced here: 209 us
  matrix products  68.4 us (33%)
  local copies, waits for them, and re-layouts  43.7 us (21%)
  other arithmetic  38.5 us (18%)
  starting transfers between devices  30.5 us (15%)
  waiting for transfers between devices  26.5 us (13%)
    dot_general x6, matrix products, tile_backward(): jnp.einsum('cqhd,ckhd->chqk', tile_grad, v, preferred_element_type=jnp.fl...  18.2 us
    ppermute x8, waiting for transfers between devices, butterfly_sum(): other = lax.ppermute(tree, axis, pairs)  17.6 us
    ppermute x8, starting transfers between devices, butterfly_sum(): other = lax.ppermute(tree, axis, pairs)  15.4 us
    ppermute x4, starting transfers between devices, shifted(): return lax.ppermute(shard, axis, pairs)  15.1 us
    dot_general x6, matrix products, block_scores(): jnp.einsum('cqhd,ckhd->chqk', tile_query, keys, preferred_element_type=jn...  14.8 us
    unnamed x107, local copies, waits for them, and re-layouts  14 us
    dot_general x6, matrix products, key_terms(): jnp.einsum('chqk,cqhd->ckhd', grad_scores, tile_query, preferred_element_...  12.5 us
    convert_element_type x2, other arithmetic, tile_backward(): (w.astype(jnp.float32) * (g - row_dot)).astype(jnp.bfloat16)  12 us
  transfers between devices with their start and end apart: 12, of which 6 were waited for; matrix products, arithmetic and copies ran while one was open for 66% of the time, Pallas kernels for 0%

commit v1 on v0

v1 whole, which is shorter than its diff:
```python
import jax
import jax.numpy as jnp
from jax import lax
from jax.sharding import PartitionSpec as P
from jax.experimental import pallas as pl
from jax.experimental.pallas import tpu as pltpu

TILE = 384
TILES_DEV = 2
REACH = 1
HEAD_SIZE = 128


adapter_scale = 0.0078125
masked_score = -1e30


def shifted(shard, axis, by):
    peers = lax.axis_size(axis)
    pairs = [(i, i + by) for i in range(peers) if 0 <= i + by < peers]
    return lax.ppermute(shard, axis, pairs)


def butterfly_sum(tree, axis):
    peers = lax.axis_size(axis)
    if peers & (peers - 1):
        return lax.psum(tree, axis)
    step = 1
    while step < peers:
        pairs = [(i, i ^ step) for i in range(peers)]
        other = lax.ppermute(tree, axis, pairs)
        tree = jax.tree.map(lambda a, b: a + b, tree, other)
        step *= 2
    return tree


def chosen_pairs(listed_key_tiles, listed_tile_count, query_tiles, key_tiles):
    total_tiles = listed_key_tiles.shape[0]
    clipped = jnp.clip(query_tiles, 0, total_tiles - 1)
    one_hot = (clipped[:, None] == jnp.arange(total_tiles, dtype=jnp.int32)[None, :]).astype(
        jnp.int32
    )
    key_lists = jnp.sum(one_hot[:, :, None] * listed_key_tiles[None, :, :], axis=1)
    counts = jnp.sum(one_hot * listed_tile_count[None, :], axis=1)
    slot_ids = jnp.arange(listed_key_tiles.shape[1], dtype=jnp.int32)
    matched = (key_lists == key_tiles[:, None]) & (slot_ids[None, :] < counts[:, None])
    inside = (query_tiles >= 0) & (query_tiles < total_tiles)
    return jnp.any(matched, axis=1) & inside


def nt_dot(a, b):
    return lax.dot_general(a, b, (((1,), (1,)), ((), ())), preferred_element_type=jnp.float32)


def tn_dot(a, b):
    return lax.dot_general(a, b, (((0,), (0,)), ((), ())), preferred_element_type=jnp.float32)


def nn_dot(a, b):
    return lax.dot_general(a, b, (((1,), (0,)), ((), ())), preferred_element_type=jnp.float32)


def tile_pass(bias_ref, first, tile_query, tile_grad, keys, values):
    score_scale = HEAD_SIZE ** (-0.5)
    scores = [
        score_scale * nt_dot(tile_query, k) + bias_ref[first + i] for i, k in enumerate(keys)
    ]
    row_max = jnp.max(scores[0], axis=-1, keepdims=True)
    for s in scores[1:]:
        row_max = jnp.maximum(row_max, jnp.max(s, axis=-1, keepdims=True))
    total = sum(jnp.sum(jnp.exp(s - row_max), axis=-1, keepdims=True) for s in scores)
    log_total = row_max + jnp.log(total)
    weights = [jnp.exp(s - log_total).astype(jnp.bfloat16) for s in scores]
    grad_weights = [nt_dot(tile_grad, v) for v in values]
    row_dot = sum(
        jnp.sum(w.astype(jnp.float32) * g, axis=-1, keepdims=True)
        for w, g in zip(weights, grad_weights)
    )
    grad_scores = [
        (w.astype(jnp.float32) * (g - row_dot)).astype(jnp.bfloat16)
        for w, g in zip(weights, grad_weights)
    ]
    query_term = score_scale * sum(nn_dot(d, k) for d, k in zip(grad_scores, keys))
    key_terms = [score_scale * tn_dot(d, tile_query) for d in grad_scores]
    value_terms = [tn_dot(w, tile_grad) for w in weights]
    return query_term, key_terms, value_terms


def attention_kernel(
    bias_ref, q_ref, g_ref, k_ref, v_ref, kl_ref, vl_ref, kr_ref, vr_ref,
    dq_ref, dk_ref, dv_ref, dkl_ref, dvl_ref, dkr_ref, dvr_ref,
):
    q_a, q_b = q_ref[0, :TILE], q_ref[0, TILE:]
    g_a, g_b = g_ref[0, :TILE], g_ref[0, TILE:]
    k_a, k_b = k_ref[0, :TILE], k_ref[0, TILE:]
    v_a, v_b = v_ref[0, :TILE], v_ref[0, TILE:]
    k_l, v_l, k_r, v_r = kl_ref[0], vl_ref[0], kr_ref[0], vr_ref[0]
    dq_a, dk_a3, dv_a3 = tile_pass(bias_ref, 0, q_a, g_a, (k_l, k_a, k_b), (v_l, v_a, v_b))
    dq_b, dk_b3, dv_b3 = tile_pass(bias_ref, 3, q_b, g_b, (k_a, k_b, k_r), (v_a, v_b, v_r))
    dq_ref[0, :TILE] = dq_a.astype(jnp.bfloat16)
    dq_ref[0, TILE:] = dq_b.astype(jnp.bfloat16)
    dk_ref[0, :TILE] = (dk_a3[1] + dk_b3[0]).astype(jnp.bfloat16)
    dk_ref[0, TILE:] = (dk_a3[2] + dk_b3[1]).astype(jnp.bfloat16)
    dv_ref[0, :TILE] = (dv_a3[1] + dv_b3[0]).astype(jnp.bfloat16)
    dv_ref[0, TILE:] = (dv_a3[2] + dv_b3[1]).astype(jnp.bfloat16)
    dkl_ref[0] = dk_a3[0].astype(jnp.bfloat16)
    dvl_ref[0] = dv_a3[0].astype(jnp.bfloat16)
    dkr_ref[0] = dk_b3[2].astype(jnp.bfloat16)
    dvr_ref[0] = dv_b3[2].astype(jnp.bfloat16)


def attention_backward(bias, queries, output_gradient, key_matrix, values, k_l, v_l, k_r, v_r):
    clip_count, block_len, width = queries.shape
    local_heads = width // HEAD_SIZE
    whole = pl.BlockSpec((1, block_len, HEAD_SIZE), lambda c, h: (c, 0, h))
    rim = pl.BlockSpec((1, TILE, HEAD_SIZE), lambda c, h: (c, 0, h))
    whole_shape = jax.ShapeDtypeStruct(queries.shape, jnp.bfloat16)
    rim_shape = jax.ShapeDtypeStruct((clip_count, TILE, width), jnp.bfloat16)
    return pl.pallas_call(
        attention_kernel,
        grid=(clip_count, local_heads),
        in_specs=[pl.BlockSpec(memory_space=pltpu.MemorySpace.SMEM)]
        + [whole] * 4
        + [rim] * 4,
        out_specs=[whole] * 3 + [rim] * 4,
        out_shape=[whole_shape] * 3 + [rim_shape] * 4,
    )(bias, queries, output_gradient, key_matrix, values, k_l, v_l, k_r, v_r)


def on_device(
    queries,
    key_matrix,
    values,
    output_gradient,
    normed,
    adapter_down_weight,
    adapter_up_weight,
    listed_key_tiles,
    listed_tile_count,
):
    block_len = queries.shape[1]
    position = lax.axis_index("seq")
    first_tile = position * TILES_DEV

    down_piece = jnp.einsum(
        "pqg,gv->pqv", normed, adapter_down_weight, preferred_element_type=jnp.float32
    )
    lowered_rows = butterfly_sum(down_piece, "head").astype(jnp.bfloat16)

    left_kv = shifted(
        jnp.stack((key_matrix[:, block_len - TILE:], values[:, block_len - TILE:]), 0), "seq", 1
    )
    right_kv = shifted(jnp.stack((key_matrix[:, :TILE], values[:, :TILE]), 0), "seq", -1)

    tile_a, tile_b = first_tile, first_tile + 1
    allowed = chosen_pairs(
        listed_key_tiles,
        listed_tile_count,
        jnp.stack([tile_a, tile_a, tile_a, tile_b, tile_b, tile_b]).astype(jnp.int32),
        jnp.stack([tile_a - 1, tile_a, tile_b, tile_a, tile_b, tile_b + 1]).astype(jnp.int32),
    )
    bias = jnp.where(allowed, 0.0, masked_score).astype(jnp.float32)

    query_grad, dk_own, dv_own, dk_l, dv_l, dk_r, dv_r = attention_backward(
        bias, queries, output_gradient, key_matrix, values,
        left_kv[0], left_kv[1], right_kv[0], right_kv[1],
    )
    from_right = shifted(jnp.stack((dk_l, dv_l), 0), "seq", -1)
    from_left = shifted(jnp.stack((dk_r, dv_r), 0), "seq", 1)
    arrived = jnp.concatenate((from_left, from_right), 2).astype(jnp.float32)
    key_grad = (dk_own.astype(jnp.float32) + arrived[0]).astype(jnp.bfloat16)
    value_gradient = (dv_own.astype(jnp.float32) + arrived[1]).astype(jnp.bfloat16)

    backward_piece = jnp.einsum(
        "dsi,ji->dsj", value_gradient, adapter_up_weight, preferred_element_type=jnp.float32
    )
    backward_rows = butterfly_sum(backward_piece, "head").astype(jnp.bfloat16)
    gradient_down_local = adapter_scale * jnp.einsum(
        "yhm,yhz->mz", normed, backward_rows, preferred_element_type=jnp.float32
    )
    gradient_up_local = adapter_scale * jnp.einsum(
        "igb,igu->bu", lowered_rows, value_gradient, preferred_element_type=jnp.float32
    )
    down_projection_grad, up_projection_grad = butterfly_sum(
        butterfly_sum((gradient_down_local, gradient_up_local), "rep"), "seq"
    )
    return (query_grad, key_grad, value_gradient, down_projection_grad, up_projection_grad)


def solution(mesh):
    in_specs = (
        P(("groups", "rep"), "seq", "head"),
        P(("groups", "rep"), "seq", "head"),
        P(("groups", "rep"), "seq", "head"),
        P(("groups", "rep"), "seq", "head"),
        P(("groups", "rep"), "seq", "head"),
        P("head", None),
        P(None, "head"),
        P("groups", None),
        P("groups"),
    )
    out_specs = (
        P(("groups", "rep"), "seq", "head"),
        P(("groups", "rep"), "seq", "head"),
        P(("groups", "rep"), "seq", "head"),
        P(("groups", "head"), None),
        P("groups", "head"),
    )
    return jax.shard_map(
        on_device, mesh=mesh, in_specs=in_specs, out_specs=out_specs, check_vma=False
    )
```

time: 210 us -> 135 us (0.64)
  matrix products: 68.4 us -> 1.64 us
  waiting for transfers between devices: 26.5 us -> 71.9 us
  local copies, waits for them, and re-layouts: 43.7 us -> 4.3 us
  other arithmetic: 38.5 us -> 8.21 us
  Pallas kernels: 0 us -> 24.8 us
  starting transfers between devices: 30.5 us -> 22.5 us
    dot_general x30 -> x0, matrix products: 63.6 us -> none  [the longest x6 18.2 us: tile_backward(): jnp.einsum('cqhd,ckhd->chqk', tile_grad, v, preferred_element_type=jnp.fl...]
    ppermute x4, waiting for transfers between devices: 8.92 us -> 47.5 us  [shifted(): return lax.ppermute(shard, axis, pairs)]
    pallas_call x0 -> x1, Pallas kernels: none -> 24.8 us  [attention_backward(): pl.pallas_call(attention_kernel, grid=(clip_count, local_heads), in_specs...]
    convert_element_type x8 -> x0, local copies, waits for them, and re-layouts: 16.6 us -> none  [the longest x4 10.8 us: finish(): own.reshape(clip_count, TILE, width).astype(jnp.bfloat16)]
    unnamed x107 -> x20, local copies, waits for them, and re-layouts: 14 us -> 0.06 us
    slice x8 -> x0, local copies, waits for them, and re-layouts: 12.2 us -> none  [the longest x2 3.02 us: heads(): x[:, t * TILE:(t + 1) * TILE]]
    convert_element_type x4 -> x2, other arithmetic: 13.6 us -> 1.98 us  [the longest x1 1.62 us: on_device(): (dv_own.astype(jnp.float32) + arrived[1]).astype(jnp.bfloat16)]
    reduce_sum x2 -> x0, other arithmetic: 8.44 us -> none  [tile_backward(): jnp.sum(jnp.exp(s - row_max), axis=-1, keepdims=True)]
  transfers between devices with their start and end apart: 12 -> 12, of which waited for: 6 -> 9; matrix products, arithmetic and copies ran while one was open for 66% -> 6% of each run, Pallas kernels for 0% -> 0%
where the time goes in v1:
time: 135 us; the launch traced here: 134 us
  waiting for transfers between devices  71.9 us (53%)
  Pallas kernels  24.8 us (18%)
  starting transfers between devices  22.5 us (17%)
  other arithmetic  8.21 us (6%)
  local copies, waits for them, and re-layouts  4.3 us (3%)
  matrix products  1.64 us (1%)
    ppermute x4, waiting for transfers between devices, shifted(): return lax.ppermute(shard, axis, pairs)  47.5 us
    pallas_call x1, Pallas kernels, attention_backward(): pl.pallas_call(attention_kernel, grid=(clip_count, local_heads), in_specs...  24.8 us
    ppermute x8, waiting for transfers between devices, butterfly_sum(): other = lax.ppermute(tree, axis, pairs)  24.4 us
    ppermute x4, starting transfers between devices, shifted(): return lax.ppermute(shard, axis, pairs)  12.2 us
    ppermute x8, starting transfers between devices, butterfly_sum(): other = lax.ppermute(tree, axis, pairs)  10.4 us
  transfers between devices with their start and end apart: 12, of which 9 were waited for; matrix products, arithmetic and copies ran while one was open for 6% of the time, Pallas kernels for 0%

profile of v1, /device:TPU:0, one launch (start us, length us, event | category | flops | bytes accessed | tf_op | source)
XLA Modules:
  0.0 134.3 jit_solution(11930675723517010815)
XLA Ops:
  0.6 1.8 %slice_bitcast_fusion.6 = (bf16[1,1,384,768]{3,2,1,0:T(8,128)(2,1)S(1)}, bf16[1,1,384,768]{3,2,1,0:T(8,128)(2,1)S(1)}, bf16[1,1,384,768]{3,2,1,0:T(8,128)(2,1)S(1)}, bf16[1,1,384,768]{3,2,1,0:T(8,128)(2,1)S(1)}) fusion(bf16[1,768,768]{2,1,0:T(8,128)(2,1)} %v_ref.1, bf16[1,768,768]{2,1,0:T(8,128)(2,1)} %k_ref.1), kind=kLoop, calls=%fused_computation.28 | loop fusion | bytes 4718592 | tf_op jit(solution)/shard_map/stack | solution.py:153
  2.5 1.1 pad_maximum_fusion
  3.6 5.0 %collective-permute-start = (bf16[2,1,384,768]{3,2,1,0:T(8,128)(2,1)}, bf16[2,1,384,768]{3,2,1,0:T(8,128)(2,1)S(1)}, u32[]{:S(2)}, u32[]{:S(2)}) collective-permute-start(bf16[2,1,384,768]{3,2,1,0:T(8,128)(2,1)} %pad_maximum_fusion), channel_id=1, source_target_pairs={{0,4},{4,8},{8,12},{1,5},{5,9},{9,13},{2,6},{6,10},{10,14},{3,7},{... | collective-permute-start | bytes 3538952 | tf_op jit(solution)/shard_map/ppermute | solution.py:21
  9.8 1.3 collective-permute-start.1
  12.2 21.9 %collective-permute-done = bf16[2,1,384,768]{3,2,1,0:T(8,128)(2,1)S(1)} collective-permute-done((bf16[2,1,384,768]{3,2,1,0:T(8,128)(2,1)}, bf16[2,1,384,768]{3,2,1,0:T(8,128)(2,1)S(1)}, u32[]{:S(2)}, u32[]{:S(2)}) %collective-permute-start) | collective-permute-done | bytes 1179680 | tf_op jit(solution)/shard_map/ppermute | solution.py:21
  34.1 1.1 slice_bitcast_fusion.4
  35.2 4.1 %collective-permute-done.1 = bf16[2,1,384,768]{3,2,1,0:T(8,128)(2,1)S(1)} collective-permute-done((bf16[2,1,384,768]{3,2,1,0:T(8,128)(2,1)}, bf16[2,1,384,768]{3,2,1,0:T(8,128)(2,1)S(1)}, u32[]{:S(2)}, u32[]{:S(2)}) %collective-permute-start.1) | collective-permute-done | bytes 1179680 | tf_op jit(solution)/shard_map/ppermute | solution.py:21
  40.4 24.8 %shard_map.128 = (bf16[1,768,768]{2,1,0:T(8,128)(2,1)}, bf16[1,768,768]{2,1,0:T(8,128)(2,1)}, bf16[1,768,768]{2,1,0:T(8,128)(2,1)}, bf16[1,384,768]{2,1,0:T(8,12...) custom-call(f32[6]{0:T(128)} %and_select_fusion.bias_ref, ...), custom_call_target="tpu_custom_call" | custom-call | tf_op jit(solution)/shard_map/pallas_call | solution.py:119
  65.2 1.4 %pad_maximum_fusion.3 = bf16[2,1,384,768]{3,2,1,0:T(8,128)(2,1)S(1)} fusion(bf16[1,1,384,768]{3,2,1,0:T(8,128)(2,1)} %bitcast.73, bf16[1,1,384,768]{3,2,1,0:T(8,128)(2,1)} %bitcast.72), kind=kLoop, calls=%fused_computation.10 | loop fusion | flops 589824 | bytes 2359296 | tf_op jit(solution)/shard_map/stack | solution.py:168
  66.6 1.3 collective-permute-start.3
  68.1 4.6 %collective-permute-start.2 = (bf16[2,1,384,768]{3,2,1,0:T(8,128)(2,1)S(1)}, bf16[2,1,384,768]{3,2,1,0:T(8,128)(2,1)S(1)}, u32[]{:S(2)}, u32[]{:S(2)}) collective-permute-start(bf16[2,1,384,768]{3,2,1,0:T(8,128)(2,1)S(1)} %pad_maximum_fusion.2), channel_id=1, source_target_pairs={{0,4},{4,8},{8,12},{1,5},{5,9},{9,13},{2,6},{6,10},{10,14},{3,7},{... | collective-permute-start | bytes 3538952 | tf_op jit(solution)/shard_map/ppermute | solution.py:21
  73.2 1.6 %collective-permute-start.8 = (f32[1,768,64]{1,2,0:T(8,128)S(1)}, f32[1,768,64]{1,2,0:T(8,128)S(1)}, u32[]{:S(2)}, u32[]{:S(2)}) collective-permute-start(f32[1,768,64]{1,2,0:T(8,128)S(1)} %fusion.15), channel_id=1, source_target_pairs={{0,2},{2,0},{1,3},{3,1},{4,6},{6,4},{5,7},{7,5},{8,10},{10,8},{9,1... | collective-permute-start | bytes 589832 | tf_op jit(solution)/shard_map/ppermute | solution.py:31
  74.8 20.2 %collective-permute-done.3 = bf16[2,1,384,768]{3,2,1,0:T(8,128)(2,1)S(1)} collective-permute-done((bf16[2,1,384,768]{3,2,1,0:T(8,128)(2,1)S(1)}, bf16[2,1,384,768]{3,2,1,0:T(8,128)(2,1)S(1)}, u32[]{:S(2)}, u32[]{:S(2)}) %collective-permute-start.3) | collective-permute-done | bytes 1179680 | tf_op jit(solution)/shard_map/ppermute | solution.py:21
  95.1 1.3 collective-permute-done.2
  96.8 1.6 %fusion.1 = (bf16[1,768,768]{2,1,0:T(8,128)(2,1)S(1)}, bf16[1,768,768]{2,1,0:T(8,128)(2,1)}) fusion(f32[2,1,768,768]{3,2,1,0:T(8,128)S(1)} %maximum_convert_fusion, bf16[1,768,768]{2,1,0:T(8,128)(2,1)S(1)} %copy-done.3, bf16[1,768,768]{2,1,0:T(8,128)(2,1)S(1)} %copy-done.2), kind=kLoop, calls=%fused_computation.2 | loop fusion | flops 3538944 | bytes 9437184 | tf_op jit(solution)/shard_map/convert_element_type | solution.py:172
  98.9 1.5 %collective-permute-start.4 = (f32[1,768,64]{1,2,0:T(8,128)S(1)}, f32[1,768,64]{1,2,0:T(8,128)S(1)}, u32[]{:S(2)}, u32[]{:S(2)}) collective-permute-start(f32[1,768,64]{1,2,0:T(8,128)S(1)} %fusion.12), channel_id=1, source_target_pairs={{0,2},{2,0},{1,3},{3,1},{4,6},{6,4},{5,7},{7,5},{8,10},{10,8},{9,1... | collective-permute-start | bytes 589832 | tf_op jit(solution)/shard_map/ppermute | solution.py:31
  100.9 3.8 %collective-permute-done.4 = f32[1,768,64]{1,2,0:T(8,128)S(1)} collective-permute-done((f32[1,768,64]{1,2,0:T(8,128)S(1)}, f32[1,768,64]{1,2,0:T(8,128)S(1)}, u32[]{:S(2)}, u32[]{:S(2)}) %collective-permute-start.4) | collective-permute-done | bytes 196640 | tf_op jit(solution)/shard_map/ppermute | solution.py:31
  105.1 2.5 %collective-permute-start.10 = (f32[64,768]{1,0:T(8,128)S(1)}, f32[64,768]{1,0:T(8,128)S(1)}, u32[]{:S(2)}, u32[]{:S(2)}) collective-permute-start(f32[64,768]{1,0:T(8,128)S(1)} %add.48), channel_id=1, source_target_pairs={{0,4},{4,0},{8,12},{12,8},{1,5},{5,1},{9,13},{13,9},{2,6},{6,2},{1... | collective-permute-start | bytes 589832 | tf_op jit(solution)/shard_map/ppermute | solution.py:31
  107.6 1.4 %collective-permute-start.6 = (f32[768,64]{0,1:T(8,128)S(1)}, f32[768,64]{0,1:T(8,128)S(1)}, u32[]{:S(2)}, u32[]{:S(2)}) collective-permute-start(f32[768,64]{0,1:T(8,128)S(1)} %add.44), channel_id=1, source_target_pairs={{0,4},{4,0},{8,12},{12,8},{1,5},{5,1},{9,13},{13,9},{2,6},{6,2},{1... | collective-permute-start | bytes 589832 | tf_op jit(solution)/shard_map/ppermute | solution.py:31
  109.0 4.3 %collective-permute-done.10 = f32[64,768]{1,0:T(8,128)S(1)} collective-permute-done((f32[64,768]{1,0:T(8,128)S(1)}, f32[64,768]{1,0:T(8,128)S(1)}, u32[]{:S(2)}, u32[]{:S(2)}) %collective-permute-start.10) | collective-permute-done | bytes 196640 | tf_op jit(solution)/shard_map/ppermute | solution.py:31
  113.4 2.9 %collective-permute-start.11 = (f32[64,768]{1,0:T(8,128)S(1)}, f32[64,768]{1,0:T(8,128)S(1)}, u32[]{:S(2)}, u32[]{:S(2)}) collective-permute-start(f32[64,768]{1,0:T(8,128)S(1)} %add.49), channel_id=1, source_target_pairs={{0,8},{4,12},{8,0},{12,4},{1,9},{5,13},{9,1},{13,5},{2,10},{6,14},... | collective-permute-start | bytes 589832 | tf_op jit(solution)/shard_map/ppermute | solution.py:31
  116.3 3.9 %collective-permute-done.6 = f32[768,64]{0,1:T(8,128)S(1)} collective-permute-done((f32[768,64]{0,1:T(8,128)S(1)}, f32[768,64]{0,1:T(8,128)S(1)}, u32[]{:S(2)}, u32[]{:S(2)}) %collective-permute-start.6) | collective-permute-done | bytes 196640 | tf_op jit(solution)/shard_map/ppermute | solution.py:31
  120.5 10.1 %collective-permute-done.11 = f32[64,768]{1,0:T(8,128)S(1)} collective-permute-done((f32[64,768]{1,0:T(8,128)S(1)}, f32[64,768]{1,0:T(8,128)S(1)}, u32[]{:S(2)}, u32[]{:S(2)}) %collective-permute-start.11) | collective-permute-done | bytes 196640 | tf_op jit(solution)/shard_map/ppermute | solution.py:31
  131.3 2.3 %collective-permute-done.7 = f32[768,64]{0,1:T(8,128)S(1)} collective-permute-done((f32[768,64]{0,1:T(8,128)S(1)}, f32[768,64]{0,1:T(8,128)S(1)}, u32[]{:S(2)}, u32[]{:S(2)}) %collective-permute-start.7) | collective-permute-done | bytes 196640 | tf_op jit(solution)/shard_map/ppermute | solution.py:31
  (48 shorter events, 7.4 us)
Async XLA Ops:
  0.6 72.1 %copy-start = (bf16[1,768,768]{2,1,0:T(8,128)(2,1)S(1)}, bf16[1,768,768]{2,1,0:T(8,128)(2,1)}, u32[]{:S(2)}) copy-start(bf16[1,768,768]{2,1,0:T(8,128)(2,1)} %param.13) | copy-start | bytes 3538948
  3.6 30.4 %collective-permute-start = (bf16[2,1,384,768]{3,2,1,0:T(8,128)(2,1)}, bf16[2,1,384,768]{3,2,1,0:T(8,128)(2,1)S(1)}, u32[]{:S(2)}, u32[]{:S(2)}) collective-permute-start(bf16[2,1,384,768]{3,2,1,0:T(8,128)(2,1)} %pad_maximum_fusion), channel_id=1, source_target_pairs={{0,4},{4,8},{8,12},{1,5},{5,9},{9,13},{2,6},{6,10},{10,14},{3,7},{... | collective-permute-start | bytes 3538952 | tf_op jit(solution)/shard_map/ppermute | solution.py:21
  8.6 2.7 %copy-start.8 = (s32[8,3]{0,1:T(4,128)S(1)}, s32[8,3]{0,1:T(4,128)}, u32[]{:S(2)}) copy-start(s32[8,3]{0,1:T(4,128)} %param.16) | copy-start | bytes 292
  8.6 2.8 %copy-start.9 = (s32[8]{0:T(128)S(1)}, s32[8]{0:T(128)}, u32[]{:S(2)}) copy-start(s32[8]{0:T(128)} %param.17) | copy-start | bytes 100
  9.8 29.5 %collective-permute-start.1 = (bf16[2,1,384,768]{3,2,1,0:T(8,128)(2,1)}, bf16[2,1,384,768]{3,2,1,0:T(8,128)(2,1)S(1)}, u32[]{:S(2)}, u32[]{:S(2)}) collective-permute-start(bf16[2,1,384,768]{3,2,1,0:T(8,128)(2,1)} %pad_maximum_fusion.1), channel_id=1, source_target_pairs={{4,0},{8,4},{12,8},{5,1},{9,5},{13,9},{6,2},{10,6},{14,10},{7,3},{... | collective-permute-start | bytes 3538952 | tf_op jit(solution)/shard_map/ppermute | solution.py:21
  65.1 2.8 %copy-start.4 = (bf16[1,384,768]{2,1,0:T(8,128)(2,1)S(1)}, bf16[1,384,768]{2,1,0:T(8,128)(2,1)}, u32[]{:S(2)}) copy-start(bf16[1,384,768]{2,1,0:T(8,128)(2,1)} %get-tuple-element.14) | copy-start | bytes 1769476
  65.2 2.8 %copy-start.5 = (bf16[1,384,768]{2,1,0:T(8,128)(2,1)S(1)}, bf16[1,384,768]{2,1,0:T(8,128)(2,1)}, u32[]{:S(2)}) copy-start(bf16[1,384,768]{2,1,0:T(8,128)(2,1)} %get-tuple-element.15) | copy-start | bytes 1769476
  66.6 28.5 %collective-permute-start.3 = (bf16[2,1,384,768]{3,2,1,0:T(8,128)(2,1)S(1)}, bf16[2,1,384,768]{3,2,1,0:T(8,128)(2,1)S(1)}, u32[]{:S(2)}, u32[]{:S(2)}) collective-permute-start(bf16[2,1,384,768]{3,2,1,0:T(8,128)(2,1)S(1)} %pad_maximum_fusion.3), channel_id=1, source_target_pairs={{4,0},{8,4},{12,8},{5,1},{9,5},{13,9},{6,2},{10,6},{14,10},{7,3},{... | collective-permute-start | bytes 3538952 | tf_op jit(solution)/shard_map/ppermute | solution.py:21
  67.9 4.8 %copy-start.6 = (bf16[768,64]{0,1:T(8,128)(2,1)S(1)}, bf16[768,64]{0,1:T(8,128)(2,1)}, u32[]{:S(2)}) copy-start(bf16[768,64]{0,1:T(8,128)(2,1)} %param.14) | copy-start | bytes 294916
  68.1 28.3 %collective-permute-start.2 = (bf16[2,1,384,768]{3,2,1,0:T(8,128)(2,1)S(1)}, bf16[2,1,384,768]{3,2,1,0:T(8,128)(2,1)S(1)}, u32[]{:S(2)}, u32[]{:S(2)}) collective-permute-start(bf16[2,1,384,768]{3,2,1,0:T(8,128)(2,1)S(1)} %pad_maximum_fusion.2), channel_id=1, source_target_pairs={{0,4},{4,8},{8,12},{1,5},{5,9},{9,13},{2,6},{6,10},{10,14},{3,7},{... | collective-permute-start | bytes 3538952 | tf_op jit(solution)/shard_map/ppermute | solution.py:21
  73.2 23.6 %copy-start.2 = (bf16[1,768,768]{2,1,0:T(8,128)(2,1)S(1)}, bf16[1,768,768]{2,1,0:T(8,128)(2,1)}, u32[]{:S(2)}) copy-start(bf16[1,768,768]{2,1,0:T(8,128)(2,1)} %get-tuple-element.13) | copy-start | bytes 3538948
  73.2 23.6 %copy-start.3 = (bf16[1,768,768]{2,1,0:T(8,128)(2,1)S(1)}, bf16[1,768,768]{2,1,0:T(8,128)(2,1)}, u32[]{:S(2)}) copy-start(bf16[1,768,768]{2,1,0:T(8,128)(2,1)} %get-tuple-element.18) | copy-start | bytes 3538948
  73.2 27.2 %collective-permute-start.8 = (f32[1,768,64]{1,2,0:T(8,128)S(1)}, f32[1,768,64]{1,2,0:T(8,128)S(1)}, u32[]{:S(2)}, u32[]{:S(2)}) collective-permute-start(f32[1,768,64]{1,2,0:T(8,128)S(1)} %fusion.15), channel_id=1, source_target_pairs={{0,2},{2,0},{1,3},{3,1},{4,6},{6,4},{5,7},{7,5},{8,10},{10,8},{9,1... | collective-permute-start | bytes 589832 | tf_op jit(solution)/shard_map/ppermute | solution.py:31
  96.8 1.6 %copy-start.7 = (bf16[64,768]{1,0:T(8,128)(2,1)S(1)}, bf16[64,768]{1,0:T(8,128)(2,1)}, u32[]{:S(2)}) copy-start(bf16[64,768]{1,0:T(8,128)(2,1)} %param.15) | copy-start | bytes 294916
  98.4 2.3 %copy-start.1 = (bf16[1,768,768]{2,1,0:T(8,128)(2,1)}, bf16[1,768,768]{2,1,0:T(8,128)(2,1)S(1)}, u32[]{:S(2)}) copy-start(bf16[1,768,768]{2,1,0:T(8,128)(2,1)S(1)} %get-tuple-element.19) | copy-start | bytes 3538948
  98.9 5.7 %collective-permute-start.4 = (f32[1,768,64]{1,2,0:T(8,128)S(1)}, f32[1,768,64]{1,2,0:T(8,128)S(1)}, u32[]{:S(2)}, u32[]{:S(2)}) collective-permute-start(f32[1,768,64]{1,2,0:T(8,128)S(1)} %fusion.12), channel_id=1, source_target_pairs={{0,2},{2,0},{1,3},{3,1},{4,6},{6,4},{5,7},{7,5},{8,10},{10,8},{9,1... | collective-permute-start | bytes 589832 | tf_op jit(solution)/shard_map/ppermute | solution.py:31
  100.8 4.2 %collective-permute-start.9 = (f32[64,768]{1,0:T(8,128)S(1)}, f32[64,768]{1,0:T(8,128)S(1)}, u32[]{:S(2)}, u32[]{:S(2)}) collective-permute-start(f32[64,768]{1,0:T(8,128)S(1)} %fusion.18), channel_id=1, source_target_pairs={{0,1},{1,0},{2,3},{3,2},{4,5},{5,4},{6,7},{7,6},{8,9},{9,8},{10,11... | collective-permute-start | bytes 589832 | tf_op jit(solution)/shard_map/ppermute | solution.py:31
  105.0 2.7 %collective-permute-start.5 = (f32[768,64]{0,1:T(8,128)S(1)}, f32[768,64]{0,1:T(8,128)S(1)}, u32[]{:S(2)}, u32[]{:S(2)}) collective-permute-start(f32[768,64]{0,1:T(8,128)S(1)} %fusion.24), channel_id=1, source_target_pairs={{0,1},{1,0},{2,3},{3,2},{4,5},{5,4},{6,7},{7,6},{8,9},{9,8},{10,11... | collective-permute-start | bytes 589832 | tf_op jit(solution)/shard_map/ppermute | solution.py:31
  105.1 8.3 %collective-permute-start.10 = (f32[64,768]{1,0:T(8,128)S(1)}, f32[64,768]{1,0:T(8,128)S(1)}, u32[]{:S(2)}, u32[]{:S(2)}) collective-permute-start(f32[64,768]{1,0:T(8,128)S(1)} %add.48), channel_id=1, source_target_pairs={{0,4},{4,0},{8,12},{12,8},{1,5},{5,1},{9,13},{13,9},{2,6},{6,2},{1... | collective-permute-start | bytes 589832 | tf_op jit(solution)/shard_map/ppermute | solution.py:31
  107.6 12.6 %collective-permute-start.6 = (f32[768,64]{0,1:T(8,128)S(1)}, f32[768,64]{0,1:T(8,128)S(1)}, u32[]{:S(2)}, u32[]{:S(2)}) collective-permute-start(f32[768,64]{0,1:T(8,128)S(1)} %add.44), channel_id=1, source_target_pairs={{0,4},{4,0},{8,12},{12,8},{1,5},{5,1},{9,13},{13,9},{2,6},{6,2},{1... | collective-permute-start | bytes 589832 | tf_op jit(solution)/shard_map/ppermute | solution.py:31
  113.4 17.2 %collective-permute-start.11 = (f32[64,768]{1,0:T(8,128)S(1)}, f32[64,768]{1,0:T(8,128)S(1)}, u32[]{:S(2)}, u32[]{:S(2)}) collective-permute-start(f32[64,768]{1,0:T(8,128)S(1)} %add.49), channel_id=1, source_target_pairs={{0,8},{4,12},{8,0},{12,4},{1,9},{5,13},{9,1},{13,5},{2,10},{6,14},... | collective-permute-start | bytes 589832 | tf_op jit(solution)/shard_map/ppermute | solution.py:31
  120.3 13.3 %collective-permute-start.7 = (f32[768,64]{0,1:T(8,128)S(1)}, f32[768,64]{0,1:T(8,128)S(1)}, u32[]{:S(2)}, u32[]{:S(2)}) collective-permute-start(f32[768,64]{0,1:T(8,128)S(1)} %add.45), channel_id=1, source_target_pairs={{0,8},{4,12},{8,0},{12,4},{1,9},{5,13},{9,1},{13,5},{2,10},{6,14},... | collective-permute-start | bytes 589832 | tf_op jit(solution)/shard_map/ppermute | solution.py:31

commit v2 on v1

--- a/solution.py
+++ b/solution.py
@@ -94,7 +94,7 @@
     g_a, g_b = g_ref[0, :TILE], g_ref[0, TILE:]
     k_a, k_b = k_ref[0, :TILE], k_ref[0, TILE:]
     v_a, v_b = v_ref[0, :TILE], v_ref[0, TILE:]
-    k_l, v_l, k_r, v_r = kl_ref[0], vl_ref[0], kr_ref[0], vr_ref[0]
+    k_l, v_l, k_r, v_r = kl_ref[0, 0], vl_ref[0, 0], kr_ref[0, 0], vr_ref[0, 0]
     dq_a, dk_a3, dv_a3 = tile_pass(bias_ref, 0, q_a, g_a, (k_l, k_a, k_b), (v_l, v_a, v_b))
     dq_b, dk_b3, dv_b3 = tile_pass(bias_ref, 3, q_b, g_b, (k_a, k_b, k_r), (v_a, v_b, v_r))
     dq_ref[0, :TILE] = dq_a.astype(jnp.bfloat16)
@@ -109,22 +109,21 @@
     dvr_ref[0] = dv_b3[2].astype(jnp.bfloat16)
 
 
-def attention_backward(bias, queries, output_gradient, key_matrix, values, k_l, v_l, k_r, v_r):
-    clip_count, block_len, width = queries.shape
-    local_heads = width // HEAD_SIZE
-    whole = pl.BlockSpec((1, block_len, HEAD_SIZE), lambda c, h: (c, 0, h))
-    rim = pl.BlockSpec((1, TILE, HEAD_SIZE), lambda c, h: (c, 0, h))
-    whole_shape = jax.ShapeDtypeStruct(queries.shape, jnp.bfloat16)
-    rim_shape = jax.ShapeDtypeStruct((clip_count, TILE, width), jnp.bfloat16)
+def attention_backward(bias, chunk, heads, queries, output_gradient, key_matrix, values, halo):
+    clip_count, block_len, _ = queries.shape
+    whole = pl.BlockSpec((1, block_len, HEAD_SIZE), lambda c, h: (c, 0, h + chunk * heads))
+    rims = [pl.BlockSpec((1, 1, TILE, HEAD_SIZE), lambda c, h, i=i: (i, c, 0, h)) for i in range(4)]
+    out_whole = pl.BlockSpec((1, block_len, HEAD_SIZE), lambda c, h: (c, 0, h))
+    out_rim = pl.BlockSpec((1, TILE, HEAD_SIZE), lambda c, h: (c, 0, h))
+    whole_shape = jax.ShapeDtypeStruct((clip_count, block_len, heads * HEAD_SIZE), jnp.bfloat16)
+    rim_shape = jax.ShapeDtypeStruct((clip_count, TILE, heads * HEAD_SIZE), jnp.bfloat16)
     return pl.pallas_call(
         attention_kernel,
-        grid=(clip_count, local_heads),
-        in_specs=[pl.BlockSpec(memory_space=pltpu.MemorySpace.SMEM)]
-        + [whole] * 4
-        + [rim] * 4,
-        out_specs=[whole] * 3 + [rim] * 4,
+        grid=(clip_count, heads),
+        in_specs=[pl.BlockSpec(memory_space=pltpu.MemorySpace.SMEM)] + [whole] * 4 + rims,
+        out_specs=[out_whole] * 3 + [out_rim] * 4,
         out_shape=[whole_shape] * 3 + [rim_shape] * 4,
-    )(bias, queries, output_gradient, key_matrix, values, k_l, v_l, k_r, v_r)
+    )(bias, queries, output_gradient, key_matrix, values, halo, halo, halo, halo)
 
 
 def on_device(
@@ -147,11 +146,6 @@
     )
     lowered_rows = butterfly_sum(down_piece, "head").astype(jnp.bfloat16)
 
-    left_kv = shifted(
-        jnp.stack((key_matrix[:, block_len - TILE:], values[:, block_len - TILE:]), 0), "seq", 1
-    )
-    right_kv = shifted(jnp.stack((key_matrix[:, :TILE], values[:, :TILE]), 0), "seq", -1)
-
     tile_a, tile_b = first_tile, first_tile + 1
     allowed = chosen_pairs(
         listed_key_tiles,
@@ -161,15 +155,33 @@
     )
     bias = jnp.where(allowed, 0.0, masked_score).astype(jnp.float32)
 
-    query_grad, dk_own, dv_own, dk_l, dv_l, dk_r, dv_r = attention_backward(
-        bias, queries, output_gradient, key_matrix, values,
-        left_kv[0], left_kv[1], right_kv[0], right_kv[1],
-    )
-    from_right = shifted(jnp.stack((dk_l, dv_l), 0), "seq", -1)
-    from_left = shifted(jnp.stack((dk_r, dv_r), 0), "seq", 1)
-    arrived = jnp.concatenate((from_left, from_right), 2).astype(jnp.float32)
-    key_grad = (dk_own.astype(jnp.float32) + arrived[0]).astype(jnp.bfloat16)
-    value_gradient = (dv_own.astype(jnp.float32) + arrived[1]).astype(jnp.bfloat16)
+    local_heads = queries.shape[2] // HEAD_SIZE
+    chunks = 3 if local_heads % 3 == 0 else (2 if local_heads % 2 == 0 else 1)
+    per_chunk = local_heads // chunks
+    outs = []
+    for chunk in range(chunks):
+        cols = slice(chunk * per_chunk * HEAD_SIZE, (chunk + 1) * per_chunk * HEAD_SIZE)
+        left_kv = shifted(
+            jnp.stack((key_matrix[:, block_len - TILE:, cols], values[:, block_len - TILE:, cols])),
+            "seq",
+            1,
+        )
+        right_kv = shifted(
+            jnp.stack((key_matrix[:, :TILE, cols], values[:, :TILE, cols]), 0), "seq", -1
+        )
+        halo = jnp.concatenate((left_kv, right_kv), 0)
+        dq, dk_own, dv_own, dk_l, dv_l, dk_r, dv_r = attention_backward(
+            bias, chunk, per_chunk, queries, output_gradient, key_matrix, values, halo
+        )
+        from_right = shifted(jnp.stack((dk_l, dv_l), 0), "seq", -1)
+        from_left = shifted(jnp.stack((dk_r, dv_r), 0), "seq", 1)
+        arrived = jnp.concatenate((from_left, from_right), 2).astype(jnp.float32)
+        dk = (dk_own.astype(jnp.float32) + arrived[0]).astype(jnp.bfloat16)
+        dv = (dv_own.astype(jnp.float32) + arrived[1]).astype(jnp.bfloat16)
+        outs.append((dq, dk, dv))
+    query_grad, key_grad, value_gradient = (
+        jnp.concatenate([o[i] for o in outs], 2) for i in range(3)
+    )
 
     backward_piece = jnp.einsum(
         "dsi,ji->dsj", value_gradient, adapter_up_weight, preferred_element_type=jnp.float32
@@ -181,9 +193,9 @@
     gradient_up_local = adapter_scale * jnp.einsum(
         "igb,igu->bu", lowered_rows, value_gradient, preferred_element_type=jnp.float32
     )
-    down_projection_grad, up_projection_grad = butterfly_sum(
-        butterfly_sum((gradient_down_local, gradient_up_local), "rep"), "seq"
-    )
+    both = jnp.stack((gradient_down_local, gradient_up_local.T), 0)
+    both = butterfly_sum(butterfly_sum(both, "rep"), "seq")
+    down_projection_grad, up_projection_grad = both[0], both[1].T
     return (query_grad, key_grad, value_gradient, down_projection_grad, up_projection_grad)
 
 

time: 135 us -> 141 us (1.044)
  waiting for transfers between devices: 71.9 us -> 39.3 us
  starting transfers between devices: 22.5 us -> 42.8 us
  other arithmetic: 8.21 us -> 21.6 us
  Pallas kernels: 24.8 us -> 29 us
    ppermute x4 -> x12, waiting for transfers between devices: 47.5 us -> 6.66 us  [shifted(): return lax.ppermute(shard, axis, pairs)]
    ppermute x4 -> x12, starting transfers between devices: 12.2 us -> 38.1 us  [shifted(): return lax.ppermute(shard, axis, pairs)]
    concatenate x0 -> x6, other arithmetic: none -> 8.33 us  [the longest x3 6.07 us: on_device(): halo = jnp.concatenate((left_kv, right_kv), 0)]
    ppermute x8 -> x5, waiting for transfers between devices: 24.4 us -> 32.6 us  [butterfly_sum(): other = lax.ppermute(tree, axis, pairs)]
    ppermute x8 -> x5, starting transfers between devices: 10.4 us -> 4.73 us  [butterfly_sum(): other = lax.ppermute(tree, axis, pairs)]
    another operation x1 -> x3, other arithmetic: 0.11 us -> 4.68 us  [on_device(): from_left = shifted(jnp.stack((dk_r, dv_r), 0), 'seq', 1)]
    pallas_call x1 -> x3, Pallas kernels: 24.8 us -> 29 us  [attention_backward(): pl.pallas_call(attention_kernel, grid=(clip_count, heads), in_specs=[pl.B...]
    another operation x1 -> x3, other arithmetic: 1.45 us -> 4.66 us  [on_device(): from_right = shifted(jnp.stack((dk_l, dv_l), 0), 'seq', -1)]
  transfers between devices with their start and end apart: 12 -> 17, of which waited for: 9 -> 6; matrix products, arithmetic and copies ran while one was open for 6% -> 16% of each run, Pallas kernels for 0% -> 21%
where the time goes in v2:
time: 141 us; the launch traced here: 140 us
  starting transfers between devices  42.8 us (30%)
  waiting for transfers between devices  39.3 us (28%)
  Pallas kernels  29 us (21%)
  other arithmetic  21.6 us (15%)
  local copies, waits for them, and re-layouts  4.73 us (3%)
  matrix products  1.65 us (1%)
    ppermute x12, starting transfers between devices, shifted(): return lax.ppermute(shard, axis, pairs)  38.1 us
    ppermute x5, waiting for transfers between devices, butterfly_sum(): other = lax.ppermute(tree, axis, pairs)  32.6 us
    pallas_call x3, Pallas kernels, attention_backward(): pl.pallas_call(attention_kernel, grid=(clip_count, heads), in_specs=[pl.B...  29 us
    ppermute x12, waiting for transfers between devices, shifted(): return lax.ppermute(shard, axis, pairs)  6.66 us
    concatenate x3, other arithmetic, on_device(): halo = jnp.concatenate((left_kv, right_kv), 0)  6.07 us
    ppermute x5, starting transfers between devices, butterfly_sum(): other = lax.ppermute(tree, axis, pairs)  4.73 us
    another operation x3, other arithmetic, on_device(): from_left = shifted(jnp.stack((dk_r, dv_r), 0), 'seq', 1)  4.68 us
    another operation x3, other arithmetic, on_device(): from_right = shifted(jnp.stack((dk_l, dv_l), 0), 'seq', -1)  4.66 us
  transfers between devices with their start and end apart: 17, of which 6 were waited for; matrix products, arithmetic and copies ran while one was open for 16% of the time, Pallas kernels for 21%

profile of v2, /device:TPU:0, one launch (start us, length us, event | category | flops | bytes accessed | tf_op | source)
XLA Modules:
  0.0 140.1 jit_solution(16079159643190006070)
XLA Ops:
  0.6 2.0 %slice_bitcast_fusion.18 = (bf16[1,1,384,256]{3,2,1,0:T(8,128)(2,1)S(1)}, bf16[1,1,384,256]{3,2,1,0:T(8,128)(2,1)S(1)}, bf16[1,1,384,256]{3,2,1,0:T(8,128)(2,1)S...) fusion(bf16[1,768,768]{2,1,0:T(8,128)(2,1)} %v_ref.5, ...), kind=kLoop, calls=%fused_computation.68 | loop fusion | bytes 4718592 | tf_op jit(solution)/shard_map/stack | solution.py:165
  3.4 5.7 %collective-permute-start = (bf16[2,1,384,256]{3,2,1,0:T(8,128)(2,1)}, bf16[2,1,384,256]{3,2,1,0:T(8,128)(2,1)}, u32[]{:S(2)}, u32[]{:S(2)}) collective-permute-start(bf16[2,1,384,256]{3,2,1,0:T(8,128)(2,1)} %pad_maximum_fusion.6), channel_id=1, source_target_pairs={{0,4},{4,8},{8,12},{1,5},{5,9},{9,13},{2,6},{6,10},{10,14},{3,7},{... | collective-permute-start | bytes 1179656 | tf_op jit(solution)/shard_map/ppermute | solution.py:21
  11.2 5.3 %collective-permute-start.2 = (bf16[2,1,384,256]{3,2,1,0:T(8,128)(2,1)S(1)}, bf16[2,1,384,256]{3,2,1,0:T(8,128)(2,1)}, u32[]{:S(2)}, u32[]{:S(2)}) collective-permute-start(bf16[2,1,384,256]{3,2,1,0:T(8,128)(2,1)S(1)} %pad_maximum_fusion.8), channel_id=1, source_target_pairs={{0,4},{4,8},{8,12},{1,5},{5,9},{9,13},{2,6},{6,10},{10,14},{3,7},{... | collective-permute-start | bytes 1179656 | tf_op jit(solution)/shard_map/ppermute | solution.py:21
  17.9 5.3 %collective-permute-start.4 = (bf16[2,1,384,256]{3,2,1,0:T(8,128)(2,1)S(1)}, bf16[2,1,384,256]{3,2,1,0:T(8,128)(2,1)}, u32[]{:S(2)}, u32[]{:S(2)}) collective-permute-start(bf16[2,1,384,256]{3,2,1,0:T(8,128)(2,1)S(1)} %pad_maximum_fusion.10), channel_id=1, source_target_pairs={{0,4},{4,8},{8,12},{1,5},{5,9},{9,13},{2,6},{6,10},{10,14},{3,7},{... | collective-permute-start | bytes 1179656 | tf_op jit(solution)/shard_map/ppermute | solution.py:21
  27.8 2.1 %pad_maximum_fusion.3.kl_ref.vl_ref.kr_ref.vr_ref = bf16[4,1,384,256]{3,2,1,0:T(8,128)(2,1)} fusion(bf16[2,1,384,256]{3,2,1,0:T(8,128)(2,1)} %collective-permute-done.1, bf16[2,1,384,256]{3,2,1,0:T(8,128)(2,1)} %collective-permute-done), kind=kLoop, calls=%fused_computation.35 | loop fusion | flops 393216 | bytes 1572864 | tf_op jit(solution)/shard_map/concatenate | solution.py:172
  29.9 9.6 %shard_map.128 = (bf16[1,768,256]{2,1,0:T(8,128)(2,1)}, bf16[1,768,256]{2,1,0:T(8,128)(2,1)}, bf16[1,768,256]{2,1,0:T(8,128)(2,1)}, bf16[1,384,256]{2,1,0:T(8,12...) custom-call(f32[6]{0:T(128)} %and_select_fusion.bias_ref, ...), custom_call_target="tpu_custom_call" | custom-call | tf_op jit(solution)/shard_map/pallas_call | solution.py:120
  39.5 1.8 %pad_maximum_fusion.12 = bf16[2,1,384,256]{3,2,1,0:T(8,128)(2,1)} fusion(bf16[1,1,384,256]{3,2,1,0:T(8,128)(2,1)} %bitcast.131, bf16[1,1,384,256]{3,2,1,0:T(8,128)(2,1)} %bitcast.130), kind=kLoop, calls=%fused_computation.47 | loop fusion | flops 196608 | bytes 786432 | tf_op jit(solution)/shard_map/stack | solution.py:177
  41.3 1.8 %pad_maximum_fusion.13 = bf16[2,1,384,256]{3,2,1,0:T(8,128)(2,1)} fusion(bf16[1,1,384,256]{3,2,1,0:T(8,128)(2,1)} %bitcast.125, bf16[1,1,384,256]{3,2,1,0:T(8,128)(2,1)} %bitcast.124), kind=kLoop, calls=%fused_computation.48 | loop fusion | flops 196608 | bytes 786432 | tf_op jit(solution)/shard_map/stack | solution.py:176
  43.2 4.6 %collective-permute-start.6 = (bf16[2,1,384,256]{3,2,1,0:T(8,128)(2,1)}, bf16[2,1,384,256]{3,2,1,0:T(8,128)(2,1)S(1)}, u32[]{:S(2)}, u32[]{:S(2)}) collective-permute-start(bf16[2,1,384,256]{3,2,1,0:T(8,128)(2,1)} %pad_maximum_fusion.12), channel_id=1, source_target_pairs={{0,4},{4,8},{8,12},{1,5},{5,9},{9,13},{2,6},{6,10},{10,14},{3,7},{... | collective-permute-start | bytes 1179656 | tf_op jit(solution)/shard_map/ppermute | solution.py:21
  49.1 2.1 %pad_maximum_fusion.4.kl_ref.vl_ref.kr_ref.vr_ref = bf16[4,1,384,256]{3,2,1,0:T(8,128)(2,1)} fusion(bf16[2,1,384,256]{3,2,1,0:T(8,128)(2,1)} %collective-permute-done.3, bf16[2,1,384,256]{3,2,1,0:T(8,128)(2,1)} %collective-permute-done.2), kind=kLoop, calls=%fused_computation.36 | loop fusion | flops 393216 | bytes 1572864 | tf_op jit(solution)/shard_map/concatenate | solution.py:172
  51.1 9.7 %shard_map.129 = (bf16[1,768,256]{2,1,0:T(8,128)(2,1)}, bf16[1,768,256]{2,1,0:T(8,128)(2,1)}, bf16[1,768,256]{2,1,0:T(8,128)(2,1)}, bf16[1,384,256]{2,1,0:T(8,12...) custom-call(f32[6]{0:T(128)} %and_select_fusion.bias_ref, ...), custom_call_target="tpu_custom_call" | custom-call | tf_op jit(solution)/shard_map/pallas_call | solution.py:120
  60.8 1.8 %pad_maximum_fusion.14 = bf16[2,1,384,256]{3,2,1,0:T(8,128)(2,1)} fusion(bf16[1,1,384,256]{3,2,1,0:T(8,128)(2,1)} %bitcast.133, bf16[1,1,384,256]{3,2,1,0:T(8,128)(2,1)} %bitcast.132), kind=kLoop, calls=%fused_computation.49 | loop fusion | flops 196608 | bytes 786432 | tf_op jit(solution)/shard_map/stack | solution.py:177
  62.6 1.8 %pad_maximum_fusion.15 = bf16[2,1,384,256]{3,2,1,0:T(8,128)(2,1)} fusion(bf16[1,1,384,256]{3,2,1,0:T(8,128)(2,1)} %bitcast.127, bf16[1,1,384,256]{3,2,1,0:T(8,128)(2,1)} %bitcast.126), kind=kLoop, calls=%fused_computation.50 | loop fusion | flops 196608 | bytes 786432 | tf_op jit(solution)/shard_map/stack | solution.py:176
  64.4 4.6 %collective-permute-start.8 = (bf16[2,1,384,256]{3,2,1,0:T(8,128)(2,1)}, bf16[2,1,384,256]{3,2,1,0:T(8,128)(2,1)S(1)}, u32[]{:S(2)}, u32[]{:S(2)}) collective-permute-start(bf16[2,1,384,256]{3,2,1,0:T(8,128)(2,1)} %pad_maximum_fusion.14), channel_id=1, source_target_pairs={{0,4},{4,8},{8,12},{1,5},{5,9},{9,13},{2,6},{6,10},{10,14},{3,7},{... | collective-permute-start | bytes 1179656 | tf_op jit(solution)/shard_map/ppermute | solution.py:21
  70.5 1.9 %pad_maximum_fusion.5.kl_ref.vl_ref.kr_ref.vr_ref = bf16[4,1,384,256]{3,2,1,0:T(8,128)(2,1)} fusion(bf16[2,1,384,256]{3,2,1,0:T(8,128)(2,1)S(1)} %collective-permute-done.5, bf16[2,1,384,256]{3,2,1,0:T(8,128)(2,1)} %collective-permute-done.4), kind=kLoop, calls=%fused_computation.37 | loop fusion | flops 393216 | bytes 1572864 | tf_op jit(solution)/shard_map/concatenate | solution.py:172
  72.4 9.7 %shard_map.130 = (bf16[1,768,256]{2,1,0:T(8,128)(2,1)}, bf16[1,768,256]{2,1,0:T(8,128)(2,1)}, bf16[1,768,256]{2,1,0:T(8,128)(2,1)}, bf16[1,384,256]{2,1,0:T(8,12...) custom-call(f32[6]{0:T(128)} %and_select_fusion.bias_ref, ...), custom_call_target="tpu_custom_call" | custom-call | tf_op jit(solution)/shard_map/pallas_call | solution.py:120
  84.3 4.7 %collective-permute-start.10 = (bf16[2,1,384,256]{3,2,1,0:T(8,128)(2,1)S(1)}, bf16[2,1,384,256]{3,2,1,0:T(8,128)(2,1)S(1)}, u32[]{:S(2)}, u32[]{:S(2)}) collective-permute-start(bf16[2,1,384,256]{3,2,1,0:T(8,128)(2,1)S(1)} %pad_maximum_fusion.16), channel_id=1, source_target_pairs={{0,4},{4,8},{8,12},{1,5},{5,9},{9,13},{2,6},{6,10},{10,14},{3,7},{... | collective-permute-start | bytes 1179656 | tf_op jit(solution)/shard_map/ppermute | solution.py:21
  92.0 2.2 %collective-permute-done.10 = bf16[2,1,384,256]{3,2,1,0:T(8,128)(2,1)S(1)} collective-permute-done((bf16[2,1,384,256]{3,2,1,0:T(8,128)(2,1)S(1)}, bf16[2,1,384,256]{3,2,1,0:T(8,128)(2,1)S(1)}, u32[]{:S(2)}, u32[]{:S(2)}) %collective-permute-start.10) | collective-permute-done | bytes 393248 | tf_op jit(solution)/shard_map/ppermute | solution.py:21
  94.3 4.4 %collective-permute-done.11 = bf16[2,1,384,256]{3,2,1,0:T(8,128)(2,1)S(1)} collective-permute-done((bf16[2,1,384,256]{3,2,1,0:T(8,128)(2,1)S(1)}, bf16[2,1,384,256]{3,2,1,0:T(8,128)(2,1)S(1)}, u32[]{:S(2)}, u32[]{:S(2)}) %collective-permute-start.11) | collective-permute-done | bytes 393248 | tf_op jit(solution)/shard_map/ppermute | solution.py:21
  101.3 4.8 %collective-permute-done.12 = f32[1,768,64]{1,2,0:T(8,128)S(1)} collective-permute-done((f32[1,768,64]{1,2,0:T(8,128)S(1)}, f32[1,768,64]{1,2,0:T(8,128)S(1)}, u32[]{:S(2)}, u32[]{:S(2)}) %collective-permute-start.12) | collective-permute-done | bytes 196640 | tf_op jit(solution)/shard_map/ppermute | solution.py:31
  106.6 1.7 %collective-permute-done.14 = f32[2,768,64]{1,2,0:T(8,128)S(1)} collective-permute-done((f32[2,768,64]{1,2,0:T(8,128)S(1)}, f32[2,768,64]{1,2,0:T(8,128)S(1)}, u32[]{:S(2)}, u32[]{:S(2)}) %collective-permute-start.14) | collective-permute-done | bytes 393248 | tf_op jit(solution)/shard_map/ppermute | solution.py:31
  108.9 10.7 %collective-permute-done.15 = f32[2,768,64]{1,2,0:T(8,128)S(1)} collective-permute-done((f32[2,768,64]{1,2,0:T(8,128)S(1)}, f32[2,768,64]{1,2,0:T(8,128)S(1)}, u32[]{:S(2)}, u32[]{:S(2)}) %collective-permute-start.15) | collective-permute-done | bytes 393248 | tf_op jit(solution)/shard_map/ppermute | solution.py:31
  119.7 2.0 %collective-permute-start.16 = (f32[2,768,64]{1,2,0:T(8,128)S(1)}, f32[2,768,64]{1,2,0:T(8,128)S(1)}, u32[]{:S(2)}, u32[]{:S(2)}) collective-permute-start(f32[2,768,64]{1,2,0:T(8,128)S(1)} %fusion.48), channel_id=1, source_target_pairs={{0,8},{4,12},{8,0},{12,4},{1,9},{5,13},{9,1},{13,5},{2,10},{6,14},... | collective-permute-start | bytes 1179656 | tf_op jit(solution)/shard_map/ppermute | solution.py:31
  123.9 15.4 %collective-permute-done.16 = f32[2,768,64]{1,2,0:T(8,128)S(1)} collective-permute-done((f32[2,768,64]{1,2,0:T(8,128)S(1)}, f32[2,768,64]{1,2,0:T(8,128)S(1)}, u32[]{:S(2)}, u32[]{:S(2)}) %collective-permute-start.16) | collective-permute-done | bytes 393248 | tf_op jit(solution)/shard_map/ppermute | solution.py:31
  (85 shorter events, 23.4 us)
Async XLA Ops:
  0.6 23.2 %copy-start = (bf16[1,768,768]{2,1,0:T(8,128)(2,1)S(1)}, bf16[1,768,768]{2,1,0:T(8,128)(2,1)}, u32[]{:S(2)}) copy-start(bf16[1,768,768]{2,1,0:T(8,128)(2,1)} %param.13) | copy-start | bytes 3538948
  3.4 21.6 %collective-permute-start = (bf16[2,1,384,256]{3,2,1,0:T(8,128)(2,1)}, bf16[2,1,384,256]{3,2,1,0:T(8,128)(2,1)}, u32[]{:S(2)}, u32[]{:S(2)}) collective-permute-start(bf16[2,1,384,256]{3,2,1,0:T(8,128)(2,1)} %pad_maximum_fusion.6), channel_id=1, source_target_pairs={{0,4},{4,8},{8,12},{1,5},{5,9},{9,13},{2,6},{6,10},{10,14},{3,7},{... | collective-permute-start | bytes 1179656 | tf_op jit(solution)/shard_map/ppermute | solution.py:21
  9.9 16.4 %collective-permute-start.1 = (bf16[2,1,384,256]{3,2,1,0:T(8,128)(2,1)}, bf16[2,1,384,256]{3,2,1,0:T(8,128)(2,1)}, u32[]{:S(2)}, u32[]{:S(2)}) collective-permute-start(bf16[2,1,384,256]{3,2,1,0:T(8,128)(2,1)} %pad_maximum_fusion.7), channel_id=1, source_target_pairs={{4,0},{8,4},{12,8},{5,1},{9,5},{13,9},{6,2},{10,6},{14,10},{7,3},{... | collective-permute-start | bytes 1179656 | tf_op jit(solution)/shard_map/ppermute | solution.py:21
  11.2 12.3 %copy-start.14 = (s32[8]{0:T(128)S(1)}, s32[8]{0:T(128)}, u32[]{:S(2)}) copy-start(s32[8]{0:T(128)} %param.17) | copy-start | bytes 100
  11.2 12.5 %copy-start.13 = (s32[8,3]{0,1:T(4,128)S(1)}, s32[8,3]{0,1:T(4,128)}, u32[]{:S(2)}) copy-start(s32[8,3]{0,1:T(4,128)} %param.16) | copy-start | bytes 292
  11.2 12.7 %copy-start.11 = (bf16[768,64]{0,1:T(8,128)(2,1)S(1)}, bf16[768,64]{0,1:T(8,128)(2,1)}, u32[]{:S(2)}) copy-start(bf16[768,64]{0,1:T(8,128)(2,1)} %param.14) | copy-start | bytes 294916
  11.2 31.9 %collective-permute-start.2 = (bf16[2,1,384,256]{3,2,1,0:T(8,128)(2,1)S(1)}, bf16[2,1,384,256]{3,2,1,0:T(8,128)(2,1)}, u32[]{:S(2)}, u32[]{:S(2)}) collective-permute-start(bf16[2,1,384,256]{3,2,1,0:T(8,128)(2,1)S(1)} %pad_maximum_fusion.8), channel_id=1, source_target_pairs={{0,4},{4,8},{8,12},{1,5},{5,9},{9,13},{2,6},{6,10},{10,14},{3,7},{... | collective-permute-start | bytes 1179656 | tf_op jit(solution)/shard_map/ppermute | solution.py:21
  16.6 31.2 %collective-permute-start.3 = (bf16[2,1,384,256]{3,2,1,0:T(8,128)(2,1)S(1)}, bf16[2,1,384,256]{3,2,1,0:T(8,128)(2,1)}, u32[]{:S(2)}, u32[]{:S(2)}) collective-permute-start(bf16[2,1,384,256]{3,2,1,0:T(8,128)(2,1)S(1)} %pad_maximum_fusion.9), channel_id=1, source_target_pairs={{4,0},{8,4},{12,8},{5,1},{9,5},{13,9},{6,2},{10,6},{14,10},{7,3},{... | collective-permute-start | bytes 1179656 | tf_op jit(solution)/shard_map/ppermute | solution.py:21
  17.9 46.5 %collective-permute-start.4 = (bf16[2,1,384,256]{3,2,1,0:T(8,128)(2,1)S(1)}, bf16[2,1,384,256]{3,2,1,0:T(8,128)(2,1)}, u32[]{:S(2)}, u32[]{:S(2)}) collective-permute-start(bf16[2,1,384,256]{3,2,1,0:T(8,128)(2,1)S(1)} %pad_maximum_fusion.10), channel_id=1, source_target_pairs={{0,4},{4,8},{8,12},{1,5},{5,9},{9,13},{2,6},{6,10},{10,14},{3,7},{... | collective-permute-start | bytes 1179656 | tf_op jit(solution)/shard_map/ppermute | solution.py:21
  25.0 44.0 %collective-permute-start.5 = (bf16[2,1,384,256]{3,2,1,0:T(8,128)(2,1)S(1)}, bf16[2,1,384,256]{3,2,1,0:T(8,128)(2,1)S(1)}, u32[]{:S(2)}, u32[]{:S(2)}) collective-permute-start(bf16[2,1,384,256]{3,2,1,0:T(8,128)(2,1)S(1)} %pad_maximum_fusion.11), channel_id=1, source_target_pairs={{4,0},{8,4},{12,8},{5,1},{9,5},{13,9},{6,2},{10,6},{14,10},{7,3},{... | collective-permute-start | bytes 1179656 | tf_op jit(solution)/shard_map/ppermute | solution.py:21
  26.3 74.7 %collective-permute-start.13 = (f32[1,768,64]{1,2,0:T(8,128)S(1)}, f32[1,768,64]{1,2,0:T(8,128)S(1)}, u32[]{:S(2)}, u32[]{:S(2)}) collective-permute-start(f32[1,768,64]{1,2,0:T(8,128)S(1)} %fusion.11), channel_id=1, source_target_pairs={{0,2},{2,0},{1,3},{3,1},{4,6},{6,4},{5,7},{7,5},{8,10},{10,8},{9,1... | collective-permute-start | bytes 589832 | tf_op jit(solution)/shard_map/ppermute | solution.py:31
  43.2 41.1 %collective-permute-start.6 = (bf16[2,1,384,256]{3,2,1,0:T(8,128)(2,1)}, bf16[2,1,384,256]{3,2,1,0:T(8,128)(2,1)S(1)}, u32[]{:S(2)}, u32[]{:S(2)}) collective-permute-start(bf16[2,1,384,256]{3,2,1,0:T(8,128)(2,1)} %pad_maximum_fusion.12), channel_id=1, source_target_pairs={{0,4},{4,8},{8,12},{1,5},{5,9},{9,13},{2,6},{6,10},{10,14},{3,7},{... | collective-permute-start | bytes 1179656 | tf_op jit(solution)/shard_map/ppermute | solution.py:21
  47.8 41.3 %collective-permute-start.7 = (bf16[2,1,384,256]{3,2,1,0:T(8,128)(2,1)}, bf16[2,1,384,256]{3,2,1,0:T(8,128)(2,1)S(1)}, u32[]{:S(2)}, u32[]{:S(2)}) collective-permute-start(bf16[2,1,384,256]{3,2,1,0:T(8,128)(2,1)} %pad_maximum_fusion.13), channel_id=1, source_target_pairs={{4,0},{8,4},{12,8},{5,1},{9,5},{13,9},{6,2},{10,6},{14,10},{7,3},{... | collective-permute-start | bytes 1179656 | tf_op jit(solution)/shard_map/ppermute | solution.py:21
  64.4 26.3 %collective-permute-start.8 = (bf16[2,1,384,256]{3,2,1,0:T(8,128)(2,1)}, bf16[2,1,384,256]{3,2,1,0:T(8,128)(2,1)S(1)}, u32[]{:S(2)}, u32[]{:S(2)}) collective-permute-start(bf16[2,1,384,256]{3,2,1,0:T(8,128)(2,1)} %pad_maximum_fusion.14), channel_id=1, source_target_pairs={{0,4},{4,8},{8,12},{1,5},{5,9},{9,13},{2,6},{6,10},{10,14},{3,7},{... | collective-permute-start | bytes 1179656 | tf_op jit(solution)/shard_map/ppermute | solution.py:21
  69.0 21.7 %collective-permute-start.9 = (bf16[2,1,384,256]{3,2,1,0:T(8,128)(2,1)}, bf16[2,1,384,256]{3,2,1,0:T(8,128)(2,1)S(1)}, u32[]{:S(2)}, u32[]{:S(2)}) collective-permute-start(bf16[2,1,384,256]{3,2,1,0:T(8,128)(2,1)} %pad_maximum_fusion.15), channel_id=1, source_target_pairs={{4,0},{8,4},{12,8},{5,1},{9,5},{13,9},{6,2},{10,6},{14,10},{7,3},{... | collective-permute-start | bytes 1179656 | tf_op jit(solution)/shard_map/ppermute | solution.py:21
  84.3 10.0 %collective-permute-start.10 = (bf16[2,1,384,256]{3,2,1,0:T(8,128)(2,1)S(1)}, bf16[2,1,384,256]{3,2,1,0:T(8,128)(2,1)S(1)}, u32[]{:S(2)}, u32[]{:S(2)}) collective-permute-start(bf16[2,1,384,256]{3,2,1,0:T(8,128)(2,1)S(1)} %pad_maximum_fusion.16), channel_id=1, source_target_pairs={{0,4},{4,8},{8,12},{1,5},{5,9},{9,13},{2,6},{6,10},{10,14},{3,7},{... | collective-permute-start | bytes 1179656 | tf_op jit(solution)/shard_map/ppermute | solution.py:21
  89.0 9.7 %collective-permute-start.11 = (bf16[2,1,384,256]{3,2,1,0:T(8,128)(2,1)S(1)}, bf16[2,1,384,256]{3,2,1,0:T(8,128)(2,1)S(1)}, u32[]{:S(2)}, u32[]{:S(2)}) collective-permute-start(bf16[2,1,384,256]{3,2,1,0:T(8,128)(2,1)S(1)} %pad_maximum_fusion.17), channel_id=1, source_target_pairs={{4,0},{8,4},{12,8},{5,1},{9,5},{13,9},{6,2},{10,6},{14,10},{7,3},{... | collective-permute-start | bytes 1179656 | tf_op jit(solution)/shard_map/ppermute | solution.py:21
  100.4 5.7 %collective-permute-start.12 = (f32[1,768,64]{1,2,0:T(8,128)S(1)}, f32[1,768,64]{1,2,0:T(8,128)S(1)}, u32[]{:S(2)}, u32[]{:S(2)}) collective-permute-start(f32[1,768,64]{1,2,0:T(8,128)S(1)} %fusion.8), channel_id=1, source_target_pairs={{0,2},{2,0},{1,3},{3,1},{4,6},{6,4},{5,7},{7,5},{8,10},{10,8},{9,1... | collective-permute-start | bytes 589832 | tf_op jit(solution)/shard_map/ppermute | solution.py:31
  106.5 15.2 %copy-start.2 = (bf16[1,768,256]{2,1,0:T(8,128)(2,1)S(1)}, bf16[1,768,256]{2,1,0:T(8,128)(2,1)}, u32[]{:S(2)}) copy-start(bf16[1,768,256]{2,1,0:T(8,128)(2,1)} %get-tuple-element.26) | copy-start | bytes 1179652
  106.5 15.2 %copy-start.3 = (bf16[1,768,256]{2,1,0:T(8,128)(2,1)S(1)}, bf16[1,768,256]{2,1,0:T(8,128)(2,1)}, u32[]{:S(2)}) copy-start(bf16[1,768,256]{2,1,0:T(8,128)(2,1)} %get-tuple-element.27) | copy-start | bytes 1179652
  106.5 15.2 %copy-start.4 = (bf16[1,768,256]{2,1,0:T(8,128)(2,1)S(1)}, bf16[1,768,256]{2,1,0:T(8,128)(2,1)}, u32[]{:S(2)}) copy-start(bf16[1,768,256]{2,1,0:T(8,128)(2,1)} %get-tuple-element.28) | copy-start | bytes 1179652
  106.5 1.8 %collective-permute-start.14 = (f32[2,768,64]{1,2,0:T(8,128)S(1)}, f32[2,768,64]{1,2,0:T(8,128)S(1)}, u32[]{:S(2)}, u32[]{:S(2)}) collective-permute-start(f32[2,768,64]{1,2,0:T(8,128)S(1)} %pad_maximum_fusion.18), channel_id=1, source_target_pairs={{0,1},{1,0},{2,3},{3,2},{4,5},{5,4},{6,7},{7,6},{8,9},{9,8},{10,11... | collective-permute-start | bytes 1179656 | tf_op jit(solution)/shard_map/ppermute | solution.py:31
  108.4 11.2 %collective-permute-start.15 = (f32[2,768,64]{1,2,0:T(8,128)S(1)}, f32[2,768,64]{1,2,0:T(8,128)S(1)}, u32[]{:S(2)}, u32[]{:S(2)}) collective-permute-start(f32[2,768,64]{1,2,0:T(8,128)S(1)} %fusion.45), channel_id=1, source_target_pairs={{0,4},{4,0},{8,12},{12,8},{1,5},{5,1},{9,13},{13,9},{2,6},{6,2},{1... | collective-permute-start | bytes 1179656 | tf_op jit(solution)/shard_map/ppermute | solution.py:31
  119.7 19.6 %collective-permute-start.16 = (f32[2,768,64]{1,2,0:T(8,128)S(1)}, f32[2,768,64]{1,2,0:T(8,128)S(1)}, u32[]{:S(2)}, u32[]{:S(2)}) collective-permute-start(f32[2,768,64]{1,2,0:T(8,128)S(1)} %fusion.48), channel_id=1, source_target_pairs={{0,8},{4,12},{8,0},{12,4},{1,9},{5,13},{9,1},{13,5},{2,10},{6,14},... | collective-permute-start | bytes 1179656 | tf_op jit(solution)/shard_map/ppermute | solution.py:31
  (8 other events, 30.3 us)

commit v3 on v2

--- a/solution.py
+++ b/solution.py
@@ -32,6 +32,48 @@
         tree = jax.tree.map(lambda a, b: a + b, tree, other)
         step *= 2
     return tree
+
+
+def scatter_sum(flat, axis, distances):
+    peers = lax.axis_size(axis)
+    index = lax.axis_index(axis)
+    for step in distances:
+        half = flat.shape[0] // 2
+        upper = (index & step) != 0
+        keep = jnp.where(upper, flat[half:], flat[:half])
+        send = jnp.where(upper, flat[:half], flat[half:])
+        flat = keep + lax.ppermute(send, axis, [(i, i ^ step) for i in range(peers)])
+    return flat
+
+
+def gather_back(flat, axis, distances):
+    peers = lax.axis_size(axis)
+    index = lax.axis_index(axis)
+    for step in reversed(distances):
+        other = lax.ppermute(flat, axis, [(i, i ^ step) for i in range(peers)])
+        upper = (index & step) != 0
+        flat = jnp.where(upper, jnp.concatenate((other, flat)), jnp.concatenate((flat, other)))
+    return flat
+
+
+def all_sum(array, axes):
+    plan = []
+    for axis in axes:
+        peers = lax.axis_size(axis)
+        if peers & (peers - 1):
+            return lax.psum(array, axes)
+        plan.append((axis, [1 << k for k in range(peers.bit_length() - 1)]))
+    pieces = 1
+    for _, distances in plan:
+        pieces *= 1 << len(distances)
+    flat = array.reshape(-1)
+    if flat.shape[0] % pieces:
+        return lax.psum(array, axes)
+    for axis, distances in plan:
+        flat = scatter_sum(flat, axis, distances)
+    for axis, distances in reversed(plan):
+        flat = gather_back(flat, axis, distances)
+    return flat.reshape(array.shape)
 
 
 def chosen_pairs(listed_key_tiles, listed_tile_count, query_tiles, key_tiles):
@@ -156,7 +198,7 @@
     bias = jnp.where(allowed, 0.0, masked_score).astype(jnp.float32)
 
     local_heads = queries.shape[2] // HEAD_SIZE
-    chunks = 3 if local_heads % 3 == 0 else (2 if local_heads % 2 == 0 else 1)
+    chunks = 1
     per_chunk = local_heads // chunks
     outs = []
     for chunk in range(chunks):
@@ -194,7 +236,7 @@
         "igb,igu->bu", lowered_rows, value_gradient, preferred_element_type=jnp.float32
     )
     both = jnp.stack((gradient_down_local, gradient_up_local.T), 0)
-    both = butterfly_sum(butterfly_sum(both, "rep"), "seq")
+    both = all_sum(both, ("rep", "seq"))
     down_projection_grad, up_projection_grad = both[0], both[1].T
     return (query_grad, key_grad, value_gradient, down_projection_grad, up_projection_grad)
 

time: 141 us -> 133 us (0.943)
  waiting for transfers between devices: 39.3 us -> 60.7 us
  starting transfers between devices: 42.8 us -> 27.4 us
  other arithmetic: 21.6 us -> 10.3 us
  Pallas kernels: 29 us -> 24.8 us
  matrix products: 1.65 us -> 3.36 us
    ppermute x12 -> x4, waiting for transfers between devices: 6.66 us -> 44.8 us  [shifted(): return lax.ppermute(shard, axis, pairs)]
    ppermute x5 -> x2, waiting for transfers between devices: 32.6 us -> 2.98 us  [butterfly_sum(): other = lax.ppermute(tree, axis, pairs)]
    ppermute x12 -> x4, starting transfers between devices: 38.1 us -> 14.4 us  [shifted(): return lax.ppermute(shard, axis, pairs)]
    ppermute x0 -> x6, waiting for transfers between devices: none -> 13 us  [the longest x3 6.61 us: scatter_sum(): lax.ppermute(send, axis, [(i, i ^ step) for i in range(peers)])]
    ppermute x0 -> x6, starting transfers between devices: none -> 10 us  [the longest x3 5.48 us: scatter_sum(): lax.ppermute(send, axis, [(i, i ^ step) for i in range(peers)])]
    pallas_call x3 -> x1, Pallas kernels: 29 us -> 24.8 us  [attention_backward(): pl.pallas_call(attention_kernel, grid=(clip_count, heads), in_specs=[pl.B...]
    another operation x3 -> x1, other arithmetic: 4.68 us -> 1.12 us  [on_device(): from_left = shifted(jnp.stack((dk_r, dv_r), 0), 'seq', 1)]
    concatenate x3 -> x1, other arithmetic: 6.07 us -> 3.26 us  [on_device(): halo = jnp.concatenate((left_kv, right_kv), 0)]
  transfers between devices with their start and end apart: 17 -> 12, of which waited for: 6 -> 11; matrix products, arithmetic and copies ran while one was open for 16% -> 6% of each run, Pallas kernels for 21% -> 0%
where the time goes in v3:
time: 133 us; the launch traced here: 132 us
  waiting for transfers between devices  60.7 us (46%)
  starting transfers between devices  27.4 us (21%)
  Pallas kernels  24.8 us (19%)
  other arithmetic  10.3 us (8%)
  local copies, waits for them, and re-layouts  4.7 us (4%)
  matrix products  3.36 us (3%)
    ppermute x4, waiting for transfers between devices, shifted(): return lax.ppermute(shard, axis, pairs)  44.8 us
    pallas_call x1, Pallas kernels, attention_backward(): pl.pallas_call(attention_kernel, grid=(clip_count, heads), in_specs=[pl.B...  24.8 us
    ppermute x4, starting transfers between devices, shifted(): return lax.ppermute(shard, axis, pairs)  14.4 us
    ppermute x3, waiting for transfers between devices, scatter_sum(): lax.ppermute(send, axis, [(i, i ^ step) for i in range(peers)])  6.61 us
    ppermute x3, waiting for transfers between devices, gather_back(): other = lax.ppermute(flat, axis, [(i, i ^ step) for i in range(peers)])  6.4 us
    ppermute x3, starting transfers between devices, scatter_sum(): lax.ppermute(send, axis, [(i, i ^ step) for i in range(peers)])  5.48 us
    ppermute x3, starting transfers between devices, gather_back(): other = lax.ppermute(flat, axis, [(i, i ^ step) for i in range(peers)])  4.51 us
    concatenate x1, other arithmetic, on_device(): halo = jnp.concatenate((left_kv, right_kv), 0)  3.26 us
  transfers between devices with their start and end apart: 12, of which 11 were waited for; matrix products, arithmetic and copies ran while one was open for 6% of the time, Pallas kernels for 0%

profile of v3, /device:TPU:0, one launch (start us, length us, event | category | flops | bytes accessed | tf_op | source)
XLA Modules:
  0.0 132.2 jit_solution(265819731275310879)
XLA Ops:
  0.6 1.8 %slice_bitcast_fusion.4 = (bf16[1,1,384,768]{3,2,1,0:T(8,128)(2,1)S(1)}, bf16[1,1,384,768]{3,2,1,0:T(8,128)(2,1)S(1)}, bf16[1,1,384,768]{3,2,1,0:T(8,128)(2,1)S(1)}, bf16[1,1,384,768]{3,2,1,0:T(8,128)(2,1)S(1)}) fusion(bf16[1,768,768]{2,1,0:T(8,128)(2,1)} %v_ref.1, bf16[1,768,768]{2,1,0:T(8,128)(2,1)} %k_ref.1), kind=kLoop, calls=%fused_computation.28 | loop fusion | bytes 4718592 | tf_op jit(solution)/shard_map/stack | solution.py:207
  2.6 1.3 collective-permute-start.1
  4.1 6.6 %collective-permute-start = (bf16[2,1,384,768]{3,2,1,0:T(8,128)(2,1)S(1)}, bf16[2,1,384,768]{3,2,1,0:T(8,128)(2,1)}, u32[]{:S(2)}, u32[]{:S(2)}) collective-permute-start(bf16[2,1,384,768]{3,2,1,0:T(8,128)(2,1)S(1)} %pad_maximum_fusion.1), channel_id=1, source_target_pairs={{0,4},{4,8},{8,12},{1,5},{5,9},{9,13},{2,6},{6,10},{10,14},{3,7},{... | collective-permute-start | bytes 3538952 | tf_op jit(solution)/shard_map/ppermute | solution.py:21
  11.8 21.8 %collective-permute-done.1 = bf16[2,1,384,768]{3,2,1,0:T(8,128)(2,1)} collective-permute-done((bf16[2,1,384,768]{3,2,1,0:T(8,128)(2,1)S(1)}, bf16[2,1,384,768]{3,2,1,0:T(8,128)(2,1)}, u32[]{:S(2)}, u32[]{:S(2)}) %collective-permute-start.1) | collective-permute-done | bytes 1179680 | tf_op jit(solution)/shard_map/ppermute | solution.py:21
  34.8 3.3 %pad_maximum_fusion.kl_ref.vl_ref.kr_ref.vr_ref = bf16[4,1,384,768]{3,2,1,0:T(8,128)(2,1)} fusion(bf16[2,1,384,768]{3,2,1,0:T(8,128)(2,1)} %collective-permute-done.1, bf16[2,1,384,768]{3,2,1,0:T(8,128)(2,1)} %collective-permute-done), kind=kLoop, calls=%fused_computation.6 | loop fusion | flops 1179648 | bytes 4718592 | tf_op jit(solution)/shard_map/concatenate | solution.py:214
  38.1 24.8 %shard_map.128 = (bf16[1,768,768]{2,1,0:T(8,128)(2,1)}, bf16[1,768,768]{2,1,0:T(8,128)(2,1)}, bf16[1,768,768]{2,1,0:T(8,128)(2,1)}, bf16[1,384,768]{2,1,0:T(8,12...) custom-call(f32[6]{0:T(128)} %and_select_fusion.bias_ref, ...), custom_call_target="tpu_custom_call" | custom-call | tf_op jit(solution)/shard_map/pallas_call | solution.py:162
  62.9 2.5 %pad_maximum_fusion.4 = bf16[2,1,384,768]{3,2,1,0:T(8,128)(2,1)} fusion(bf16[1,1,384,768]{3,2,1,0:T(8,128)(2,1)} %bitcast.71, bf16[1,1,384,768]{3,2,1,0:T(8,128)(2,1)} %bitcast.70), kind=kLoop, calls=%fused_computation.11 | loop fusion | flops 589824 | bytes 2359296 | tf_op jit(solution)/shard_map/stack | solution.py:218
  65.4 1.3 collective-permute-start.3
  67.9 5.2 %collective-permute-start.2 = (bf16[2,1,384,768]{3,2,1,0:T(8,128)(2,1)}, bf16[2,1,384,768]{3,2,1,0:T(8,128)(2,1)S(1)}, u32[]{:S(2)}, u32[]{:S(2)}) collective-permute-start(bf16[2,1,384,768]{3,2,1,0:T(8,128)(2,1)} %pad_maximum_fusion.3), channel_id=1, source_target_pairs={{0,4},{4,8},{8,12},{1,5},{5,9},{9,13},{2,6},{6,10},{10,14},{3,7},{... | collective-permute-start | bytes 3538952 | tf_op jit(solution)/shard_map/ppermute | solution.py:21
  74.3 1.6 %collective-permute-start.4 = (f32[1,768,64]{1,2,0:T(8,128)}, f32[1,768,64]{1,2,0:T(8,128)}, u32[]{:S(2)}, u32[]{:S(2)}) collective-permute-start(f32[1,768,64]{1,2,0:T(8,128)} %fusion.15), channel_id=1, source_target_pairs={{0,2},{2,0},{1,3},{3,1},{4,6},{6,4},{5,7},{7,5},{8,10},{10,8},{9,1... | collective-permute-start | bytes 589832 | tf_op jit(solution)/shard_map/ppermute | solution.py:31
  75.9 19.3 %collective-permute-done.3 = bf16[2,1,384,768]{3,2,1,0:T(8,128)(2,1)S(1)} collective-permute-done((bf16[2,1,384,768]{3,2,1,0:T(8,128)(2,1)}, bf16[2,1,384,768]{3,2,1,0:T(8,128)(2,1)S(1)}, u32[]{:S(2)}, u32[]{:S(2)}) %collective-permute-start.3) | collective-permute-done | bytes 1179680 | tf_op jit(solution)/shard_map/ppermute | solution.py:21
  95.2 2.4 %collective-permute-done.2 = bf16[2,1,384,768]{3,2,1,0:T(8,128)(2,1)S(1)} collective-permute-done((bf16[2,1,384,768]{3,2,1,0:T(8,128)(2,1)}, bf16[2,1,384,768]{3,2,1,0:T(8,128)(2,1)S(1)}, u32[]{:S(2)}, u32[]{:S(2)}) %collective-permute-start.2) | collective-permute-done | bytes 1179680 | tf_op jit(solution)/shard_map/ppermute | solution.py:21
  98.1 1.6 %fusion.1 = (bf16[1,768,768]{2,1,0:T(8,128)(2,1)S(1)}, bf16[1,768,768]{2,1,0:T(8,128)(2,1)}) fusion(f32[2,1,768,768]{3,2,1,0:T(8,128)S(1)} %maximum_convert_fusion, bf16[1,768,768]{2,1,0:T(8,128)(2,1)S(1)} %copy-done.3, bf16[1,768,768]{2,1,0:T(8,128)(2,1)S(1)} %copy-done.2), kind=kLoop, calls=%fused_computation.2 | loop fusion | flops 3538944 | bytes 9437184 | tf_op jit(solution)/shard_map/convert_element_type | solution.py:222
  100.2 1.4 %collective-permute-start.5 = (f32[1,768,64]{1,2,0:T(8,128)S(1)}, f32[1,768,64]{1,2,0:T(8,128)S(1)}, u32[]{:S(2)}, u32[]{:S(2)}) collective-permute-start(f32[1,768,64]{1,2,0:T(8,128)S(1)} %fusion.12), channel_id=1, source_target_pairs={{0,2},{2,0},{1,3},{3,1},{4,6},{6,4},{5,7},{7,5},{8,10},{10,8},{9,1... | collective-permute-start | bytes 589832 | tf_op jit(solution)/shard_map/ppermute | solution.py:31
  101.5 1.4 %fusion.18 = f32[768,64]{0,1:T(8,128)S(1)} fusion(bf16[1,768,768]{2,1,0:T(8,128)(2,1)S(1)} %get-tuple-element.29, f32[1,768,64]{1,2,0:T(8,128)} %fusion.15, f32[1,768,64]{1,2,0:T(8,128)} %collective-permute-done.4), kind=kOutput, calls=%fused_computation.22 | convolution fusion | flops 75644928 | bytes 1769472 | tf_op jit(solution)/shard_map/igb,igu->bu/dot_general | solution.py:235
  102.9 3.0 %collective-permute-done.5 = f32[1,768,64]{1,2,0:T(8,128)S(1)} collective-permute-done((f32[1,768,64]{1,2,0:T(8,128)S(1)}, f32[1,768,64]{1,2,0:T(8,128)S(1)}, u32[]{:S(2)}, u32[]{:S(2)}) %collective-permute-start.5) | collective-permute-done | bytes 196640 | tf_op jit(solution)/shard_map/ppermute | solution.py:31
  108.1 2.4 %collective-permute-start.7 = (f32[24576]{0:T(1024)S(1)}, f32[24576]{0:T(1024)S(1)}, u32[]{:S(2)}, u32[]{:S(2)}) collective-permute-start(f32[24576]{0:T(1024)S(1)} %slice_select_fusion), channel_id=1, source_target_pairs={{0,4},{4,0},{8,12},{12,8},{1,5},{5,1},{9,13},{13,9},{2,6},{6,2},{1... | collective-permute-start | bytes 294920 | tf_op jit(solution)/shard_map/ppermute | solution.py:45
  110.5 3.1 %collective-permute-done.7 = f32[24576]{0:T(1024)S(1)} collective-permute-done((f32[24576]{0:T(1024)S(1)}, f32[24576]{0:T(1024)S(1)}, u32[]{:S(2)}, u32[]{:S(2)}) %collective-permute-start.7) | collective-permute-done | bytes 98336 | tf_op jit(solution)/shard_map/ppermute | solution.py:45
  113.6 3.0 %collective-permute-start.8 = (f32[12288]{0:T(1024)S(1)}, f32[12288]{0:T(1024)S(1)}, u32[]{:S(2)}, u32[]{:S(2)}) collective-permute-start(f32[12288]{0:T(1024)S(1)} %slice_select_fusion.1), channel_id=1, source_target_pairs={{0,8},{4,12},{8,0},{12,4},{1,9},{5,13},{9,1},{13,5},{2,10},{6,14},... | collective-permute-start | bytes 147464 | tf_op jit(solution)/shard_map/ppermute | solution.py:45
  116.6 2.4 %collective-permute-done.8 = f32[12288]{0:T(1024)S(1)} collective-permute-done((f32[12288]{0:T(1024)S(1)}, f32[12288]{0:T(1024)S(1)}, u32[]{:S(2)}, u32[]{:S(2)}) %collective-permute-start.8) | collective-permute-done | bytes 49184 | tf_op jit(solution)/shard_map/ppermute | solution.py:45
  119.0 2.7 %collective-permute-start.9 = (f32[12288]{0:T(1024)S(1)}, f32[12288]{0:T(1024)S(1)}, u32[]{:S(2)}, u32[]{:S(2)}) collective-permute-start(f32[12288]{0:T(1024)S(1)} %select_add_fusion.1), channel_id=1, source_target_pairs={{0,8},{4,12},{8,0},{12,4},{1,9},{5,13},{9,1},{13,5},{2,10},{6,14},... | collective-permute-start | bytes 147464 | tf_op jit(solution)/shard_map/ppermute | solution.py:53
  121.7 2.4 %collective-permute-done.9 = f32[12288]{0:T(1024)S(1)} collective-permute-done((f32[12288]{0:T(1024)S(1)}, f32[12288]{0:T(1024)S(1)}, u32[]{:S(2)}, u32[]{:S(2)}) %collective-permute-start.9) | collective-permute-done | bytes 49184 | tf_op jit(solution)/shard_map/ppermute | solution.py:53
  124.1 1.7 %collective-permute-start.10 = (f32[24576]{0:T(1024)S(1)}, f32[24576]{0:T(1024)S(1)}, u32[]{:S(2)}, u32[]{:S(2)}) collective-permute-start(f32[24576]{0:T(1024)S(1)} %maximum_select_fusion.4), channel_id=1, source_target_pairs={{0,4},{4,0},{8,12},{12,8},{1,5},{5,1},{9,13},{13,9},{2,6},{6,2},{1... | collective-permute-start | bytes 294920 | tf_op jit(solution)/shard_map/ppermute | solution.py:53
  126.0 2.8 %collective-permute-done.10 = f32[24576]{0:T(1024)S(1)} collective-permute-done((f32[24576]{0:T(1024)S(1)}, f32[24576]{0:T(1024)S(1)}, u32[]{:S(2)}, u32[]{:S(2)}) %collective-permute-start.10) | collective-permute-done | bytes 98336 | tf_op jit(solution)/shard_map/ppermute | solution.py:53
  (62 shorter events, 11.5 us)
Async XLA Ops:
  0.6 72.5 %copy-start = (bf16[1,768,768]{2,1,0:T(8,128)(2,1)S(1)}, bf16[1,768,768]{2,1,0:T(8,128)(2,1)}, u32[]{:S(2)}) copy-start(bf16[1,768,768]{2,1,0:T(8,128)(2,1)} %param.13) | copy-start | bytes 3538948
  2.6 31.0 %collective-permute-start.1 = (bf16[2,1,384,768]{3,2,1,0:T(8,128)(2,1)S(1)}, bf16[2,1,384,768]{3,2,1,0:T(8,128)(2,1)}, u32[]{:S(2)}, u32[]{:S(2)}) collective-permute-start(bf16[2,1,384,768]{3,2,1,0:T(8,128)(2,1)S(1)} %pad_maximum_fusion.2), channel_id=1, source_target_pairs={{4,0},{8,4},{12,8},{5,1},{9,5},{13,9},{6,2},{10,6},{14,10},{7,3},{... | collective-permute-start | bytes 3538952 | tf_op jit(solution)/shard_map/ppermute | solution.py:21
  3.9 7.0 %copy-start.8 = (s32[8,3]{0,1:T(4,128)S(1)}, s32[8,3]{0,1:T(4,128)}, u32[]{:S(2)}) copy-start(s32[8,3]{0,1:T(4,128)} %param.16) | copy-start | bytes 292
  3.9 7.1 %copy-start.9 = (s32[8]{0:T(128)S(1)}, s32[8]{0:T(128)}, u32[]{:S(2)}) copy-start(s32[8]{0:T(128)} %param.17) | copy-start | bytes 100
  4.1 30.8 %collective-permute-start = (bf16[2,1,384,768]{3,2,1,0:T(8,128)(2,1)S(1)}, bf16[2,1,384,768]{3,2,1,0:T(8,128)(2,1)}, u32[]{:S(2)}, u32[]{:S(2)}) collective-permute-start(bf16[2,1,384,768]{3,2,1,0:T(8,128)(2,1)S(1)} %pad_maximum_fusion.1), channel_id=1, source_target_pairs={{0,4},{4,8},{8,12},{1,5},{5,9},{9,13},{2,6},{6,10},{10,14},{3,7},{... | collective-permute-start | bytes 3538952 | tf_op jit(solution)/shard_map/ppermute | solution.py:21
  62.9 3.8 %copy-start.4 = (bf16[1,384,768]{2,1,0:T(8,128)(2,1)S(1)}, bf16[1,384,768]{2,1,0:T(8,128)(2,1)}, u32[]{:S(2)}) copy-start(bf16[1,384,768]{2,1,0:T(8,128)(2,1)} %get-tuple-element.14) | copy-start | bytes 1769476
  62.9 3.8 %copy-start.5 = (bf16[1,384,768]{2,1,0:T(8,128)(2,1)S(1)}, bf16[1,384,768]{2,1,0:T(8,128)(2,1)}, u32[]{:S(2)}) copy-start(bf16[1,384,768]{2,1,0:T(8,128)(2,1)} %get-tuple-element.15) | copy-start | bytes 1769476
  65.4 29.8 %collective-permute-start.3 = (bf16[2,1,384,768]{3,2,1,0:T(8,128)(2,1)}, bf16[2,1,384,768]{3,2,1,0:T(8,128)(2,1)S(1)}, u32[]{:S(2)}, u32[]{:S(2)}) collective-permute-start(bf16[2,1,384,768]{3,2,1,0:T(8,128)(2,1)} %pad_maximum_fusion.4), channel_id=1, source_target_pairs={{4,0},{8,4},{12,8},{5,1},{9,5},{13,9},{6,2},{10,6},{14,10},{7,3},{... | collective-permute-start | bytes 3538952 | tf_op jit(solution)/shard_map/ppermute | solution.py:21
  66.7 6.3 %copy-start.6 = (bf16[768,64]{0,1:T(8,128)(2,1)S(1)}, bf16[768,64]{0,1:T(8,128)(2,1)}, u32[]{:S(2)}) copy-start(bf16[768,64]{0,1:T(8,128)(2,1)} %param.14) | copy-start | bytes 294916
  67.9 29.8 %collective-permute-start.2 = (bf16[2,1,384,768]{3,2,1,0:T(8,128)(2,1)}, bf16[2,1,384,768]{3,2,1,0:T(8,128)(2,1)S(1)}, u32[]{:S(2)}, u32[]{:S(2)}) collective-permute-start(bf16[2,1,384,768]{3,2,1,0:T(8,128)(2,1)} %pad_maximum_fusion.3), channel_id=1, source_target_pairs={{0,4},{4,8},{8,12},{1,5},{5,9},{9,13},{2,6},{6,10},{10,14},{3,7},{... | collective-permute-start | bytes 3538952 | tf_op jit(solution)/shard_map/ppermute | solution.py:21
  74.3 27.2 %collective-permute-start.4 = (f32[1,768,64]{1,2,0:T(8,128)}, f32[1,768,64]{1,2,0:T(8,128)}, u32[]{:S(2)}, u32[]{:S(2)}) collective-permute-start(f32[1,768,64]{1,2,0:T(8,128)} %fusion.15), channel_id=1, source_target_pairs={{0,2},{2,0},{1,3},{3,1},{4,6},{6,4},{5,7},{7,5},{8,10},{10,8},{9,1... | collective-permute-start | bytes 589832 | tf_op jit(solution)/shard_map/ppermute | solution.py:31
  75.9 22.1 %copy-start.2 = (bf16[1,768,768]{2,1,0:T(8,128)(2,1)S(1)}, bf16[1,768,768]{2,1,0:T(8,128)(2,1)}, u32[]{:S(2)}) copy-start(bf16[1,768,768]{2,1,0:T(8,128)(2,1)} %get-tuple-element.13) | copy-start | bytes 3538948
  75.9 22.1 %copy-start.3 = (bf16[1,768,768]{2,1,0:T(8,128)(2,1)S(1)}, bf16[1,768,768]{2,1,0:T(8,128)(2,1)}, u32[]{:S(2)}) copy-start(bf16[1,768,768]{2,1,0:T(8,128)(2,1)} %get-tuple-element.18) | copy-start | bytes 3538948
  98.0 1.6 %copy-start.7 = (bf16[64,768]{1,0:T(8,128)(2,1)S(1)}, bf16[64,768]{1,0:T(8,128)(2,1)}, u32[]{:S(2)}) copy-start(bf16[64,768]{1,0:T(8,128)(2,1)} %param.15) | copy-start | bytes 294916
  99.7 3.2 %copy-start.1 = (bf16[1,768,768]{2,1,0:T(8,128)(2,1)}, bf16[1,768,768]{2,1,0:T(8,128)(2,1)S(1)}, u32[]{:S(2)}) copy-start(bf16[1,768,768]{2,1,0:T(8,128)(2,1)S(1)} %get-tuple-element.29) | copy-start | bytes 3538948
  100.2 5.7 %collective-permute-start.5 = (f32[1,768,64]{1,2,0:T(8,128)S(1)}, f32[1,768,64]{1,2,0:T(8,128)S(1)}, u32[]{:S(2)}, u32[]{:S(2)}) collective-permute-start(f32[1,768,64]{1,2,0:T(8,128)S(1)} %fusion.12), channel_id=1, source_target_pairs={{0,2},{2,0},{1,3},{3,1},{4,6},{6,4},{5,7},{7,5},{8,10},{10,8},{9,1... | collective-permute-start | bytes 589832 | tf_op jit(solution)/shard_map/ppermute | solution.py:31
  106.5 1.5 %collective-permute-start.6 = (f32[49152]{0:T(1024)S(1)}, f32[49152]{0:T(1024)S(1)}, u32[]{:S(2)}, u32[]{:S(2)}) collective-permute-start(f32[49152]{0:T(1024)S(1)} %select_n.88), channel_id=1, source_target_pairs={{0,1},{1,0},{2,3},{3,2},{4,5},{5,4},{6,7},{7,6},{8,9},{9,8},{10,11... | collective-permute-start | bytes 589832 | tf_op jit(solution)/shard_map/ppermute | solution.py:45
  108.1 5.5 %collective-permute-start.7 = (f32[24576]{0:T(1024)S(1)}, f32[24576]{0:T(1024)S(1)}, u32[]{:S(2)}, u32[]{:S(2)}) collective-permute-start(f32[24576]{0:T(1024)S(1)} %slice_select_fusion), channel_id=1, source_target_pairs={{0,4},{4,0},{8,12},{12,8},{1,5},{5,1},{9,13},{13,9},{2,6},{6,2},{1... | collective-permute-start | bytes 294920 | tf_op jit(solution)/shard_map/ppermute | solution.py:45
  113.6 5.4 %collective-permute-start.8 = (f32[12288]{0:T(1024)S(1)}, f32[12288]{0:T(1024)S(1)}, u32[]{:S(2)}, u32[]{:S(2)}) collective-permute-start(f32[12288]{0:T(1024)S(1)} %slice_select_fusion.1), channel_id=1, source_target_pairs={{0,8},{4,12},{8,0},{12,4},{1,9},{5,13},{9,1},{13,5},{2,10},{6,14},... | collective-permute-start | bytes 147464 | tf_op jit(solution)/shard_map/ppermute | solution.py:45
  119.0 5.1 %collective-permute-start.9 = (f32[12288]{0:T(1024)S(1)}, f32[12288]{0:T(1024)S(1)}, u32[]{:S(2)}, u32[]{:S(2)}) collective-permute-start(f32[12288]{0:T(1024)S(1)} %select_add_fusion.1), channel_id=1, source_target_pairs={{0,8},{4,12},{8,0},{12,4},{1,9},{5,13},{9,1},{13,5},{2,10},{6,14},... | collective-permute-start | bytes 147464 | tf_op jit(solution)/shard_map/ppermute | solution.py:53
  124.1 4.7 %collective-permute-start.10 = (f32[24576]{0:T(1024)S(1)}, f32[24576]{0:T(1024)S(1)}, u32[]{:S(2)}, u32[]{:S(2)}) collective-permute-start(f32[24576]{0:T(1024)S(1)} %maximum_select_fusion.4), channel_id=1, source_target_pairs={{0,4},{4,0},{8,12},{12,8},{1,5},{5,1},{9,13},{13,9},{2,6},{6,2},{1... | collective-permute-start | bytes 294920 | tf_op jit(solution)/shard_map/ppermute | solution.py:53
  128.8 1.5 %collective-permute-start.11 = (f32[49152]{0:T(1024)S(1)}, f32[49152]{0:T(1024)S(1)}, u32[]{:S(2)}, u32[]{:S(2)}) collective-permute-start(f32[49152]{0:T(1024)S(1)} %maximum_select_fusion.2), channel_id=1, source_target_pairs={{0,1},{1,0},{2,3},{3,2},{4,5},{5,4},{6,7},{7,6},{8,9},{9,8},{10,11... | collective-permute-start | bytes 589832 | tf_op jit(solution)/shard_map/ppermute | solution.py:53

commit v4 on v3

--- a/solution.py
+++ b/solution.py
@@ -197,44 +197,43 @@
     )
     bias = jnp.where(allowed, 0.0, masked_score).astype(jnp.float32)
 
-    local_heads = queries.shape[2] // HEAD_SIZE
-    chunks = 1
-    per_chunk = local_heads // chunks
-    outs = []
-    for chunk in range(chunks):
-        cols = slice(chunk * per_chunk * HEAD_SIZE, (chunk + 1) * per_chunk * HEAD_SIZE)
-        left_kv = shifted(
-            jnp.stack((key_matrix[:, block_len - TILE:, cols], values[:, block_len - TILE:, cols])),
-            "seq",
-            1,
+    low_left = shifted(lowered_rows[:, block_len - TILE:], "seq", 1)
+    low_right = shifted(lowered_rows[:, :TILE], "seq", -1)
+
+    left_kv = shifted(
+        jnp.stack((key_matrix[:, block_len - TILE:], values[:, block_len - TILE:])), "seq", 1
+    )
+    right_kv = shifted(jnp.stack((key_matrix[:, :TILE], values[:, :TILE])), "seq", -1)
+    halo = jnp.concatenate((left_kv, right_kv), 0)
+    query_grad, dk_own, dv_own, dk_l, dv_l, dk_r, dv_r = attention_backward(
+        bias, 0, queries.shape[2] // HEAD_SIZE, queries, output_gradient, key_matrix, values, halo
+    )
+
+    def project(term):
+        return jnp.einsum(
+            "dsi,ji->dsj", term, adapter_up_weight, preferred_element_type=jnp.float32
         )
-        right_kv = shifted(
-            jnp.stack((key_matrix[:, :TILE, cols], values[:, :TILE, cols]), 0), "seq", -1
-        )
-        halo = jnp.concatenate((left_kv, right_kv), 0)
-        dq, dk_own, dv_own, dk_l, dv_l, dk_r, dv_r = attention_backward(
-            bias, chunk, per_chunk, queries, output_gradient, key_matrix, values, halo
-        )
-        from_right = shifted(jnp.stack((dk_l, dv_l), 0), "seq", -1)
-        from_left = shifted(jnp.stack((dk_r, dv_r), 0), "seq", 1)
-        arrived = jnp.concatenate((from_left, from_right), 2).astype(jnp.float32)
-        dk = (dk_own.astype(jnp.float32) + arrived[0]).astype(jnp.bfloat16)
-        dv = (dv_own.astype(jnp.float32) + arrived[1]).astype(jnp.bfloat16)
-        outs.append((dq, dk, dv))
-    query_grad, key_grad, value_gradient = (
-        jnp.concatenate([o[i] for o in outs], 2) for i in range(3)
-    )
-
-    backward_piece = jnp.einsum(
-        "dsi,ji->dsj", value_gradient, adapter_up_weight, preferred_element_type=jnp.float32
-    )
+
+    proj_from_right = shifted(project(dv_l), "seq", -1)
+    proj_from_left = shifted(project(dv_r), "seq", 1)
+    backward_piece = project(dv_own) + jnp.concatenate((proj_from_left, proj_from_right), 1)
     backward_rows = butterfly_sum(backward_piece, "head").astype(jnp.bfloat16)
     gradient_down_local = adapter_scale * jnp.einsum(
         "yhm,yhz->mz", normed, backward_rows, preferred_element_type=jnp.float32
     )
-    gradient_up_local = adapter_scale * jnp.einsum(
-        "igb,igu->bu", lowered_rows, value_gradient, preferred_element_type=jnp.float32
-    )
+    up_terms = (
+        jnp.einsum("igb,igu->bu", lowered_rows, dv_own, preferred_element_type=jnp.float32)
+        + jnp.einsum("igb,igu->bu", low_left, dv_l, preferred_element_type=jnp.float32)
+        + jnp.einsum("igb,igu->bu", low_right, dv_r, preferred_element_type=jnp.float32)
+    )
+    gradient_up_local = adapter_scale * up_terms
+
+    from_right = shifted(jnp.stack((dk_l, dv_l), 0), "seq", -1)
+    from_left = shifted(jnp.stack((dk_r, dv_r), 0), "seq", 1)
+    arrived = jnp.concatenate((from_left, from_right), 2).astype(jnp.float32)
+    key_grad = (dk_own.astype(jnp.float32) + arrived[0]).astype(jnp.bfloat16)
+    value_gradient = (dv_own.astype(jnp.float32) + arrived[1]).astype(jnp.bfloat16)
+
     both = jnp.stack((gradient_down_local, gradient_up_local.T), 0)
     both = all_sum(both, ("rep", "seq"))
     down_projection_grad, up_projection_grad = both[0], both[1].T

time: 133 us -> 154 us (1.16)
  local copies, waits for them, and re-layouts: 4.7 us -> 15.3 us
  waiting for transfers between devices: 60.7 us -> 51.1 us
  starting transfers between devices: 27.4 us -> 35.6 us
  other arithmetic: 10.3 us -> 16.6 us
  matrix products: 3.36 us -> 8.99 us
    ppermute x4 -> x8, waiting for transfers between devices: 44.8 us -> 16.3 us  [shifted(): return lax.ppermute(shard, axis, pairs)]
    ppermute x3, waiting for transfers between devices: 6.4 us -> 23 us  [gather_back(): other = lax.ppermute(flat, axis, [(i, i ^ step) for i in range(peers)])]
    ppermute x4 -> x8, starting transfers between devices: 14.4 us -> 21.9 us  [shifted(): return lax.ppermute(shard, axis, pairs)]
    dot_general x2 -> x6, matrix products: 1.84 us -> 5.84 us  [the longest x3 3.45 us: project(): jnp.einsum('dsi,ji->dsj', term, adapter_up_weight, preferred_element_type...]
    select_n x2, local copies, waits for them, and re-layouts: 0.28 us -> 3.64 us  [scatter_sum(): send = jnp.where(upper, flat[:half], flat[half:])]
    select_n x2, local copies, waits for them, and re-layouts: 0.28 us -> 3.63 us  [scatter_sum(): keep = jnp.where(upper, flat[half:], flat[:half])]
    add x3, other arithmetic: 0.05 us -> 2.06 us  [scatter_sum(): keep + lax.ppermute(send, axis, [(i, i ^ step) for i in range(peers)])]
    ppermute x2, waiting for transfers between devices: 2.98 us -> 4.95 us  [butterfly_sum(): other = lax.ppermute(tree, axis, pairs)]
  transfers between devices with their start and end apart: 12 -> 16, of which waited for: 11 -> 9; matrix products, arithmetic and copies ran while one was open for 6% -> 16% of each run, Pallas kernels for 0% -> 16%
where the time goes in v4:
time: 154 us; the launch traced here: 153 us
  waiting for transfers between devices  51.1 us (33%)
  starting transfers between devices  35.6 us (23%)
  Pallas kernels  24.9 us (16%)
  other arithmetic  16.6 us (11%)
  local copies, waits for them, and re-layouts  15.3 us (10%)
  matrix products  8.99 us (6%)
    pallas_call x1, Pallas kernels, attention_backward(): pl.pallas_call(attention_kernel, grid=(clip_count, heads), in_specs=[pl.B...  24.9 us
    ppermute x3, waiting for transfers between devices, gather_back(): other = lax.ppermute(flat, axis, [(i, i ^ step) for i in range(peers)])  23 us
    ppermute x8, starting transfers between devices, shifted(): return lax.ppermute(shard, axis, pairs)  21.9 us
    ppermute x8, waiting for transfers between devices, shifted(): return lax.ppermute(shard, axis, pairs)  16.3 us
    ppermute x3, waiting for transfers between devices, scatter_sum(): lax.ppermute(send, axis, [(i, i ^ step) for i in range(peers)])  6.9 us
    ppermute x3, starting transfers between devices, scatter_sum(): lax.ppermute(send, axis, [(i, i ^ step) for i in range(peers)])  5.66 us
    ppermute x2, waiting for transfers between devices, butterfly_sum(): other = lax.ppermute(tree, axis, pairs)  4.95 us
    ppermute x3, starting transfers between devices, gather_back(): other = lax.ppermute(flat, axis, [(i, i ^ step) for i in range(peers)])  4.72 us
  transfers between devices with their start and end apart: 16, of which 9 were waited for; matrix products, arithmetic and copies ran while one was open for 16% of the time, Pallas kernels for 16%

profile of v4, /device:TPU:0, one launch (start us, length us, event | category | flops | bytes accessed | tf_op | source)
XLA Modules:
  0.0 153.4 jit_solution(7448456535007944122)
XLA Ops:
  1.9 2.1 %fusion.12 = f32[1,768,64]{1,2,0:T(8,128)} fusion(bf16[768,64]{0,1:T(8,128)(2,1)} %param.14, bf16[1,768,768]{2,1,0:T(8,128)(2,1)S(1)} %copy-done), kind=kOutput, calls=%fused_computation.20 | convolution fusion | flops 75497472 | bytes 1474560 | tf_op jit(solution)/shard_map/pqg,gv->pqv/dot_general | solution.py:186
  4.0 2.9 %collective-permute-start.4 = (f32[1,768,64]{1,2,0:T(8,128)}, f32[1,768,64]{1,2,0:T(8,128)}, u32[]{:S(2)}, u32[]{:S(2)}) collective-permute-start(f32[1,768,64]{1,2,0:T(8,128)} %fusion.12), channel_id=1, source_target_pairs={{0,2},{2,0},{1,3},{3,1},{4,6},{6,4},{5,7},{7,5},{8,10},{10,8},{9,1... | collective-permute-start | bytes 589832 | tf_op jit(solution)/shard_map/ppermute | solution.py:31
  9.9 5.6 %collective-permute-start = (bf16[2,1,384,768]{3,2,1,0:T(8,128)(2,1)S(1)}, bf16[2,1,384,768]{3,2,1,0:T(8,128)(2,1)}, u32[]{:S(2)}, u32[]{:S(2)}) collective-permute-start(bf16[2,1,384,768]{3,2,1,0:T(8,128)(2,1)S(1)} %pad_maximum_fusion.1), channel_id=1, source_target_pairs={{0,4},{4,8},{8,12},{1,5},{5,9},{9,13},{2,6},{6,10},{10,14},{3,7},{... | collective-permute-start | bytes 3538952 | tf_op jit(solution)/shard_map/ppermute | solution.py:21
  19.0 3.1 %collective-permute-start.5 = (bf16[1,384,64]{1,2,0:T(8,128)(2,1)}, bf16[1,384,64]{1,2,0:T(8,128)(2,1)}, u32[]{:S(2)}, u32[]{:S(2)}) collective-permute-start(bf16[1,384,64]{1,2,0:T(8,128)(2,1)} %get-tuple-element.39), channel_id=1, source_target_pairs={{0,4},{4,8},{8,12},{1,5},{5,9},{9,13},{2,6},{6,10},{10,14},{3,7},{... | collective-permute-start | bytes 147464 | tf_op jit(solution)/shard_map/ppermute | solution.py:21
  23.4 15.0 %collective-permute-done.1 = bf16[2,1,384,768]{3,2,1,0:T(8,128)(2,1)} collective-permute-done((bf16[2,1,384,768]{3,2,1,0:T(8,128)(2,1)S(1)}, bf16[2,1,384,768]{3,2,1,0:T(8,128)(2,1)}, u32[]{:S(2)}, u32[]{:S(2)}) %collective-permute-start.1) | collective-permute-done | bytes 1179680 | tf_op jit(solution)/shard_map/ppermute | solution.py:21
  39.6 3.3 %pad_maximum_fusion.kl_ref.vl_ref.kr_ref.vr_ref = bf16[4,1,384,768]{3,2,1,0:T(8,128)(2,1)} fusion(bf16[2,1,384,768]{3,2,1,0:T(8,128)(2,1)} %collective-permute-done.1, bf16[2,1,384,768]{3,2,1,0:T(8,128)(2,1)} %collective-permute-done), kind=kLoop, calls=%fused_computation.6 | loop fusion | flops 1179648 | bytes 4718592 | tf_op jit(solution)/shard_map/concatenate | solution.py:207
  42.9 24.9 %shard_map.128 = (bf16[1,768,768]{2,1,0:T(8,128)(2,1)}, bf16[1,768,768]{2,1,0:T(8,128)(2,1)}, bf16[1,768,768]{2,1,0:T(8,128)(2,1)}, bf16[1,384,768]{2,1,0:T(8,12...) custom-call(f32[6]{0:T(128)} %and_select_fusion.bias_ref, ...), custom_call_target="tpu_custom_call" | custom-call | tf_op jit(solution)/shard_map/pallas_call | solution.py:162
  72.0 5.1 %collective-permute-start.7 = (f32[1,384,64]{1,2,0:T(8,128)S(1)}, f32[1,384,64]{1,2,0:T(8,128)S(1)}, u32[]{:S(2)}, u32[]{:S(2)}) collective-permute-start(f32[1,384,64]{1,2,0:T(8,128)S(1)} %convolution_bitcast_fusion.1), channel_id=1, source_target_pairs={{0,4},{4,8},{8,12},{1,5},{5,9},{9,13},{2,6},{6,10},{10,14},{3,7},{... | collective-permute-start | bytes 294920 | tf_op jit(solution)/shard_map/ppermute | solution.py:21
  80.6 4.9 %collective-permute-done.9 = f32[1,768,64]{1,2,0:T(8,128)S(1)} collective-permute-done((f32[1,768,64]{1,2,0:T(8,128)S(1)}, f32[1,768,64]{1,2,0:T(8,128)S(1)}, u32[]{:S(2)}, u32[]{:S(2)}) %collective-permute-start.9) | collective-permute-done | bytes 196640 | tf_op jit(solution)/shard_map/ppermute | solution.py:31
  86.6 1.8 %copy.21 = f32[768,64]{1,0:T(8,128)} copy(f32[768,64]{0,1:T(8,128)} %get-tuple-element.37) | data formatting | bytes 393216 | tf_op jit(solution)/shard_map/jit(_where)/select_n | solution.py:44
  88.5 1.8 %select_n.88 = f32[49152]{0:T(1024)} reshape(f32[768,64]{1,0:T(8,128)} %copy.21) | data formatting | bytes 393216 | tf_op jit(solution)/shard_map/jit(_where)/select_n | solution.py:44
  90.3 1.8 %copy.20 = f32[768,64]{1,0:T(8,128)} copy(f32[768,64]{0,1:T(8,128)} %get-tuple-element.38) | data formatting | bytes 393216 | tf_op jit(solution)/shard_map/jit(_where)/select_n | solution.py:43
  92.1 1.8 %select_n.86 = f32[49152]{0:T(1024)} reshape(f32[768,64]{1,0:T(8,128)} %copy.20) | data formatting | bytes 393216 | tf_op jit(solution)/shard_map/jit(_where)/select_n | solution.py:43
  96.3 2.4 %collective-permute-start.11 = (f32[24576]{0:T(1024)}, f32[24576]{0:T(1024)}, u32[]{:S(2)}, u32[]{:S(2)}) collective-permute-start(f32[24576]{0:T(1024)} %slice_select_fusion), channel_id=1, source_target_pairs={{0,4},{4,0},{8,12},{12,8},{1,5},{5,1},{9,13},{13,9},{2,6},{6,2},{1... | collective-permute-start | bytes 294920 | tf_op jit(solution)/shard_map/ppermute | solution.py:45
  98.7 3.8 %collective-permute-done.11 = f32[24576]{0:T(1024)} collective-permute-done((f32[24576]{0:T(1024)}, f32[24576]{0:T(1024)}, u32[]{:S(2)}, u32[]{:S(2)}) %collective-permute-start.11) | collective-permute-done | bytes 98336 | tf_op jit(solution)/shard_map/ppermute | solution.py:45
  103.5 3.3 %collective-permute-start.12 = (f32[12288]{0:T(1024)S(1)}, f32[12288]{0:T(1024)S(1)}, u32[]{:S(2)}, u32[]{:S(2)}) collective-permute-start(f32[12288]{0:T(1024)S(1)} %slice_select_fusion.1), channel_id=1, source_target_pairs={{0,8},{4,12},{8,0},{12,4},{1,9},{5,13},{9,1},{13,5},{2,10},{6,14},... | collective-permute-start | bytes 147464 | tf_op jit(solution)/shard_map/ppermute | solution.py:45
  106.8 3.1 %collective-permute-done.12 = f32[12288]{0:T(1024)S(1)} collective-permute-done((f32[12288]{0:T(1024)S(1)}, f32[12288]{0:T(1024)S(1)}, u32[]{:S(2)}, u32[]{:S(2)}) %collective-permute-start.12) | collective-permute-done | bytes 49184 | tf_op jit(solution)/shard_map/ppermute | solution.py:45
  109.9 2.0 %collective-permute-start.13 = (f32[12288]{0:T(1024)S(1)}, f32[12288]{0:T(1024)S(1)}, u32[]{:S(2)}, u32[]{:S(2)}) collective-permute-start(f32[12288]{0:T(1024)S(1)} %select_add_fusion.1), channel_id=1, source_target_pairs={{0,8},{4,12},{8,0},{12,4},{1,9},{5,13},{9,1},{13,5},{2,10},{6,14},... | collective-permute-start | bytes 147464 | tf_op jit(solution)/shard_map/ppermute | solution.py:53
  111.9 2.2 %pad_maximum_fusion.4 = bf16[2,1,384,768]{3,2,1,0:T(8,128)(2,1)} fusion(bf16[1,1,384,768]{3,2,1,0:T(8,128)(2,1)S(1)} %bitcast.99, bf16[1,1,384,768]{3,2,1,0:T(8,128)(2,1)} %bitcast.101), kind=kLoop, calls=%fused_computation.11 | loop fusion | flops 589824 | bytes 2359296 | tf_op jit(solution)/shard_map/stack | solution.py:231
  115.5 2.7 %collective-permute-start.14 = (f32[24576]{0:T(1024)S(1)}, f32[24576]{0:T(1024)S(1)}, u32[]{:S(2)}, u32[]{:S(2)}) collective-permute-start(f32[24576]{0:T(1024)S(1)} %maximum_select_fusion.4), channel_id=1, source_target_pairs={{0,4},{4,0},{8,12},{12,8},{1,5},{5,1},{9,13},{13,9},{2,6},{6,2},{1... | collective-permute-start | bytes 294920 | tf_op jit(solution)/shard_map/ppermute | solution.py:53
  119.3 3.0 %collective-permute-start.2 = (bf16[2,1,384,768]{3,2,1,0:T(8,128)(2,1)}, bf16[2,1,384,768]{3,2,1,0:T(8,128)(2,1)}, u32[]{:S(2)}, u32[]{:S(2)}) collective-permute-start(bf16[2,1,384,768]{3,2,1,0:T(8,128)(2,1)} %pad_maximum_fusion.3), channel_id=1, source_target_pairs={{0,4},{4,8},{8,12},{1,5},{5,9},{9,13},{2,6},{6,10},{10,14},{3,7},{... | collective-permute-start | bytes 3538952 | tf_op jit(solution)/shard_map/ppermute | solution.py:21
  123.2 21.5 %collective-permute-done.14 = f32[24576]{0:T(1024)S(1)} collective-permute-done((f32[24576]{0:T(1024)S(1)}, f32[24576]{0:T(1024)S(1)}, u32[]{:S(2)}, u32[]{:S(2)}) %collective-permute-start.14) | collective-permute-done | bytes 98336 | tf_op jit(solution)/shard_map/ppermute | solution.py:53
  149.2 2.1 %maximum_convert_fusion = f32[2,1,768,768]{3,2,1,0:T(8,128)S(1)} fusion(bf16[2,1,384,768]{3,2,1,0:T(8,128)(2,1)} %collective-permute-done.3, bf16[2,1,384,768]{3,2,1,0:T(8,128)(2,1)} %collective-permute-done.2), kind=kLoop, calls=%fused_computation.7 | loop fusion | flops 4718592 | bytes 7077888 | tf_op jit(solution)/shard_map/convert_element_type | solution.py:233
  151.3 2.0 %fusion.1 = (bf16[1,768,768]{2,1,0:T(8,128)(2,1)}, bf16[1,768,768]{2,1,0:T(8,128)(2,1)}) fusion(f32[2,1,768,768]{3,2,1,0:T(8,128)S(1)} %maximum_convert_fusion, bf16[1,768,768]{2,1,0:T(8,128)(2,1)S(1)} %copy-done.1, bf16[1,768,768]{2,1,0:T(8,128)(2,1)S(1)} %copy-done.6), kind=kLoop, calls=%fused_computation.2 | loop fusion | flops 3538944 | bytes 9437184 | tf_op jit(solution)/shard_map/convert_element_type | solution.py:235
  (88 shorter events, 30.3 us)
Async XLA Ops:
  0.6 6.3 %copy-start.4 = (bf16[1,768,768]{2,1,0:T(8,128)(2,1)S(1)}, bf16[1,768,768]{2,1,0:T(8,128)(2,1)}, u32[]{:S(2)}) copy-start(bf16[1,768,768]{2,1,0:T(8,128)(2,1)} %k_ref.1) | copy-start | bytes 3538948
  4.0 13.3 %collective-permute-start.4 = (f32[1,768,64]{1,2,0:T(8,128)}, f32[1,768,64]{1,2,0:T(8,128)}, u32[]{:S(2)}, u32[]{:S(2)}) collective-permute-start(f32[1,768,64]{1,2,0:T(8,128)} %fusion.12), channel_id=1, source_target_pairs={{0,2},{2,0},{1,3},{3,1},{4,6},{6,4},{5,7},{7,5},{8,10},{10,8},{9,1... | collective-permute-start | bytes 589832 | tf_op jit(solution)/shard_map/ppermute | solution.py:31
  8.4 30.0 %collective-permute-start.1 = (bf16[2,1,384,768]{3,2,1,0:T(8,128)(2,1)S(1)}, bf16[2,1,384,768]{3,2,1,0:T(8,128)(2,1)}, u32[]{:S(2)}, u32[]{:S(2)}) collective-permute-start(bf16[2,1,384,768]{3,2,1,0:T(8,128)(2,1)S(1)} %pad_maximum_fusion.2), channel_id=1, source_target_pairs={{4,0},{8,4},{12,8},{5,1},{9,5},{13,9},{6,2},{10,6},{14,10},{7,3},{... | collective-permute-start | bytes 3538952 | tf_op jit(solution)/shard_map/ppermute | solution.py:21
  9.9 29.7 %collective-permute-start = (bf16[2,1,384,768]{3,2,1,0:T(8,128)(2,1)S(1)}, bf16[2,1,384,768]{3,2,1,0:T(8,128)(2,1)}, u32[]{:S(2)}, u32[]{:S(2)}) collective-permute-start(bf16[2,1,384,768]{3,2,1,0:T(8,128)(2,1)S(1)} %pad_maximum_fusion.1), channel_id=1, source_target_pairs={{0,4},{4,8},{8,12},{1,5},{5,9},{9,13},{2,6},{6,10},{10,14},{3,7},{... | collective-permute-start | bytes 3538952 | tf_op jit(solution)/shard_map/ppermute | solution.py:21
  18.4 20.0 %copy-start.7 = (bf16[1,768,64]{1,2,0:T(8,128)(2,1)}, bf16[1,768,64]{1,2,0:T(8,128)(2,1)S(1)}, u32[]{:S(2)}) copy-start(bf16[1,768,64]{1,2,0:T(8,128)(2,1)S(1)} %add_convert_fusion.1) | copy-start | bytes 294916
  19.0 59.1 %collective-permute-start.5 = (bf16[1,384,64]{1,2,0:T(8,128)(2,1)}, bf16[1,384,64]{1,2,0:T(8,128)(2,1)}, u32[]{:S(2)}, u32[]{:S(2)}) collective-permute-start(bf16[1,384,64]{1,2,0:T(8,128)(2,1)} %get-tuple-element.39), channel_id=1, source_target_pairs={{0,4},{4,8},{8,12},{1,5},{5,9},{9,13},{2,6},{6,10},{10,14},{3,7},{... | collective-permute-start | bytes 147464 | tf_op jit(solution)/shard_map/ppermute | solution.py:21
  22.1 55.0 %collective-permute-start.6 = (bf16[1,384,64]{1,2,0:T(8,128)(2,1)}, bf16[1,384,64]{1,2,0:T(8,128)(2,1)}, u32[]{:S(2)}, u32[]{:S(2)}) collective-permute-start(bf16[1,384,64]{1,2,0:T(8,128)(2,1)} %get-tuple-element.40), channel_id=1, source_target_pairs={{4,0},{8,4},{12,8},{5,1},{9,5},{13,9},{6,2},{10,6},{14,10},{7,3},{... | collective-permute-start | bytes 147464 | tf_op jit(solution)/shard_map/ppermute | solution.py:21
  42.9 24.9 %copy-start.9 = (bf16[64,768]{1,0:T(8,128)(2,1)S(1)}, bf16[64,768]{1,0:T(8,128)(2,1)}, u32[]{:S(2)}) copy-start(bf16[64,768]{1,0:T(8,128)(2,1)} %param.15) | copy-start | bytes 294916
  67.7 9.4 %copy-start.2 = (bf16[1,384,768]{2,1,0:T(8,128)(2,1)S(1)}, bf16[1,384,768]{2,1,0:T(8,128)(2,1)}, u32[]{:S(2)}) copy-start(bf16[1,384,768]{2,1,0:T(8,128)(2,1)} %get-tuple-element.15) | copy-start | bytes 1769476
  67.7 10.4 %copy-start.3 = (bf16[1,384,768]{2,1,0:T(8,128)(2,1)S(1)}, bf16[1,384,768]{2,1,0:T(8,128)(2,1)}, u32[]{:S(2)}) copy-start(bf16[1,384,768]{2,1,0:T(8,128)(2,1)} %get-tuple-element.17) | copy-start | bytes 1769476
  69.2 10.1 %copy-start.1 = (bf16[1,768,768]{2,1,0:T(8,128)(2,1)S(1)}, bf16[1,768,768]{2,1,0:T(8,128)(2,1)}, u32[]{:S(2)}) copy-start(bf16[1,768,768]{2,1,0:T(8,128)(2,1)} %get-tuple-element.18) | copy-start | bytes 3538948
  69.2 10.1 %copy-start.10 = (bf16[64,768]{1,0:T(8,128)(2,1)S(1)}, bf16[64,768]{1,0:T(8,128)(2,1)}, u32[]{:S(2)}) copy-start(bf16[64,768]{1,0:T(8,128)(2,1)} %param.15) | copy-start | bytes 294916
  70.7 8.5 %collective-permute-start.8 = (f32[1,384,64]{1,2,0:T(8,128)S(1)}, f32[1,384,64]{1,2,0:T(8,128)S(1)}, u32[]{:S(2)}, u32[]{:S(2)}) collective-permute-start(f32[1,384,64]{1,2,0:T(8,128)S(1)} %convolution_bitcast_fusion), channel_id=1, source_target_pairs={{4,0},{8,4},{12,8},{5,1},{9,5},{13,9},{6,2},{10,6},{14,10},{7,3},{... | collective-permute-start | bytes 294920 | tf_op jit(solution)/shard_map/ppermute | solution.py:21
  72.0 7.3 %collective-permute-start.7 = (f32[1,384,64]{1,2,0:T(8,128)S(1)}, f32[1,384,64]{1,2,0:T(8,128)S(1)}, u32[]{:S(2)}, u32[]{:S(2)}) collective-permute-start(f32[1,384,64]{1,2,0:T(8,128)S(1)} %convolution_bitcast_fusion.1), channel_id=1, source_target_pairs={{0,4},{4,8},{8,12},{1,5},{5,9},{9,13},{2,6},{6,10},{10,14},{3,7},{... | collective-permute-start | bytes 294920 | tf_op jit(solution)/shard_map/ppermute | solution.py:21
  79.8 5.7 %collective-permute-start.9 = (f32[1,768,64]{1,2,0:T(8,128)S(1)}, f32[1,768,64]{1,2,0:T(8,128)S(1)}, u32[]{:S(2)}, u32[]{:S(2)}) collective-permute-start(f32[1,768,64]{1,2,0:T(8,128)S(1)} %fusion.27), channel_id=1, source_target_pairs={{0,2},{2,0},{1,3},{3,1},{4,6},{6,4},{5,7},{7,5},{8,10},{10,8},{9,1... | collective-permute-start | bytes 589832 | tf_op jit(solution)/shard_map/ppermute | solution.py:31
  90.3 3.6 %collective-permute-start.10 = (f32[49152]{0:T(1024)}, f32[49152]{0:T(1024)}, u32[]{:S(2)}, u32[]{:S(2)}) collective-permute-start(f32[49152]{0:T(1024)} %select_n.88), channel_id=1, source_target_pairs={{0,1},{1,0},{2,3},{3,2},{4,5},{5,4},{6,7},{7,6},{8,9},{9,8},{10,11... | collective-permute-start | bytes 589832 | tf_op jit(solution)/shard_map/ppermute | solution.py:45
  96.3 6.2 %collective-permute-start.11 = (f32[24576]{0:T(1024)}, f32[24576]{0:T(1024)}, u32[]{:S(2)}, u32[]{:S(2)}) collective-permute-start(f32[24576]{0:T(1024)} %slice_select_fusion), channel_id=1, source_target_pairs={{0,4},{4,0},{8,12},{12,8},{1,5},{5,1},{9,13},{13,9},{2,6},{6,2},{1... | collective-permute-start | bytes 294920 | tf_op jit(solution)/shard_map/ppermute | solution.py:45
  103.5 6.4 %collective-permute-start.12 = (f32[12288]{0:T(1024)S(1)}, f32[12288]{0:T(1024)S(1)}, u32[]{:S(2)}, u32[]{:S(2)}) collective-permute-start(f32[12288]{0:T(1024)S(1)} %slice_select_fusion.1), channel_id=1, source_target_pairs={{0,8},{4,12},{8,0},{12,4},{1,9},{5,13},{9,1},{13,5},{2,10},{6,14},... | collective-permute-start | bytes 147464 | tf_op jit(solution)/shard_map/ppermute | solution.py:45
  109.9 5.6 %collective-permute-start.13 = (f32[12288]{0:T(1024)S(1)}, f32[12288]{0:T(1024)S(1)}, u32[]{:S(2)}, u32[]{:S(2)}) collective-permute-start(f32[12288]{0:T(1024)S(1)} %select_add_fusion.1), channel_id=1, source_target_pairs={{0,8},{4,12},{8,0},{12,4},{1,9},{5,13},{9,1},{13,5},{2,10},{6,14},... | collective-permute-start | bytes 147464 | tf_op jit(solution)/shard_map/ppermute | solution.py:53
  111.9 6.3 %copy-start.11 = (bf16[1,384,768]{2,1,0:T(8,128)(2,1)S(1)}, bf16[1,384,768]{2,1,0:T(8,128)(2,1)}, u32[]{:S(2)}) copy-start(bf16[1,384,768]{2,1,0:T(8,128)(2,1)} %get-tuple-element.14) | copy-start | bytes 1769476
  114.1 35.1 %collective-permute-start.3 = (bf16[2,1,384,768]{3,2,1,0:T(8,128)(2,1)}, bf16[2,1,384,768]{3,2,1,0:T(8,128)(2,1)}, u32[]{:S(2)}, u32[]{:S(2)}) collective-permute-start(bf16[2,1,384,768]{3,2,1,0:T(8,128)(2,1)} %pad_maximum_fusion.4), channel_id=1, source_target_pairs={{4,0},{8,4},{12,8},{5,1},{9,5},{13,9},{6,2},{10,6},{14,10},{7,3},{... | collective-permute-start | bytes 3538952 | tf_op jit(solution)/shard_map/ppermute | solution.py:21
  115.5 29.2 %collective-permute-start.14 = (f32[24576]{0:T(1024)S(1)}, f32[24576]{0:T(1024)S(1)}, u32[]{:S(2)}, u32[]{:S(2)}) collective-permute-start(f32[24576]{0:T(1024)S(1)} %maximum_select_fusion.4), channel_id=1, source_target_pairs={{0,4},{4,0},{8,12},{12,8},{1,5},{5,1},{9,13},{13,9},{2,6},{6,2},{1... | collective-permute-start | bytes 294920 | tf_op jit(solution)/shard_map/ppermute | solution.py:53
  119.3 30.0 %collective-permute-start.2 = (bf16[2,1,384,768]{3,2,1,0:T(8,128)(2,1)}, bf16[2,1,384,768]{3,2,1,0:T(8,128)(2,1)}, u32[]{:S(2)}, u32[]{:S(2)}) collective-permute-start(bf16[2,1,384,768]{3,2,1,0:T(8,128)(2,1)} %pad_maximum_fusion.3), channel_id=1, source_target_pairs={{0,4},{4,8},{8,12},{1,5},{5,9},{9,13},{2,6},{6,10},{10,14},{3,7},{... | collective-permute-start | bytes 3538952 | tf_op jit(solution)/shard_map/ppermute | solution.py:21
  144.7 1.6 %collective-permute-start.15 = (f32[49152]{0:T(1024)S(1)}, f32[49152]{0:T(1024)}, u32[]{:S(2)}, u32[]{:S(2)}) collective-permute-start(f32[49152]{0:T(1024)S(1)} %maximum_select_fusion.2), channel_id=1, source_target_pairs={{0,1},{1,0},{2,3},{3,2},{4,5},{5,4},{6,7},{7,6},{8,9},{9,8},{10,11... | collective-permute-start | bytes 589832 | tf_op jit(solution)/shard_map/ppermute | solution.py:53
  (8 other events, 25.6 us)

commit v5 on v4

--- a/solution.py
+++ b/solution.py
@@ -230,11 +230,12 @@
 
     from_right = shifted(jnp.stack((dk_l, dv_l), 0), "seq", -1)
     from_left = shifted(jnp.stack((dk_r, dv_r), 0), "seq", 1)
+    both = jnp.stack((gradient_down_local, gradient_up_local.T), 0)
+    both, from_left, from_right = lax.optimization_barrier((both, from_left, from_right))
     arrived = jnp.concatenate((from_left, from_right), 2).astype(jnp.float32)
     key_grad = (dk_own.astype(jnp.float32) + arrived[0]).astype(jnp.bfloat16)
     value_gradient = (dv_own.astype(jnp.float32) + arrived[1]).astype(jnp.bfloat16)
 
-    both = jnp.stack((gradient_down_local, gradient_up_local.T), 0)
     both = all_sum(both, ("rep", "seq"))
     down_projection_grad, up_projection_grad = both[0], both[1].T
     return (query_grad, key_grad, value_gradient, down_projection_grad, up_projection_grad)

time: 154 us -> 136 us (0.88)
  local copies, waits for them, and re-layouts: 15.3 us -> 7.53 us
  other arithmetic: 16.6 us -> 12 us
  waiting for transfers between devices: 51.1 us -> 47 us
  matrix products: 8.99 us -> 5.9 us
  starting transfers between devices: 35.6 us -> 37.5 us
    ppermute x3, waiting for transfers between devices: 23 us -> 2.41 us  [gather_back(): other = lax.ppermute(flat, axis, [(i, i ^ step) for i in range(peers)])]
    ppermute x8, waiting for transfers between devices: 16.3 us -> 34.3 us  [shifted(): return lax.ppermute(shard, axis, pairs)]
    select_n x2, local copies, waits for them, and re-layouts: 3.64 us -> 0.28 us  [scatter_sum(): send = jnp.where(upper, flat[:half], flat[half:])]
    select_n x2, local copies, waits for them, and re-layouts: 3.63 us -> 0.28 us  [scatter_sum(): keep = jnp.where(upper, flat[half:], flat[:half])]
    dot_general x3, matrix products: 3.45 us -> 1.12 us  [project(): jnp.einsum('dsi,ji->dsj', term, adapter_up_weight, preferred_element_type...]
    add x3, other arithmetic: 2.06 us -> 0.05 us  [scatter_sum(): keep + lax.ppermute(send, axis, [(i, i ^ step) for i in range(peers)])]
    ppermute x8, starting transfers between devices: 21.9 us -> 23.7 us  [shifted(): return lax.ppermute(shard, axis, pairs)]
    concatenate x4, local copies, waits for them, and re-layouts: 2.09 us -> 0.36 us  [gather_back(): jnp.concatenate((other, flat))]
  transfers between devices with their start and end apart: 16 -> 16, of which waited for: 9 -> 11; matrix products, arithmetic and copies ran while one was open for 16% -> 14% of each run, Pallas kernels for 16% -> 18%
where the time goes in v5:
time: 136 us
  waiting for transfers between devices  47 us (35%)
  starting transfers between devices  37.5 us (28%)
  Pallas kernels  24.8 us (18%)
  other arithmetic  12 us (9%)
  local copies, waits for them, and re-layouts  7.53 us (6%)
  matrix products  5.9 us (4%)
    ppermute x8, waiting for transfers between devices, shifted(): return lax.ppermute(shard, axis, pairs)  34.3 us
    pallas_call x1, Pallas kernels, attention_backward(): pl.pallas_call(attention_kernel, grid=(clip_count, heads), in_specs=[pl.B...  24.8 us
    ppermute x8, starting transfers between devices, shifted(): return lax.ppermute(shard, axis, pairs)  23.7 us
    ppermute x3, waiting for transfers between devices, scatter_sum(): lax.ppermute(send, axis, [(i, i ^ step) for i in range(peers)])  6.62 us
    ppermute x3, starting transfers between devices, scatter_sum(): lax.ppermute(send, axis, [(i, i ^ step) for i in range(peers)])  5.71 us
    ppermute x3, starting transfers between devices, gather_back(): other = lax.ppermute(flat, axis, [(i, i ^ step) for i in range(peers)])  4.49 us
    unnamed x28, local copies, waits for them, and re-layouts  4.35 us
    ppermute x2, starting transfers between devices, butterfly_sum(): other = lax.ppermute(tree, axis, pairs)  3.65 us
  transfers between devices with their start and end apart: 16, of which 11 were waited for; matrix products, arithmetic and copies ran while one was open for 14% of the time, Pallas kernels for 18%

profile of v5, /device:TPU:0, one launch (start us, length us, event | category | flops | bytes accessed | tf_op | source)
XLA Modules:
  0.0 135.9 jit_solution(5891235098995299286)
XLA Ops:
  1.9 2.1 %fusion.12 = f32[1,768,64]{1,2,0:T(8,128)} fusion(bf16[768,64]{0,1:T(8,128)(2,1)} %param.14, bf16[1,768,768]{2,1,0:T(8,128)(2,1)S(1)} %copy-done), kind=kOutput, calls=%fused_computation.20 | convolution fusion | flops 75497472 | bytes 1474560 | tf_op jit(solution)/shard_map/pqg,gv->pqv/dot_general | solution.py:186
  4.0 2.9 %collective-permute-start.5 = (f32[1,768,64]{1,2,0:T(8,128)}, f32[1,768,64]{1,2,0:T(8,128)}, u32[]{:S(2)}, u32[]{:S(2)}) collective-permute-start(f32[1,768,64]{1,2,0:T(8,128)} %fusion.12), channel_id=1, source_target_pairs={{0,2},{2,0},{1,3},{3,1},{4,6},{6,4},{5,7},{7,5},{8,10},{10,8},{9,1... | collective-permute-start | bytes 589832 | tf_op jit(solution)/shard_map/ppermute | solution.py:31
  6.9 1.4 %slice_bitcast_fusion.4 = (bf16[1,1,384,768]{3,2,1,0:T(8,128)(2,1)S(1)}, bf16[1,1,384,768]{3,2,1,0:T(8,128)(2,1)S(1)}, bf16[1,1,384,768]{3,2,1,0:T(8,128)(2,1)S(1)}, bf16[1,1,384,768]{3,2,1,0:T(8,128)(2,1)S(1)}) fusion(bf16[1,768,768]{2,1,0:T(8,128)(2,1)} %v_ref.1, bf16[1,768,768]{2,1,0:T(8,128)(2,1)S(1)} %copy-done.4), kind=kLoop, calls=%fused_computation.40 | loop fusion | bytes 4718592 | tf_op jit(solution)/shard_map/stack | solution.py:204
  8.4 1.3 collective-permute-start.1
  9.9 5.6 %collective-permute-start = (bf16[2,1,384,768]{3,2,1,0:T(8,128)(2,1)S(1)}, bf16[2,1,384,768]{3,2,1,0:T(8,128)(2,1)}, u32[]{:S(2)}, u32[]{:S(2)}) collective-permute-start(bf16[2,1,384,768]{3,2,1,0:T(8,128)(2,1)S(1)} %pad_maximum_fusion.1), channel_id=1, source_target_pairs={{0,4},{4,8},{8,12},{1,5},{5,9},{9,13},{2,6},{6,10},{10,14},{3,7},{... | collective-permute-start | bytes 3538952 | tf_op jit(solution)/shard_map/ppermute | solution.py:21
  19.0 3.1 %collective-permute-start.6 = (bf16[1,384,64]{1,2,0:T(8,128)(2,1)}, bf16[1,384,64]{1,2,0:T(8,128)(2,1)}, u32[]{:S(2)}, u32[]{:S(2)}) collective-permute-start(bf16[1,384,64]{1,2,0:T(8,128)(2,1)} %get-tuple-element.45), channel_id=1, source_target_pairs={{0,4},{4,8},{8,12},{1,5},{5,9},{9,13},{2,6},{6,10},{10,14},{3,7},{... | collective-permute-start | bytes 147464 | tf_op jit(solution)/shard_map/ppermute | solution.py:21
  23.3 15.1 %collective-permute-done.1 = bf16[2,1,384,768]{3,2,1,0:T(8,128)(2,1)} collective-permute-done((bf16[2,1,384,768]{3,2,1,0:T(8,128)(2,1)S(1)}, bf16[2,1,384,768]{3,2,1,0:T(8,128)(2,1)}, u32[]{:S(2)}, u32[]{:S(2)}) %collective-permute-start.1) | collective-permute-done | bytes 1179680 | tf_op jit(solution)/shard_map/ppermute | solution.py:21
  39.6 3.3 %pad_maximum_fusion.kl_ref.vl_ref.kr_ref.vr_ref = bf16[4,1,384,768]{3,2,1,0:T(8,128)(2,1)} fusion(bf16[2,1,384,768]{3,2,1,0:T(8,128)(2,1)} %collective-permute-done.1, bf16[2,1,384,768]{3,2,1,0:T(8,128)(2,1)} %collective-permute-done), kind=kLoop, calls=%fused_computation.6 | loop fusion | flops 1179648 | bytes 4718592 | tf_op jit(solution)/shard_map/concatenate | solution.py:207
  42.9 24.8 %shard_map.128 = (bf16[1,768,768]{2,1,0:T(8,128)(2,1)}, bf16[1,768,768]{2,1,0:T(8,128)(2,1)}, bf16[1,768,768]{2,1,0:T(8,128)(2,1)}, bf16[1,384,768]{2,1,0:T(8,12...) custom-call(f32[6]{0:T(128)} %and_select_fusion.bias_ref, ...), custom_call_target="tpu_custom_call" | custom-call | tf_op jit(solution)/shard_map/pallas_call | solution.py:162
  67.7 1.4 %pad_maximum_fusion.4 = bf16[2,1,384,768]{3,2,1,0:T(8,128)(2,1)S(1)} fusion(bf16[1,1,384,768]{3,2,1,0:T(8,128)(2,1)} %bitcast.100, bf16[1,1,384,768]{3,2,1,0:T(8,128)(2,1)} %bitcast.103), kind=kLoop, calls=%fused_computation.11 | loop fusion | flops 589824 | bytes 2359296 | tf_op jit(solution)/shard_map/stack | solution.py:231
  69.2 1.3 collective-permute-start.9
  71.0 5.3 %collective-permute-start.8 = (bf16[2,1,384,768]{3,2,1,0:T(8,128)(2,1)S(1)}, bf16[2,1,384,768]{3,2,1,0:T(8,128)(2,1)S(1)}, u32[]{:S(2)}, u32[]{:S(2)}) collective-permute-start(bf16[2,1,384,768]{3,2,1,0:T(8,128)(2,1)S(1)} %pad_maximum_fusion.3), channel_id=1, source_target_pairs={{0,4},{4,8},{8,12},{1,5},{5,9},{9,13},{2,6},{6,10},{10,14},{3,7},{... | collective-permute-start | bytes 3538952 | tf_op jit(solution)/shard_map/ppermute | solution.py:21
  77.9 4.6 %collective-permute-start.2 = (f32[1,384,64]{1,2,0:T(8,128)S(1)}, f32[1,384,64]{1,2,0:T(8,128)S(1)}, u32[]{:S(2)}, u32[]{:S(2)}) collective-permute-start(f32[1,384,64]{1,2,0:T(8,128)S(1)} %convolution_bitcast_fusion.1), channel_id=1, source_target_pairs={{0,4},{4,8},{8,12},{1,5},{5,9},{9,13},{2,6},{6,10},{10,14},{3,7},{... | collective-permute-start | bytes 294920 | tf_op jit(solution)/shard_map/ppermute | solution.py:21
  83.5 16.3 %collective-permute-done.3 = f32[1,384,64]{1,2,0:T(8,128)S(1)} collective-permute-done((f32[1,384,64]{1,2,0:T(8,128)S(1)}, f32[1,384,64]{1,2,0:T(8,128)S(1)}, u32[]{:S(2)}, u32[]{:S(2)}) %collective-permute-start.3) | collective-permute-done | bytes 98336 | tf_op jit(solution)/shard_map/ppermute | solution.py:21
  99.7 1.8 %collective-permute-done.2 = f32[1,384,64]{1,2,0:T(8,128)S(1)} collective-permute-done((f32[1,384,64]{1,2,0:T(8,128)S(1)}, f32[1,384,64]{1,2,0:T(8,128)S(1)}, u32[]{:S(2)}, u32[]{:S(2)}) %collective-permute-start.2) | collective-permute-done | bytes 98336 | tf_op jit(solution)/shard_map/ppermute | solution.py:21
  104.1 3.6 %collective-permute-done.4 = f32[1,768,64]{1,2,0:T(8,128)S(1)} collective-permute-done((f32[1,768,64]{1,2,0:T(8,128)S(1)}, f32[1,768,64]{1,2,0:T(8,128)S(1)}, u32[]{:S(2)}, u32[]{:S(2)}) %collective-permute-start.4) | collective-permute-done | bytes 196640 | tf_op jit(solution)/shard_map/ppermute | solution.py:31
  111.4 2.5 %collective-permute-start.11 = (f32[24576]{0:T(1024)S(1)}, f32[24576]{0:T(1024)S(1)}, u32[]{:S(2)}, u32[]{:S(2)}) collective-permute-start(f32[24576]{0:T(1024)S(1)} %slice_select_fusion.2), channel_id=1, source_target_pairs={{0,4},{4,0},{8,12},{12,8},{1,5},{5,1},{9,13},{13,9},{2,6},{6,2},{1... | collective-permute-start | bytes 294920 | tf_op jit(solution)/shard_map/ppermute | solution.py:45
  114.0 3.1 %collective-permute-done.11 = f32[24576]{0:T(1024)S(1)} collective-permute-done((f32[24576]{0:T(1024)S(1)}, f32[24576]{0:T(1024)S(1)}, u32[]{:S(2)}, u32[]{:S(2)}) %collective-permute-start.11) | collective-permute-done | bytes 98336 | tf_op jit(solution)/shard_map/ppermute | solution.py:45
  117.1 3.1 %collective-permute-start.12 = (f32[12288]{0:T(1024)S(1)}, f32[12288]{0:T(1024)S(1)}, u32[]{:S(2)}, u32[]{:S(2)}) collective-permute-start(f32[12288]{0:T(1024)S(1)} %slice_select_fusion.3), channel_id=1, source_target_pairs={{0,8},{4,12},{8,0},{12,4},{1,9},{5,13},{9,1},{13,5},{2,10},{6,14},... | collective-permute-start | bytes 147464 | tf_op jit(solution)/shard_map/ppermute | solution.py:45
  120.2 2.4 %collective-permute-done.12 = f32[12288]{0:T(1024)S(1)} collective-permute-done((f32[12288]{0:T(1024)S(1)}, f32[12288]{0:T(1024)S(1)}, u32[]{:S(2)}, u32[]{:S(2)}) %collective-permute-start.12) | collective-permute-done | bytes 49184 | tf_op jit(solution)/shard_map/ppermute | solution.py:45
  122.6 2.7 %collective-permute-start.13 = (f32[12288]{0:T(1024)S(1)}, f32[12288]{0:T(1024)S(1)}, u32[]{:S(2)}, u32[]{:S(2)}) collective-permute-start(f32[12288]{0:T(1024)S(1)} %select_add_fusion.1), channel_id=1, source_target_pairs={{0,8},{4,12},{8,0},{12,4},{1,9},{5,13},{9,1},{13,5},{2,10},{6,14},... | collective-permute-start | bytes 147464 | tf_op jit(solution)/shard_map/ppermute | solution.py:53
  125.3 2.0 %maximum_convert_fusion = f32[2,1,768,768]{3,2,1,0:T(8,128)S(1)} fusion(bf16[2,1,384,768]{3,2,1,0:T(8,128)(2,1)} %copy-done.6, bf16[2,1,384,768]{3,2,1,0:T(8,128)(2,1)} %copy-done.7), kind=kLoop, calls=%fused_computation.7 | loop fusion | flops 4718592 | bytes 7077888 | tf_op jit(solution)/shard_map/convert_element_type | solution.py:235
  127.7 1.7 %collective-permute-start.14 = (f32[24576]{0:T(1024)S(1)}, f32[24576]{0:T(1024)S(1)}, u32[]{:S(2)}, u32[]{:S(2)}) collective-permute-start(f32[24576]{0:T(1024)S(1)} %maximum_select_fusion.4), channel_id=1, source_target_pairs={{0,4},{4,0},{8,12},{12,8},{1,5},{5,1},{9,13},{13,9},{2,6},{6,2},{1... | collective-permute-start | bytes 294920 | tf_op jit(solution)/shard_map/ppermute | solution.py:53
  129.4 2.0 %fusion.1 = (bf16[1,768,768]{2,1,0:T(8,128)(2,1)}, bf16[1,768,768]{2,1,0:T(8,128)(2,1)}) fusion(f32[2,1,768,768]{3,2,1,0:T(8,128)S(1)} %maximum_convert_fusion, bf16[1,768,768]{2,1,0:T(8,128)(2,1)S(1)} %copy-done.1, bf16[1,768,768]{2,1,0:T(8,128)(2,1)S(1)} %copy-done.5), kind=kLoop, calls=%fused_computation.2 | loop fusion | flops 3538944 | bytes 9437184 | tf_op jit(solution)/shard_map/convert_element_type | solution.py:237
  (84 shorter events, 21.5 us)
Async XLA Ops:
  0.6 6.3 %copy-start.4 = (bf16[1,768,768]{2,1,0:T(8,128)(2,1)S(1)}, bf16[1,768,768]{2,1,0:T(8,128)(2,1)}, u32[]{:S(2)}) copy-start(bf16[1,768,768]{2,1,0:T(8,128)(2,1)} %k_ref.1) | copy-start | bytes 3538948
  4.0 13.3 %collective-permute-start.5 = (f32[1,768,64]{1,2,0:T(8,128)}, f32[1,768,64]{1,2,0:T(8,128)}, u32[]{:S(2)}, u32[]{:S(2)}) collective-permute-start(f32[1,768,64]{1,2,0:T(8,128)} %fusion.12), channel_id=1, source_target_pairs={{0,2},{2,0},{1,3},{3,1},{4,6},{6,4},{5,7},{7,5},{8,10},{10,8},{9,1... | collective-permute-start | bytes 589832 | tf_op jit(solution)/shard_map/ppermute | solution.py:31
  8.4 30.0 %collective-permute-start.1 = (bf16[2,1,384,768]{3,2,1,0:T(8,128)(2,1)S(1)}, bf16[2,1,384,768]{3,2,1,0:T(8,128)(2,1)}, u32[]{:S(2)}, u32[]{:S(2)}) collective-permute-start(bf16[2,1,384,768]{3,2,1,0:T(8,128)(2,1)S(1)} %pad_maximum_fusion.2), channel_id=1, source_target_pairs={{4,0},{8,4},{12,8},{5,1},{9,5},{13,9},{6,2},{10,6},{14,10},{7,3},{... | collective-permute-start | bytes 3538952 | tf_op jit(solution)/shard_map/ppermute | solution.py:21
  9.7 6.0 %copy-start.12 = (s32[8,3]{0,1:T(4,128)S(1)}, s32[8,3]{0,1:T(4,128)}, u32[]{:S(2)}) copy-start(s32[8,3]{0,1:T(4,128)} %param.16) | copy-start | bytes 292
  9.9 29.7 %collective-permute-start = (bf16[2,1,384,768]{3,2,1,0:T(8,128)(2,1)S(1)}, bf16[2,1,384,768]{3,2,1,0:T(8,128)(2,1)}, u32[]{:S(2)}, u32[]{:S(2)}) collective-permute-start(bf16[2,1,384,768]{3,2,1,0:T(8,128)(2,1)S(1)} %pad_maximum_fusion.1), channel_id=1, source_target_pairs={{0,4},{4,8},{8,12},{1,5},{5,9},{9,13},{2,6},{6,10},{10,14},{3,7},{... | collective-permute-start | bytes 3538952 | tf_op jit(solution)/shard_map/ppermute | solution.py:21
  18.3 20.1 %copy-start.8 = (bf16[1,768,64]{1,2,0:T(8,128)(2,1)}, bf16[1,768,64]{1,2,0:T(8,128)(2,1)S(1)}, u32[]{:S(2)}) copy-start(bf16[1,768,64]{1,2,0:T(8,128)(2,1)S(1)} %add_convert_fusion) | copy-start | bytes 294916
  19.0 83.8 %collective-permute-start.6 = (bf16[1,384,64]{1,2,0:T(8,128)(2,1)}, bf16[1,384,64]{1,2,0:T(8,128)(2,1)}, u32[]{:S(2)}, u32[]{:S(2)}) collective-permute-start(bf16[1,384,64]{1,2,0:T(8,128)(2,1)} %get-tuple-element.45), channel_id=1, source_target_pairs={{0,4},{4,8},{8,12},{1,5},{5,9},{9,13},{2,6},{6,10},{10,14},{3,7},{... | collective-permute-start | bytes 147464 | tf_op jit(solution)/shard_map/ppermute | solution.py:21
  22.1 55.9 %collective-permute-start.7 = (bf16[1,384,64]{1,2,0:T(8,128)(2,1)}, bf16[1,384,64]{1,2,0:T(8,128)(2,1)}, u32[]{:S(2)}, u32[]{:S(2)}) collective-permute-start(bf16[1,384,64]{1,2,0:T(8,128)(2,1)} %get-tuple-element.46), channel_id=1, source_target_pairs={{4,0},{8,4},{12,8},{5,1},{9,5},{13,9},{6,2},{10,6},{14,10},{7,3},{... | collective-permute-start | bytes 147464 | tf_op jit(solution)/shard_map/ppermute | solution.py:21
  67.7 2.8 %copy-start.3 = (bf16[1,384,768]{2,1,0:T(8,128)(2,1)S(1)}, bf16[1,384,768]{2,1,0:T(8,128)(2,1)}, u32[]{:S(2)}) copy-start(bf16[1,384,768]{2,1,0:T(8,128)(2,1)} %get-tuple-element.18) | copy-start | bytes 1769476
  67.7 3.1 %copy-start.11 = (bf16[1,384,768]{2,1,0:T(8,128)(2,1)S(1)}, bf16[1,384,768]{2,1,0:T(8,128)(2,1)}, u32[]{:S(2)}) copy-start(bf16[1,384,768]{2,1,0:T(8,128)(2,1)} %get-tuple-element.20) | copy-start | bytes 1769476
  69.2 38.9 %collective-permute-start.9 = (bf16[2,1,384,768]{3,2,1,0:T(8,128)(2,1)S(1)}, bf16[2,1,384,768]{3,2,1,0:T(8,128)(2,1)S(1)}, u32[]{:S(2)}, u32[]{:S(2)}) collective-permute-start(bf16[2,1,384,768]{3,2,1,0:T(8,128)(2,1)S(1)} %pad_maximum_fusion.4), channel_id=1, source_target_pairs={{4,0},{8,4},{12,8},{5,1},{9,5},{13,9},{6,2},{10,6},{14,10},{7,3},{... | collective-permute-start | bytes 3538952 | tf_op jit(solution)/shard_map/ppermute | solution.py:21
  70.8 5.5 %copy-start.2 = (bf16[1,384,768]{2,1,0:T(8,128)(2,1)S(1)}, bf16[1,384,768]{2,1,0:T(8,128)(2,1)}, u32[]{:S(2)}) copy-start(bf16[1,384,768]{2,1,0:T(8,128)(2,1)} %get-tuple-element.19) | copy-start | bytes 1769476
  71.0 30.6 %copy-start.1 = (bf16[1,768,768]{2,1,0:T(8,128)(2,1)S(1)}, bf16[1,768,768]{2,1,0:T(8,128)(2,1)}, u32[]{:S(2)}) copy-start(bf16[1,768,768]{2,1,0:T(8,128)(2,1)} %get-tuple-element.17) | copy-start | bytes 3538948
  71.0 37.2 %collective-permute-start.8 = (bf16[2,1,384,768]{3,2,1,0:T(8,128)(2,1)S(1)}, bf16[2,1,384,768]{3,2,1,0:T(8,128)(2,1)S(1)}, u32[]{:S(2)}, u32[]{:S(2)}) collective-permute-start(bf16[2,1,384,768]{3,2,1,0:T(8,128)(2,1)S(1)} %pad_maximum_fusion.3), channel_id=1, source_target_pairs={{0,4},{4,8},{8,12},{1,5},{5,9},{9,13},{2,6},{6,10},{10,14},{3,7},{... | collective-permute-start | bytes 3538952 | tf_op jit(solution)/shard_map/ppermute | solution.py:21
  76.6 23.1 %collective-permute-start.3 = (f32[1,384,64]{1,2,0:T(8,128)S(1)}, f32[1,384,64]{1,2,0:T(8,128)S(1)}, u32[]{:S(2)}, u32[]{:S(2)}) collective-permute-start(f32[1,384,64]{1,2,0:T(8,128)S(1)} %convolution_bitcast_fusion), channel_id=1, source_target_pairs={{4,0},{8,4},{12,8},{5,1},{9,5},{13,9},{6,2},{10,6},{14,10},{7,3},{... | collective-permute-start | bytes 294920 | tf_op jit(solution)/shard_map/ppermute | solution.py:21
  77.9 23.6 %collective-permute-start.2 = (f32[1,384,64]{1,2,0:T(8,128)S(1)}, f32[1,384,64]{1,2,0:T(8,128)S(1)}, u32[]{:S(2)}, u32[]{:S(2)}) collective-permute-start(f32[1,384,64]{1,2,0:T(8,128)S(1)} %convolution_bitcast_fusion.1), channel_id=1, source_target_pairs={{0,4},{4,8},{8,12},{1,5},{5,9},{9,13},{2,6},{6,10},{10,14},{3,7},{... | collective-permute-start | bytes 294920 | tf_op jit(solution)/shard_map/ppermute | solution.py:21
  102.0 5.7 %collective-permute-start.4 = (f32[1,768,64]{1,2,0:T(8,128)S(1)}, f32[1,768,64]{1,2,0:T(8,128)S(1)}, u32[]{:S(2)}, u32[]{:S(2)}) collective-permute-start(f32[1,768,64]{1,2,0:T(8,128)S(1)} %fusion.18), channel_id=1, source_target_pairs={{0,2},{2,0},{1,3},{3,1},{4,6},{6,4},{5,7},{7,5},{8,10},{10,8},{9,1... | collective-permute-start | bytes 589832 | tf_op jit(solution)/shard_map/ppermute | solution.py:31
  109.9 1.5 %collective-permute-start.10 = (f32[49152]{0:T(1024)S(1)}, f32[49152]{0:T(1024)S(1)}, u32[]{:S(2)}, u32[]{:S(2)}) collective-permute-start(f32[49152]{0:T(1024)S(1)} %select_n.88), channel_id=1, source_target_pairs={{0,1},{1,0},{2,3},{3,2},{4,5},{5,4},{6,7},{7,6},{8,9},{9,8},{10,11... | collective-permute-start | bytes 589832 | tf_op jit(solution)/shard_map/ppermute | solution.py:45
  111.4 5.6 %collective-permute-start.11 = (f32[24576]{0:T(1024)S(1)}, f32[24576]{0:T(1024)S(1)}, u32[]{:S(2)}, u32[]{:S(2)}) collective-permute-start(f32[24576]{0:T(1024)S(1)} %slice_select_fusion.2), channel_id=1, source_target_pairs={{0,4},{4,0},{8,12},{12,8},{1,5},{5,1},{9,13},{13,9},{2,6},{6,2},{1... | collective-permute-start | bytes 294920 | tf_op jit(solution)/shard_map/ppermute | solution.py:45
  117.1 5.5 %collective-permute-start.12 = (f32[12288]{0:T(1024)S(1)}, f32[12288]{0:T(1024)S(1)}, u32[]{:S(2)}, u32[]{:S(2)}) collective-permute-start(f32[12288]{0:T(1024)S(1)} %slice_select_fusion.3), channel_id=1, source_target_pairs={{0,8},{4,12},{8,0},{12,4},{1,9},{5,13},{9,1},{13,5},{2,10},{6,14},... | collective-permute-start | bytes 147464 | tf_op jit(solution)/shard_map/ppermute | solution.py:45
  122.6 6.8 %copy-start.5 = (bf16[1,768,768]{2,1,0:T(8,128)(2,1)S(1)}, bf16[1,768,768]{2,1,0:T(8,128)(2,1)}, u32[]{:S(2)}) copy-start(bf16[1,768,768]{2,1,0:T(8,128)(2,1)} %get-tuple-element.16) | copy-start | bytes 3538948
  122.6 5.1 %collective-permute-start.13 = (f32[12288]{0:T(1024)S(1)}, f32[12288]{0:T(1024)S(1)}, u32[]{:S(2)}, u32[]{:S(2)}) collective-permute-start(f32[12288]{0:T(1024)S(1)} %select_add_fusion.1), channel_id=1, source_target_pairs={{0,8},{4,12},{8,0},{12,4},{1,9},{5,13},{9,1},{13,5},{2,10},{6,14},... | collective-permute-start | bytes 147464 | tf_op jit(solution)/shard_map/ppermute | solution.py:53
  127.7 4.7 %collective-permute-start.14 = (f32[24576]{0:T(1024)S(1)}, f32[24576]{0:T(1024)S(1)}, u32[]{:S(2)}, u32[]{:S(2)}) collective-permute-start(f32[24576]{0:T(1024)S(1)} %maximum_select_fusion.4), channel_id=1, source_target_pairs={{0,4},{4,0},{8,12},{12,8},{1,5},{5,1},{9,13},{13,9},{2,6},{6,2},{1... | collective-permute-start | bytes 294920 | tf_op jit(solution)/shard_map/ppermute | solution.py:53
  132.4 1.5 %collective-permute-start.15 = (f32[49152]{0:T(1024)S(1)}, f32[49152]{0:T(1024)S(1)}, u32[]{:S(2)}, u32[]{:S(2)}) collective-permute-start(f32[49152]{0:T(1024)S(1)} %maximum_select_fusion.2), channel_id=1, source_target_pairs={{0,1},{1,0},{2,3},{3,2},{4,5},{5,4},{6,7},{7,6},{8,9},{9,8},{10,11... | collective-permute-start | bytes 589832 | tf_op jit(solution)/shard_map/ppermute | solution.py:53
  (5 other events, 8.7 us)

commit v6 on v3

--- a/solution.py
+++ b/solution.py
@@ -129,14 +129,14 @@
 
 
 def attention_kernel(
-    bias_ref, q_ref, g_ref, k_ref, v_ref, kl_ref, vl_ref, kr_ref, vr_ref,
-    dq_ref, dk_ref, dv_ref, dkl_ref, dvl_ref, dkr_ref, dvr_ref,
+    bias_ref, q_ref, g_ref, k_ref, v_ref, left_ref, right_ref,
+    dq_ref, dk_ref, dv_ref, to_left_ref, to_right_ref,
 ):
     q_a, q_b = q_ref[0, :TILE], q_ref[0, TILE:]
     g_a, g_b = g_ref[0, :TILE], g_ref[0, TILE:]
     k_a, k_b = k_ref[0, :TILE], k_ref[0, TILE:]
     v_a, v_b = v_ref[0, :TILE], v_ref[0, TILE:]
-    k_l, v_l, k_r, v_r = kl_ref[0, 0], vl_ref[0, 0], kr_ref[0, 0], vr_ref[0, 0]
+    k_l, v_l, k_r, v_r = left_ref[0, 0], left_ref[1, 0], right_ref[0, 0], right_ref[1, 0]
     dq_a, dk_a3, dv_a3 = tile_pass(bias_ref, 0, q_a, g_a, (k_l, k_a, k_b), (v_l, v_a, v_b))
     dq_b, dk_b3, dv_b3 = tile_pass(bias_ref, 3, q_b, g_b, (k_a, k_b, k_r), (v_a, v_b, v_r))
     dq_ref[0, :TILE] = dq_a.astype(jnp.bfloat16)
@@ -145,27 +145,26 @@
     dk_ref[0, TILE:] = (dk_a3[2] + dk_b3[1]).astype(jnp.bfloat16)
     dv_ref[0, :TILE] = (dv_a3[1] + dv_b3[0]).astype(jnp.bfloat16)
     dv_ref[0, TILE:] = (dv_a3[2] + dv_b3[1]).astype(jnp.bfloat16)
-    dkl_ref[0] = dk_a3[0].astype(jnp.bfloat16)
-    dvl_ref[0] = dv_a3[0].astype(jnp.bfloat16)
-    dkr_ref[0] = dk_b3[2].astype(jnp.bfloat16)
-    dvr_ref[0] = dv_b3[2].astype(jnp.bfloat16)
-
-
-def attention_backward(bias, chunk, heads, queries, output_gradient, key_matrix, values, halo):
+    to_left_ref[0, 0] = dk_a3[0].astype(jnp.bfloat16)
+    to_left_ref[1, 0] = dv_a3[0].astype(jnp.bfloat16)
+    to_right_ref[0, 0] = dk_b3[2].astype(jnp.bfloat16)
+    to_right_ref[1, 0] = dv_b3[2].astype(jnp.bfloat16)
+
+
+def attention_backward(bias, chunk, heads, queries, output_gradient, key_matrix, values, left, right):
     clip_count, block_len, _ = queries.shape
     whole = pl.BlockSpec((1, block_len, HEAD_SIZE), lambda c, h: (c, 0, h + chunk * heads))
-    rims = [pl.BlockSpec((1, 1, TILE, HEAD_SIZE), lambda c, h, i=i: (i, c, 0, h)) for i in range(4)]
+    rim = pl.BlockSpec((2, 1, TILE, HEAD_SIZE), lambda c, h: (0, c, 0, h))
     out_whole = pl.BlockSpec((1, block_len, HEAD_SIZE), lambda c, h: (c, 0, h))
-    out_rim = pl.BlockSpec((1, TILE, HEAD_SIZE), lambda c, h: (c, 0, h))
     whole_shape = jax.ShapeDtypeStruct((clip_count, block_len, heads * HEAD_SIZE), jnp.bfloat16)
-    rim_shape = jax.ShapeDtypeStruct((clip_count, TILE, heads * HEAD_SIZE), jnp.bfloat16)
+    rim_shape = jax.ShapeDtypeStruct((2, clip_count, TILE, heads * HEAD_SIZE), jnp.bfloat16)
     return pl.pallas_call(
         attention_kernel,
         grid=(clip_count, heads),
-        in_specs=[pl.BlockSpec(memory_space=pltpu.MemorySpace.SMEM)] + [whole] * 4 + rims,
-        out_specs=[out_whole] * 3 + [out_rim] * 4,
-        out_shape=[whole_shape] * 3 + [rim_shape] * 4,
-    )(bias, queries, output_gradient, key_matrix, values, halo, halo, halo, halo)
+        in_specs=[pl.BlockSpec(memory_space=pltpu.MemorySpace.SMEM)] + [whole] * 4 + [rim] * 2,
+        out_specs=[out_whole] * 3 + [rim] * 2,
+        out_shape=[whole_shape] * 3 + [rim_shape] * 2,
+    )(bias, queries, output_gradient, key_matrix, values, left, right)
 
 
 def on_device(
@@ -211,12 +210,11 @@
         right_kv = shifted(
             jnp.stack((key_matrix[:, :TILE, cols], values[:, :TILE, cols]), 0), "seq", -1
         )
-        halo = jnp.concatenate((left_kv, right_kv), 0)
-        dq, dk_own, dv_own, dk_l, dv_l, dk_r, dv_r = attention_backward(
-            bias, chunk, per_chunk, queries, output_gradient, key_matrix, values, halo
+        dq, dk_own, dv_own, to_left, to_right = attention_backward(
+            bias, chunk, per_chunk, queries, output_gradient, key_matrix, values, left_kv, right_kv
         )
-        from_right = shifted(jnp.stack((dk_l, dv_l), 0), "seq", -1)
-        from_left = shifted(jnp.stack((dk_r, dv_r), 0), "seq", 1)
+        from_right = shifted(to_left, "seq", -1)
+        from_left = shifted(to_right, "seq", 1)
         arrived = jnp.concatenate((from_left, from_right), 2).astype(jnp.float32)
         dk = (dk_own.astype(jnp.float32) + arrived[0]).astype(jnp.bfloat16)
         dv = (dv_own.astype(jnp.float32) + arrived[1]).astype(jnp.bfloat16)

time: 133 us -> 130 us (0.977)
  other arithmetic: 10.3 us -> 5.42 us
  waiting for transfers between devices: 60.7 us -> 63.1 us
  starting transfers between devices: 27.4 us -> 25.1 us
    another operation x2 -> x0, other arithmetic: 3.62 us -> none  [the longest x1 2.5 us: on_device(): from_right = shifted(jnp.stack((dk_l, dv_l), 0), 'seq', -1)]
    concatenate x1 -> x0, other arithmetic: 3.26 us -> none  [on_device(): halo = jnp.concatenate((left_kv, right_kv), 0)]
    ppermute x4, waiting for transfers between devices: 44.8 us -> 47.4 us  [shifted(): return lax.ppermute(shard, axis, pairs)]
    ppermute x4, starting transfers between devices: 14.4 us -> 12.2 us  [shifted(): return lax.ppermute(shard, axis, pairs)]
    unnamed x22 -> x20, local copies, waits for them, and re-layouts: 1.71 us -> 2.71 us
  transfers between devices with their start and end apart: 12 -> 12, of which waited for: 11 -> 11; matrix products, arithmetic and copies ran while one was open for 6% -> 7% of each run, Pallas kernels for 0% -> 0%
where the time goes in v6:
time: 130 us; the launch traced here: 129 us
  waiting for transfers between devices  63.1 us (49%)
  starting transfers between devices  25.1 us (19%)
  Pallas kernels  24.8 us (19%)
  local copies, waits for them, and re-layouts  5.71 us (4%)
  other arithmetic  5.42 us (4%)
  matrix products  4.26 us (3%)
    ppermute x4, waiting for transfers between devices, shifted(): return lax.ppermute(shard, axis, pairs)  47.4 us
    pallas_call x1, Pallas kernels, attention_backward(): pl.pallas_call(attention_kernel, grid=(clip_count, heads), in_specs=[pl.B...  24.8 us
    ppermute x4, starting transfers between devices, shifted(): return lax.ppermute(shard, axis, pairs)  12.2 us
    ppermute x3, waiting for transfers between devices, scatter_sum(): lax.ppermute(send, axis, [(i, i ^ step) for i in range(peers)])  6.57 us
    ppermute x3, waiting for transfers between devices, gather_back(): other = lax.ppermute(flat, axis, [(i, i ^ step) for i in range(peers)])  6.31 us
    ppermute x3, starting transfers between devices, scatter_sum(): lax.ppermute(send, axis, [(i, i ^ step) for i in range(peers)])  5.27 us
    ppermute x3, starting transfers between devices, gather_back(): other = lax.ppermute(flat, axis, [(i, i ^ step) for i in range(peers)])  4.6 us
    ppermute x2, starting transfers between devices, butterfly_sum(): other = lax.ppermute(tree, axis, pairs)  3.05 us
  transfers between devices with their start and end apart: 12, of which 11 were waited for; matrix products, arithmetic and copies ran while one was open for 7% of the time, Pallas kernels for 0%

profile of v6, /device:TPU:0, one launch (start us, length us, event | category | flops | bytes accessed | tf_op | source)
XLA Modules:
  0.0 129.3 jit_solution(13309468546718865144)
XLA Ops:
  0.6 1.8 %slice_bitcast_fusion.2 = (bf16[1,1,384,768]{3,2,1,0:T(8,128)(2,1)S(1)}, bf16[1,1,384,768]{3,2,1,0:T(8,128)(2,1)S(1)}, bf16[1,1,384,768]{3,2,1,0:T(8,128)(2,1)S(1)}, bf16[1,1,384,768]{3,2,1,0:T(8,128)(2,1)S(1)}) fusion(bf16[1,768,768]{2,1,0:T(8,128)(2,1)} %v_ref.1, bf16[1,768,768]{2,1,0:T(8,128)(2,1)} %k_ref.1), kind=kLoop, calls=%fused_computation.23 | loop fusion | bytes 4718592 | tf_op jit(solution)/shard_map/stack | solution.py:211
  3.6 5.0 %collective-permute-start = (bf16[2,1,384,768]{3,2,1,0:T(8,128)(2,1)}, bf16[2,1,384,768]{3,2,1,0:T(8,128)(2,1)S(1)}, u32[]{:S(2)}, u32[]{:S(2)}) collective-permute-start(bf16[2,1,384,768]{3,2,1,0:T(8,128)(2,1)} %pad_maximum_fusion), channel_id=1, source_target_pairs={{0,4},{4,8},{8,12},{1,5},{5,9},{9,13},{2,6},{6,10},{10,14},{3,7},{... | collective-permute-start | bytes 3538952 | tf_op jit(solution)/shard_map/ppermute | solution.py:21
  9.8 1.3 collective-permute-start.1
  12.2 21.9 %collective-permute-done.left_ref = bf16[2,1,384,768]{3,2,1,0:T(8,128)(2,1)S(1)} collective-permute-done((bf16[2,1,384,768]{3,2,1,0:T(8,128)(2,1)}, bf16[2,1,384,768]{3,2,1,0:T(8,128)(2,1)S(1)}, u32[]{:S(2)}, u32[]{:S(2)}) %collective-permute-start) | collective-permute-done | bytes 1179680 | tf_op jit(solution)/shard_map/ppermute | solution.py:21
  34.1 5.2 %collective-permute-done.1.right_ref = bf16[2,1,384,768]{3,2,1,0:T(8,128)(2,1)S(1)} collective-permute-done((bf16[2,1,384,768]{3,2,1,0:T(8,128)(2,1)}, bf16[2,1,384,768]{3,2,1,0:T(8,128)(2,1)S(1)}, u32[]{:S(2)}, u32[]{:S(2)}) %collective-permute-start.1) | collective-permute-done | bytes 1179680 | tf_op jit(solution)/shard_map/ppermute | solution.py:21
  40.3 24.8 %shard_map.128 = (bf16[1,768,768]{2,1,0:T(8,128)(2,1)}, bf16[1,768,768]{2,1,0:T(8,128)(2,1)}, bf16[1,768,768]{2,1,0:T(8,128)(2,1)}, bf16[2,1,384,768]{3,2,1,0:T(8,128)(2,1)}, bf16[2,1,384,768]{3,2,1,0:T(8,128)(2,1)}) custom-call(f32[6]{0:T(128)} %and_select_fusion.bias_ref, bf16[1,768,768]{2,1,0:T(8,128)(2,1)} %q_ref.1, bf16[1,768,768]{2,1,0:T(8,128)(2,1)} %g_ref.1, ...), custom_call_target="tpu_custom_call" | custom-call | tf_op jit(solution)/shard_map/pallas_call | solution.py:161
  65.1 1.3 collective-permute-start.3
  66.4 4.6 %collective-permute-start.2 = (bf16[2,1,384,768]{3,2,1,0:T(8,128)(2,1)}, bf16[2,1,384,768]{3,2,1,0:T(8,128)(2,1)S(1)}, u32[]{:S(2)}, u32[]{:S(2)}) collective-permute-start(bf16[2,1,384,768]{3,2,1,0:T(8,128)(2,1)} %get-tuple-element.12), channel_id=1, source_target_pairs={{0,4},{4,8},{8,12},{1,5},{5,9},{9,13},{2,6},{6,10},{10,14},{3,7},{... | collective-permute-start | bytes 3538952 | tf_op jit(solution)/shard_map/ppermute | solution.py:21
  71.0 2.1 %fusion.15 = f32[1,768,64]{1,2,0:T(8,128)} fusion(bf16[768,64]{0,1:T(8,128)(2,1)} %param.14, bf16[1,768,768]{2,1,0:T(8,128)(2,1)S(1)} %copy-done), kind=kOutput, calls=%fused_computation.18 | convolution fusion | flops 75497472 | bytes 1474560 | tf_op jit(solution)/shard_map/pqg,gv->pqv/dot_general | solution.py:185
  73.1 1.5 %collective-permute-start.4 = (f32[1,768,64]{1,2,0:T(8,128)}, f32[1,768,64]{1,2,0:T(8,128)}, u32[]{:S(2)}, u32[]{:S(2)}) collective-permute-start(f32[1,768,64]{1,2,0:T(8,128)} %fusion.15), channel_id=1, source_target_pairs={{0,2},{2,0},{1,3},{3,1},{4,6},{6,4},{5,7},{7,5},{8,10},{10,8},{9,1... | collective-permute-start | bytes 589832 | tf_op jit(solution)/shard_map/ppermute | solution.py:31
  74.6 19.1 %collective-permute-done.3 = bf16[2,1,384,768]{3,2,1,0:T(8,128)(2,1)S(1)} collective-permute-done((bf16[2,1,384,768]{3,2,1,0:T(8,128)(2,1)}, bf16[2,1,384,768]{3,2,1,0:T(8,128)(2,1)S(1)}, u32[]{:S(2)}, u32[]{:S(2)}) %collective-permute-start.3) | collective-permute-done | bytes 1179680 | tf_op jit(solution)/shard_map/ppermute | solution.py:21
  93.7 1.3 collective-permute-done.2
  95.4 1.6 %fusion.1 = (bf16[1,768,768]{2,1,0:T(8,128)(2,1)S(1)}, bf16[1,768,768]{2,1,0:T(8,128)(2,1)}) fusion(f32[2,1,768,768]{3,2,1,0:T(8,128)S(1)} %maximum_convert_fusion, bf16[1,768,768]{2,1,0:T(8,128)(2,1)S(1)} %copy-done.3, bf16[1,768,768]{2,1,0:T(8,128)(2,1)S(1)} %copy-done.2), kind=kLoop, calls=%fused_computation.2 | loop fusion | flops 3538944 | bytes 9437184 | tf_op jit(solution)/shard_map/convert_element_type | solution.py:220
  97.5 1.5 %collective-permute-start.5 = (f32[1,768,64]{1,2,0:T(8,128)S(1)}, f32[1,768,64]{1,2,0:T(8,128)S(1)}, u32[]{:S(2)}, u32[]{:S(2)}) collective-permute-start(f32[1,768,64]{1,2,0:T(8,128)S(1)} %fusion.12), channel_id=1, source_target_pairs={{0,2},{2,0},{1,3},{3,1},{4,6},{6,4},{5,7},{7,5},{8,10},{10,8},{9,1... | collective-permute-start | bytes 589832 | tf_op jit(solution)/shard_map/ppermute | solution.py:31
  99.0 1.4 %fusion.18 = f32[768,64]{0,1:T(8,128)S(1)} fusion(bf16[1,768,768]{2,1,0:T(8,128)(2,1)S(1)} %get-tuple-element.25, f32[1,768,64]{1,2,0:T(8,128)} %fusion.15, f32[1,768,64]{1,2,0:T(8,128)} %collective-permute-done.4), kind=kOutput, calls=%fused_computation.19 | convolution fusion | flops 75644928 | bytes 1769472 | tf_op jit(solution)/shard_map/igb,igu->bu/dot_general | solution.py:233
  100.4 2.8 %collective-permute-done.5 = f32[1,768,64]{1,2,0:T(8,128)S(1)} collective-permute-done((f32[1,768,64]{1,2,0:T(8,128)S(1)}, f32[1,768,64]{1,2,0:T(8,128)S(1)}, u32[]{:S(2)}, u32[]{:S(2)}) %collective-permute-start.5) | collective-permute-done | bytes 196640 | tf_op jit(solution)/shard_map/ppermute | solution.py:31
  105.4 2.4 %collective-permute-start.7 = (f32[24576]{0:T(1024)S(1)}, f32[24576]{0:T(1024)S(1)}, u32[]{:S(2)}, u32[]{:S(2)}) collective-permute-start(f32[24576]{0:T(1024)S(1)} %slice_select_fusion), channel_id=1, source_target_pairs={{0,4},{4,0},{8,12},{12,8},{1,5},{5,1},{9,13},{13,9},{2,6},{6,2},{1... | collective-permute-start | bytes 294920 | tf_op jit(solution)/shard_map/ppermute | solution.py:45
  107.8 3.1 %collective-permute-done.7 = f32[24576]{0:T(1024)S(1)} collective-permute-done((f32[24576]{0:T(1024)S(1)}, f32[24576]{0:T(1024)S(1)}, u32[]{:S(2)}, u32[]{:S(2)}) %collective-permute-start.7) | collective-permute-done | bytes 98336 | tf_op jit(solution)/shard_map/ppermute | solution.py:45
  111.0 2.8 %collective-permute-start.8 = (f32[12288]{0:T(1024)S(1)}, f32[12288]{0:T(1024)S(1)}, u32[]{:S(2)}, u32[]{:S(2)}) collective-permute-start(f32[12288]{0:T(1024)S(1)} %slice_select_fusion.1), channel_id=1, source_target_pairs={{0,8},{4,12},{8,0},{12,4},{1,9},{5,13},{9,1},{13,5},{2,10},{6,14},... | collective-permute-start | bytes 147464 | tf_op jit(solution)/shard_map/ppermute | solution.py:45
  113.7 2.3 %collective-permute-done.8 = f32[12288]{0:T(1024)S(1)} collective-permute-done((f32[12288]{0:T(1024)S(1)}, f32[12288]{0:T(1024)S(1)}, u32[]{:S(2)}, u32[]{:S(2)}) %collective-permute-start.8) | collective-permute-done | bytes 49184 | tf_op jit(solution)/shard_map/ppermute | solution.py:45
  116.1 2.7 %collective-permute-start.9 = (f32[12288]{0:T(1024)S(1)}, f32[12288]{0:T(1024)S(1)}, u32[]{:S(2)}, u32[]{:S(2)}) collective-permute-start(f32[12288]{0:T(1024)S(1)} %select_add_fusion.1), channel_id=1, source_target_pairs={{0,8},{4,12},{8,0},{12,4},{1,9},{5,13},{9,1},{13,5},{2,10},{6,14},... | collective-permute-start | bytes 147464 | tf_op jit(solution)/shard_map/ppermute | solution.py:53
  118.8 2.3 %collective-permute-done.9 = f32[12288]{0:T(1024)S(1)} collective-permute-done((f32[12288]{0:T(1024)S(1)}, f32[12288]{0:T(1024)S(1)}, u32[]{:S(2)}, u32[]{:S(2)}) %collective-permute-start.9) | collective-permute-done | bytes 49184 | tf_op jit(solution)/shard_map/ppermute | solution.py:53
  121.1 1.8 %collective-permute-start.10 = (f32[24576]{0:T(1024)S(1)}, f32[24576]{0:T(1024)S(1)}, u32[]{:S(2)}, u32[]{:S(2)}) collective-permute-start(f32[24576]{0:T(1024)S(1)} %maximum_select_fusion.4), channel_id=1, source_target_pairs={{0,4},{4,0},{8,12},{12,8},{1,5},{5,1},{9,13},{13,9},{2,6},{6,2},{1... | collective-permute-start | bytes 294920 | tf_op jit(solution)/shard_map/ppermute | solution.py:53
  123.1 2.7 %collective-permute-done.10 = f32[24576]{0:T(1024)S(1)} collective-permute-done((f32[24576]{0:T(1024)S(1)}, f32[24576]{0:T(1024)S(1)}, u32[]{:S(2)}, u32[]{:S(2)}) %collective-permute-start.10) | collective-permute-done | bytes 98336 | tf_op jit(solution)/shard_map/ppermute | solution.py:53
  (57 shorter events, 11.0 us)
Async XLA Ops:
  0.6 70.4 %copy-start = (bf16[1,768,768]{2,1,0:T(8,128)(2,1)S(1)}, bf16[1,768,768]{2,1,0:T(8,128)(2,1)}, u32[]{:S(2)}) copy-start(bf16[1,768,768]{2,1,0:T(8,128)(2,1)} %param.13) | copy-start | bytes 3538948
  3.6 30.4 %collective-permute-start = (bf16[2,1,384,768]{3,2,1,0:T(8,128)(2,1)}, bf16[2,1,384,768]{3,2,1,0:T(8,128)(2,1)S(1)}, u32[]{:S(2)}, u32[]{:S(2)}) collective-permute-start(bf16[2,1,384,768]{3,2,1,0:T(8,128)(2,1)} %pad_maximum_fusion), channel_id=1, source_target_pairs={{0,4},{4,8},{8,12},{1,5},{5,9},{9,13},{2,6},{6,10},{10,14},{3,7},{... | collective-permute-start | bytes 3538952 | tf_op jit(solution)/shard_map/ppermute | solution.py:21
  8.6 2.7 %copy-start.7 = (s32[8,3]{0,1:T(4,128)S(1)}, s32[8,3]{0,1:T(4,128)}, u32[]{:S(2)}) copy-start(s32[8,3]{0,1:T(4,128)} %param.16) | copy-start | bytes 292
  8.6 2.8 %copy-start.8 = (s32[8]{0:T(128)S(1)}, s32[8]{0:T(128)}, u32[]{:S(2)}) copy-start(s32[8]{0:T(128)} %param.17) | copy-start | bytes 100
  9.8 29.5 %collective-permute-start.1 = (bf16[2,1,384,768]{3,2,1,0:T(8,128)(2,1)}, bf16[2,1,384,768]{3,2,1,0:T(8,128)(2,1)S(1)}, u32[]{:S(2)}, u32[]{:S(2)}) collective-permute-start(bf16[2,1,384,768]{3,2,1,0:T(8,128)(2,1)} %pad_maximum_fusion.1), channel_id=1, source_target_pairs={{4,0},{8,4},{12,8},{5,1},{9,5},{13,9},{6,2},{10,6},{14,10},{7,3},{... | collective-permute-start | bytes 3538952 | tf_op jit(solution)/shard_map/ppermute | solution.py:21
  34.1 5.2 %copy-start.4 = (bf16[2,1,384,768]{3,2,1,0:T(8,128)(2,1)}, bf16[2,1,384,768]{3,2,1,0:T(8,128)(2,1)S(1)}, u32[]{:S(2)}) copy-start(bf16[2,1,384,768]{3,2,1,0:T(8,128)(2,1)S(1)} %collective-permute-done.left_ref) | copy-start | bytes 3538948
  39.3 1.0 copy-start.5
  65.1 28.6 %collective-permute-start.3 = (bf16[2,1,384,768]{3,2,1,0:T(8,128)(2,1)}, bf16[2,1,384,768]{3,2,1,0:T(8,128)(2,1)S(1)}, u32[]{:S(2)}, u32[]{:S(2)}) collective-permute-start(bf16[2,1,384,768]{3,2,1,0:T(8,128)(2,1)} %get-tuple-element.13), channel_id=1, source_target_pairs={{4,0},{8,4},{12,8},{5,1},{9,5},{13,9},{6,2},{10,6},{14,10},{7,3},{... | collective-permute-start | bytes 3538952 | tf_op jit(solution)/shard_map/ppermute | solution.py:21
  66.4 28.6 %collective-permute-start.2 = (bf16[2,1,384,768]{3,2,1,0:T(8,128)(2,1)}, bf16[2,1,384,768]{3,2,1,0:T(8,128)(2,1)S(1)}, u32[]{:S(2)}, u32[]{:S(2)}) collective-permute-start(bf16[2,1,384,768]{3,2,1,0:T(8,128)(2,1)} %get-tuple-element.12), channel_id=1, source_target_pairs={{0,4},{4,8},{8,12},{1,5},{5,9},{9,13},{2,6},{6,10},{10,14},{3,7},{... | collective-permute-start | bytes 3538952 | tf_op jit(solution)/shard_map/ppermute | solution.py:21
  73.1 25.9 %collective-permute-start.4 = (f32[1,768,64]{1,2,0:T(8,128)}, f32[1,768,64]{1,2,0:T(8,128)}, u32[]{:S(2)}, u32[]{:S(2)}) collective-permute-start(f32[1,768,64]{1,2,0:T(8,128)} %fusion.15), channel_id=1, source_target_pairs={{0,2},{2,0},{1,3},{3,1},{4,6},{6,4},{5,7},{7,5},{8,10},{10,8},{9,1... | collective-permute-start | bytes 589832 | tf_op jit(solution)/shard_map/ppermute | solution.py:31
  74.6 20.7 %copy-start.2 = (bf16[1,768,768]{2,1,0:T(8,128)(2,1)S(1)}, bf16[1,768,768]{2,1,0:T(8,128)(2,1)}, u32[]{:S(2)}) copy-start(bf16[1,768,768]{2,1,0:T(8,128)(2,1)} %get-tuple-element.11) | copy-start | bytes 3538948
  74.6 20.7 %copy-start.3 = (bf16[1,768,768]{2,1,0:T(8,128)(2,1)S(1)}, bf16[1,768,768]{2,1,0:T(8,128)(2,1)}, u32[]{:S(2)}) copy-start(bf16[1,768,768]{2,1,0:T(8,128)(2,1)} %get-tuple-element.14) | copy-start | bytes 3538948
  95.4 1.6 %copy-start.6 = (bf16[64,768]{1,0:T(8,128)(2,1)S(1)}, bf16[64,768]{1,0:T(8,128)(2,1)}, u32[]{:S(2)}) copy-start(bf16[64,768]{1,0:T(8,128)(2,1)} %param.15) | copy-start | bytes 294916
  97.0 3.4 %copy-start.1 = (bf16[1,768,768]{2,1,0:T(8,128)(2,1)}, bf16[1,768,768]{2,1,0:T(8,128)(2,1)S(1)}, u32[]{:S(2)}) copy-start(bf16[1,768,768]{2,1,0:T(8,128)(2,1)S(1)} %get-tuple-element.25) | copy-start | bytes 3538948
  97.5 5.7 %collective-permute-start.5 = (f32[1,768,64]{1,2,0:T(8,128)S(1)}, f32[1,768,64]{1,2,0:T(8,128)S(1)}, u32[]{:S(2)}, u32[]{:S(2)}) collective-permute-start(f32[1,768,64]{1,2,0:T(8,128)S(1)} %fusion.12), channel_id=1, source_target_pairs={{0,2},{2,0},{1,3},{3,1},{4,6},{6,4},{5,7},{7,5},{8,10},{10,8},{9,1... | collective-permute-start | bytes 589832 | tf_op jit(solution)/shard_map/ppermute | solution.py:31
  103.8 1.5 %collective-permute-start.6 = (f32[49152]{0:T(1024)S(1)}, f32[49152]{0:T(1024)S(1)}, u32[]{:S(2)}, u32[]{:S(2)}) collective-permute-start(f32[49152]{0:T(1024)S(1)} %select_n.88), channel_id=1, source_target_pairs={{0,1},{1,0},{2,3},{3,2},{4,5},{5,4},{6,7},{7,6},{8,9},{9,8},{10,11... | collective-permute-start | bytes 589832 | tf_op jit(solution)/shard_map/ppermute | solution.py:45
  105.4 5.5 %collective-permute-start.7 = (f32[24576]{0:T(1024)S(1)}, f32[24576]{0:T(1024)S(1)}, u32[]{:S(2)}, u32[]{:S(2)}) collective-permute-start(f32[24576]{0:T(1024)S(1)} %slice_select_fusion), channel_id=1, source_target_pairs={{0,4},{4,0},{8,12},{12,8},{1,5},{5,1},{9,13},{13,9},{2,6},{6,2},{1... | collective-permute-start | bytes 294920 | tf_op jit(solution)/shard_map/ppermute | solution.py:45
  111.0 5.1 %collective-permute-start.8 = (f32[12288]{0:T(1024)S(1)}, f32[12288]{0:T(1024)S(1)}, u32[]{:S(2)}, u32[]{:S(2)}) collective-permute-start(f32[12288]{0:T(1024)S(1)} %slice_select_fusion.1), channel_id=1, source_target_pairs={{0,8},{4,12},{8,0},{12,4},{1,9},{5,13},{9,1},{13,5},{2,10},{6,14},... | collective-permute-start | bytes 147464 | tf_op jit(solution)/shard_map/ppermute | solution.py:45
  116.1 5.1 %collective-permute-start.9 = (f32[12288]{0:T(1024)S(1)}, f32[12288]{0:T(1024)S(1)}, u32[]{:S(2)}, u32[]{:S(2)}) collective-permute-start(f32[12288]{0:T(1024)S(1)} %select_add_fusion.1), channel_id=1, source_target_pairs={{0,8},{4,12},{8,0},{12,4},{1,9},{5,13},{9,1},{13,5},{2,10},{6,14},... | collective-permute-start | bytes 147464 | tf_op jit(solution)/shard_map/ppermute | solution.py:53
  121.1 4.7 %collective-permute-start.10 = (f32[24576]{0:T(1024)S(1)}, f32[24576]{0:T(1024)S(1)}, u32[]{:S(2)}, u32[]{:S(2)}) collective-permute-start(f32[24576]{0:T(1024)S(1)} %maximum_select_fusion.4), channel_id=1, source_target_pairs={{0,4},{4,0},{8,12},{12,8},{1,5},{5,1},{9,13},{13,9},{2,6},{6,2},{1... | collective-permute-start | bytes 294920 | tf_op jit(solution)/shard_map/ppermute | solution.py:53
  125.8 1.5 %collective-permute-start.11 = (f32[49152]{0:T(1024)S(1)}, f32[49152]{0:T(1024)S(1)}, u32[]{:S(2)}, u32[]{:S(2)}) collective-permute-start(f32[49152]{0:T(1024)S(1)} %maximum_select_fusion.2), channel_id=1, source_target_pairs={{0,1},{1,0},{2,3},{3,2},{4,5},{5,4},{6,7},{7,6},{8,9},{9,8},{10,11... | collective-permute-start | bytes 589832 | tf_op jit(solution)/shard_map/ppermute | solution.py:53

commit v7 on v6

--- a/solution.py
+++ b/solution.py
@@ -197,7 +197,7 @@
     bias = jnp.where(allowed, 0.0, masked_score).astype(jnp.float32)
 
     local_heads = queries.shape[2] // HEAD_SIZE
-    chunks = 1
+    chunks = 2 if local_heads % 2 == 0 else 1
     per_chunk = local_heads // chunks
     outs = []
     for chunk in range(chunks):

time: 130 us -> 118 us (0.908)
  waiting for transfers between devices: 63.1 us -> 34.8 us
  other arithmetic: 5.42 us -> 11.9 us
  local copies, waits for them, and re-layouts: 5.71 us -> 10.2 us
  starting transfers between devices: 25.1 us -> 28.9 us
  Pallas kernels: 24.8 us -> 26.8 us
    ppermute x4 -> x8, waiting for transfers between devices: 47.4 us -> 13.7 us  [shifted(): return lax.ppermute(shard, axis, pairs)]
    ppermute x4 -> x8, starting transfers between devices: 12.2 us -> 24.3 us  [shifted(): return lax.ppermute(shard, axis, pairs)]
    ppermute x3, starting transfers between devices: 4.6 us -> 0.23 us  [gather_back(): other = lax.ppermute(flat, axis, [(i, i ^ step) for i in range(peers)])]
    ppermute x3, waiting for transfers between devices: 6.57 us -> 10.6 us  [scatter_sum(): lax.ppermute(send, axis, [(i, i ^ step) for i in range(peers)])]
    ppermute x3, starting transfers between devices: 5.27 us -> 1.35 us  [scatter_sum(): lax.ppermute(send, axis, [(i, i ^ step) for i in range(peers)])]
    unnamed x20 -> x30, local copies, waits for them, and re-layouts: 2.71 us -> 6.43 us
    concatenate x0 -> x3, other arithmetic: none -> 3.38 us  [on_device(): jnp.concatenate([o[i] for o in outs], 2)]
    pallas_call x1 -> x2, Pallas kernels: 24.8 us -> 26.8 us  [attention_backward(): pl.pallas_call(attention_kernel, grid=(clip_count, heads), in_specs=[pl.B...]
  transfers between devices with their start and end apart: 12 -> 16, of which waited for: 11 -> 11; matrix products, arithmetic and copies ran while one was open for 7% -> 12% of each run, Pallas kernels for 0% -> 23%
where the time goes in v7:
time: 118 us
  waiting for transfers between devices  34.8 us (29%)
  starting transfers between devices  28.9 us (24%)
  Pallas kernels  26.8 us (23%)
  other arithmetic  11.9 us (10%)
  local copies, waits for them, and re-layouts  10.2 us (9%)
  matrix products  4.25 us (4%)
    pallas_call x2, Pallas kernels, attention_backward(): pl.pallas_call(attention_kernel, grid=(clip_count, heads), in_specs=[pl.B...  26.8 us
    ppermute x8, starting transfers between devices, shifted(): return lax.ppermute(shard, axis, pairs)  24.3 us
    ppermute x8, waiting for transfers between devices, shifted(): return lax.ppermute(shard, axis, pairs)  13.7 us
    ppermute x3, waiting for transfers between devices, scatter_sum(): lax.ppermute(send, axis, [(i, i ^ step) for i in range(peers)])  10.6 us
    ppermute x3, waiting for transfers between devices, gather_back(): other = lax.ppermute(flat, axis, [(i, i ^ step) for i in range(peers)])  7.67 us
    unnamed x30, local copies, waits for them, and re-layouts  6.43 us
    concatenate x3, other arithmetic, on_device(): jnp.concatenate([o[i] for o in outs], 2)  3.38 us
    ppermute x2, starting transfers between devices, butterfly_sum(): other = lax.ppermute(tree, axis, pairs)  3.01 us
  transfers between devices with their start and end apart: 16, of which 11 were waited for; matrix products, arithmetic and copies ran while one was open for 12% of the time, Pallas kernels for 23%

profile of v7, /device:TPU:0, one launch (start us, length us, event | category | flops | bytes accessed | tf_op | source)
XLA Modules:
  0.0 117.9 jit_solution(7564300624410342087)
XLA Ops:
  0.6 1.9 %slice_bitcast_fusion.9 = (bf16[1,1,384,384]{3,2,1,0:T(8,128)(2,1)S(1)}, bf16[1,1,384,384]{3,2,1,0:T(8,128)(2,1)S(1)}, bf16[1,1,384,384]{3,2,1,0:T(8,128)(2,1)S(...) fusion(bf16[1,768,768]{2,1,0:T(8,128)(2,1)} %v_ref.3, ...), kind=kLoop, calls=%fused_computation.41 | loop fusion | bytes 4718592 | tf_op jit(solution)/shard_map/stack | solution.py:211
  3.5 5.0 %collective-permute-start = (bf16[2,1,384,384]{3,2,1,0:T(8,128)(2,1)}, bf16[2,1,384,384]{3,2,1,0:T(8,128)(2,1)S(1)}, u32[]{:S(2)}, u32[]{:S(2)}) collective-permute-start(bf16[2,1,384,384]{3,2,1,0:T(8,128)(2,1)} %pad_maximum_fusion.3), channel_id=1, source_target_pairs={{0,4},{4,8},{8,12},{1,5},{5,9},{9,13},{2,6},{6,10},{10,14},{3,7},{... | collective-permute-start | bytes 1769480 | tf_op jit(solution)/shard_map/ppermute | solution.py:21
  13.7 5.2 %collective-permute-start.2 = (bf16[2,1,384,384]{3,2,1,0:T(8,128)(2,1)}, bf16[2,1,384,384]{3,2,1,0:T(8,128)(2,1)S(1)}, u32[]{:S(2)}, u32[]{:S(2)}) collective-permute-start(bf16[2,1,384,384]{3,2,1,0:T(8,128)(2,1)} %pad_maximum_fusion.5), channel_id=1, source_target_pairs={{0,4},{4,8},{8,12},{1,5},{5,9},{9,13},{2,6},{6,10},{10,14},{3,7},{... | collective-permute-start | bytes 1769480 | tf_op jit(solution)/shard_map/ppermute | solution.py:21
  22.4 5.3 %collective-permute-done.1.right_ref = bf16[2,1,384,384]{3,2,1,0:T(8,128)(2,1)S(1)} collective-permute-done((bf16[2,1,384,384]{3,2,1,0:T(8,128)(2,1)}, bf16[2,1,384,384]{3,2,1,0:T(8,128)(2,1)S(1)}, u32[]{:S(2)}, u32[]{:S(2)}) %collective-permute-start.1) | collective-permute-done | bytes 589856 | tf_op jit(solution)/shard_map/ppermute | solution.py:21
  28.5 13.4 %shard_map.128 = (bf16[1,768,384]{2,1,0:T(8,128)(2,1)}, bf16[1,768,384]{2,1,0:T(8,128)(2,1)}, bf16[1,768,384]{2,1,0:T(8,128)(2,1)}, bf16[2,1,384,384]{3,2,1,0:T(8,128)(2,1)}, bf16[2,1,384,384]{3,2,1,0:T(8,128)(2,1)}) custom-call(f32[6]{0:T(128)} %and_select_fusion.bias_ref, bf16[1,768,768]{2,1,0:T(8,128)(2,1)} %q_ref.3, bf16[1,768,768]{2,1,0:T(8,128)(2,1)} %g_ref.3, ...), custom_call_target="tpu_custom_call" | custom-call | tf_op jit(solution)/shard_map/pallas_call | solution.py:161
  41.9 3.5 %collective-permute-start.4 = (bf16[2,1,384,384]{3,2,1,0:T(8,128)(2,1)}, bf16[2,1,384,384]{3,2,1,0:T(8,128)(2,1)S(1)}, u32[]{:S(2)}, u32[]{:S(2)}) collective-permute-start(bf16[2,1,384,384]{3,2,1,0:T(8,128)(2,1)} %get-tuple-element.18), channel_id=1, source_target_pairs={{0,4},{4,8},{8,12},{1,5},{5,9},{9,13},{2,6},{6,10},{10,14},{3,7},{... | collective-permute-start | bytes 1769480 | tf_op jit(solution)/shard_map/ppermute | solution.py:21
  45.4 1.3 %collective-permute-start.5 = (bf16[2,1,384,384]{3,2,1,0:T(8,128)(2,1)}, bf16[2,1,384,384]{3,2,1,0:T(8,128)(2,1)S(1)}, u32[]{:S(2)}, u32[]{:S(2)}) collective-permute-start(bf16[2,1,384,384]{3,2,1,0:T(8,128)(2,1)} %get-tuple-element.19), channel_id=1, source_target_pairs={{4,0},{8,4},{12,8},{5,1},{9,5},{13,9},{6,2},{10,6},{14,10},{7,3},{... | collective-permute-start | bytes 1769480 | tf_op jit(solution)/shard_map/ppermute | solution.py:21
  48.4 13.4 %shard_map.129 = (bf16[1,768,384]{2,1,0:T(8,128)(2,1)}, bf16[1,768,384]{2,1,0:T(8,128)(2,1)}, bf16[1,768,384]{2,1,0:T(8,128)(2,1)}, bf16[2,1,384,384]{3,2,1,0:T(8,128)(2,1)}, bf16[2,1,384,384]{3,2,1,0:T(8,128)(2,1)}) custom-call(f32[6]{0:T(128)} %and_select_fusion.bias_ref, bf16[1,768,768]{2,1,0:T(8,128)(2,1)} %q_ref.3, bf16[1,768,768]{2,1,0:T(8,128)(2,1)} %g_ref.3, ...), custom_call_target="tpu_custom_call" | custom-call | tf_op jit(solution)/shard_map/pallas_call | solution.py:161
  61.8 5.4 %collective-permute-start.6 = (bf16[2,1,384,384]{3,2,1,0:T(8,128)(2,1)}, bf16[2,1,384,384]{3,2,1,0:T(8,128)(2,1)}, u32[]{:S(2)}, u32[]{:S(2)}) collective-permute-start(bf16[2,1,384,384]{3,2,1,0:T(8,128)(2,1)} %get-tuple-element.21), channel_id=1, source_target_pairs={{0,4},{4,8},{8,12},{1,5},{5,9},{9,13},{2,6},{6,10},{10,14},{3,7},{... | collective-permute-start | bytes 1769480 | tf_op jit(solution)/shard_map/ppermute | solution.py:21
  67.2 1.5 %collective-permute-start.7 = (bf16[2,1,384,384]{3,2,1,0:T(8,128)(2,1)}, bf16[2,1,384,384]{3,2,1,0:T(8,128)(2,1)}, u32[]{:S(2)}, u32[]{:S(2)}) collective-permute-start(bf16[2,1,384,384]{3,2,1,0:T(8,128)(2,1)} %get-tuple-element.22), channel_id=1, source_target_pairs={{4,0},{8,4},{12,8},{5,1},{9,5},{13,9},{6,2},{10,6},{14,10},{7,3},{... | collective-permute-start | bytes 1769480 | tf_op jit(solution)/shard_map/ppermute | solution.py:21
  68.6 2.1 %fusion.19 = f32[1,768,64]{1,2,0:T(8,128)} fusion(bf16[768,64]{0,1:T(8,128)(2,1)} %param.14, bf16[1,768,768]{2,1,0:T(8,128)(2,1)S(1)} %copy-done), kind=kOutput, calls=%fused_computation.26 | convolution fusion | flops 75497472 | bytes 1474560 | tf_op jit(solution)/shard_map/pqg,gv->pqv/dot_general | solution.py:185
  70.7 1.5 %collective-permute-start.8 = (f32[1,768,64]{1,2,0:T(8,128)}, f32[1,768,64]{1,2,0:T(8,128)}, u32[]{:S(2)}, u32[]{:S(2)}) collective-permute-start(f32[1,768,64]{1,2,0:T(8,128)} %fusion.19), channel_id=1, source_target_pairs={{0,2},{2,0},{1,3},{3,1},{4,6},{6,4},{5,7},{7,5},{8,10},{10,8},{9,1... | collective-permute-start | bytes 589832 | tf_op jit(solution)/shard_map/ppermute | solution.py:31
  73.8 2.2 %collective-permute-done.6 = bf16[2,1,384,384]{3,2,1,0:T(8,128)(2,1)} collective-permute-done((bf16[2,1,384,384]{3,2,1,0:T(8,128)(2,1)}, bf16[2,1,384,384]{3,2,1,0:T(8,128)(2,1)}, u32[]{:S(2)}, u32[]{:S(2)}) %collective-permute-start.6) | collective-permute-done | bytes 589856 | tf_op jit(solution)/shard_map/ppermute | solution.py:21
  76.0 4.9 %collective-permute-done.7 = bf16[2,1,384,384]{3,2,1,0:T(8,128)(2,1)} collective-permute-done((bf16[2,1,384,384]{3,2,1,0:T(8,128)(2,1)}, bf16[2,1,384,384]{3,2,1,0:T(8,128)(2,1)}, u32[]{:S(2)}, u32[]{:S(2)}) %collective-permute-start.7) | collective-permute-done | bytes 589856 | tf_op jit(solution)/shard_map/ppermute | solution.py:21
  81.0 1.4 %maximum_convert_fusion.1 = f32[2,1,768,384]{3,2,1,0:T(8,128)S(1)} fusion(bf16[2,1,384,384]{3,2,1,0:T(8,128)(2,1)} %collective-permute-done.7, bf16[2,1,384,384]{3,2,1,0:T(8,128)(2,1)} %collective-permute-done.6), kind=kLoop, calls=%fused_computation.14 | loop fusion | flops 2359296 | bytes 3538944 | tf_op jit(solution)/shard_map/convert_element_type | solution.py:218
  84.1 1.5 %collective-permute-start.9 = (f32[1,768,64]{1,2,0:T(8,128)S(1)}, f32[1,768,64]{1,2,0:T(8,128)S(1)}, u32[]{:S(2)}, u32[]{:S(2)}) collective-permute-start(f32[1,768,64]{1,2,0:T(8,128)S(1)} %fusion.16), channel_id=1, source_target_pairs={{0,2},{2,0},{1,3},{3,1},{4,6},{6,4},{5,7},{7,5},{8,10},{10,8},{9,1... | collective-permute-start | bytes 589832 | tf_op jit(solution)/shard_map/ppermute | solution.py:31
  85.6 1.4 %fusion.22 = f32[768,64]{0,1:T(8,128)S(1)} fusion(bf16[1,768,768]{2,1,0:T(8,128)(2,1)S(1)} %pad_maximum_fusion.2, f32[1,768,64]{1,2,0:T(8,128)} %fusion.19, f32[1,768,64]{1,2,0:T(8,128)} %collective-permute-done.8), kind=kOutput, calls=%fused_computation.27 | convolution fusion | flops 75644928 | bytes 1769472 | tf_op jit(solution)/shard_map/igb,igu->bu/dot_general | solution.py:233
  87.0 2.8 %collective-permute-done.9 = f32[1,768,64]{1,2,0:T(8,128)S(1)} collective-permute-done((f32[1,768,64]{1,2,0:T(8,128)S(1)}, f32[1,768,64]{1,2,0:T(8,128)S(1)}, u32[]{:S(2)}, u32[]{:S(2)}) %collective-permute-start.9) | collective-permute-done | bytes 196640 | tf_op jit(solution)/shard_map/ppermute | solution.py:31
  91.4 1.5 %collective-permute-done.10 = f32[49152]{0:T(1024)} collective-permute-done((f32[49152]{0:T(1024)}, f32[49152]{0:T(1024)}, u32[]{:S(2)}, u32[]{:S(2)}) %collective-permute-start.10) | collective-permute-done | bytes 196640 | tf_op jit(solution)/shard_map/ppermute | solution.py:45
  94.7 4.1 %collective-permute-done.11 = f32[24576]{0:T(1024)S(1)} collective-permute-done((f32[24576]{0:T(1024)S(1)}, f32[24576]{0:T(1024)S(1)}, u32[]{:S(2)}, u32[]{:S(2)}) %collective-permute-start.11) | collective-permute-done | bytes 98336 | tf_op jit(solution)/shard_map/ppermute | solution.py:45
  99.4 5.0 %collective-permute-done.12 = f32[12288]{0:T(1024)S(1)} collective-permute-done((f32[12288]{0:T(1024)S(1)}, f32[12288]{0:T(1024)S(1)}, u32[]{:S(2)}, u32[]{:S(2)}) %collective-permute-start.12) | collective-permute-done | bytes 49184 | tf_op jit(solution)/shard_map/ppermute | solution.py:45
  104.5 2.2 %pad_maximum_fusion = bf16[1,768,768]{2,1,0:T(8,128)(2,1)} fusion(bf16[1,768,384]{2,1,0:T(8,128)(2,1)} %get-tuple-element.16, bf16[1,768,384]{2,1,0:T(8,128)(2,1)S(1)} %copy-done.10), kind=kLoop, calls=%fused_computation.12 | loop fusion | flops 2359296 | bytes 2359296 | tf_op jit(solution)/shard_map/concatenate | solution.py:223
  106.7 3.1 %collective-permute-done.13 = f32[12288]{0:T(1024)S(1)} collective-permute-done((f32[12288]{0:T(1024)S(1)}, f32[12288]{0:T(1024)S(1)}, u32[]{:S(2)}, u32[]{:S(2)}) %collective-permute-start.13) | collective-permute-done | bytes 49184 | tf_op jit(solution)/shard_map/ppermute | solution.py:53
  111.1 3.3 %collective-permute-done.14 = f32[24576]{0:T(1024)S(1)} collective-permute-done((f32[24576]{0:T(1024)S(1)}, f32[24576]{0:T(1024)S(1)}, u32[]{:S(2)}, u32[]{:S(2)}) %collective-permute-start.14) | collective-permute-done | bytes 98336 | tf_op jit(solution)/shard_map/ppermute | solution.py:53
  (83 shorter events, 24.1 us)
Async XLA Ops:
  0.6 68.0 %copy-start = (bf16[1,768,768]{2,1,0:T(8,128)(2,1)S(1)}, bf16[1,768,768]{2,1,0:T(8,128)(2,1)}, u32[]{:S(2)}) copy-start(bf16[1,768,768]{2,1,0:T(8,128)(2,1)} %param.13) | copy-start | bytes 3538948
  3.5 19.0 %collective-permute-start = (bf16[2,1,384,384]{3,2,1,0:T(8,128)(2,1)}, bf16[2,1,384,384]{3,2,1,0:T(8,128)(2,1)S(1)}, u32[]{:S(2)}, u32[]{:S(2)}) collective-permute-start(bf16[2,1,384,384]{3,2,1,0:T(8,128)(2,1)} %pad_maximum_fusion.3), channel_id=1, source_target_pairs={{0,4},{4,8},{8,12},{1,5},{5,9},{9,13},{2,6},{6,10},{10,14},{3,7},{... | collective-permute-start | bytes 1769480 | tf_op jit(solution)/shard_map/ppermute | solution.py:21
  9.3 18.3 %collective-permute-start.1 = (bf16[2,1,384,384]{3,2,1,0:T(8,128)(2,1)}, bf16[2,1,384,384]{3,2,1,0:T(8,128)(2,1)S(1)}, u32[]{:S(2)}, u32[]{:S(2)}) collective-permute-start(bf16[2,1,384,384]{3,2,1,0:T(8,128)(2,1)} %pad_maximum_fusion.4), channel_id=1, source_target_pairs={{4,0},{8,4},{12,8},{5,1},{9,5},{13,9},{6,2},{10,6},{14,10},{7,3},{... | collective-permute-start | bytes 1769480 | tf_op jit(solution)/shard_map/ppermute | solution.py:21
  10.6 9.0 %copy-start.12 = (s32[8,3]{0,1:T(4,128)S(1)}, s32[8,3]{0,1:T(4,128)}, u32[]{:S(2)}) copy-start(s32[8,3]{0,1:T(4,128)} %param.16) | copy-start | bytes 292
  11.5 35.2 %collective-permute-start.3 = (bf16[2,1,384,384]{3,2,1,0:T(8,128)(2,1)}, bf16[2,1,384,384]{3,2,1,0:T(8,128)(2,1)S(1)}, u32[]{:S(2)}, u32[]{:S(2)}) collective-permute-start(bf16[2,1,384,384]{3,2,1,0:T(8,128)(2,1)} %pad_maximum_fusion.6), channel_id=1, source_target_pairs={{4,0},{8,4},{12,8},{5,1},{9,5},{13,9},{6,2},{10,6},{14,10},{7,3},{... | collective-permute-start | bytes 1769480 | tf_op jit(solution)/shard_map/ppermute | solution.py:21
  13.7 33.1 %collective-permute-start.2 = (bf16[2,1,384,384]{3,2,1,0:T(8,128)(2,1)}, bf16[2,1,384,384]{3,2,1,0:T(8,128)(2,1)S(1)}, u32[]{:S(2)}, u32[]{:S(2)}) collective-permute-start(bf16[2,1,384,384]{3,2,1,0:T(8,128)(2,1)} %pad_maximum_fusion.5), channel_id=1, source_target_pairs={{0,4},{4,8},{8,12},{1,5},{5,9},{9,13},{2,6},{6,10},{10,14},{3,7},{... | collective-permute-start | bytes 1769480 | tf_op jit(solution)/shard_map/ppermute | solution.py:21
  22.4 5.3 %copy-start.4 = (bf16[2,1,384,384]{3,2,1,0:T(8,128)(2,1)}, bf16[2,1,384,384]{3,2,1,0:T(8,128)(2,1)S(1)}, u32[]{:S(2)}) copy-start(bf16[2,1,384,384]{3,2,1,0:T(8,128)(2,1)S(1)} %collective-permute-done.left_ref) | copy-start | bytes 1769476
  41.9 30.3 %collective-permute-start.4 = (bf16[2,1,384,384]{3,2,1,0:T(8,128)(2,1)}, bf16[2,1,384,384]{3,2,1,0:T(8,128)(2,1)S(1)}, u32[]{:S(2)}, u32[]{:S(2)}) collective-permute-start(bf16[2,1,384,384]{3,2,1,0:T(8,128)(2,1)} %get-tuple-element.18), channel_id=1, source_target_pairs={{0,4},{4,8},{8,12},{1,5},{5,9},{9,13},{2,6},{6,10},{10,14},{3,7},{... | collective-permute-start | bytes 1769480 | tf_op jit(solution)/shard_map/ppermute | solution.py:21
  45.4 26.8 %collective-permute-start.5 = (bf16[2,1,384,384]{3,2,1,0:T(8,128)(2,1)}, bf16[2,1,384,384]{3,2,1,0:T(8,128)(2,1)S(1)}, u32[]{:S(2)}, u32[]{:S(2)}) collective-permute-start(bf16[2,1,384,384]{3,2,1,0:T(8,128)(2,1)} %get-tuple-element.19), channel_id=1, source_target_pairs={{4,0},{8,4},{12,8},{5,1},{9,5},{13,9},{6,2},{10,6},{14,10},{7,3},{... | collective-permute-start | bytes 1769480 | tf_op jit(solution)/shard_map/ppermute | solution.py:21
  61.8 14.2 %collective-permute-start.6 = (bf16[2,1,384,384]{3,2,1,0:T(8,128)(2,1)}, bf16[2,1,384,384]{3,2,1,0:T(8,128)(2,1)}, u32[]{:S(2)}, u32[]{:S(2)}) collective-permute-start(bf16[2,1,384,384]{3,2,1,0:T(8,128)(2,1)} %get-tuple-element.21), channel_id=1, source_target_pairs={{0,4},{4,8},{8,12},{1,5},{5,9},{9,13},{2,6},{6,10},{10,14},{3,7},{... | collective-permute-start | bytes 1769480 | tf_op jit(solution)/shard_map/ppermute | solution.py:21
  67.2 13.8 %collective-permute-start.7 = (bf16[2,1,384,384]{3,2,1,0:T(8,128)(2,1)}, bf16[2,1,384,384]{3,2,1,0:T(8,128)(2,1)}, u32[]{:S(2)}, u32[]{:S(2)}) collective-permute-start(bf16[2,1,384,384]{3,2,1,0:T(8,128)(2,1)} %get-tuple-element.22), channel_id=1, source_target_pairs={{4,0},{8,4},{12,8},{5,1},{9,5},{13,9},{6,2},{10,6},{14,10},{7,3},{... | collective-permute-start | bytes 1769480 | tf_op jit(solution)/shard_map/ppermute | solution.py:21
  70.7 14.9 %collective-permute-start.8 = (f32[1,768,64]{1,2,0:T(8,128)}, f32[1,768,64]{1,2,0:T(8,128)}, u32[]{:S(2)}, u32[]{:S(2)}) collective-permute-start(f32[1,768,64]{1,2,0:T(8,128)} %fusion.19), channel_id=1, source_target_pairs={{0,2},{2,0},{1,3},{3,1},{4,6},{6,4},{5,7},{7,5},{8,10},{10,8},{9,1... | collective-permute-start | bytes 589832 | tf_op jit(solution)/shard_map/ppermute | solution.py:31
  72.2 1.2 %copy-start.6 = (bf16[1,768,384]{2,1,0:T(8,128)(2,1)S(1)}, bf16[1,768,384]{2,1,0:T(8,128)(2,1)}, u32[]{:S(2)}) copy-start(bf16[1,768,384]{2,1,0:T(8,128)(2,1)} %get-tuple-element.23) | copy-start | bytes 1769476
  73.8 8.6 %copy-start.8 = (bf16[1,768,384]{2,1,0:T(8,128)(2,1)S(1)}, bf16[1,768,384]{2,1,0:T(8,128)(2,1)}, u32[]{:S(2)}) copy-start(bf16[1,768,384]{2,1,0:T(8,128)(2,1)} %get-tuple-element.20) | copy-start | bytes 1769476
  73.8 8.6 %copy-start.9 = (bf16[1,768,384]{2,1,0:T(8,128)(2,1)S(1)}, bf16[1,768,384]{2,1,0:T(8,128)(2,1)}, u32[]{:S(2)}) copy-start(bf16[1,768,384]{2,1,0:T(8,128)(2,1)} %get-tuple-element.24) | copy-start | bytes 1769476
  83.6 3.4 %copy-start.1 = (bf16[1,768,768]{2,1,0:T(8,128)(2,1)}, bf16[1,768,768]{2,1,0:T(8,128)(2,1)S(1)}, u32[]{:S(2)}) copy-start(bf16[1,768,768]{2,1,0:T(8,128)(2,1)S(1)} %pad_maximum_fusion.2) | copy-start | bytes 3538948
  84.1 5.7 %collective-permute-start.9 = (f32[1,768,64]{1,2,0:T(8,128)S(1)}, f32[1,768,64]{1,2,0:T(8,128)S(1)}, u32[]{:S(2)}, u32[]{:S(2)}) collective-permute-start(f32[1,768,64]{1,2,0:T(8,128)S(1)} %fusion.16), channel_id=1, source_target_pairs={{0,2},{2,0},{1,3},{3,1},{4,6},{6,4},{5,7},{7,5},{8,10},{10,8},{9,1... | collective-permute-start | bytes 589832 | tf_op jit(solution)/shard_map/ppermute | solution.py:31
  91.1 1.8 %collective-permute-start.10 = (f32[49152]{0:T(1024)}, f32[49152]{0:T(1024)}, u32[]{:S(2)}, u32[]{:S(2)}) collective-permute-start(f32[49152]{0:T(1024)} %select_n.88), channel_id=1, source_target_pairs={{0,1},{1,0},{2,3},{3,2},{4,5},{5,4},{6,7},{7,6},{8,9},{9,8},{10,11... | collective-permute-start | bytes 589832 | tf_op jit(solution)/shard_map/ppermute | solution.py:45
  91.3 13.2 %copy-start.10 = (bf16[1,768,384]{2,1,0:T(8,128)(2,1)S(1)}, bf16[1,768,384]{2,1,0:T(8,128)(2,1)}, u32[]{:S(2)}) copy-start(bf16[1,768,384]{2,1,0:T(8,128)(2,1)} %get-tuple-element.15) | copy-start | bytes 1769476
  93.9 4.9 %collective-permute-start.11 = (f32[24576]{0:T(1024)S(1)}, f32[24576]{0:T(1024)S(1)}, u32[]{:S(2)}, u32[]{:S(2)}) collective-permute-start(f32[24576]{0:T(1024)S(1)} %slice_select_fusion), channel_id=1, source_target_pairs={{0,4},{4,0},{8,12},{12,8},{1,5},{5,1},{9,13},{13,9},{2,6},{6,2},{1... | collective-permute-start | bytes 294920 | tf_op jit(solution)/shard_map/ppermute | solution.py:45
  98.8 5.6 %collective-permute-start.12 = (f32[12288]{0:T(1024)S(1)}, f32[12288]{0:T(1024)S(1)}, u32[]{:S(2)}, u32[]{:S(2)}) collective-permute-start(f32[12288]{0:T(1024)S(1)} %slice_select_fusion.1), channel_id=1, source_target_pairs={{0,8},{4,12},{8,0},{12,4},{1,9},{5,13},{9,1},{13,5},{2,10},{6,14},... | collective-permute-start | bytes 147464 | tf_op jit(solution)/shard_map/ppermute | solution.py:45
  104.4 5.3 %collective-permute-start.13 = (f32[12288]{0:T(1024)S(1)}, f32[12288]{0:T(1024)S(1)}, u32[]{:S(2)}, u32[]{:S(2)}) collective-permute-start(f32[12288]{0:T(1024)S(1)} %select_add_fusion.1), channel_id=1, source_target_pairs={{0,8},{4,12},{8,0},{12,4},{1,9},{5,13},{9,1},{13,5},{2,10},{6,14},... | collective-permute-start | bytes 147464 | tf_op jit(solution)/shard_map/ppermute | solution.py:53
  109.8 4.7 %collective-permute-start.14 = (f32[24576]{0:T(1024)S(1)}, f32[24576]{0:T(1024)S(1)}, u32[]{:S(2)}, u32[]{:S(2)}) collective-permute-start(f32[24576]{0:T(1024)S(1)} %maximum_select_fusion.4), channel_id=1, source_target_pairs={{0,4},{4,0},{8,12},{12,8},{1,5},{5,1},{9,13},{13,9},{2,6},{6,2},{1... | collective-permute-start | bytes 294920 | tf_op jit(solution)/shard_map/ppermute | solution.py:53
  114.5 1.5 %collective-permute-start.15 = (f32[49152]{0:T(1024)S(1)}, f32[49152]{0:T(1024)S(1)}, u32[]{:S(2)}, u32[]{:S(2)}) collective-permute-start(f32[49152]{0:T(1024)S(1)} %maximum_select_fusion.2), channel_id=1, source_target_pairs={{0,1},{1,0},{2,3},{3,2},{4,5},{5,4},{6,7},{7,6},{8,9},{9,8},{10,11... | collective-permute-start | bytes 589832 | tf_op jit(solution)/shard_map/ppermute | solution.py:53
  (6 other events, 4.9 us)

commit v8 on v7

--- a/solution.py
+++ b/solution.py
@@ -54,6 +54,32 @@
         upper = (index & step) != 0
         flat = jnp.where(upper, jnp.concatenate((other, flat)), jnp.concatenate((flat, other)))
     return flat
+
+
+def one_round_sum(flat, axis):
+    peers = lax.axis_size(axis)
+    index = lax.axis_index(axis)
+    pieces = flat.reshape(peers, -1)
+    slot = lax.broadcasted_iota(jnp.int32, pieces.shape, 0)
+
+    def piece(at):
+        return lax.dynamic_index_in_dim(pieces, at % peers, 0, keepdims=False)
+
+    total = piece(index)
+    for step in range(1, peers):
+        total = total + lax.ppermute(
+            piece(index + step), axis, [(j, j + step) for j in range(peers - step)]
+        )
+        total = total + lax.ppermute(
+            piece(index - step), axis, [(j, j - step) for j in range(step, peers)]
+        )
+    whole = jnp.where(slot == index, total[None], 0.0)
+    for step in range(1, peers):
+        up = lax.ppermute(total, axis, [(j, j + step) for j in range(peers - step)])
+        down = lax.ppermute(total, axis, [(j, j - step) for j in range(step, peers)])
+        whole = whole + jnp.where(slot == index - step, up[None], 0.0)
+        whole = whole + jnp.where(slot == index + step, down[None], 0.0)
+    return whole.reshape(-1)
 
 
 def all_sum(array, axes):
@@ -69,10 +95,15 @@
     flat = array.reshape(-1)
     if flat.shape[0] % pieces:
         return lax.psum(array, axes)
-    for axis, distances in plan:
-        flat = scatter_sum(flat, axis, distances)
-    for axis, distances in reversed(plan):
-        flat = gather_back(flat, axis, distances)
+    inner, outer = plan[0], plan[1:]
+    flat = scatter_sum(flat, inner[0], inner[1])
+    for axis, distances in outer:
+        if lax.axis_size(axis) <= 4:
+            flat = one_round_sum(flat, axis)
+        else:
+            flat = scatter_sum(flat, axis, distances)
+            flat = gather_back(flat, axis, distances)
+    flat = gather_back(flat, inner[0], inner[1])
     return flat.reshape(array.shape)
 
 

time: 118 us -> 145 us (1.23)
  starting transfers between devices: 28.9 us -> 58.6 us
  waiting for transfers between devices: 34.8 us -> 29.2 us
  local copies, waits for them, and re-layouts: 10.2 us -> 13 us
    ppermute x0 -> x12, starting transfers between devices: none -> 31.2 us  [the longest x3 11.9 us: one_round_sum(): lax.ppermute(piece(index + step), axis, [(j, j + step) for j in range(pee...]
    ppermute x0 -> x12, waiting for transfers between devices: none -> 11.8 us  [the longest x3 6.07 us: one_round_sum(): lax.ppermute(piece(index - step), axis, [(j, j - step) for j in range(ste...]
    ppermute x3 -> x1, waiting for transfers between devices: 10.6 us -> 1.02 us  [scatter_sum(): lax.ppermute(send, axis, [(i, i ^ step) for i in range(peers)])]
    ppermute x3 -> x1, waiting for transfers between devices: 7.67 us -> 0.01 us  [gather_back(): other = lax.ppermute(flat, axis, [(i, i ^ step) for i in range(peers)])]
    unnamed x30 -> x33, local copies, waits for them, and re-layouts: 6.43 us -> 7.2 us
  transfers between devices with their start and end apart: 16 -> 24, of which waited for: 11 -> 9; matrix products, arithmetic and copies ran while one was open for 12% -> 11% of each run, Pallas kernels for 23% -> 19%
where the time goes in v8:
time: 145 us; the launch traced here: 144 us
  starting transfers between devices  58.6 us (40%)
  waiting for transfers between devices  29.2 us (20%)
  Pallas kernels  26.9 us (19%)
  local copies, waits for them, and re-layouts  13 us (9%)
  other arithmetic  10.8 us (7%)
  matrix products  4.26 us (3%)
    pallas_call x2, Pallas kernels, attention_backward(): pl.pallas_call(attention_kernel, grid=(clip_count, heads), in_specs=[pl.B...  26.9 us
    ppermute x8, starting transfers between devices, shifted(): return lax.ppermute(shard, axis, pairs)  24.3 us
    ppermute x8, waiting for transfers between devices, shifted(): return lax.ppermute(shard, axis, pairs)  13.7 us
    ppermute x3, starting transfers between devices, one_round_sum(): lax.ppermute(piece(index + step), axis, [(j, j + step) for j in range(pee...  11.9 us
    ppermute x3, starting transfers between devices, one_round_sum(): up = lax.ppermute(total, axis, [(j, j + step) for j in range(peers - step)])  11.6 us
    unnamed x33, local copies, waits for them, and re-layouts  7.2 us
    ppermute x3, waiting for transfers between devices, one_round_sum(): lax.ppermute(piece(index - step), axis, [(j, j - step) for j in range(ste...  6.07 us
    ppermute x3, waiting for transfers between devices, one_round_sum(): lax.ppermute(total, axis, [(j, j - step) for j in range(step, peers)])  5.3 us
  transfers between devices with their start and end apart: 24, of which 9 were waited for; matrix products, arithmetic and copies ran while one was open for 11% of the time, Pallas kernels for 19%

profile of v8, /device:TPU:0, one launch (start us, length us, event | category | flops | bytes accessed | tf_op | source)
XLA Modules:
  0.0 144.1 jit_solution(12415303076236763514)
XLA Ops:
  0.6 1.9 %slice_bitcast_fusion.9 = (bf16[1,1,384,384]{3,2,1,0:T(8,128)(2,1)S(1)}, bf16[1,1,384,384]{3,2,1,0:T(8,128)(2,1)S(1)}, bf16[1,1,384,384]{3,2,1,0:T(8,128)(2,1)S(...) fusion(bf16[1,768,768]{2,1,0:T(8,128)(2,1)} %v_ref.3, ...), kind=kLoop, calls=%fused_computation.53 | loop fusion | bytes 4718592 | tf_op jit(solution)/shard_map/stack | solution.py:242
  3.5 5.0 %collective-permute-start = (bf16[2,1,384,384]{3,2,1,0:T(8,128)(2,1)}, bf16[2,1,384,384]{3,2,1,0:T(8,128)(2,1)S(1)}, u32[]{:S(2)}, u32[]{:S(2)}) collective-permute-start(bf16[2,1,384,384]{3,2,1,0:T(8,128)(2,1)} %pad_maximum_fusion.3), channel_id=1, source_target_pairs={{0,4},{4,8},{8,12},{1,5},{5,9},{9,13},{2,6},{6,10},{10,14},{3,7},{... | collective-permute-start | bytes 1769480 | tf_op jit(solution)/shard_map/ppermute | solution.py:21
  13.7 5.2 %collective-permute-start.2 = (bf16[2,1,384,384]{3,2,1,0:T(8,128)(2,1)}, bf16[2,1,384,384]{3,2,1,0:T(8,128)(2,1)S(1)}, u32[]{:S(2)}, u32[]{:S(2)}) collective-permute-start(bf16[2,1,384,384]{3,2,1,0:T(8,128)(2,1)} %pad_maximum_fusion.5), channel_id=1, source_target_pairs={{0,4},{4,8},{8,12},{1,5},{5,9},{9,13},{2,6},{6,10},{10,14},{3,7},{... | collective-permute-start | bytes 1769480 | tf_op jit(solution)/shard_map/ppermute | solution.py:21
  22.4 5.2 %collective-permute-done.1.right_ref = bf16[2,1,384,384]{3,2,1,0:T(8,128)(2,1)S(1)} collective-permute-done((bf16[2,1,384,384]{3,2,1,0:T(8,128)(2,1)}, bf16[2,1,384,384]{3,2,1,0:T(8,128)(2,1)S(1)}, u32[]{:S(2)}, u32[]{:S(2)}) %collective-permute-start.1) | collective-permute-done | bytes 589856 | tf_op jit(solution)/shard_map/ppermute | solution.py:21
  28.5 13.4 %shard_map.128 = (bf16[1,768,384]{2,1,0:T(8,128)(2,1)}, bf16[1,768,384]{2,1,0:T(8,128)(2,1)}, bf16[1,768,384]{2,1,0:T(8,128)(2,1)}, bf16[2,1,384,384]{3,2,1,0:T(8,128)(2,1)}, bf16[2,1,384,384]{3,2,1,0:T(8,128)(2,1)}) custom-call(f32[6]{0:T(128)} %and_select_fusion.bias_ref, bf16[1,768,768]{2,1,0:T(8,128)(2,1)} %q_ref.3, bf16[1,768,768]{2,1,0:T(8,128)(2,1)} %g_ref.3, ...), custom_call_target="tpu_custom_call" | custom-call | tf_op jit(solution)/shard_map/pallas_call | solution.py:192
  41.9 3.5 %collective-permute-start.4 = (bf16[2,1,384,384]{3,2,1,0:T(8,128)(2,1)}, bf16[2,1,384,384]{3,2,1,0:T(8,128)(2,1)S(1)}, u32[]{:S(2)}, u32[]{:S(2)}) collective-permute-start(bf16[2,1,384,384]{3,2,1,0:T(8,128)(2,1)} %get-tuple-element.18), channel_id=1, source_target_pairs={{0,4},{4,8},{8,12},{1,5},{5,9},{9,13},{2,6},{6,10},{10,14},{3,7},{... | collective-permute-start | bytes 1769480 | tf_op jit(solution)/shard_map/ppermute | solution.py:21
  48.3 13.5 %shard_map.129 = (bf16[1,768,384]{2,1,0:T(8,128)(2,1)}, bf16[1,768,384]{2,1,0:T(8,128)(2,1)}, bf16[1,768,384]{2,1,0:T(8,128)(2,1)}, bf16[2,1,384,384]{3,2,1,0:T(8,128)(2,1)}, bf16[2,1,384,384]{3,2,1,0:T(8,128)(2,1)}) custom-call(f32[6]{0:T(128)} %and_select_fusion.bias_ref, bf16[1,768,768]{2,1,0:T(8,128)(2,1)} %q_ref.3, bf16[1,768,768]{2,1,0:T(8,128)(2,1)} %g_ref.3, ...), custom_call_target="tpu_custom_call" | custom-call | tf_op jit(solution)/shard_map/pallas_call | solution.py:192
  61.8 5.3 %collective-permute-start.6 = (bf16[2,1,384,384]{3,2,1,0:T(8,128)(2,1)}, bf16[2,1,384,384]{3,2,1,0:T(8,128)(2,1)}, u32[]{:S(2)}, u32[]{:S(2)}) collective-permute-start(bf16[2,1,384,384]{3,2,1,0:T(8,128)(2,1)} %get-tuple-element.21), channel_id=1, source_target_pairs={{0,4},{4,8},{8,12},{1,5},{5,9},{9,13},{2,6},{6,10},{10,14},{3,7},{... | collective-permute-start | bytes 1769480 | tf_op jit(solution)/shard_map/ppermute | solution.py:21
  67.2 1.5 %collective-permute-start.7 = (bf16[2,1,384,384]{3,2,1,0:T(8,128)(2,1)}, bf16[2,1,384,384]{3,2,1,0:T(8,128)(2,1)}, u32[]{:S(2)}, u32[]{:S(2)}) collective-permute-start(bf16[2,1,384,384]{3,2,1,0:T(8,128)(2,1)} %get-tuple-element.22), channel_id=1, source_target_pairs={{4,0},{8,4},{12,8},{5,1},{9,5},{13,9},{6,2},{10,6},{14,10},{7,3},{... | collective-permute-start | bytes 1769480 | tf_op jit(solution)/shard_map/ppermute | solution.py:21
  68.6 2.1 %fusion.19 = f32[1,768,64]{1,2,0:T(8,128)} fusion(bf16[768,64]{0,1:T(8,128)(2,1)} %param.14, bf16[1,768,768]{2,1,0:T(8,128)(2,1)S(1)} %copy-done), kind=kOutput, calls=%fused_computation.26 | convolution fusion | flops 75497472 | bytes 1474560 | tf_op jit(solution)/shard_map/pqg,gv->pqv/dot_general | solution.py:216
  70.7 1.5 %collective-permute-start.8 = (f32[1,768,64]{1,2,0:T(8,128)}, f32[1,768,64]{1,2,0:T(8,128)}, u32[]{:S(2)}, u32[]{:S(2)}) collective-permute-start(f32[1,768,64]{1,2,0:T(8,128)} %fusion.19), channel_id=1, source_target_pairs={{0,2},{2,0},{1,3},{3,1},{4,6},{6,4},{5,7},{7,5},{8,10},{10,8},{9,1... | collective-permute-start | bytes 589832 | tf_op jit(solution)/shard_map/ppermute | solution.py:31
  73.7 2.3 %collective-permute-done.6 = bf16[2,1,384,384]{3,2,1,0:T(8,128)(2,1)} collective-permute-done((bf16[2,1,384,384]{3,2,1,0:T(8,128)(2,1)}, bf16[2,1,384,384]{3,2,1,0:T(8,128)(2,1)}, u32[]{:S(2)}, u32[]{:S(2)}) %collective-permute-start.6) | collective-permute-done | bytes 589856 | tf_op jit(solution)/shard_map/ppermute | solution.py:21
  76.0 4.9 %collective-permute-done.7 = bf16[2,1,384,384]{3,2,1,0:T(8,128)(2,1)} collective-permute-done((bf16[2,1,384,384]{3,2,1,0:T(8,128)(2,1)}, bf16[2,1,384,384]{3,2,1,0:T(8,128)(2,1)}, u32[]{:S(2)}, u32[]{:S(2)}) %collective-permute-start.7) | collective-permute-done | bytes 589856 | tf_op jit(solution)/shard_map/ppermute | solution.py:21
  80.9 1.4 maximum_convert_fusion.1
  84.0 1.5 %collective-permute-start.9 = (f32[1,768,64]{1,2,0:T(8,128)S(1)}, f32[1,768,64]{1,2,0:T(8,128)S(1)}, u32[]{:S(2)}, u32[]{:S(2)}) collective-permute-start(f32[1,768,64]{1,2,0:T(8,128)S(1)} %fusion.16), channel_id=1, source_target_pairs={{0,2},{2,0},{1,3},{3,1},{4,6},{6,4},{5,7},{7,5},{8,10},{10,8},{9,1... | collective-permute-start | bytes 589832 | tf_op jit(solution)/shard_map/ppermute | solution.py:31
  85.5 1.4 fusion.22
  86.9 2.8 %collective-permute-done.9 = f32[1,768,64]{1,2,0:T(8,128)S(1)} collective-permute-done((f32[1,768,64]{1,2,0:T(8,128)S(1)}, f32[1,768,64]{1,2,0:T(8,128)S(1)}, u32[]{:S(2)}, u32[]{:S(2)}) %collective-permute-start.9) | collective-permute-done | bytes 196640 | tf_op jit(solution)/shard_map/ppermute | solution.py:31
  92.3 2.7 %collective-permute-start.11 = (f32[12288]{0:T(1024)S(1)}, f32[12288]{0:T(1024)S(1)}, u32[]{:S(2)}, u32[]{:S(2)}) collective-permute-start(f32[12288]{0:T(1024)S(1)} %bitcast.138), channel_id=1, source_target_pairs={{0,4},{4,8},{8,12},{1,5},{5,9},{9,13},{2,6},{6,10},{10,14},{3,7},{... | collective-permute-start | bytes 147464 | tf_op jit(solution)/shard_map/ppermute | solution.py:70
  96.3 4.3 %collective-permute-start.13 = (f32[12288]{0:T(1024)S(1)}, f32[12288]{0:T(1024)S(1)}, u32[]{:S(2)}, u32[]{:S(2)}) collective-permute-start(f32[12288]{0:T(1024)S(1)} %bitcast.136), channel_id=1, source_target_pairs={{0,8},{4,12},{1,9},{5,13},{2,10},{6,14},{3,11},{7,15},{16,24},{20,... | collective-permute-start | bytes 147464 | tf_op jit(solution)/shard_map/ppermute | solution.py:70
  101.9 4.9 %collective-permute-start.15 = (f32[12288]{0:T(1024)S(1)}, f32[12288]{0:T(1024)S(1)}, u32[]{:S(2)}, u32[]{:S(2)}) collective-permute-start(f32[12288]{0:T(1024)S(1)} %bitcast.134), channel_id=1, source_target_pairs={{0,12},{1,13},{2,14},{3,15},{16,28},{17,29},{18,30},{19,31}} | collective-permute-start | bytes 147464 | tf_op jit(solution)/shard_map/ppermute | solution.py:70
  108.5 6.1 %collective-permute-done.16 = f32[12288]{0:T(1024)S(1)} collective-permute-done((f32[12288]{0:T(1024)S(1)}, f32[12288]{0:T(1024)S(1)}, u32[]{:S(2)}, u32[]{:S(2)}) %collective-permute-start.16) | collective-permute-done | bytes 49184 | tf_op jit(solution)/shard_map/ppermute | solution.py:73
  117.2 3.4 %collective-permute-start.19 = (f32[12288]{0:T(1024)S(1)}, f32[12288]{0:T(1024)S(1)}, u32[]{:S(2)}, u32[]{:S(2)}) collective-permute-start(f32[12288]{0:T(1024)S(1)} %add_add_fusion), channel_id=1, source_target_pairs={{0,8},{4,12},{1,9},{5,13},{2,10},{6,14},{3,11},{7,15},{16,24},{20,... | collective-permute-start | bytes 147464 | tf_op jit(solution)/shard_map/ppermute | solution.py:78
  121.9 6.9 %collective-permute-start.21 = (f32[12288]{0:T(1024)S(1)}, f32[12288]{0:T(1024)S(1)}, u32[]{:S(2)}, u32[]{:S(2)}) collective-permute-start(f32[12288]{0:T(1024)S(1)} %add_add_fusion), channel_id=1, source_target_pairs={{0,12},{1,13},{2,14},{3,15},{16,28},{17,29},{18,30},{19,31}} | collective-permute-start | bytes 147464 | tf_op jit(solution)/shard_map/ppermute | solution.py:78
  131.3 5.3 %collective-permute-done.22 = f32[12288]{0:T(1024)S(1)} collective-permute-done((f32[12288]{0:T(1024)S(1)}, f32[12288]{0:T(1024)S(1)}, u32[]{:S(2)}, u32[]{:S(2)}) %collective-permute-start.22) | collective-permute-done | bytes 49184 | tf_op jit(solution)/shard_map/ppermute | solution.py:79
  (121 shorter events, 37.0 us)
Async XLA Ops:
  3.5 19.0 %collective-permute-start = (bf16[2,1,384,384]{3,2,1,0:T(8,128)(2,1)}, bf16[2,1,384,384]{3,2,1,0:T(8,128)(2,1)S(1)}, u32[]{:S(2)}, u32[]{:S(2)}) collective-permute-start(bf16[2,1,384,384]{3,2,1,0:T(8,128)(2,1)} %pad_maximum_fusion.3), channel_id=1, source_target_pairs={{0,4},{4,8},{8,12},{1,5},{5,9},{9,13},{2,6},{6,10},{10,14},{3,7},{... | collective-permute-start | bytes 1769480 | tf_op jit(solution)/shard_map/ppermute | solution.py:21
  9.3 18.3 %collective-permute-start.1 = (bf16[2,1,384,384]{3,2,1,0:T(8,128)(2,1)}, bf16[2,1,384,384]{3,2,1,0:T(8,128)(2,1)S(1)}, u32[]{:S(2)}, u32[]{:S(2)}) collective-permute-start(bf16[2,1,384,384]{3,2,1,0:T(8,128)(2,1)} %pad_maximum_fusion.4), channel_id=1, source_target_pairs={{4,0},{8,4},{12,8},{5,1},{9,5},{13,9},{6,2},{10,6},{14,10},{7,3},{... | collective-permute-start | bytes 1769480 | tf_op jit(solution)/shard_map/ppermute | solution.py:21
  11.5 35.2 %collective-permute-start.3 = (bf16[2,1,384,384]{3,2,1,0:T(8,128)(2,1)}, bf16[2,1,384,384]{3,2,1,0:T(8,128)(2,1)S(1)}, u32[]{:S(2)}, u32[]{:S(2)}) collective-permute-start(bf16[2,1,384,384]{3,2,1,0:T(8,128)(2,1)} %pad_maximum_fusion.6), channel_id=1, source_target_pairs={{4,0},{8,4},{12,8},{5,1},{9,5},{13,9},{6,2},{10,6},{14,10},{7,3},{... | collective-permute-start | bytes 1769480 | tf_op jit(solution)/shard_map/ppermute | solution.py:21
  13.7 33.1 %collective-permute-start.2 = (bf16[2,1,384,384]{3,2,1,0:T(8,128)(2,1)}, bf16[2,1,384,384]{3,2,1,0:T(8,128)(2,1)S(1)}, u32[]{:S(2)}, u32[]{:S(2)}) collective-permute-start(bf16[2,1,384,384]{3,2,1,0:T(8,128)(2,1)} %pad_maximum_fusion.5), channel_id=1, source_target_pairs={{0,4},{4,8},{8,12},{1,5},{5,9},{9,13},{2,6},{6,10},{10,14},{3,7},{... | collective-permute-start | bytes 1769480 | tf_op jit(solution)/shard_map/ppermute | solution.py:21
  41.9 30.3 %collective-permute-start.4 = (bf16[2,1,384,384]{3,2,1,0:T(8,128)(2,1)}, bf16[2,1,384,384]{3,2,1,0:T(8,128)(2,1)S(1)}, u32[]{:S(2)}, u32[]{:S(2)}) collective-permute-start(bf16[2,1,384,384]{3,2,1,0:T(8,128)(2,1)} %get-tuple-element.18), channel_id=1, source_target_pairs={{0,4},{4,8},{8,12},{1,5},{5,9},{9,13},{2,6},{6,10},{10,14},{3,7},{... | collective-permute-start | bytes 1769480 | tf_op jit(solution)/shard_map/ppermute | solution.py:21
  45.4 26.8 %collective-permute-start.5 = (bf16[2,1,384,384]{3,2,1,0:T(8,128)(2,1)}, bf16[2,1,384,384]{3,2,1,0:T(8,128)(2,1)S(1)}, u32[]{:S(2)}, u32[]{:S(2)}) collective-permute-start(bf16[2,1,384,384]{3,2,1,0:T(8,128)(2,1)} %get-tuple-element.19), channel_id=1, source_target_pairs={{4,0},{8,4},{12,8},{5,1},{9,5},{13,9},{6,2},{10,6},{14,10},{7,3},{... | collective-permute-start | bytes 1769480 | tf_op jit(solution)/shard_map/ppermute | solution.py:21
  61.8 14.2 %collective-permute-start.6 = (bf16[2,1,384,384]{3,2,1,0:T(8,128)(2,1)}, bf16[2,1,384,384]{3,2,1,0:T(8,128)(2,1)}, u32[]{:S(2)}, u32[]{:S(2)}) collective-permute-start(bf16[2,1,384,384]{3,2,1,0:T(8,128)(2,1)} %get-tuple-element.21), channel_id=1, source_target_pairs={{0,4},{4,8},{8,12},{1,5},{5,9},{9,13},{2,6},{6,10},{10,14},{3,7},{... | collective-permute-start | bytes 1769480 | tf_op jit(solution)/shard_map/ppermute | solution.py:21
  67.2 13.8 %collective-permute-start.7 = (bf16[2,1,384,384]{3,2,1,0:T(8,128)(2,1)}, bf16[2,1,384,384]{3,2,1,0:T(8,128)(2,1)}, u32[]{:S(2)}, u32[]{:S(2)}) collective-permute-start(bf16[2,1,384,384]{3,2,1,0:T(8,128)(2,1)} %get-tuple-element.22), channel_id=1, source_target_pairs={{4,0},{8,4},{12,8},{5,1},{9,5},{13,9},{6,2},{10,6},{14,10},{7,3},{... | collective-permute-start | bytes 1769480 | tf_op jit(solution)/shard_map/ppermute | solution.py:21
  70.7 14.8 %collective-permute-start.8 = (f32[1,768,64]{1,2,0:T(8,128)}, f32[1,768,64]{1,2,0:T(8,128)}, u32[]{:S(2)}, u32[]{:S(2)}) collective-permute-start(f32[1,768,64]{1,2,0:T(8,128)} %fusion.19), channel_id=1, source_target_pairs={{0,2},{2,0},{1,3},{3,1},{4,6},{6,4},{5,7},{7,5},{8,10},{10,8},{9,1... | collective-permute-start | bytes 589832 | tf_op jit(solution)/shard_map/ppermute | solution.py:31
  84.0 5.7 %collective-permute-start.9 = (f32[1,768,64]{1,2,0:T(8,128)S(1)}, f32[1,768,64]{1,2,0:T(8,128)S(1)}, u32[]{:S(2)}, u32[]{:S(2)}) collective-permute-start(f32[1,768,64]{1,2,0:T(8,128)S(1)} %fusion.16), channel_id=1, source_target_pairs={{0,2},{2,0},{1,3},{3,1},{4,6},{6,4},{5,7},{7,5},{8,10},{10,8},{9,1... | collective-permute-start | bytes 589832 | tf_op jit(solution)/shard_map/ppermute | solution.py:31
  90.3 1.5 %collective-permute-start.10 = (f32[49152]{0:T(1024)S(1)}, f32[49152]{0:T(1024)S(1)}, u32[]{:S(2)}, u32[]{:S(2)}) collective-permute-start(f32[49152]{0:T(1024)S(1)} %select_n.154), channel_id=1, source_target_pairs={{0,1},{1,0},{2,3},{3,2},{4,5},{5,4},{6,7},{7,6},{8,9},{9,8},{10,11... | collective-permute-start | bytes 589832 | tf_op jit(solution)/shard_map/ppermute | solution.py:45
  92.3 14.5 %collective-permute-start.11 = (f32[12288]{0:T(1024)S(1)}, f32[12288]{0:T(1024)S(1)}, u32[]{:S(2)}, u32[]{:S(2)}) collective-permute-start(f32[12288]{0:T(1024)S(1)} %bitcast.138), channel_id=1, source_target_pairs={{0,4},{4,8},{8,12},{1,5},{5,9},{9,13},{2,6},{6,10},{10,14},{3,7},{... | collective-permute-start | bytes 147464 | tf_op jit(solution)/shard_map/ppermute | solution.py:70
  95.0 13.1 %collective-permute-start.12 = (f32[12288]{0:T(1024)S(1)}, f32[12288]{0:T(1024)S(1)}, u32[]{:S(2)}, u32[]{:S(2)}) collective-permute-start(f32[12288]{0:T(1024)S(1)} %bitcast.137), channel_id=1, source_target_pairs={{4,0},{8,4},{12,8},{5,1},{9,5},{13,9},{6,2},{10,6},{14,10},{7,3},{... | collective-permute-start | bytes 147464 | tf_op jit(solution)/shard_map/ppermute | solution.py:73
  96.3 11.8 %collective-permute-start.13 = (f32[12288]{0:T(1024)S(1)}, f32[12288]{0:T(1024)S(1)}, u32[]{:S(2)}, u32[]{:S(2)}) collective-permute-start(f32[12288]{0:T(1024)S(1)} %bitcast.136), channel_id=1, source_target_pairs={{0,8},{4,12},{1,9},{5,13},{2,10},{6,14},{3,11},{7,15},{16,24},{20,... | collective-permute-start | bytes 147464 | tf_op jit(solution)/shard_map/ppermute | solution.py:70
  100.6 7.5 %collective-permute-start.14 = (f32[12288]{0:T(1024)S(1)}, f32[12288]{0:T(1024)S(1)}, u32[]{:S(2)}, u32[]{:S(2)}) collective-permute-start(f32[12288]{0:T(1024)S(1)} %bitcast.135), channel_id=1, source_target_pairs={{8,0},{12,4},{9,1},{13,5},{10,2},{14,6},{11,3},{15,7},{24,16},{28,... | collective-permute-start | bytes 147464 | tf_op jit(solution)/shard_map/ppermute | solution.py:73
  101.9 6.6 %collective-permute-start.15 = (f32[12288]{0:T(1024)S(1)}, f32[12288]{0:T(1024)S(1)}, u32[]{:S(2)}, u32[]{:S(2)}) collective-permute-start(f32[12288]{0:T(1024)S(1)} %bitcast.134), channel_id=1, source_target_pairs={{0,12},{1,13},{2,14},{3,15},{16,28},{17,29},{18,30},{19,31}} | collective-permute-start | bytes 147464 | tf_op jit(solution)/shard_map/ppermute | solution.py:70
  106.8 7.8 %collective-permute-start.16 = (f32[12288]{0:T(1024)S(1)}, f32[12288]{0:T(1024)S(1)}, u32[]{:S(2)}, u32[]{:S(2)}) collective-permute-start(f32[12288]{0:T(1024)S(1)} %bitcast.133), channel_id=1, source_target_pairs={{12,0},{13,1},{14,2},{15,3},{28,16},{29,17},{30,18},{31,19}} | collective-permute-start | bytes 147464 | tf_op jit(solution)/shard_map/ppermute | solution.py:73
  114.6 14.2 %collective-permute-start.17 = (f32[12288]{0:T(1024)S(1)}, f32[12288]{0:T(1024)S(1)}, u32[]{:S(2)}, u32[]{:S(2)}) collective-permute-start(f32[12288]{0:T(1024)S(1)} %add_add_fusion), channel_id=1, source_target_pairs={{0,4},{4,8},{8,12},{1,5},{5,9},{9,13},{2,6},{6,10},{10,14},{3,7},{... | collective-permute-start | bytes 147464 | tf_op jit(solution)/shard_map/ppermute | solution.py:78
  115.9 15.4 %collective-permute-start.18 = (f32[12288]{0:T(1024)S(1)}, f32[12288]{0:T(1024)S(1)}, u32[]{:S(2)}, u32[]{:S(2)}) collective-permute-start(f32[12288]{0:T(1024)S(1)} %add_add_fusion), channel_id=1, source_target_pairs={{4,0},{8,4},{12,8},{5,1},{9,5},{13,9},{6,2},{10,6},{14,10},{7,3},{... | collective-permute-start | bytes 147464 | tf_op jit(solution)/shard_map/ppermute | solution.py:79
  117.2 14.1 %collective-permute-start.19 = (f32[12288]{0:T(1024)S(1)}, f32[12288]{0:T(1024)S(1)}, u32[]{:S(2)}, u32[]{:S(2)}) collective-permute-start(f32[12288]{0:T(1024)S(1)} %add_add_fusion), channel_id=1, source_target_pairs={{0,8},{4,12},{1,9},{5,13},{2,10},{6,14},{3,11},{7,15},{16,24},{20,... | collective-permute-start | bytes 147464 | tf_op jit(solution)/shard_map/ppermute | solution.py:78
  120.6 10.7 %collective-permute-start.20 = (f32[12288]{0:T(1024)S(1)}, f32[12288]{0:T(1024)S(1)}, u32[]{:S(2)}, u32[]{:S(2)}) collective-permute-start(f32[12288]{0:T(1024)S(1)} %add_add_fusion), channel_id=1, source_target_pairs={{8,0},{12,4},{9,1},{13,5},{10,2},{14,6},{11,3},{15,7},{24,16},{28,... | collective-permute-start | bytes 147464 | tf_op jit(solution)/shard_map/ppermute | solution.py:79
  121.9 9.4 %collective-permute-start.21 = (f32[12288]{0:T(1024)S(1)}, f32[12288]{0:T(1024)S(1)}, u32[]{:S(2)}, u32[]{:S(2)}) collective-permute-start(f32[12288]{0:T(1024)S(1)} %add_add_fusion), channel_id=1, source_target_pairs={{0,12},{1,13},{2,14},{3,15},{16,28},{17,29},{18,30},{19,31}} | collective-permute-start | bytes 147464 | tf_op jit(solution)/shard_map/ppermute | solution.py:78
  128.8 7.8 %collective-permute-start.22 = (f32[12288]{0:T(1024)S(1)}, f32[12288]{0:T(1024)S(1)}, u32[]{:S(2)}, u32[]{:S(2)}) collective-permute-start(f32[12288]{0:T(1024)S(1)} %add_add_fusion), channel_id=1, source_target_pairs={{12,0},{13,1},{14,2},{15,3},{28,16},{29,17},{30,18},{31,19}} | collective-permute-start | bytes 147464 | tf_op jit(solution)/shard_map/ppermute | solution.py:79
  137.6 3.6 %collective-permute-start.23 = (f32[49152]{0:T(1024)}, f32[49152]{0:T(1024)}, u32[]{:S(2)}, u32[]{:S(2)}) collective-permute-start(f32[49152]{0:T(1024)} %bitcast.39), channel_id=1, source_target_pairs={{0,1},{1,0},{2,3},{3,2},{4,5},{5,4},{6,7},{7,6},{8,9},{9,8},{10,11... | collective-permute-start | bytes 589832 | tf_op jit(solution)/shard_map/ppermute | solution.py:53
  (15 other events, 161.1 us)

commit v9 on v7

--- a/solution.py
+++ b/solution.py
@@ -69,10 +69,17 @@
     flat = array.reshape(-1)
     if flat.shape[0] % pieces:
         return lax.psum(array, axes)
-    for axis, distances in plan:
-        flat = scatter_sum(flat, axis, distances)
-    for axis, distances in reversed(plan):
-        flat = gather_back(flat, axis, distances)
+    inner, outer = plan[0], plan[1:]
+    flat = scatter_sum(flat, inner[0], inner[1])
+    for axis, distances in outer:
+        flat = scatter_sum(flat, axis, distances[:-1])
+        if distances:
+            step = distances[-1]
+            flat = flat + lax.ppermute(
+                flat, axis, [(i, i ^ step) for i in range(lax.axis_size(axis))]
+            )
+        flat = gather_back(flat, axis, distances[:-1])
+    flat = gather_back(flat, inner[0], inner[1])
     return flat.reshape(array.shape)
 
 
@@ -218,21 +225,23 @@
         arrived = jnp.concatenate((from_left, from_right), 2).astype(jnp.float32)
         dk = (dk_own.astype(jnp.float32) + arrived[0]).astype(jnp.bfloat16)
         dv = (dv_own.astype(jnp.float32) + arrived[1]).astype(jnp.bfloat16)
-        outs.append((dq, dk, dv))
+        piece = jnp.einsum(
+            "dsi,ji->dsj", dv, adapter_up_weight[:, cols], preferred_element_type=jnp.float32
+        )
+        up = jnp.einsum("igb,igu->bu", lowered_rows, dv, preferred_element_type=jnp.float32)
+        outs.append((dq, dk, dv, piece, up))
     query_grad, key_grad, value_gradient = (
         jnp.concatenate([o[i] for o in outs], 2) for i in range(3)
     )
 
-    backward_piece = jnp.einsum(
-        "dsi,ji->dsj", value_gradient, adapter_up_weight, preferred_element_type=jnp.float32
-    )
+    backward_piece = outs[0][3]
+    for o in outs[1:]:
+        backward_piece = backward_piece + o[3]
     backward_rows = butterfly_sum(backward_piece, "head").astype(jnp.bfloat16)
     gradient_down_local = adapter_scale * jnp.einsum(
         "yhm,yhz->mz", normed, backward_rows, preferred_element_type=jnp.float32
     )
-    gradient_up_local = adapter_scale * jnp.einsum(
-        "igb,igu->bu", lowered_rows, value_gradient, preferred_element_type=jnp.float32
-    )
+    gradient_up_local = adapter_scale * jnp.concatenate([o[4] for o in outs], 1)
     both = jnp.stack((gradient_down_local, gradient_up_local.T), 0)
     both = all_sum(both, ("rep", "seq"))
     down_projection_grad, up_projection_grad = both[0], both[1].T

time: 118 us -> 138 us (1.17)
  waiting for transfers between devices: 34.8 us -> 47.7 us
  local copies, waits for them, and re-layouts: 10.2 us -> 15.9 us
  starting transfers between devices: 28.9 us -> 31.5 us
  matrix products: 4.25 us -> 2.63 us
    ppermute x8, waiting for transfers between devices: 13.7 us -> 28.3 us  [shifted(): return lax.ppermute(shard, axis, pairs)]
    ppermute x3 -> x2, waiting for transfers between devices: 10.6 us -> 3.58 us  [scatter_sum(): lax.ppermute(send, axis, [(i, i ^ step) for i in range(peers)])]
    ppermute x2, waiting for transfers between devices: 2.83 us -> 7.88 us  [butterfly_sum(): other = lax.ppermute(tree, axis, pairs)]
    ppermute x0 -> x1, waiting for transfers between devices: none -> 4.35 us  [all_sum(): lax.ppermute(flat, axis, [(i, i ^ step) for i in range(lax.axis_size(axis...]
    ppermute x3 -> x2, waiting for transfers between devices: 7.67 us -> 3.5 us  [gather_back(): other = lax.ppermute(flat, axis, [(i, i ^ step) for i in range(peers)])]
    select_n x2, local copies, waits for them, and re-layouts: 0.28 us -> 3.63 us  [scatter_sum(): keep = jnp.where(upper, flat[half:], flat[:half])]
    select_n x2, local copies, waits for them, and re-layouts: 0.97 us -> 3.63 us  [scatter_sum(): send = jnp.where(upper, flat[:half], flat[half:])]
    ppermute x0 -> x1, starting transfers between devices: none -> 2.11 us  [all_sum(): lax.ppermute(flat, axis, [(i, i ^ step) for i in range(lax.axis_size(axis...]
  transfers between devices with their start and end apart: 16 -> 15, of which waited for: 11 -> 8; matrix products, arithmetic and copies ran while one was open for 12% -> 11% of each run, Pallas kernels for 23% -> 20%
where the time goes in v9:
time: 138 us; the launch traced here: 137 us
  waiting for transfers between devices  47.7 us (35%)
  starting transfers between devices  31.5 us (23%)
  Pallas kernels  26.9 us (19%)
  local copies, waits for them, and re-layouts  15.9 us (12%)
  other arithmetic  11.7 us (8%)
  matrix products  2.63 us (2%)
    ppermute x8, waiting for transfers between devices, shifted(): return lax.ppermute(shard, axis, pairs)  28.3 us
    pallas_call x2, Pallas kernels, attention_backward(): pl.pallas_call(attention_kernel, grid=(clip_count, heads), in_specs=[pl.B...  26.9 us
    ppermute x8, starting transfers between devices, shifted(): return lax.ppermute(shard, axis, pairs)  24.5 us
    ppermute x2, waiting for transfers between devices, butterfly_sum(): other = lax.ppermute(tree, axis, pairs)  7.88 us
    unnamed x38, local copies, waits for them, and re-layouts  5.32 us
    ppermute x1, waiting for transfers between devices, all_sum(): lax.ppermute(flat, axis, [(i, i ^ step) for i in range(lax.axis_size(axis...  4.35 us
    select_n x2, local copies, waits for them, and re-layouts, scatter_sum(): keep = jnp.where(upper, flat[half:], flat[:half])  3.63 us
    select_n x2, local copies, waits for them, and re-layouts, scatter_sum(): send = jnp.where(upper, flat[:half], flat[half:])  3.63 us
  transfers between devices with their start and end apart: 15, of which 8 were waited for; matrix products, arithmetic and copies ran while one was open for 11% of the time, Pallas kernels for 20%

profile of v9, /device:TPU:0, one launch (start us, length us, event | category | flops | bytes accessed | tf_op | source)
XLA Modules:
  0.0 137.3 jit_solution(6664280073616446439)
XLA Ops:
  0.6 1.9 %slice_bitcast_fusion.9 = (bf16[1,1,384,384]{3,2,1,0:T(8,128)(2,1)S(1)}, bf16[1,1,384,384]{3,2,1,0:T(8,128)(2,1)S(1)}, bf16[1,1,384,384]{3,2,1,0:T(8,128)(2,1)S(...) fusion(bf16[1,768,768]{2,1,0:T(8,128)(2,1)} %v_ref.3, ...), kind=kLoop, calls=%fused_computation.43 | loop fusion | bytes 4718592 | tf_op jit(solution)/shard_map/stack | solution.py:218
  3.5 5.0 %collective-permute-start = (bf16[2,1,384,384]{3,2,1,0:T(8,128)(2,1)}, bf16[2,1,384,384]{3,2,1,0:T(8,128)(2,1)S(1)}, u32[]{:S(2)}, u32[]{:S(2)}) collective-permute-start(bf16[2,1,384,384]{3,2,1,0:T(8,128)(2,1)} %pad_maximum_fusion.3), channel_id=1, source_target_pairs={{0,4},{4,8},{8,12},{1,5},{5,9},{9,13},{2,6},{6,10},{10,14},{3,7},{... | collective-permute-start | bytes 1769480 | tf_op jit(solution)/shard_map/ppermute | solution.py:21
  13.7 6.0 %collective-permute-start.2 = (bf16[2,1,384,384]{3,2,1,0:T(8,128)(2,1)}, bf16[2,1,384,384]{3,2,1,0:T(8,128)(2,1)}, u32[]{:S(2)}, u32[]{:S(2)}) collective-permute-start(bf16[2,1,384,384]{3,2,1,0:T(8,128)(2,1)} %pad_maximum_fusion.5), channel_id=1, source_target_pairs={{0,4},{4,8},{8,12},{1,5},{5,9},{9,13},{2,6},{6,10},{10,14},{3,7},{... | collective-permute-start | bytes 1769480 | tf_op jit(solution)/shard_map/ppermute | solution.py:21
  20.8 18.0 %collective-permute-done.3.right_ref = bf16[2,1,384,384]{3,2,1,0:T(8,128)(2,1)S(1)} collective-permute-done((bf16[2,1,384,384]{3,2,1,0:T(8,128)(2,1)}, bf16[2,1,384,384]{3,2,1,0:T(8,128)(2,1)S(1)}, u32[]{:S(2)}, u32[]{:S(2)}) %collective-permute-start.3) | collective-permute-done | bytes 589856 | tf_op jit(solution)/shard_map/ppermute | solution.py:21
  39.6 13.4 %shard_map.129 = (bf16[1,768,384]{2,1,0:T(8,128)(2,1)}, bf16[1,768,384]{2,1,0:T(8,128)(2,1)}, bf16[1,768,384]{2,1,0:T(8,128)(2,1)}, bf16[2,1,384,384]{3,2,1,0:T(8,128)(2,1)}, bf16[2,1,384,384]{3,2,1,0:T(8,128)(2,1)}) custom-call(f32[6]{0:T(128)} %and_select_fusion.bias_ref, bf16[1,768,768]{2,1,0:T(8,128)(2,1)} %q_ref.3, bf16[1,768,768]{2,1,0:T(8,128)(2,1)} %g_ref.3, ...), custom_call_target="tpu_custom_call" | custom-call | tf_op jit(solution)/shard_map/pallas_call | solution.py:168
  53.1 3.5 %collective-permute-start.6 = (bf16[2,1,384,384]{3,2,1,0:T(8,128)(2,1)}, bf16[2,1,384,384]{3,2,1,0:T(8,128)(2,1)S(1)}, u32[]{:S(2)}, u32[]{:S(2)}) collective-permute-start(bf16[2,1,384,384]{3,2,1,0:T(8,128)(2,1)} %get-tuple-element.21), channel_id=1, source_target_pairs={{0,4},{4,8},{8,12},{1,5},{5,9},{9,13},{2,6},{6,10},{10,14},{3,7},{... | collective-permute-start | bytes 1769480 | tf_op jit(solution)/shard_map/ppermute | solution.py:21
  58.4 1.5 %collective-permute-start.8 = (f32[1,768,64]{1,2,0:T(8,128)S(1)}, f32[1,768,64]{1,2,0:T(8,128)S(1)}, u32[]{:S(2)}, u32[]{:S(2)}) collective-permute-start(f32[1,768,64]{1,2,0:T(8,128)S(1)} %fusion.13), channel_id=1, source_target_pairs={{0,2},{2,0},{1,3},{3,1},{4,6},{6,4},{5,7},{7,5},{8,10},{10,8},{9,1... | collective-permute-start | bytes 589832 | tf_op jit(solution)/shard_map/ppermute | solution.py:31
  59.9 4.2 %collective-permute-done.8 = f32[1,768,64]{1,2,0:T(8,128)S(1)} collective-permute-done((f32[1,768,64]{1,2,0:T(8,128)S(1)}, f32[1,768,64]{1,2,0:T(8,128)S(1)}, u32[]{:S(2)}, u32[]{:S(2)}) %collective-permute-start.8) | collective-permute-done | bytes 196640 | tf_op jit(solution)/shard_map/ppermute | solution.py:31
  66.4 13.4 %shard_map.128 = (bf16[1,768,384]{2,1,0:T(8,128)(2,1)}, bf16[1,768,384]{2,1,0:T(8,128)(2,1)}, bf16[1,768,384]{2,1,0:T(8,128)(2,1)}, bf16[2,1,384,384]{3,2,1,0:T(8,128)(2,1)}, bf16[2,1,384,384]{3,2,1,0:T(8,128)(2,1)}) custom-call(f32[6]{0:T(128)} %and_select_fusion.bias_ref, bf16[1,768,768]{2,1,0:T(8,128)(2,1)} %q_ref.3, bf16[1,768,768]{2,1,0:T(8,128)(2,1)} %g_ref.3, ...), custom_call_target="tpu_custom_call" | custom-call | tf_op jit(solution)/shard_map/pallas_call | solution.py:168
  79.8 4.6 %collective-permute-start.4 = (bf16[2,1,384,384]{3,2,1,0:T(8,128)(2,1)}, bf16[2,1,384,384]{3,2,1,0:T(8,128)(2,1)S(1)}, u32[]{:S(2)}, u32[]{:S(2)}) collective-permute-start(bf16[2,1,384,384]{3,2,1,0:T(8,128)(2,1)} %get-tuple-element.18), channel_id=1, source_target_pairs={{0,4},{4,8},{8,12},{1,5},{5,9},{9,13},{2,6},{6,10},{10,14},{3,7},{... | collective-permute-start | bytes 1769480 | tf_op jit(solution)/shard_map/ppermute | solution.py:21
  84.4 1.6 %collective-permute-start.5 = (bf16[2,1,384,384]{3,2,1,0:T(8,128)(2,1)}, bf16[2,1,384,384]{3,2,1,0:T(8,128)(2,1)S(1)}, u32[]{:S(2)}, u32[]{:S(2)}) collective-permute-start(bf16[2,1,384,384]{3,2,1,0:T(8,128)(2,1)} %get-tuple-element.19), channel_id=1, source_target_pairs={{4,0},{8,4},{12,8},{5,1},{9,5},{13,9},{6,2},{10,6},{14,10},{7,3},{... | collective-permute-start | bytes 1769480 | tf_op jit(solution)/shard_map/ppermute | solution.py:21
  88.5 6.1 %collective-permute-done.4 = bf16[2,1,384,384]{3,2,1,0:T(8,128)(2,1)S(1)} collective-permute-done((bf16[2,1,384,384]{3,2,1,0:T(8,128)(2,1)}, bf16[2,1,384,384]{3,2,1,0:T(8,128)(2,1)S(1)}, u32[]{:S(2)}, u32[]{:S(2)}) %collective-permute-start.4) | collective-permute-done | bytes 589856 | tf_op jit(solution)/shard_map/ppermute | solution.py:21
  94.7 4.2 %collective-permute-done.5 = bf16[2,1,384,384]{3,2,1,0:T(8,128)(2,1)S(1)} collective-permute-done((bf16[2,1,384,384]{3,2,1,0:T(8,128)(2,1)}, bf16[2,1,384,384]{3,2,1,0:T(8,128)(2,1)S(1)}, u32[]{:S(2)}, u32[]{:S(2)}) %collective-permute-start.5) | collective-permute-done | bytes 589856 | tf_op jit(solution)/shard_map/ppermute | solution.py:21
  99.6 1.6 %collective-permute-start.9 = (f32[1,768,64]{1,2,0:T(8,128)S(1)}, f32[1,768,64]{1,2,0:T(8,128)S(1)}, u32[]{:S(2)}, u32[]{:S(2)}) collective-permute-start(f32[1,768,64]{1,2,0:T(8,128)S(1)} %fusion.12), channel_id=1, source_target_pairs={{0,2},{2,0},{1,3},{3,1},{4,6},{6,4},{5,7},{7,5},{8,10},{10,8},{9,1... | collective-permute-start | bytes 589832 | tf_op jit(solution)/shard_map/ppermute | solution.py:31
  101.6 3.7 %collective-permute-done.9 = f32[1,768,64]{1,2,0:T(8,128)S(1)} collective-permute-done((f32[1,768,64]{1,2,0:T(8,128)S(1)}, f32[1,768,64]{1,2,0:T(8,128)S(1)}, u32[]{:S(2)}, u32[]{:S(2)}) %collective-permute-start.9) | collective-permute-done | bytes 196640 | tf_op jit(solution)/shard_map/ppermute | solution.py:31
  106.5 1.8 %copy.21 = f32[768,64]{1,0:T(8,128)} copy(f32[768,64]{0,1:T(8,128)} %get-tuple-element.49) | data formatting | bytes 393216 | tf_op jit(solution)/shard_map/jit(_where)/select_n | solution.py:44
  108.3 1.8 %select_n.71 = f32[49152]{0:T(1024)} reshape(f32[768,64]{1,0:T(8,128)} %copy.21) | data formatting | bytes 393216 | tf_op jit(solution)/shard_map/jit(_where)/select_n | solution.py:44
  110.1 1.8 %copy.20 = f32[768,64]{1,0:T(8,128)} copy(f32[768,64]{0,1:T(8,128)} %get-tuple-element.50) | data formatting | bytes 393216 | tf_op jit(solution)/shard_map/jit(_where)/select_n | solution.py:43
  111.9 1.8 %select_n.68 = f32[49152]{0:T(1024)} reshape(f32[768,64]{1,0:T(8,128)} %copy.20) | data formatting | bytes 393216 | tf_op jit(solution)/shard_map/jit(_where)/select_n | solution.py:43
  114.9 1.7 %collective-permute-start.11 = (f32[24576]{0:T(1024)S(1)}, f32[24576]{0:T(1024)S(1)}, u32[]{:S(2)}, u32[]{:S(2)}) collective-permute-start(f32[24576]{0:T(1024)S(1)} %slice_select_fusion), channel_id=1, source_target_pairs={{0,4},{4,0},{8,12},{12,8},{1,5},{5,1},{9,13},{13,9},{2,6},{6,2},{1... | collective-permute-start | bytes 294920 | tf_op jit(solution)/shard_map/ppermute | solution.py:45
  116.6 3.6 %collective-permute-done.11 = f32[24576]{0:T(1024)S(1)} collective-permute-done((f32[24576]{0:T(1024)S(1)}, f32[24576]{0:T(1024)S(1)}, u32[]{:S(2)}, u32[]{:S(2)}) %collective-permute-start.11) | collective-permute-done | bytes 98336 | tf_op jit(solution)/shard_map/ppermute | solution.py:45
  120.2 2.1 %collective-permute-start.12 = (f32[24576]{0:T(1024)S(1)}, f32[24576]{0:T(1024)S(1)}, u32[]{:S(2)}, u32[]{:S(2)}) collective-permute-start(f32[24576]{0:T(1024)S(1)} %select_add_fusion), channel_id=1, source_target_pairs={{0,8},{4,12},{8,0},{12,4},{1,9},{5,13},{9,1},{13,5},{2,10},{6,14},... | collective-permute-start | bytes 294920 | tf_op jit(solution)/shard_map/ppermute | solution.py:78
  123.4 4.4 %collective-permute-done.12 = f32[24576]{0:T(1024)S(1)} collective-permute-done((f32[24576]{0:T(1024)S(1)}, f32[24576]{0:T(1024)S(1)}, u32[]{:S(2)}, u32[]{:S(2)}) %collective-permute-start.12) | collective-permute-done | bytes 98336 | tf_op jit(solution)/shard_map/ppermute | solution.py:78
  129.0 3.5 %collective-permute-done.13 = f32[24576]{0:T(1024)S(1)} collective-permute-done((f32[24576]{0:T(1024)S(1)}, f32[24576]{0:T(1024)S(1)}, u32[]{:S(2)}, u32[]{:S(2)}) %collective-permute-start.13) | collective-permute-done | bytes 98336 | tf_op jit(solution)/shard_map/ppermute | solution.py:53
  (88 shorter events, 25.1 us)
Async XLA Ops:
  0.6 57.2 %copy-start = (bf16[1,768,768]{2,1,0:T(8,128)(2,1)S(1)}, bf16[1,768,768]{2,1,0:T(8,128)(2,1)}, u32[]{:S(2)}) copy-start(bf16[1,768,768]{2,1,0:T(8,128)(2,1)} %param.13) | copy-start | bytes 3538948
  3.5 61.3 %collective-permute-start = (bf16[2,1,384,384]{3,2,1,0:T(8,128)(2,1)}, bf16[2,1,384,384]{3,2,1,0:T(8,128)(2,1)S(1)}, u32[]{:S(2)}, u32[]{:S(2)}) collective-permute-start(bf16[2,1,384,384]{3,2,1,0:T(8,128)(2,1)} %pad_maximum_fusion.3), channel_id=1, source_target_pairs={{0,4},{4,8},{8,12},{1,5},{5,9},{9,13},{2,6},{6,10},{10,14},{3,7},{... | collective-permute-start | bytes 1769480 | tf_op jit(solution)/shard_map/ppermute | solution.py:21
  9.3 55.4 %collective-permute-start.1 = (bf16[2,1,384,384]{3,2,1,0:T(8,128)(2,1)}, bf16[2,1,384,384]{3,2,1,0:T(8,128)(2,1)S(1)}, u32[]{:S(2)}, u32[]{:S(2)}) collective-permute-start(bf16[2,1,384,384]{3,2,1,0:T(8,128)(2,1)} %pad_maximum_fusion.4), channel_id=1, source_target_pairs={{4,0},{8,4},{12,8},{5,1},{9,5},{13,9},{6,2},{10,6},{14,10},{7,3},{... | collective-permute-start | bytes 1769480 | tf_op jit(solution)/shard_map/ppermute | solution.py:21
  10.6 9.3 %copy-start.16 = (s32[8,3]{0,1:T(4,128)S(1)}, s32[8,3]{0,1:T(4,128)}, u32[]{:S(2)}) copy-start(s32[8,3]{0,1:T(4,128)} %param.16) | copy-start | bytes 292
  10.6 9.5 %copy-start.17 = (s32[8]{0:T(128)S(1)}, s32[8]{0:T(128)}, u32[]{:S(2)}) copy-start(s32[8]{0:T(128)} %param.17) | copy-start | bytes 100
  11.5 27.3 %collective-permute-start.3 = (bf16[2,1,384,384]{3,2,1,0:T(8,128)(2,1)}, bf16[2,1,384,384]{3,2,1,0:T(8,128)(2,1)S(1)}, u32[]{:S(2)}, u32[]{:S(2)}) collective-permute-start(bf16[2,1,384,384]{3,2,1,0:T(8,128)(2,1)} %pad_maximum_fusion.6), channel_id=1, source_target_pairs={{4,0},{8,4},{12,8},{5,1},{9,5},{13,9},{6,2},{10,6},{14,10},{7,3},{... | collective-permute-start | bytes 1769480 | tf_op jit(solution)/shard_map/ppermute | solution.py:21
  13.7 25.2 %collective-permute-start.2 = (bf16[2,1,384,384]{3,2,1,0:T(8,128)(2,1)}, bf16[2,1,384,384]{3,2,1,0:T(8,128)(2,1)}, u32[]{:S(2)}, u32[]{:S(2)}) collective-permute-start(bf16[2,1,384,384]{3,2,1,0:T(8,128)(2,1)} %pad_maximum_fusion.5), channel_id=1, source_target_pairs={{0,4},{4,8},{8,12},{1,5},{5,9},{9,13},{2,6},{6,10},{10,14},{3,7},{... | collective-permute-start | bytes 1769480 | tf_op jit(solution)/shard_map/ppermute | solution.py:21
  20.8 37.1 %copy-start.15 = (bf16[768,64]{0,1:T(8,128)(2,1)S(1)}, bf16[768,64]{0,1:T(8,128)(2,1)}, u32[]{:S(2)}) copy-start(bf16[768,64]{0,1:T(8,128)(2,1)} %param.14) | copy-start | bytes 294916
  53.1 33.0 %collective-permute-start.6 = (bf16[2,1,384,384]{3,2,1,0:T(8,128)(2,1)}, bf16[2,1,384,384]{3,2,1,0:T(8,128)(2,1)S(1)}, u32[]{:S(2)}, u32[]{:S(2)}) collective-permute-start(bf16[2,1,384,384]{3,2,1,0:T(8,128)(2,1)} %get-tuple-element.21), channel_id=1, source_target_pairs={{0,4},{4,8},{8,12},{1,5},{5,9},{9,13},{2,6},{6,10},{10,14},{3,7},{... | collective-permute-start | bytes 1769480 | tf_op jit(solution)/shard_map/ppermute | solution.py:21
  56.6 29.5 %collective-permute-start.7 = (bf16[2,1,384,384]{3,2,1,0:T(8,128)(2,1)}, bf16[2,1,384,384]{3,2,1,0:T(8,128)(2,1)}, u32[]{:S(2)}, u32[]{:S(2)}) collective-permute-start(bf16[2,1,384,384]{3,2,1,0:T(8,128)(2,1)} %get-tuple-element.22), channel_id=1, source_target_pairs={{4,0},{8,4},{12,8},{5,1},{9,5},{13,9},{6,2},{10,6},{14,10},{7,3},{... | collective-permute-start | bytes 1769480 | tf_op jit(solution)/shard_map/ppermute | solution.py:21
  58.4 5.7 %collective-permute-start.8 = (f32[1,768,64]{1,2,0:T(8,128)S(1)}, f32[1,768,64]{1,2,0:T(8,128)S(1)}, u32[]{:S(2)}, u32[]{:S(2)}) collective-permute-start(f32[1,768,64]{1,2,0:T(8,128)S(1)} %fusion.13), channel_id=1, source_target_pairs={{0,2},{2,0},{1,3},{3,1},{4,6},{6,4},{5,7},{7,5},{8,10},{10,8},{9,1... | collective-permute-start | bytes 589832 | tf_op jit(solution)/shard_map/ppermute | solution.py:31
  79.8 14.8 %collective-permute-start.4 = (bf16[2,1,384,384]{3,2,1,0:T(8,128)(2,1)}, bf16[2,1,384,384]{3,2,1,0:T(8,128)(2,1)S(1)}, u32[]{:S(2)}, u32[]{:S(2)}) collective-permute-start(bf16[2,1,384,384]{3,2,1,0:T(8,128)(2,1)} %get-tuple-element.18), channel_id=1, source_target_pairs={{0,4},{4,8},{8,12},{1,5},{5,9},{9,13},{2,6},{6,10},{10,14},{3,7},{... | collective-permute-start | bytes 1769480 | tf_op jit(solution)/shard_map/ppermute | solution.py:21
  84.4 14.4 %collective-permute-start.5 = (bf16[2,1,384,384]{3,2,1,0:T(8,128)(2,1)}, bf16[2,1,384,384]{3,2,1,0:T(8,128)(2,1)S(1)}, u32[]{:S(2)}, u32[]{:S(2)}) collective-permute-start(bf16[2,1,384,384]{3,2,1,0:T(8,128)(2,1)} %get-tuple-element.19), channel_id=1, source_target_pairs={{4,0},{8,4},{12,8},{5,1},{9,5},{13,9},{6,2},{10,6},{14,10},{7,3},{... | collective-permute-start | bytes 1769480 | tf_op jit(solution)/shard_map/ppermute | solution.py:21
  88.5 10.5 %copy-start.9 = (bf16[1,768,384]{2,1,0:T(8,128)(2,1)S(1)}, bf16[1,768,384]{2,1,0:T(8,128)(2,1)}, u32[]{:S(2)}) copy-start(bf16[1,768,384]{2,1,0:T(8,128)(2,1)} %get-tuple-element.17) | copy-start | bytes 1769476
  88.5 10.5 %copy-start.10 = (bf16[1,768,384]{2,1,0:T(8,128)(2,1)S(1)}, bf16[1,768,384]{2,1,0:T(8,128)(2,1)}, u32[]{:S(2)}) copy-start(bf16[1,768,384]{2,1,0:T(8,128)(2,1)} %get-tuple-element.23) | copy-start | bytes 1769476
  99.6 5.7 %collective-permute-start.9 = (f32[1,768,64]{1,2,0:T(8,128)S(1)}, f32[1,768,64]{1,2,0:T(8,128)S(1)}, u32[]{:S(2)}, u32[]{:S(2)}) collective-permute-start(f32[1,768,64]{1,2,0:T(8,128)S(1)} %fusion.12), channel_id=1, source_target_pairs={{0,2},{2,0},{1,3},{3,1},{4,6},{6,4},{5,7},{7,5},{8,10},{10,8},{9,1... | collective-permute-start | bytes 589832 | tf_op jit(solution)/shard_map/ppermute | solution.py:31
  110.1 3.6 %collective-permute-start.10 = (f32[49152]{0:T(1024)}, f32[49152]{0:T(1024)}, u32[]{:S(2)}, u32[]{:S(2)}) collective-permute-start(f32[49152]{0:T(1024)} %select_n.71), channel_id=1, source_target_pairs={{0,1},{1,0},{2,3},{3,2},{4,5},{5,4},{6,7},{7,6},{8,9},{9,8},{10,11... | collective-permute-start | bytes 589832 | tf_op jit(solution)/shard_map/ppermute | solution.py:45
  113.7 8.6 %copy-start.11 = (bf16[1,768,384]{2,1,0:T(8,128)(2,1)S(1)}, bf16[1,768,384]{2,1,0:T(8,128)(2,1)}, u32[]{:S(2)}) copy-start(bf16[1,768,384]{2,1,0:T(8,128)(2,1)} %get-tuple-element.16) | copy-start | bytes 1769476
  113.7 8.6 %copy-start.12 = (bf16[1,768,384]{2,1,0:T(8,128)(2,1)S(1)}, bf16[1,768,384]{2,1,0:T(8,128)(2,1)}, u32[]{:S(2)}) copy-start(bf16[1,768,384]{2,1,0:T(8,128)(2,1)} %get-tuple-element.15) | copy-start | bytes 1769476
  114.9 5.3 %collective-permute-start.11 = (f32[24576]{0:T(1024)S(1)}, f32[24576]{0:T(1024)S(1)}, u32[]{:S(2)}, u32[]{:S(2)}) collective-permute-start(f32[24576]{0:T(1024)S(1)} %slice_select_fusion), channel_id=1, source_target_pairs={{0,4},{4,0},{8,12},{12,8},{1,5},{5,1},{9,13},{13,9},{2,6},{6,2},{1... | collective-permute-start | bytes 294920 | tf_op jit(solution)/shard_map/ppermute | solution.py:45
  120.2 7.6 %collective-permute-start.12 = (f32[24576]{0:T(1024)S(1)}, f32[24576]{0:T(1024)S(1)}, u32[]{:S(2)}, u32[]{:S(2)}) collective-permute-start(f32[24576]{0:T(1024)S(1)} %select_add_fusion), channel_id=1, source_target_pairs={{0,8},{4,12},{8,0},{12,4},{1,9},{5,13},{9,1},{13,5},{2,10},{6,14},... | collective-permute-start | bytes 294920 | tf_op jit(solution)/shard_map/ppermute | solution.py:78
  127.8 4.7 %copy-start.2 = (f32[24576]{0:T(1024)}, f32[24576]{0:T(1024)S(1)}, u32[]{:S(2)}) copy-start(f32[24576]{0:T(1024)S(1)} %add.54) | copy-start | bytes 294916
  127.8 4.7 %collective-permute-start.13 = (f32[24576]{0:T(1024)S(1)}, f32[24576]{0:T(1024)S(1)}, u32[]{:S(2)}, u32[]{:S(2)}) collective-permute-start(f32[24576]{0:T(1024)S(1)} %add.54), channel_id=1, source_target_pairs={{0,4},{4,0},{8,12},{12,8},{1,5},{5,1},{9,13},{13,9},{2,6},{6,2},{1... | collective-permute-start | bytes 294920 | tf_op jit(solution)/shard_map/ppermute | solution.py:53
  132.5 2.9 %collective-permute-start.14 = (f32[49152]{0:T(1024)S(1)}, f32[49152]{0:T(1024)S(1)}, u32[]{:S(2)}, u32[]{:S(2)}) collective-permute-start(f32[49152]{0:T(1024)S(1)} %maximum_select_fusion.2), channel_id=1, source_target_pairs={{0,1},{1,0},{2,3},{3,2},{4,5},{5,4},{6,7},{7,6},{8,9},{9,8},{10,11... | collective-permute-start | bytes 589832 | tf_op jit(solution)/shard_map/ppermute | solution.py:53
  (9 other events, 13.0 us)

commit v10 on v7

--- a/solution.py
+++ b/solution.py
@@ -69,10 +69,17 @@
     flat = array.reshape(-1)
     if flat.shape[0] % pieces:
         return lax.psum(array, axes)
-    for axis, distances in plan:
-        flat = scatter_sum(flat, axis, distances)
-    for axis, distances in reversed(plan):
-        flat = gather_back(flat, axis, distances)
+    inner, outer = plan[0], plan[1:]
+    flat = scatter_sum(flat, inner[0], inner[1])
+    for axis, distances in outer:
+        flat = scatter_sum(flat, axis, distances[:-1])
+        if distances:
+            step = distances[-1]
+            flat = flat + lax.ppermute(
+                flat, axis, [(i, i ^ step) for i in range(lax.axis_size(axis))]
+            )
+        flat = gather_back(flat, axis, distances[:-1])
+    flat = gather_back(flat, inner[0], inner[1])
     return flat.reshape(array.shape)
 
 

time: 118 us -> 116 us (0.983)
  waiting for transfers between devices: 34.8 us -> 32.3 us
    ppermute x0 -> x1, waiting for transfers between devices: none -> 6.53 us  [all_sum(): lax.ppermute(flat, axis, [(i, i ^ step) for i in range(lax.axis_size(axis...]
    ppermute x3 -> x2, waiting for transfers between devices: 10.6 us -> 5.61 us  [scatter_sum(): lax.ppermute(send, axis, [(i, i ^ step) for i in range(peers)])]
    ppermute x3 -> x2, waiting for transfers between devices: 7.67 us -> 3.68 us  [gather_back(): other = lax.ppermute(flat, axis, [(i, i ^ step) for i in range(peers)])]
    unnamed x30 -> x32, local copies, waits for them, and re-layouts: 6.43 us -> 6.51 us
  transfers between devices with their start and end apart: 16 -> 15, of which waited for: 11 -> 10; matrix products, arithmetic and copies ran while one was open for 12% -> 12% of each run, Pallas kernels for 23% -> 23%
where the time goes in v10:
time: 116 us; the launch traced here: 115 us
  waiting for transfers between devices  32.3 us (28%)
  starting transfers between devices  28.8 us (25%)
  Pallas kernels  26.8 us (23%)
  local copies, waits for them, and re-layouts  11.1 us (10%)
  other arithmetic  10.8 us (9%)
  matrix products  4.26 us (4%)
    pallas_call x2, Pallas kernels, attention_backward(): pl.pallas_call(attention_kernel, grid=(clip_count, heads), in_specs=[pl.B...  26.8 us
    ppermute x8, starting transfers between devices, shifted(): return lax.ppermute(shard, axis, pairs)  24.3 us
    ppermute x8, waiting for transfers between devices, shifted(): return lax.ppermute(shard, axis, pairs)  13.6 us
    ppermute x1, waiting for transfers between devices, all_sum(): lax.ppermute(flat, axis, [(i, i ^ step) for i in range(lax.axis_size(axis...  6.53 us
    unnamed x32, local copies, waits for them, and re-layouts  6.51 us
    ppermute x2, waiting for transfers between devices, scatter_sum(): lax.ppermute(send, axis, [(i, i ^ step) for i in range(peers)])  5.61 us
    ppermute x2, waiting for transfers between devices, gather_back(): other = lax.ppermute(flat, axis, [(i, i ^ step) for i in range(peers)])  3.68 us
    ppermute x2, starting transfers between devices, butterfly_sum(): other = lax.ppermute(tree, axis, pairs)  3 us
  transfers between devices with their start and end apart: 15, of which 10 were waited for; matrix products, arithmetic and copies ran while one was open for 12% of the time, Pallas kernels for 23%

profile of v10, /device:TPU:0, one launch (start us, length us, event | category | flops | bytes accessed | tf_op | source)
XLA Modules:
  0.0 115.1 jit_solution(1850046219058016555)
XLA Ops:
  0.6 1.9 %slice_bitcast_fusion.9 = (bf16[1,1,384,384]{3,2,1,0:T(8,128)(2,1)S(1)}, bf16[1,1,384,384]{3,2,1,0:T(8,128)(2,1)S(1)}, bf16[1,1,384,384]{3,2,1,0:T(8,128)(2,1)S(...) fusion(bf16[1,768,768]{2,1,0:T(8,128)(2,1)} %v_ref.3, ...), kind=kLoop, calls=%fused_computation.41 | loop fusion | bytes 4718592 | tf_op jit(solution)/shard_map/stack | solution.py:218
  3.5 5.0 %collective-permute-start = (bf16[2,1,384,384]{3,2,1,0:T(8,128)(2,1)}, bf16[2,1,384,384]{3,2,1,0:T(8,128)(2,1)S(1)}, u32[]{:S(2)}, u32[]{:S(2)}) collective-permute-start(bf16[2,1,384,384]{3,2,1,0:T(8,128)(2,1)} %pad_maximum_fusion.3), channel_id=1, source_target_pairs={{0,4},{4,8},{8,12},{1,5},{5,9},{9,13},{2,6},{6,10},{10,14},{3,7},{... | collective-permute-start | bytes 1769480 | tf_op jit(solution)/shard_map/ppermute | solution.py:21
  9.3 1.3 %collective-permute-start.1 = (bf16[2,1,384,384]{3,2,1,0:T(8,128)(2,1)}, bf16[2,1,384,384]{3,2,1,0:T(8,128)(2,1)S(1)}, u32[]{:S(2)}, u32[]{:S(2)}) collective-permute-start(bf16[2,1,384,384]{3,2,1,0:T(8,128)(2,1)} %pad_maximum_fusion.4), channel_id=1, source_target_pairs={{4,0},{8,4},{12,8},{5,1},{9,5},{13,9},{6,2},{10,6},{14,10},{7,3},{... | collective-permute-start | bytes 1769480 | tf_op jit(solution)/shard_map/ppermute | solution.py:21
  11.5 1.3 %collective-permute-start.3 = (bf16[2,1,384,384]{3,2,1,0:T(8,128)(2,1)}, bf16[2,1,384,384]{3,2,1,0:T(8,128)(2,1)S(1)}, u32[]{:S(2)}, u32[]{:S(2)}) collective-permute-start(bf16[2,1,384,384]{3,2,1,0:T(8,128)(2,1)} %pad_maximum_fusion.6), channel_id=1, source_target_pairs={{4,0},{8,4},{12,8},{5,1},{9,5},{13,9},{6,2},{10,6},{14,10},{7,3},{... | collective-permute-start | bytes 1769480 | tf_op jit(solution)/shard_map/ppermute | solution.py:21
  13.7 5.2 %collective-permute-start.2 = (bf16[2,1,384,384]{3,2,1,0:T(8,128)(2,1)}, bf16[2,1,384,384]{3,2,1,0:T(8,128)(2,1)S(1)}, u32[]{:S(2)}, u32[]{:S(2)}) collective-permute-start(bf16[2,1,384,384]{3,2,1,0:T(8,128)(2,1)} %pad_maximum_fusion.5), channel_id=1, source_target_pairs={{0,4},{4,8},{8,12},{1,5},{5,9},{9,13},{2,6},{6,10},{10,14},{3,7},{... | collective-permute-start | bytes 1769480 | tf_op jit(solution)/shard_map/ppermute | solution.py:21
  22.4 5.3 %collective-permute-done.1.right_ref = bf16[2,1,384,384]{3,2,1,0:T(8,128)(2,1)S(1)} collective-permute-done((bf16[2,1,384,384]{3,2,1,0:T(8,128)(2,1)}, bf16[2,1,384,384]{3,2,1,0:T(8,128)(2,1)S(1)}, u32[]{:S(2)}, u32[]{:S(2)}) %collective-permute-start.1) | collective-permute-done | bytes 589856 | tf_op jit(solution)/shard_map/ppermute | solution.py:21
  28.5 13.4 %shard_map.128 = (bf16[1,768,384]{2,1,0:T(8,128)(2,1)}, bf16[1,768,384]{2,1,0:T(8,128)(2,1)}, bf16[1,768,384]{2,1,0:T(8,128)(2,1)}, bf16[2,1,384,384]{3,2,1,0:T(8,128)(2,1)}, bf16[2,1,384,384]{3,2,1,0:T(8,128)(2,1)}) custom-call(f32[6]{0:T(128)} %and_select_fusion.bias_ref, bf16[1,768,768]{2,1,0:T(8,128)(2,1)} %q_ref.3, bf16[1,768,768]{2,1,0:T(8,128)(2,1)} %g_ref.3, ...), custom_call_target="tpu_custom_call" | custom-call | tf_op jit(solution)/shard_map/pallas_call | solution.py:168
  41.9 3.5 %collective-permute-start.4 = (bf16[2,1,384,384]{3,2,1,0:T(8,128)(2,1)}, bf16[2,1,384,384]{3,2,1,0:T(8,128)(2,1)S(1)}, u32[]{:S(2)}, u32[]{:S(2)}) collective-permute-start(bf16[2,1,384,384]{3,2,1,0:T(8,128)(2,1)} %get-tuple-element.18), channel_id=1, source_target_pairs={{0,4},{4,8},{8,12},{1,5},{5,9},{9,13},{2,6},{6,10},{10,14},{3,7},{... | collective-permute-start | bytes 1769480 | tf_op jit(solution)/shard_map/ppermute | solution.py:21
  45.4 1.3 %collective-permute-start.5 = (bf16[2,1,384,384]{3,2,1,0:T(8,128)(2,1)}, bf16[2,1,384,384]{3,2,1,0:T(8,128)(2,1)S(1)}, u32[]{:S(2)}, u32[]{:S(2)}) collective-permute-start(bf16[2,1,384,384]{3,2,1,0:T(8,128)(2,1)} %get-tuple-element.19), channel_id=1, source_target_pairs={{4,0},{8,4},{12,8},{5,1},{9,5},{13,9},{6,2},{10,6},{14,10},{7,3},{... | collective-permute-start | bytes 1769480 | tf_op jit(solution)/shard_map/ppermute | solution.py:21
  48.4 13.4 %shard_map.129 = (bf16[1,768,384]{2,1,0:T(8,128)(2,1)}, bf16[1,768,384]{2,1,0:T(8,128)(2,1)}, bf16[1,768,384]{2,1,0:T(8,128)(2,1)}, bf16[2,1,384,384]{3,2,1,0:T(8,128)(2,1)}, bf16[2,1,384,384]{3,2,1,0:T(8,128)(2,1)}) custom-call(f32[6]{0:T(128)} %and_select_fusion.bias_ref, bf16[1,768,768]{2,1,0:T(8,128)(2,1)} %q_ref.3, bf16[1,768,768]{2,1,0:T(8,128)(2,1)} %g_ref.3, ...), custom_call_target="tpu_custom_call" | custom-call | tf_op jit(solution)/shard_map/pallas_call | solution.py:168
  61.8 5.4 %collective-permute-start.6 = (bf16[2,1,384,384]{3,2,1,0:T(8,128)(2,1)}, bf16[2,1,384,384]{3,2,1,0:T(8,128)(2,1)}, u32[]{:S(2)}, u32[]{:S(2)}) collective-permute-start(bf16[2,1,384,384]{3,2,1,0:T(8,128)(2,1)} %get-tuple-element.21), channel_id=1, source_target_pairs={{0,4},{4,8},{8,12},{1,5},{5,9},{9,13},{2,6},{6,10},{10,14},{3,7},{... | collective-permute-start | bytes 1769480 | tf_op jit(solution)/shard_map/ppermute | solution.py:21
  67.2 1.5 %collective-permute-start.7 = (bf16[2,1,384,384]{3,2,1,0:T(8,128)(2,1)}, bf16[2,1,384,384]{3,2,1,0:T(8,128)(2,1)}, u32[]{:S(2)}, u32[]{:S(2)}) collective-permute-start(bf16[2,1,384,384]{3,2,1,0:T(8,128)(2,1)} %get-tuple-element.22), channel_id=1, source_target_pairs={{4,0},{8,4},{12,8},{5,1},{9,5},{13,9},{6,2},{10,6},{14,10},{7,3},{... | collective-permute-start | bytes 1769480 | tf_op jit(solution)/shard_map/ppermute | solution.py:21
  68.7 2.1 %fusion.19 = f32[1,768,64]{1,2,0:T(8,128)} fusion(bf16[768,64]{0,1:T(8,128)(2,1)} %param.14, bf16[1,768,768]{2,1,0:T(8,128)(2,1)S(1)} %copy-done), kind=kOutput, calls=%fused_computation.26 | convolution fusion | flops 75497472 | bytes 1474560 | tf_op jit(solution)/shard_map/pqg,gv->pqv/dot_general | solution.py:192
  70.7 1.5 %collective-permute-start.8 = (f32[1,768,64]{1,2,0:T(8,128)}, f32[1,768,64]{1,2,0:T(8,128)}, u32[]{:S(2)}, u32[]{:S(2)}) collective-permute-start(f32[1,768,64]{1,2,0:T(8,128)} %fusion.19), channel_id=1, source_target_pairs={{0,2},{2,0},{1,3},{3,1},{4,6},{6,4},{5,7},{7,5},{8,10},{10,8},{9,1... | collective-permute-start | bytes 589832 | tf_op jit(solution)/shard_map/ppermute | solution.py:31
  73.8 2.2 %collective-permute-done.6 = bf16[2,1,384,384]{3,2,1,0:T(8,128)(2,1)} collective-permute-done((bf16[2,1,384,384]{3,2,1,0:T(8,128)(2,1)}, bf16[2,1,384,384]{3,2,1,0:T(8,128)(2,1)}, u32[]{:S(2)}, u32[]{:S(2)}) %collective-permute-start.6) | collective-permute-done | bytes 589856 | tf_op jit(solution)/shard_map/ppermute | solution.py:21
  76.0 4.9 %collective-permute-done.7 = bf16[2,1,384,384]{3,2,1,0:T(8,128)(2,1)} collective-permute-done((bf16[2,1,384,384]{3,2,1,0:T(8,128)(2,1)}, bf16[2,1,384,384]{3,2,1,0:T(8,128)(2,1)}, u32[]{:S(2)}, u32[]{:S(2)}) %collective-permute-start.7) | collective-permute-done | bytes 589856 | tf_op jit(solution)/shard_map/ppermute | solution.py:21
  81.0 1.4 %maximum_convert_fusion.1 = f32[2,1,768,384]{3,2,1,0:T(8,128)S(1)} fusion(bf16[2,1,384,384]{3,2,1,0:T(8,128)(2,1)} %collective-permute-done.7, bf16[2,1,384,384]{3,2,1,0:T(8,128)(2,1)} %collective-permute-done.6), kind=kLoop, calls=%fused_computation.14 | loop fusion | flops 2359296 | bytes 3538944 | tf_op jit(solution)/shard_map/convert_element_type | solution.py:225
  84.0 1.5 %collective-permute-start.9 = (f32[1,768,64]{1,2,0:T(8,128)S(1)}, f32[1,768,64]{1,2,0:T(8,128)S(1)}, u32[]{:S(2)}, u32[]{:S(2)}) collective-permute-start(f32[1,768,64]{1,2,0:T(8,128)S(1)} %fusion.16), channel_id=1, source_target_pairs={{0,2},{2,0},{1,3},{3,1},{4,6},{6,4},{5,7},{7,5},{8,10},{10,8},{9,1... | collective-permute-start | bytes 589832 | tf_op jit(solution)/shard_map/ppermute | solution.py:31
  85.5 1.4 %fusion.22 = f32[768,64]{0,1:T(8,128)S(1)} fusion(bf16[1,768,768]{2,1,0:T(8,128)(2,1)S(1)} %pad_maximum_fusion.2, f32[1,768,64]{1,2,0:T(8,128)} %fusion.19, f32[1,768,64]{1,2,0:T(8,128)} %collective-permute-done.8), kind=kOutput, calls=%fused_computation.27 | convolution fusion | flops 75644928 | bytes 1769472 | tf_op jit(solution)/shard_map/igb,igu->bu/dot_general | solution.py:240
  86.9 2.8 %collective-permute-done.9 = f32[1,768,64]{1,2,0:T(8,128)S(1)} collective-permute-done((f32[1,768,64]{1,2,0:T(8,128)S(1)}, f32[1,768,64]{1,2,0:T(8,128)S(1)}, u32[]{:S(2)}, u32[]{:S(2)}) %collective-permute-start.9) | collective-permute-done | bytes 196640 | tf_op jit(solution)/shard_map/ppermute | solution.py:31
  91.4 1.5 %collective-permute-done.10 = f32[49152]{0:T(1024)} collective-permute-done((f32[49152]{0:T(1024)}, f32[49152]{0:T(1024)}, u32[]{:S(2)}, u32[]{:S(2)}) %collective-permute-start.10) | collective-permute-done | bytes 196640 | tf_op jit(solution)/shard_map/ppermute | solution.py:45
  94.6 4.1 %collective-permute-done.11 = f32[24576]{0:T(1024)S(1)} collective-permute-done((f32[24576]{0:T(1024)S(1)}, f32[24576]{0:T(1024)S(1)}, u32[]{:S(2)}, u32[]{:S(2)}) %collective-permute-start.11) | collective-permute-done | bytes 98336 | tf_op jit(solution)/shard_map/ppermute | solution.py:45
  99.3 6.5 %collective-permute-done.12 = f32[24576]{0:T(1024)S(1)} collective-permute-done((f32[24576]{0:T(1024)S(1)}, f32[24576]{0:T(1024)S(1)}, u32[]{:S(2)}, u32[]{:S(2)}) %collective-permute-start.12) | collective-permute-done | bytes 98336 | tf_op jit(solution)/shard_map/ppermute | solution.py:78
  107.1 3.5 %collective-permute-done.13 = f32[24576]{0:T(1024)S(1)} collective-permute-done((f32[24576]{0:T(1024)S(1)}, f32[24576]{0:T(1024)S(1)}, u32[]{:S(2)}, u32[]{:S(2)}) %collective-permute-start.13) | collective-permute-done | bytes 98336 | tf_op jit(solution)/shard_map/ppermute | solution.py:53
  (79 shorter events, 22.3 us)
Async XLA Ops:
  0.6 68.0 %copy-start = (bf16[1,768,768]{2,1,0:T(8,128)(2,1)S(1)}, bf16[1,768,768]{2,1,0:T(8,128)(2,1)}, u32[]{:S(2)}) copy-start(bf16[1,768,768]{2,1,0:T(8,128)(2,1)} %param.13) | copy-start | bytes 3538948
  3.5 19.0 %collective-permute-start = (bf16[2,1,384,384]{3,2,1,0:T(8,128)(2,1)}, bf16[2,1,384,384]{3,2,1,0:T(8,128)(2,1)S(1)}, u32[]{:S(2)}, u32[]{:S(2)}) collective-permute-start(bf16[2,1,384,384]{3,2,1,0:T(8,128)(2,1)} %pad_maximum_fusion.3), channel_id=1, source_target_pairs={{0,4},{4,8},{8,12},{1,5},{5,9},{9,13},{2,6},{6,10},{10,14},{3,7},{... | collective-permute-start | bytes 1769480 | tf_op jit(solution)/shard_map/ppermute | solution.py:21
  9.3 18.3 %collective-permute-start.1 = (bf16[2,1,384,384]{3,2,1,0:T(8,128)(2,1)}, bf16[2,1,384,384]{3,2,1,0:T(8,128)(2,1)S(1)}, u32[]{:S(2)}, u32[]{:S(2)}) collective-permute-start(bf16[2,1,384,384]{3,2,1,0:T(8,128)(2,1)} %pad_maximum_fusion.4), channel_id=1, source_target_pairs={{4,0},{8,4},{12,8},{5,1},{9,5},{13,9},{6,2},{10,6},{14,10},{7,3},{... | collective-permute-start | bytes 1769480 | tf_op jit(solution)/shard_map/ppermute | solution.py:21
  10.6 9.0 %copy-start.13 = (s32[8,3]{0,1:T(4,128)S(1)}, s32[8,3]{0,1:T(4,128)}, u32[]{:S(2)}) copy-start(s32[8,3]{0,1:T(4,128)} %param.16) | copy-start | bytes 292
  11.5 35.2 %collective-permute-start.3 = (bf16[2,1,384,384]{3,2,1,0:T(8,128)(2,1)}, bf16[2,1,384,384]{3,2,1,0:T(8,128)(2,1)S(1)}, u32[]{:S(2)}, u32[]{:S(2)}) collective-permute-start(bf16[2,1,384,384]{3,2,1,0:T(8,128)(2,1)} %pad_maximum_fusion.6), channel_id=1, source_target_pairs={{4,0},{8,4},{12,8},{5,1},{9,5},{13,9},{6,2},{10,6},{14,10},{7,3},{... | collective-permute-start | bytes 1769480 | tf_op jit(solution)/shard_map/ppermute | solution.py:21
  13.7 33.1 %collective-permute-start.2 = (bf16[2,1,384,384]{3,2,1,0:T(8,128)(2,1)}, bf16[2,1,384,384]{3,2,1,0:T(8,128)(2,1)S(1)}, u32[]{:S(2)}, u32[]{:S(2)}) collective-permute-start(bf16[2,1,384,384]{3,2,1,0:T(8,128)(2,1)} %pad_maximum_fusion.5), channel_id=1, source_target_pairs={{0,4},{4,8},{8,12},{1,5},{5,9},{9,13},{2,6},{6,10},{10,14},{3,7},{... | collective-permute-start | bytes 1769480 | tf_op jit(solution)/shard_map/ppermute | solution.py:21
  22.4 5.3 %copy-start.4 = (bf16[2,1,384,384]{3,2,1,0:T(8,128)(2,1)}, bf16[2,1,384,384]{3,2,1,0:T(8,128)(2,1)S(1)}, u32[]{:S(2)}) copy-start(bf16[2,1,384,384]{3,2,1,0:T(8,128)(2,1)S(1)} %collective-permute-done.left_ref) | copy-start | bytes 1769476
  41.9 30.3 %collective-permute-start.4 = (bf16[2,1,384,384]{3,2,1,0:T(8,128)(2,1)}, bf16[2,1,384,384]{3,2,1,0:T(8,128)(2,1)S(1)}, u32[]{:S(2)}, u32[]{:S(2)}) collective-permute-start(bf16[2,1,384,384]{3,2,1,0:T(8,128)(2,1)} %get-tuple-element.18), channel_id=1, source_target_pairs={{0,4},{4,8},{8,12},{1,5},{5,9},{9,13},{2,6},{6,10},{10,14},{3,7},{... | collective-permute-start | bytes 1769480 | tf_op jit(solution)/shard_map/ppermute | solution.py:21
  45.4 26.8 %collective-permute-start.5 = (bf16[2,1,384,384]{3,2,1,0:T(8,128)(2,1)}, bf16[2,1,384,384]{3,2,1,0:T(8,128)(2,1)S(1)}, u32[]{:S(2)}, u32[]{:S(2)}) collective-permute-start(bf16[2,1,384,384]{3,2,1,0:T(8,128)(2,1)} %get-tuple-element.19), channel_id=1, source_target_pairs={{4,0},{8,4},{12,8},{5,1},{9,5},{13,9},{6,2},{10,6},{14,10},{7,3},{... | collective-permute-start | bytes 1769480 | tf_op jit(solution)/shard_map/ppermute | solution.py:21
  61.8 14.2 %collective-permute-start.6 = (bf16[2,1,384,384]{3,2,1,0:T(8,128)(2,1)}, bf16[2,1,384,384]{3,2,1,0:T(8,128)(2,1)}, u32[]{:S(2)}, u32[]{:S(2)}) collective-permute-start(bf16[2,1,384,384]{3,2,1,0:T(8,128)(2,1)} %get-tuple-element.21), channel_id=1, source_target_pairs={{0,4},{4,8},{8,12},{1,5},{5,9},{9,13},{2,6},{6,10},{10,14},{3,7},{... | collective-permute-start | bytes 1769480 | tf_op jit(solution)/shard_map/ppermute | solution.py:21
  67.2 13.8 %collective-permute-start.7 = (bf16[2,1,384,384]{3,2,1,0:T(8,128)(2,1)}, bf16[2,1,384,384]{3,2,1,0:T(8,128)(2,1)}, u32[]{:S(2)}, u32[]{:S(2)}) collective-permute-start(bf16[2,1,384,384]{3,2,1,0:T(8,128)(2,1)} %get-tuple-element.22), channel_id=1, source_target_pairs={{4,0},{8,4},{12,8},{5,1},{9,5},{13,9},{6,2},{10,6},{14,10},{7,3},{... | collective-permute-start | bytes 1769480 | tf_op jit(solution)/shard_map/ppermute | solution.py:21
  70.7 14.8 %collective-permute-start.8 = (f32[1,768,64]{1,2,0:T(8,128)}, f32[1,768,64]{1,2,0:T(8,128)}, u32[]{:S(2)}, u32[]{:S(2)}) collective-permute-start(f32[1,768,64]{1,2,0:T(8,128)} %fusion.19), channel_id=1, source_target_pairs={{0,2},{2,0},{1,3},{3,1},{4,6},{6,4},{5,7},{7,5},{8,10},{10,8},{9,1... | collective-permute-start | bytes 589832 | tf_op jit(solution)/shard_map/ppermute | solution.py:31
  72.3 1.2 %copy-start.6 = (bf16[1,768,384]{2,1,0:T(8,128)(2,1)S(1)}, bf16[1,768,384]{2,1,0:T(8,128)(2,1)}, u32[]{:S(2)}) copy-start(bf16[1,768,384]{2,1,0:T(8,128)(2,1)} %get-tuple-element.23) | copy-start | bytes 1769476
  73.8 8.6 %copy-start.8 = (bf16[1,768,384]{2,1,0:T(8,128)(2,1)S(1)}, bf16[1,768,384]{2,1,0:T(8,128)(2,1)}, u32[]{:S(2)}) copy-start(bf16[1,768,384]{2,1,0:T(8,128)(2,1)} %get-tuple-element.20) | copy-start | bytes 1769476
  73.8 8.6 %copy-start.9 = (bf16[1,768,384]{2,1,0:T(8,128)(2,1)S(1)}, bf16[1,768,384]{2,1,0:T(8,128)(2,1)}, u32[]{:S(2)}) copy-start(bf16[1,768,384]{2,1,0:T(8,128)(2,1)} %get-tuple-element.24) | copy-start | bytes 1769476
  83.6 3.4 %copy-start.1 = (bf16[1,768,768]{2,1,0:T(8,128)(2,1)}, bf16[1,768,768]{2,1,0:T(8,128)(2,1)S(1)}, u32[]{:S(2)}) copy-start(bf16[1,768,768]{2,1,0:T(8,128)(2,1)S(1)} %pad_maximum_fusion.2) | copy-start | bytes 3538948
  84.0 5.7 %collective-permute-start.9 = (f32[1,768,64]{1,2,0:T(8,128)S(1)}, f32[1,768,64]{1,2,0:T(8,128)S(1)}, u32[]{:S(2)}, u32[]{:S(2)}) collective-permute-start(f32[1,768,64]{1,2,0:T(8,128)S(1)} %fusion.16), channel_id=1, source_target_pairs={{0,2},{2,0},{1,3},{3,1},{4,6},{6,4},{5,7},{7,5},{8,10},{10,8},{9,1... | collective-permute-start | bytes 589832 | tf_op jit(solution)/shard_map/ppermute | solution.py:31
  91.1 1.8 %collective-permute-start.10 = (f32[49152]{0:T(1024)}, f32[49152]{0:T(1024)}, u32[]{:S(2)}, u32[]{:S(2)}) collective-permute-start(f32[49152]{0:T(1024)} %select_n.63), channel_id=1, source_target_pairs={{0,1},{1,0},{2,3},{3,2},{4,5},{5,4},{6,7},{7,6},{8,9},{9,8},{10,11... | collective-permute-start | bytes 589832 | tf_op jit(solution)/shard_map/ppermute | solution.py:45
  91.2 14.7 %copy-start.10 = (bf16[1,768,384]{2,1,0:T(8,128)(2,1)S(1)}, bf16[1,768,384]{2,1,0:T(8,128)(2,1)}, u32[]{:S(2)}) copy-start(bf16[1,768,384]{2,1,0:T(8,128)(2,1)} %get-tuple-element.15) | copy-start | bytes 1769476
  91.4 14.6 %copy-start.11 = (bf16[1,768,384]{2,1,0:T(8,128)(2,1)S(1)}, bf16[1,768,384]{2,1,0:T(8,128)(2,1)}, u32[]{:S(2)}) copy-start(bf16[1,768,384]{2,1,0:T(8,128)(2,1)} %get-tuple-element.16) | copy-start | bytes 1769476
  93.8 4.9 %collective-permute-start.11 = (f32[24576]{0:T(1024)S(1)}, f32[24576]{0:T(1024)S(1)}, u32[]{:S(2)}, u32[]{:S(2)}) collective-permute-start(f32[24576]{0:T(1024)S(1)} %slice_select_fusion), channel_id=1, source_target_pairs={{0,4},{4,0},{8,12},{12,8},{1,5},{5,1},{9,13},{13,9},{2,6},{6,2},{1... | collective-permute-start | bytes 294920 | tf_op jit(solution)/shard_map/ppermute | solution.py:45
  98.8 7.1 %collective-permute-start.12 = (f32[24576]{0:T(1024)S(1)}, f32[24576]{0:T(1024)S(1)}, u32[]{:S(2)}, u32[]{:S(2)}) collective-permute-start(f32[24576]{0:T(1024)S(1)} %select_add_fusion), channel_id=1, source_target_pairs={{0,8},{4,12},{8,0},{12,4},{1,9},{5,13},{9,1},{13,5},{2,10},{6,14},... | collective-permute-start | bytes 294920 | tf_op jit(solution)/shard_map/ppermute | solution.py:78
  105.8 4.7 %collective-permute-start.13 = (f32[24576]{0:T(1024)S(1)}, f32[24576]{0:T(1024)S(1)}, u32[]{:S(2)}, u32[]{:S(2)}) collective-permute-start(f32[24576]{0:T(1024)S(1)} %add.46), channel_id=1, source_target_pairs={{0,4},{4,0},{8,12},{12,8},{1,5},{5,1},{9,13},{13,9},{2,6},{6,2},{1... | collective-permute-start | bytes 294920 | tf_op jit(solution)/shard_map/ppermute | solution.py:53
  110.6 1.6 %collective-permute-start.14 = (f32[49152]{0:T(1024)S(1)}, f32[49152]{0:T(1024)}, u32[]{:S(2)}, u32[]{:S(2)}) collective-permute-start(f32[49152]{0:T(1024)S(1)} %maximum_select_fusion.2), channel_id=1, source_target_pairs={{0,1},{1,0},{2,3},{3,2},{4,5},{5,4},{6,7},{7,6},{8,9},{9,8},{10,11... | collective-permute-start | bytes 589832 | tf_op jit(solution)/shard_map/ppermute | solution.py:53
  (6 other events, 4.9 us)

commit v11 on v10

--- a/solution.py
+++ b/solution.py
@@ -111,15 +111,14 @@
 
 def tile_pass(bias_ref, first, tile_query, tile_grad, keys, values):
     score_scale = HEAD_SIZE ** (-0.5)
-    scores = [
-        score_scale * nt_dot(tile_query, k) + bias_ref[first + i] for i, k in enumerate(keys)
-    ]
-    row_max = jnp.max(scores[0], axis=-1, keepdims=True)
-    for s in scores[1:]:
-        row_max = jnp.maximum(row_max, jnp.max(s, axis=-1, keepdims=True))
-    total = sum(jnp.sum(jnp.exp(s - row_max), axis=-1, keepdims=True) for s in scores)
-    log_total = row_max + jnp.log(total)
-    weights = [jnp.exp(s - log_total).astype(jnp.bfloat16) for s in scores]
+    scores = [score_scale * nt_dot(tile_query, k) for k in keys]
+    row_max = jnp.max(scores[0], axis=-1, keepdims=True) + bias_ref[first]
+    for i, s in enumerate(scores[1:], 1):
+        row_max = jnp.maximum(row_max, jnp.max(s, axis=-1, keepdims=True) + bias_ref[first + i])
+    probs = [jnp.exp(s - (row_max - bias_ref[first + i])) for i, s in enumerate(scores)]
+    total = sum(jnp.sum(p, axis=-1, keepdims=True) for p in probs)
+    inverse = 1.0 / total
+    weights = [(p * inverse).astype(jnp.bfloat16) for p in probs]
     grad_weights = [nt_dot(tile_grad, v) for v in values]
     row_dot = sum(
         jnp.sum(w.astype(jnp.float32) * g, axis=-1, keepdims=True)

time: 116 us -> 116 us (level)
  no operation moved by 1% of the time
where the time goes in v11:
time: 116 us; the launch traced here: 115 us
  waiting for transfers between devices  32.2 us (28%)
  starting transfers between devices  28.8 us (25%)
  Pallas kernels  27 us (23%)
  local copies, waits for them, and re-layouts  11.1 us (10%)
  other arithmetic  10.8 us (9%)
  matrix products  4.26 us (4%)
    pallas_call x2, Pallas kernels, attention_backward(): pl.pallas_call(attention_kernel, grid=(clip_count, heads), in_specs=[pl.B...  27 us
    ppermute x8, starting transfers between devices, shifted(): return lax.ppermute(shard, axis, pairs)  24.3 us
    ppermute x8, waiting for transfers between devices, shifted(): return lax.ppermute(shard, axis, pairs)  13.6 us
    ppermute x1, waiting for transfers between devices, all_sum(): lax.ppermute(flat, axis, [(i, i ^ step) for i in range(lax.axis_size(axis...  6.54 us
    unnamed x32, local copies, waits for them, and re-layouts  6.51 us
    ppermute x2, waiting for transfers between devices, scatter_sum(): lax.ppermute(send, axis, [(i, i ^ step) for i in range(peers)])  5.58 us
    ppermute x2, waiting for transfers between devices, gather_back(): other = lax.ppermute(flat, axis, [(i, i ^ step) for i in range(peers)])  3.68 us
    ppermute x2, starting transfers between devices, butterfly_sum(): other = lax.ppermute(tree, axis, pairs)  3.03 us
  transfers between devices with their start and end apart: 15, of which 10 were waited for; matrix products, arithmetic and copies ran while one was open for 12% of the time, Pallas kernels for 23%

profile of v11, /device:TPU:0, one launch (start us, length us, event | category | flops | bytes accessed | tf_op | source)
XLA Modules:
  0.0 115.2 jit_solution(9638940966917904528)
XLA Ops:
  0.6 1.9 %slice_bitcast_fusion.9 = (bf16[1,1,384,384]{3,2,1,0:T(8,128)(2,1)S(1)}, bf16[1,1,384,384]{3,2,1,0:T(8,128)(2,1)S(1)}, bf16[1,1,384,384]{3,2,1,0:T(8,128)(2,1)S(...) fusion(bf16[1,768,768]{2,1,0:T(8,128)(2,1)} %v_ref.3, ...), kind=kLoop, calls=%fused_computation.41 | loop fusion | bytes 4718592 | tf_op jit(solution)/shard_map/stack | solution.py:217
  3.5 5.0 %collective-permute-start = (bf16[2,1,384,384]{3,2,1,0:T(8,128)(2,1)}, bf16[2,1,384,384]{3,2,1,0:T(8,128)(2,1)S(1)}, u32[]{:S(2)}, u32[]{:S(2)}) collective-permute-start(bf16[2,1,384,384]{3,2,1,0:T(8,128)(2,1)} %pad_maximum_fusion.3), channel_id=1, source_target_pairs={{0,4},{4,8},{8,12},{1,5},{5,9},{9,13},{2,6},{6,10},{10,14},{3,7},{... | collective-permute-start | bytes 1769480 | tf_op jit(solution)/shard_map/ppermute | solution.py:21
  9.3 1.3 %collective-permute-start.1 = (bf16[2,1,384,384]{3,2,1,0:T(8,128)(2,1)}, bf16[2,1,384,384]{3,2,1,0:T(8,128)(2,1)S(1)}, u32[]{:S(2)}, u32[]{:S(2)}) collective-permute-start(bf16[2,1,384,384]{3,2,1,0:T(8,128)(2,1)} %pad_maximum_fusion.4), channel_id=1, source_target_pairs={{4,0},{8,4},{12,8},{5,1},{9,5},{13,9},{6,2},{10,6},{14,10},{7,3},{... | collective-permute-start | bytes 1769480 | tf_op jit(solution)/shard_map/ppermute | solution.py:21
  11.5 1.3 %collective-permute-start.3 = (bf16[2,1,384,384]{3,2,1,0:T(8,128)(2,1)}, bf16[2,1,384,384]{3,2,1,0:T(8,128)(2,1)S(1)}, u32[]{:S(2)}, u32[]{:S(2)}) collective-permute-start(bf16[2,1,384,384]{3,2,1,0:T(8,128)(2,1)} %pad_maximum_fusion.6), channel_id=1, source_target_pairs={{4,0},{8,4},{12,8},{5,1},{9,5},{13,9},{6,2},{10,6},{14,10},{7,3},{... | collective-permute-start | bytes 1769480 | tf_op jit(solution)/shard_map/ppermute | solution.py:21
  13.7 5.2 %collective-permute-start.2 = (bf16[2,1,384,384]{3,2,1,0:T(8,128)(2,1)}, bf16[2,1,384,384]{3,2,1,0:T(8,128)(2,1)S(1)}, u32[]{:S(2)}, u32[]{:S(2)}) collective-permute-start(bf16[2,1,384,384]{3,2,1,0:T(8,128)(2,1)} %pad_maximum_fusion.5), channel_id=1, source_target_pairs={{0,4},{4,8},{8,12},{1,5},{5,9},{9,13},{2,6},{6,10},{10,14},{3,7},{... | collective-permute-start | bytes 1769480 | tf_op jit(solution)/shard_map/ppermute | solution.py:21
  22.4 5.3 %collective-permute-done.1.right_ref = bf16[2,1,384,384]{3,2,1,0:T(8,128)(2,1)S(1)} collective-permute-done((bf16[2,1,384,384]{3,2,1,0:T(8,128)(2,1)}, bf16[2,1,384,384]{3,2,1,0:T(8,128)(2,1)S(1)}, u32[]{:S(2)}, u32[]{:S(2)}) %collective-permute-start.1) | collective-permute-done | bytes 589856 | tf_op jit(solution)/shard_map/ppermute | solution.py:21
  28.5 13.5 %shard_map.128 = (bf16[1,768,384]{2,1,0:T(8,128)(2,1)}, bf16[1,768,384]{2,1,0:T(8,128)(2,1)}, bf16[1,768,384]{2,1,0:T(8,128)(2,1)}, bf16[2,1,384,384]{3,2,1,0:T(8,128)(2,1)}, bf16[2,1,384,384]{3,2,1,0:T(8,128)(2,1)}) custom-call(f32[6]{0:T(128)} %and_select_fusion.bias_ref, bf16[1,768,768]{2,1,0:T(8,128)(2,1)} %q_ref.3, bf16[1,768,768]{2,1,0:T(8,128)(2,1)} %g_ref.3, ...), custom_call_target="tpu_custom_call" | custom-call | tf_op jit(solution)/shard_map/pallas_call | solution.py:167
  42.0 3.5 %collective-permute-start.4 = (bf16[2,1,384,384]{3,2,1,0:T(8,128)(2,1)}, bf16[2,1,384,384]{3,2,1,0:T(8,128)(2,1)S(1)}, u32[]{:S(2)}, u32[]{:S(2)}) collective-permute-start(bf16[2,1,384,384]{3,2,1,0:T(8,128)(2,1)} %get-tuple-element.18), channel_id=1, source_target_pairs={{0,4},{4,8},{8,12},{1,5},{5,9},{9,13},{2,6},{6,10},{10,14},{3,7},{... | collective-permute-start | bytes 1769480 | tf_op jit(solution)/shard_map/ppermute | solution.py:21
  45.5 1.3 %collective-permute-start.5 = (bf16[2,1,384,384]{3,2,1,0:T(8,128)(2,1)}, bf16[2,1,384,384]{3,2,1,0:T(8,128)(2,1)S(1)}, u32[]{:S(2)}, u32[]{:S(2)}) collective-permute-start(bf16[2,1,384,384]{3,2,1,0:T(8,128)(2,1)} %get-tuple-element.19), channel_id=1, source_target_pairs={{4,0},{8,4},{12,8},{5,1},{9,5},{13,9},{6,2},{10,6},{14,10},{7,3},{... | collective-permute-start | bytes 1769480 | tf_op jit(solution)/shard_map/ppermute | solution.py:21
  48.5 13.5 %shard_map.129 = (bf16[1,768,384]{2,1,0:T(8,128)(2,1)}, bf16[1,768,384]{2,1,0:T(8,128)(2,1)}, bf16[1,768,384]{2,1,0:T(8,128)(2,1)}, bf16[2,1,384,384]{3,2,1,0:T(8,128)(2,1)}, bf16[2,1,384,384]{3,2,1,0:T(8,128)(2,1)}) custom-call(f32[6]{0:T(128)} %and_select_fusion.bias_ref, bf16[1,768,768]{2,1,0:T(8,128)(2,1)} %q_ref.3, bf16[1,768,768]{2,1,0:T(8,128)(2,1)} %g_ref.3, ...), custom_call_target="tpu_custom_call" | custom-call | tf_op jit(solution)/shard_map/pallas_call | solution.py:167
  62.0 5.4 %collective-permute-start.6 = (bf16[2,1,384,384]{3,2,1,0:T(8,128)(2,1)}, bf16[2,1,384,384]{3,2,1,0:T(8,128)(2,1)}, u32[]{:S(2)}, u32[]{:S(2)}) collective-permute-start(bf16[2,1,384,384]{3,2,1,0:T(8,128)(2,1)} %get-tuple-element.21), channel_id=1, source_target_pairs={{0,4},{4,8},{8,12},{1,5},{5,9},{9,13},{2,6},{6,10},{10,14},{3,7},{... | collective-permute-start | bytes 1769480 | tf_op jit(solution)/shard_map/ppermute | solution.py:21
  67.4 1.5 %collective-permute-start.7 = (bf16[2,1,384,384]{3,2,1,0:T(8,128)(2,1)}, bf16[2,1,384,384]{3,2,1,0:T(8,128)(2,1)}, u32[]{:S(2)}, u32[]{:S(2)}) collective-permute-start(bf16[2,1,384,384]{3,2,1,0:T(8,128)(2,1)} %get-tuple-element.22), channel_id=1, source_target_pairs={{4,0},{8,4},{12,8},{5,1},{9,5},{13,9},{6,2},{10,6},{14,10},{7,3},{... | collective-permute-start | bytes 1769480 | tf_op jit(solution)/shard_map/ppermute | solution.py:21
  68.8 2.1 %fusion.19 = f32[1,768,64]{1,2,0:T(8,128)} fusion(bf16[768,64]{0,1:T(8,128)(2,1)} %param.14, bf16[1,768,768]{2,1,0:T(8,128)(2,1)S(1)} %copy-done), kind=kOutput, calls=%fused_computation.26 | convolution fusion | flops 75497472 | bytes 1474560 | tf_op jit(solution)/shard_map/pqg,gv->pqv/dot_general | solution.py:191
  70.9 1.5 %collective-permute-start.8 = (f32[1,768,64]{1,2,0:T(8,128)}, f32[1,768,64]{1,2,0:T(8,128)}, u32[]{:S(2)}, u32[]{:S(2)}) collective-permute-start(f32[1,768,64]{1,2,0:T(8,128)} %fusion.19), channel_id=1, source_target_pairs={{0,2},{2,0},{1,3},{3,1},{4,6},{6,4},{5,7},{7,5},{8,10},{10,8},{9,1... | collective-permute-start | bytes 589832 | tf_op jit(solution)/shard_map/ppermute | solution.py:31
  74.0 2.2 %collective-permute-done.6 = bf16[2,1,384,384]{3,2,1,0:T(8,128)(2,1)} collective-permute-done((bf16[2,1,384,384]{3,2,1,0:T(8,128)(2,1)}, bf16[2,1,384,384]{3,2,1,0:T(8,128)(2,1)}, u32[]{:S(2)}, u32[]{:S(2)}) %collective-permute-start.6) | collective-permute-done | bytes 589856 | tf_op jit(solution)/shard_map/ppermute | solution.py:21
  76.2 4.9 %collective-permute-done.7 = bf16[2,1,384,384]{3,2,1,0:T(8,128)(2,1)} collective-permute-done((bf16[2,1,384,384]{3,2,1,0:T(8,128)(2,1)}, bf16[2,1,384,384]{3,2,1,0:T(8,128)(2,1)}, u32[]{:S(2)}, u32[]{:S(2)}) %collective-permute-start.7) | collective-permute-done | bytes 589856 | tf_op jit(solution)/shard_map/ppermute | solution.py:21
  81.2 1.4 %maximum_convert_fusion.1 = f32[2,1,768,384]{3,2,1,0:T(8,128)S(1)} fusion(bf16[2,1,384,384]{3,2,1,0:T(8,128)(2,1)} %collective-permute-done.7, bf16[2,1,384,384]{3,2,1,0:T(8,128)(2,1)} %collective-permute-done.6), kind=kLoop, calls=%fused_computation.14 | loop fusion | flops 2359296 | bytes 3538944 | tf_op jit(solution)/shard_map/convert_element_type | solution.py:224
  84.2 1.5 %collective-permute-start.9 = (f32[1,768,64]{1,2,0:T(8,128)S(1)}, f32[1,768,64]{1,2,0:T(8,128)S(1)}, u32[]{:S(2)}, u32[]{:S(2)}) collective-permute-start(f32[1,768,64]{1,2,0:T(8,128)S(1)} %fusion.16), channel_id=1, source_target_pairs={{0,2},{2,0},{1,3},{3,1},{4,6},{6,4},{5,7},{7,5},{8,10},{10,8},{9,1... | collective-permute-start | bytes 589832 | tf_op jit(solution)/shard_map/ppermute | solution.py:31
  85.8 1.4 %fusion.22 = f32[768,64]{0,1:T(8,128)S(1)} fusion(bf16[1,768,768]{2,1,0:T(8,128)(2,1)S(1)} %pad_maximum_fusion.2, f32[1,768,64]{1,2,0:T(8,128)} %fusion.19, f32[1,768,64]{1,2,0:T(8,128)} %collective-permute-done.8), kind=kOutput, calls=%fused_computation.27 | convolution fusion | flops 75644928 | bytes 1769472 | tf_op jit(solution)/shard_map/igb,igu->bu/dot_general | solution.py:239
  87.1 2.8 %collective-permute-done.9 = f32[1,768,64]{1,2,0:T(8,128)S(1)} collective-permute-done((f32[1,768,64]{1,2,0:T(8,128)S(1)}, f32[1,768,64]{1,2,0:T(8,128)S(1)}, u32[]{:S(2)}, u32[]{:S(2)}) %collective-permute-start.9) | collective-permute-done | bytes 196640 | tf_op jit(solution)/shard_map/ppermute | solution.py:31
  91.6 1.5 %collective-permute-done.10 = f32[49152]{0:T(1024)} collective-permute-done((f32[49152]{0:T(1024)}, f32[49152]{0:T(1024)}, u32[]{:S(2)}, u32[]{:S(2)}) %collective-permute-start.10) | collective-permute-done | bytes 196640 | tf_op jit(solution)/shard_map/ppermute | solution.py:45
  94.8 4.1 %collective-permute-done.11 = f32[24576]{0:T(1024)S(1)} collective-permute-done((f32[24576]{0:T(1024)S(1)}, f32[24576]{0:T(1024)S(1)}, u32[]{:S(2)}, u32[]{:S(2)}) %collective-permute-start.11) | collective-permute-done | bytes 98336 | tf_op jit(solution)/shard_map/ppermute | solution.py:45
  99.5 6.5 %collective-permute-done.12 = f32[24576]{0:T(1024)S(1)} collective-permute-done((f32[24576]{0:T(1024)S(1)}, f32[24576]{0:T(1024)S(1)}, u32[]{:S(2)}, u32[]{:S(2)}) %collective-permute-start.12) | collective-permute-done | bytes 98336 | tf_op jit(solution)/shard_map/ppermute | solution.py:78
  107.2 3.5 %collective-permute-done.13 = f32[24576]{0:T(1024)S(1)} collective-permute-done((f32[24576]{0:T(1024)S(1)}, f32[24576]{0:T(1024)S(1)}, u32[]{:S(2)}, u32[]{:S(2)}) %collective-permute-start.13) | collective-permute-done | bytes 98336 | tf_op jit(solution)/shard_map/ppermute | solution.py:53
  (79 shorter events, 22.3 us)
Async XLA Ops:
  0.6 68.2 %copy-start = (bf16[1,768,768]{2,1,0:T(8,128)(2,1)S(1)}, bf16[1,768,768]{2,1,0:T(8,128)(2,1)}, u32[]{:S(2)}) copy-start(bf16[1,768,768]{2,1,0:T(8,128)(2,1)} %param.13) | copy-start | bytes 3538948
  3.5 19.0 %collective-permute-start = (bf16[2,1,384,384]{3,2,1,0:T(8,128)(2,1)}, bf16[2,1,384,384]{3,2,1,0:T(8,128)(2,1)S(1)}, u32[]{:S(2)}, u32[]{:S(2)}) collective-permute-start(bf16[2,1,384,384]{3,2,1,0:T(8,128)(2,1)} %pad_maximum_fusion.3), channel_id=1, source_target_pairs={{0,4},{4,8},{8,12},{1,5},{5,9},{9,13},{2,6},{6,10},{10,14},{3,7},{... | collective-permute-start | bytes 1769480 | tf_op jit(solution)/shard_map/ppermute | solution.py:21
  9.3 18.3 %collective-permute-start.1 = (bf16[2,1,384,384]{3,2,1,0:T(8,128)(2,1)}, bf16[2,1,384,384]{3,2,1,0:T(8,128)(2,1)S(1)}, u32[]{:S(2)}, u32[]{:S(2)}) collective-permute-start(bf16[2,1,384,384]{3,2,1,0:T(8,128)(2,1)} %pad_maximum_fusion.4), channel_id=1, source_target_pairs={{4,0},{8,4},{12,8},{5,1},{9,5},{13,9},{6,2},{10,6},{14,10},{7,3},{... | collective-permute-start | bytes 1769480 | tf_op jit(solution)/shard_map/ppermute | solution.py:21
  10.6 9.0 %copy-start.13 = (s32[8,3]{0,1:T(4,128)S(1)}, s32[8,3]{0,1:T(4,128)}, u32[]{:S(2)}) copy-start(s32[8,3]{0,1:T(4,128)} %param.16) | copy-start | bytes 292
  11.5 35.3 %collective-permute-start.3 = (bf16[2,1,384,384]{3,2,1,0:T(8,128)(2,1)}, bf16[2,1,384,384]{3,2,1,0:T(8,128)(2,1)S(1)}, u32[]{:S(2)}, u32[]{:S(2)}) collective-permute-start(bf16[2,1,384,384]{3,2,1,0:T(8,128)(2,1)} %pad_maximum_fusion.6), channel_id=1, source_target_pairs={{4,0},{8,4},{12,8},{5,1},{9,5},{13,9},{6,2},{10,6},{14,10},{7,3},{... | collective-permute-start | bytes 1769480 | tf_op jit(solution)/shard_map/ppermute | solution.py:21
  13.7 33.2 %collective-permute-start.2 = (bf16[2,1,384,384]{3,2,1,0:T(8,128)(2,1)}, bf16[2,1,384,384]{3,2,1,0:T(8,128)(2,1)S(1)}, u32[]{:S(2)}, u32[]{:S(2)}) collective-permute-start(bf16[2,1,384,384]{3,2,1,0:T(8,128)(2,1)} %pad_maximum_fusion.5), channel_id=1, source_target_pairs={{0,4},{4,8},{8,12},{1,5},{5,9},{9,13},{2,6},{6,10},{10,14},{3,7},{... | collective-permute-start | bytes 1769480 | tf_op jit(solution)/shard_map/ppermute | solution.py:21
  22.4 5.3 %copy-start.4 = (bf16[2,1,384,384]{3,2,1,0:T(8,128)(2,1)}, bf16[2,1,384,384]{3,2,1,0:T(8,128)(2,1)S(1)}, u32[]{:S(2)}) copy-start(bf16[2,1,384,384]{3,2,1,0:T(8,128)(2,1)S(1)} %collective-permute-done.left_ref) | copy-start | bytes 1769476
  42.0 30.4 %collective-permute-start.4 = (bf16[2,1,384,384]{3,2,1,0:T(8,128)(2,1)}, bf16[2,1,384,384]{3,2,1,0:T(8,128)(2,1)S(1)}, u32[]{:S(2)}, u32[]{:S(2)}) collective-permute-start(bf16[2,1,384,384]{3,2,1,0:T(8,128)(2,1)} %get-tuple-element.18), channel_id=1, source_target_pairs={{0,4},{4,8},{8,12},{1,5},{5,9},{9,13},{2,6},{6,10},{10,14},{3,7},{... | collective-permute-start | bytes 1769480 | tf_op jit(solution)/shard_map/ppermute | solution.py:21
  45.5 26.9 %collective-permute-start.5 = (bf16[2,1,384,384]{3,2,1,0:T(8,128)(2,1)}, bf16[2,1,384,384]{3,2,1,0:T(8,128)(2,1)S(1)}, u32[]{:S(2)}, u32[]{:S(2)}) collective-permute-start(bf16[2,1,384,384]{3,2,1,0:T(8,128)(2,1)} %get-tuple-element.19), channel_id=1, source_target_pairs={{4,0},{8,4},{12,8},{5,1},{9,5},{13,9},{6,2},{10,6},{14,10},{7,3},{... | collective-permute-start | bytes 1769480 | tf_op jit(solution)/shard_map/ppermute | solution.py:21
  62.0 14.2 %collective-permute-start.6 = (bf16[2,1,384,384]{3,2,1,0:T(8,128)(2,1)}, bf16[2,1,384,384]{3,2,1,0:T(8,128)(2,1)}, u32[]{:S(2)}, u32[]{:S(2)}) collective-permute-start(bf16[2,1,384,384]{3,2,1,0:T(8,128)(2,1)} %get-tuple-element.21), channel_id=1, source_target_pairs={{0,4},{4,8},{8,12},{1,5},{5,9},{9,13},{2,6},{6,10},{10,14},{3,7},{... | collective-permute-start | bytes 1769480 | tf_op jit(solution)/shard_map/ppermute | solution.py:21
  67.4 13.8 %collective-permute-start.7 = (bf16[2,1,384,384]{3,2,1,0:T(8,128)(2,1)}, bf16[2,1,384,384]{3,2,1,0:T(8,128)(2,1)}, u32[]{:S(2)}, u32[]{:S(2)}) collective-permute-start(bf16[2,1,384,384]{3,2,1,0:T(8,128)(2,1)} %get-tuple-element.22), channel_id=1, source_target_pairs={{4,0},{8,4},{12,8},{5,1},{9,5},{13,9},{6,2},{10,6},{14,10},{7,3},{... | collective-permute-start | bytes 1769480 | tf_op jit(solution)/shard_map/ppermute | solution.py:21
  70.9 14.8 %collective-permute-start.8 = (f32[1,768,64]{1,2,0:T(8,128)}, f32[1,768,64]{1,2,0:T(8,128)}, u32[]{:S(2)}, u32[]{:S(2)}) collective-permute-start(f32[1,768,64]{1,2,0:T(8,128)} %fusion.19), channel_id=1, source_target_pairs={{0,2},{2,0},{1,3},{3,1},{4,6},{6,4},{5,7},{7,5},{8,10},{10,8},{9,1... | collective-permute-start | bytes 589832 | tf_op jit(solution)/shard_map/ppermute | solution.py:31
  72.4 1.2 %copy-start.6 = (bf16[1,768,384]{2,1,0:T(8,128)(2,1)S(1)}, bf16[1,768,384]{2,1,0:T(8,128)(2,1)}, u32[]{:S(2)}) copy-start(bf16[1,768,384]{2,1,0:T(8,128)(2,1)} %get-tuple-element.23) | copy-start | bytes 1769476
  74.0 8.6 %copy-start.8 = (bf16[1,768,384]{2,1,0:T(8,128)(2,1)S(1)}, bf16[1,768,384]{2,1,0:T(8,128)(2,1)}, u32[]{:S(2)}) copy-start(bf16[1,768,384]{2,1,0:T(8,128)(2,1)} %get-tuple-element.20) | copy-start | bytes 1769476
  74.0 8.6 %copy-start.9 = (bf16[1,768,384]{2,1,0:T(8,128)(2,1)S(1)}, bf16[1,768,384]{2,1,0:T(8,128)(2,1)}, u32[]{:S(2)}) copy-start(bf16[1,768,384]{2,1,0:T(8,128)(2,1)} %get-tuple-element.24) | copy-start | bytes 1769476
  83.7 3.4 %copy-start.1 = (bf16[1,768,768]{2,1,0:T(8,128)(2,1)}, bf16[1,768,768]{2,1,0:T(8,128)(2,1)S(1)}, u32[]{:S(2)}) copy-start(bf16[1,768,768]{2,1,0:T(8,128)(2,1)S(1)} %pad_maximum_fusion.2) | copy-start | bytes 3538948
  84.2 5.7 %collective-permute-start.9 = (f32[1,768,64]{1,2,0:T(8,128)S(1)}, f32[1,768,64]{1,2,0:T(8,128)S(1)}, u32[]{:S(2)}, u32[]{:S(2)}) collective-permute-start(f32[1,768,64]{1,2,0:T(8,128)S(1)} %fusion.16), channel_id=1, source_target_pairs={{0,2},{2,0},{1,3},{3,1},{4,6},{6,4},{5,7},{7,5},{8,10},{10,8},{9,1... | collective-permute-start | bytes 589832 | tf_op jit(solution)/shard_map/ppermute | solution.py:31
  91.2 1.8 %collective-permute-start.10 = (f32[49152]{0:T(1024)}, f32[49152]{0:T(1024)}, u32[]{:S(2)}, u32[]{:S(2)}) collective-permute-start(f32[49152]{0:T(1024)} %select_n.63), channel_id=1, source_target_pairs={{0,1},{1,0},{2,3},{3,2},{4,5},{5,4},{6,7},{7,6},{8,9},{9,8},{10,11... | collective-permute-start | bytes 589832 | tf_op jit(solution)/shard_map/ppermute | solution.py:45
  91.4 14.7 %copy-start.10 = (bf16[1,768,384]{2,1,0:T(8,128)(2,1)S(1)}, bf16[1,768,384]{2,1,0:T(8,128)(2,1)}, u32[]{:S(2)}) copy-start(bf16[1,768,384]{2,1,0:T(8,128)(2,1)} %get-tuple-element.15) | copy-start | bytes 1769476
  91.5 14.6 %copy-start.11 = (bf16[1,768,384]{2,1,0:T(8,128)(2,1)S(1)}, bf16[1,768,384]{2,1,0:T(8,128)(2,1)}, u32[]{:S(2)}) copy-start(bf16[1,768,384]{2,1,0:T(8,128)(2,1)} %get-tuple-element.16) | copy-start | bytes 1769476
  94.0 4.9 %collective-permute-start.11 = (f32[24576]{0:T(1024)S(1)}, f32[24576]{0:T(1024)S(1)}, u32[]{:S(2)}, u32[]{:S(2)}) collective-permute-start(f32[24576]{0:T(1024)S(1)} %slice_select_fusion), channel_id=1, source_target_pairs={{0,4},{4,0},{8,12},{12,8},{1,5},{5,1},{9,13},{13,9},{2,6},{6,2},{1... | collective-permute-start | bytes 294920 | tf_op jit(solution)/shard_map/ppermute | solution.py:45
  98.9 7.1 %collective-permute-start.12 = (f32[24576]{0:T(1024)S(1)}, f32[24576]{0:T(1024)S(1)}, u32[]{:S(2)}, u32[]{:S(2)}) collective-permute-start(f32[24576]{0:T(1024)S(1)} %select_add_fusion), channel_id=1, source_target_pairs={{0,8},{4,12},{8,0},{12,4},{1,9},{5,13},{9,1},{13,5},{2,10},{6,14},... | collective-permute-start | bytes 294920 | tf_op jit(solution)/shard_map/ppermute | solution.py:78
  106.0 4.7 %collective-permute-start.13 = (f32[24576]{0:T(1024)S(1)}, f32[24576]{0:T(1024)S(1)}, u32[]{:S(2)}, u32[]{:S(2)}) collective-permute-start(f32[24576]{0:T(1024)S(1)} %add.46), channel_id=1, source_target_pairs={{0,4},{4,0},{8,12},{12,8},{1,5},{5,1},{9,13},{13,9},{2,6},{6,2},{1... | collective-permute-start | bytes 294920 | tf_op jit(solution)/shard_map/ppermute | solution.py:53
  110.7 1.6 %collective-permute-start.14 = (f32[49152]{0:T(1024)S(1)}, f32[49152]{0:T(1024)}, u32[]{:S(2)}, u32[]{:S(2)}) collective-permute-start(f32[49152]{0:T(1024)S(1)} %maximum_select_fusion.2), channel_id=1, source_target_pairs={{0,1},{1,0},{2,3},{3,2},{4,5},{5,4},{6,7},{7,6},{8,9},{9,8},{10,11... | collective-permute-start | bytes 589832 | tf_op jit(solution)/shard_map/ppermute | solution.py:53
  (6 other events, 4.9 us)

commit v12 on v10

--- a/solution.py
+++ b/solution.py
@@ -240,9 +240,9 @@
     gradient_up_local = adapter_scale * jnp.einsum(
         "igb,igu->bu", lowered_rows, value_gradient, preferred_element_type=jnp.float32
     )
-    both = jnp.stack((gradient_down_local, gradient_up_local.T), 0)
+    both = jnp.stack((gradient_down_local.T, gradient_up_local), 0)
     both = all_sum(both, ("rep", "seq"))
-    down_projection_grad, up_projection_grad = both[0], both[1].T
+    down_projection_grad, up_projection_grad = both[0].T, both[1]
     return (query_grad, key_grad, value_gradient, down_projection_grad, up_projection_grad)
 
 

time: 116 us -> 112 us (0.966)
  local copies, waits for them, and re-layouts: 11.1 us -> 7.82 us
    unnamed x32 -> x30, local copies, waits for them, and re-layouts: 6.51 us -> 4.85 us
  transfers between devices with their start and end apart: 15 -> 15, of which waited for: 10 -> 10; matrix products, arithmetic and copies ran while one was open for 12% -> 12% of each run, Pallas kernels for 23% -> 24%
where the time goes in v12:
time: 112 us
  waiting for transfers between devices  32.4 us (29%)
  starting transfers between devices  28.9 us (26%)
  Pallas kernels  26.8 us (24%)
  other arithmetic  10.7 us (10%)
  local copies, waits for them, and re-layouts  7.82 us (7%)
  matrix products  4.26 us (4%)
    pallas_call x2, Pallas kernels, attention_backward(): pl.pallas_call(attention_kernel, grid=(clip_count, heads), in_specs=[pl.B...  26.8 us
    ppermute x8, starting transfers between devices, shifted(): return lax.ppermute(shard, axis, pairs)  24.3 us
    ppermute x8, waiting for transfers between devices, shifted(): return lax.ppermute(shard, axis, pairs)  13.6 us
    ppermute x1, waiting for transfers between devices, all_sum(): lax.ppermute(flat, axis, [(i, i ^ step) for i in range(lax.axis_size(axis...  6.53 us
    ppermute x2, waiting for transfers between devices, scatter_sum(): lax.ppermute(send, axis, [(i, i ^ step) for i in range(peers)])  5.66 us
    unnamed x30, local copies, waits for them, and re-layouts  4.85 us
    ppermute x2, waiting for transfers between devices, gather_back(): other = lax.ppermute(flat, axis, [(i, i ^ step) for i in range(peers)])  3.72 us
    ppermute x2, starting transfers between devices, butterfly_sum(): other = lax.ppermute(tree, axis, pairs)  3 us
  transfers between devices with their start and end apart: 15, of which 10 were waited for; matrix products, arithmetic and copies ran while one was open for 12% of the time, Pallas kernels for 24%

profile of v12, /device:TPU:0, one launch (start us, length us, event | category | flops | bytes accessed | tf_op | source)
XLA Modules:
  0.0 111.8 jit_solution(18422387397902661869)
XLA Ops:
  0.6 1.9 %slice_bitcast_fusion.8 = (bf16[1,1,384,384]{3,2,1,0:T(8,128)(2,1)S(1)}, bf16[1,1,384,384]{3,2,1,0:T(8,128)(2,1)S(1)}, bf16[1,1,384,384]{3,2,1,0:T(8,128)(2,1)S(...) fusion(bf16[1,768,768]{2,1,0:T(8,128)(2,1)} %v_ref.3, ...), kind=kLoop, calls=%fused_computation.38 | loop fusion | bytes 4718592 | tf_op jit(solution)/shard_map/stack | solution.py:218
  3.5 5.0 %collective-permute-start = (bf16[2,1,384,384]{3,2,1,0:T(8,128)(2,1)}, bf16[2,1,384,384]{3,2,1,0:T(8,128)(2,1)S(1)}, u32[]{:S(2)}, u32[]{:S(2)}) collective-permute-start(bf16[2,1,384,384]{3,2,1,0:T(8,128)(2,1)} %pad_maximum_fusion.3), channel_id=1, source_target_pairs={{0,4},{4,8},{8,12},{1,5},{5,9},{9,13},{2,6},{6,10},{10,14},{3,7},{... | collective-permute-start | bytes 1769480 | tf_op jit(solution)/shard_map/ppermute | solution.py:21
  9.3 1.3 %collective-permute-start.1 = (bf16[2,1,384,384]{3,2,1,0:T(8,128)(2,1)}, bf16[2,1,384,384]{3,2,1,0:T(8,128)(2,1)S(1)}, u32[]{:S(2)}, u32[]{:S(2)}) collective-permute-start(bf16[2,1,384,384]{3,2,1,0:T(8,128)(2,1)} %pad_maximum_fusion.4), channel_id=1, source_target_pairs={{4,0},{8,4},{12,8},{5,1},{9,5},{13,9},{6,2},{10,6},{14,10},{7,3},{... | collective-permute-start | bytes 1769480 | tf_op jit(solution)/shard_map/ppermute | solution.py:21
  11.5 1.3 %collective-permute-start.3 = (bf16[2,1,384,384]{3,2,1,0:T(8,128)(2,1)}, bf16[2,1,384,384]{3,2,1,0:T(8,128)(2,1)S(1)}, u32[]{:S(2)}, u32[]{:S(2)}) collective-permute-start(bf16[2,1,384,384]{3,2,1,0:T(8,128)(2,1)} %pad_maximum_fusion.6), channel_id=1, source_target_pairs={{4,0},{8,4},{12,8},{5,1},{9,5},{13,9},{6,2},{10,6},{14,10},{7,3},{... | collective-permute-start | bytes 1769480 | tf_op jit(solution)/shard_map/ppermute | solution.py:21
  13.7 5.2 %collective-permute-start.2 = (bf16[2,1,384,384]{3,2,1,0:T(8,128)(2,1)}, bf16[2,1,384,384]{3,2,1,0:T(8,128)(2,1)S(1)}, u32[]{:S(2)}, u32[]{:S(2)}) collective-permute-start(bf16[2,1,384,384]{3,2,1,0:T(8,128)(2,1)} %pad_maximum_fusion.5), channel_id=1, source_target_pairs={{0,4},{4,8},{8,12},{1,5},{5,9},{9,13},{2,6},{6,10},{10,14},{3,7},{... | collective-permute-start | bytes 1769480 | tf_op jit(solution)/shard_map/ppermute | solution.py:21
  22.4 5.3 %collective-permute-done.1.right_ref = bf16[2,1,384,384]{3,2,1,0:T(8,128)(2,1)S(1)} collective-permute-done((bf16[2,1,384,384]{3,2,1,0:T(8,128)(2,1)}, bf16[2,1,384,384]{3,2,1,0:T(8,128)(2,1)S(1)}, u32[]{:S(2)}, u32[]{:S(2)}) %collective-permute-start.1) | collective-permute-done | bytes 589856 | tf_op jit(solution)/shard_map/ppermute | solution.py:21
  28.5 13.4 %shard_map.128 = (bf16[1,768,384]{2,1,0:T(8,128)(2,1)}, bf16[1,768,384]{2,1,0:T(8,128)(2,1)}, bf16[1,768,384]{2,1,0:T(8,128)(2,1)}, bf16[2,1,384,384]{3,2,1,0:T(8,128)(2,1)}, bf16[2,1,384,384]{3,2,1,0:T(8,128)(2,1)}) custom-call(f32[6]{0:T(128)} %and_select_fusion.bias_ref, bf16[1,768,768]{2,1,0:T(8,128)(2,1)} %q_ref.3, bf16[1,768,768]{2,1,0:T(8,128)(2,1)} %g_ref.3, ...), custom_call_target="tpu_custom_call" | custom-call | tf_op jit(solution)/shard_map/pallas_call | solution.py:168
  41.9 3.5 %collective-permute-start.4 = (bf16[2,1,384,384]{3,2,1,0:T(8,128)(2,1)}, bf16[2,1,384,384]{3,2,1,0:T(8,128)(2,1)S(1)}, u32[]{:S(2)}, u32[]{:S(2)}) collective-permute-start(bf16[2,1,384,384]{3,2,1,0:T(8,128)(2,1)} %get-tuple-element.18), channel_id=1, source_target_pairs={{0,4},{4,8},{8,12},{1,5},{5,9},{9,13},{2,6},{6,10},{10,14},{3,7},{... | collective-permute-start | bytes 1769480 | tf_op jit(solution)/shard_map/ppermute | solution.py:21
  45.4 1.3 %collective-permute-start.5 = (bf16[2,1,384,384]{3,2,1,0:T(8,128)(2,1)}, bf16[2,1,384,384]{3,2,1,0:T(8,128)(2,1)S(1)}, u32[]{:S(2)}, u32[]{:S(2)}) collective-permute-start(bf16[2,1,384,384]{3,2,1,0:T(8,128)(2,1)} %get-tuple-element.19), channel_id=1, source_target_pairs={{4,0},{8,4},{12,8},{5,1},{9,5},{13,9},{6,2},{10,6},{14,10},{7,3},{... | collective-permute-start | bytes 1769480 | tf_op jit(solution)/shard_map/ppermute | solution.py:21
  48.4 13.4 %shard_map.129 = (bf16[1,768,384]{2,1,0:T(8,128)(2,1)}, bf16[1,768,384]{2,1,0:T(8,128)(2,1)}, bf16[1,768,384]{2,1,0:T(8,128)(2,1)}, bf16[2,1,384,384]{3,2,1,0:T(8,128)(2,1)}, bf16[2,1,384,384]{3,2,1,0:T(8,128)(2,1)}) custom-call(f32[6]{0:T(128)} %and_select_fusion.bias_ref, bf16[1,768,768]{2,1,0:T(8,128)(2,1)} %q_ref.3, bf16[1,768,768]{2,1,0:T(8,128)(2,1)} %g_ref.3, ...), custom_call_target="tpu_custom_call" | custom-call | tf_op jit(solution)/shard_map/pallas_call | solution.py:168
  61.8 5.4 %collective-permute-start.6 = (bf16[2,1,384,384]{3,2,1,0:T(8,128)(2,1)}, bf16[2,1,384,384]{3,2,1,0:T(8,128)(2,1)}, u32[]{:S(2)}, u32[]{:S(2)}) collective-permute-start(bf16[2,1,384,384]{3,2,1,0:T(8,128)(2,1)} %get-tuple-element.21), channel_id=1, source_target_pairs={{0,4},{4,8},{8,12},{1,5},{5,9},{9,13},{2,6},{6,10},{10,14},{3,7},{... | collective-permute-start | bytes 1769480 | tf_op jit(solution)/shard_map/ppermute | solution.py:21
  67.2 1.5 %collective-permute-start.7 = (bf16[2,1,384,384]{3,2,1,0:T(8,128)(2,1)}, bf16[2,1,384,384]{3,2,1,0:T(8,128)(2,1)}, u32[]{:S(2)}, u32[]{:S(2)}) collective-permute-start(bf16[2,1,384,384]{3,2,1,0:T(8,128)(2,1)} %get-tuple-element.22), channel_id=1, source_target_pairs={{4,0},{8,4},{12,8},{5,1},{9,5},{13,9},{6,2},{10,6},{14,10},{7,3},{... | collective-permute-start | bytes 1769480 | tf_op jit(solution)/shard_map/ppermute | solution.py:21
  68.7 2.1 %fusion.16 = f32[1,768,64]{1,2,0:T(8,128)} fusion(bf16[768,64]{0,1:T(8,128)(2,1)} %param.14, bf16[1,768,768]{2,1,0:T(8,128)(2,1)S(1)} %copy-done), kind=kOutput, calls=%fused_computation.25 | convolution fusion | flops 75497472 | bytes 1474560 | tf_op jit(solution)/shard_map/pqg,gv->pqv/dot_general | solution.py:192
  70.7 1.5 %collective-permute-start.8 = (f32[1,768,64]{1,2,0:T(8,128)}, f32[1,768,64]{1,2,0:T(8,128)}, u32[]{:S(2)}, u32[]{:S(2)}) collective-permute-start(f32[1,768,64]{1,2,0:T(8,128)} %fusion.16), channel_id=1, source_target_pairs={{0,2},{2,0},{1,3},{3,1},{4,6},{6,4},{5,7},{7,5},{8,10},{10,8},{9,1... | collective-permute-start | bytes 589832 | tf_op jit(solution)/shard_map/ppermute | solution.py:31
  73.8 2.2 %collective-permute-done.6 = bf16[2,1,384,384]{3,2,1,0:T(8,128)(2,1)} collective-permute-done((bf16[2,1,384,384]{3,2,1,0:T(8,128)(2,1)}, bf16[2,1,384,384]{3,2,1,0:T(8,128)(2,1)}, u32[]{:S(2)}, u32[]{:S(2)}) %collective-permute-start.6) | collective-permute-done | bytes 589856 | tf_op jit(solution)/shard_map/ppermute | solution.py:21
  76.0 4.9 %collective-permute-done.7 = bf16[2,1,384,384]{3,2,1,0:T(8,128)(2,1)} collective-permute-done((bf16[2,1,384,384]{3,2,1,0:T(8,128)(2,1)}, bf16[2,1,384,384]{3,2,1,0:T(8,128)(2,1)}, u32[]{:S(2)}, u32[]{:S(2)}) %collective-permute-start.7) | collective-permute-done | bytes 589856 | tf_op jit(solution)/shard_map/ppermute | solution.py:21
  81.0 1.4 %maximum_convert_fusion.1 = f32[2,1,768,384]{3,2,1,0:T(8,128)S(1)} fusion(bf16[2,1,384,384]{3,2,1,0:T(8,128)(2,1)} %collective-permute-done.7, bf16[2,1,384,384]{3,2,1,0:T(8,128)(2,1)} %collective-permute-done.6), kind=kLoop, calls=%fused_computation.14 | loop fusion | flops 2359296 | bytes 3538944 | tf_op jit(solution)/shard_map/convert_element_type | solution.py:225
  84.0 1.5 %collective-permute-start.9 = (f32[1,768,64]{1,2,0:T(8,128)S(1)}, f32[1,768,64]{1,2,0:T(8,128)S(1)}, u32[]{:S(2)}, u32[]{:S(2)}) collective-permute-start(f32[1,768,64]{1,2,0:T(8,128)S(1)} %fusion.19), channel_id=1, source_target_pairs={{0,2},{2,0},{1,3},{3,1},{4,6},{6,4},{5,7},{7,5},{8,10},{10,8},{9,1... | collective-permute-start | bytes 589832 | tf_op jit(solution)/shard_map/ppermute | solution.py:31
  85.5 1.4 %fusion.25 = f32[64,768]{1,0:T(8,128)S(1)} fusion(bf16[1,768,768]{2,1,0:T(8,128)(2,1)S(1)} %pad_maximum_fusion.2, f32[1,768,64]{1,2,0:T(8,128)} %fusion.16, f32[1,768,64]{1,2,0:T(8,128)} %collective-permute-done.8), kind=kOutput, calls=%fused_computation.28 | convolution fusion | flops 75644928 | bytes 1769472 | tf_op jit(solution)/shard_map/igb,igu->bu/dot_general | solution.py:240
  86.9 2.8 %collective-permute-done.9 = f32[1,768,64]{1,2,0:T(8,128)S(1)} collective-permute-done((f32[1,768,64]{1,2,0:T(8,128)S(1)}, f32[1,768,64]{1,2,0:T(8,128)S(1)}, u32[]{:S(2)}, u32[]{:S(2)}) %collective-permute-start.9) | collective-permute-done | bytes 196640 | tf_op jit(solution)/shard_map/ppermute | solution.py:31
  90.3 1.5 %collective-permute-done.10 = f32[49152]{0:T(1024)} collective-permute-done((f32[49152]{0:T(1024)S(1)}, f32[49152]{0:T(1024)}, u32[]{:S(2)}, u32[]{:S(2)}) %collective-permute-start.10) | collective-permute-done | bytes 196640 | tf_op jit(solution)/shard_map/ppermute | solution.py:45
  93.5 4.1 %collective-permute-done.11 = f32[24576]{0:T(1024)S(1)} collective-permute-done((f32[24576]{0:T(1024)S(1)}, f32[24576]{0:T(1024)S(1)}, u32[]{:S(2)}, u32[]{:S(2)}) %collective-permute-start.11) | collective-permute-done | bytes 98336 | tf_op jit(solution)/shard_map/ppermute | solution.py:45
  98.2 6.5 %collective-permute-done.12 = f32[24576]{0:T(1024)S(1)} collective-permute-done((f32[24576]{0:T(1024)S(1)}, f32[24576]{0:T(1024)S(1)}, u32[]{:S(2)}, u32[]{:S(2)}) %collective-permute-start.12) | collective-permute-done | bytes 98336 | tf_op jit(solution)/shard_map/ppermute | solution.py:78
  106.0 3.5 %collective-permute-done.13 = f32[24576]{0:T(1024)S(1)} collective-permute-done((f32[24576]{0:T(1024)S(1)}, f32[24576]{0:T(1024)S(1)}, u32[]{:S(2)}, u32[]{:S(2)}) %collective-permute-start.13) | collective-permute-done | bytes 98336 | tf_op jit(solution)/shard_map/ppermute | solution.py:53
  (75 shorter events, 19.0 us)
Async XLA Ops:
  0.6 68.0 %copy-start = (bf16[1,768,768]{2,1,0:T(8,128)(2,1)S(1)}, bf16[1,768,768]{2,1,0:T(8,128)(2,1)}, u32[]{:S(2)}) copy-start(bf16[1,768,768]{2,1,0:T(8,128)(2,1)} %param.13) | copy-start | bytes 3538948
  3.5 19.0 %collective-permute-start = (bf16[2,1,384,384]{3,2,1,0:T(8,128)(2,1)}, bf16[2,1,384,384]{3,2,1,0:T(8,128)(2,1)S(1)}, u32[]{:S(2)}, u32[]{:S(2)}) collective-permute-start(bf16[2,1,384,384]{3,2,1,0:T(8,128)(2,1)} %pad_maximum_fusion.3), channel_id=1, source_target_pairs={{0,4},{4,8},{8,12},{1,5},{5,9},{9,13},{2,6},{6,10},{10,14},{3,7},{... | collective-permute-start | bytes 1769480 | tf_op jit(solution)/shard_map/ppermute | solution.py:21
  9.3 18.3 %collective-permute-start.1 = (bf16[2,1,384,384]{3,2,1,0:T(8,128)(2,1)}, bf16[2,1,384,384]{3,2,1,0:T(8,128)(2,1)S(1)}, u32[]{:S(2)}, u32[]{:S(2)}) collective-permute-start(bf16[2,1,384,384]{3,2,1,0:T(8,128)(2,1)} %pad_maximum_fusion.4), channel_id=1, source_target_pairs={{4,0},{8,4},{12,8},{5,1},{9,5},{13,9},{6,2},{10,6},{14,10},{7,3},{... | collective-permute-start | bytes 1769480 | tf_op jit(solution)/shard_map/ppermute | solution.py:21
  10.6 9.0 %copy-start.13 = (s32[8,3]{0,1:T(4,128)S(1)}, s32[8,3]{0,1:T(4,128)}, u32[]{:S(2)}) copy-start(s32[8,3]{0,1:T(4,128)} %param.16) | copy-start | bytes 292
  11.5 35.2 %collective-permute-start.3 = (bf16[2,1,384,384]{3,2,1,0:T(8,128)(2,1)}, bf16[2,1,384,384]{3,2,1,0:T(8,128)(2,1)S(1)}, u32[]{:S(2)}, u32[]{:S(2)}) collective-permute-start(bf16[2,1,384,384]{3,2,1,0:T(8,128)(2,1)} %pad_maximum_fusion.6), channel_id=1, source_target_pairs={{4,0},{8,4},{12,8},{5,1},{9,5},{13,9},{6,2},{10,6},{14,10},{7,3},{... | collective-permute-start | bytes 1769480 | tf_op jit(solution)/shard_map/ppermute | solution.py:21
  13.7 33.1 %collective-permute-start.2 = (bf16[2,1,384,384]{3,2,1,0:T(8,128)(2,1)}, bf16[2,1,384,384]{3,2,1,0:T(8,128)(2,1)S(1)}, u32[]{:S(2)}, u32[]{:S(2)}) collective-permute-start(bf16[2,1,384,384]{3,2,1,0:T(8,128)(2,1)} %pad_maximum_fusion.5), channel_id=1, source_target_pairs={{0,4},{4,8},{8,12},{1,5},{5,9},{9,13},{2,6},{6,10},{10,14},{3,7},{... | collective-permute-start | bytes 1769480 | tf_op jit(solution)/shard_map/ppermute | solution.py:21
  22.4 5.3 %copy-start.4 = (bf16[2,1,384,384]{3,2,1,0:T(8,128)(2,1)}, bf16[2,1,384,384]{3,2,1,0:T(8,128)(2,1)S(1)}, u32[]{:S(2)}) copy-start(bf16[2,1,384,384]{3,2,1,0:T(8,128)(2,1)S(1)} %collective-permute-done.left_ref) | copy-start | bytes 1769476
  41.9 30.3 %collective-permute-start.4 = (bf16[2,1,384,384]{3,2,1,0:T(8,128)(2,1)}, bf16[2,1,384,384]{3,2,1,0:T(8,128)(2,1)S(1)}, u32[]{:S(2)}, u32[]{:S(2)}) collective-permute-start(bf16[2,1,384,384]{3,2,1,0:T(8,128)(2,1)} %get-tuple-element.18), channel_id=1, source_target_pairs={{0,4},{4,8},{8,12},{1,5},{5,9},{9,13},{2,6},{6,10},{10,14},{3,7},{... | collective-permute-start | bytes 1769480 | tf_op jit(solution)/shard_map/ppermute | solution.py:21
  45.4 26.8 %collective-permute-start.5 = (bf16[2,1,384,384]{3,2,1,0:T(8,128)(2,1)}, bf16[2,1,384,384]{3,2,1,0:T(8,128)(2,1)S(1)}, u32[]{:S(2)}, u32[]{:S(2)}) collective-permute-start(bf16[2,1,384,384]{3,2,1,0:T(8,128)(2,1)} %get-tuple-element.19), channel_id=1, source_target_pairs={{4,0},{8,4},{12,8},{5,1},{9,5},{13,9},{6,2},{10,6},{14,10},{7,3},{... | collective-permute-start | bytes 1769480 | tf_op jit(solution)/shard_map/ppermute | solution.py:21
  61.8 14.2 %collective-permute-start.6 = (bf16[2,1,384,384]{3,2,1,0:T(8,128)(2,1)}, bf16[2,1,384,384]{3,2,1,0:T(8,128)(2,1)}, u32[]{:S(2)}, u32[]{:S(2)}) collective-permute-start(bf16[2,1,384,384]{3,2,1,0:T(8,128)(2,1)} %get-tuple-element.21), channel_id=1, source_target_pairs={{0,4},{4,8},{8,12},{1,5},{5,9},{9,13},{2,6},{6,10},{10,14},{3,7},{... | collective-permute-start | bytes 1769480 | tf_op jit(solution)/shard_map/ppermute | solution.py:21
  67.2 13.8 %collective-permute-start.7 = (bf16[2,1,384,384]{3,2,1,0:T(8,128)(2,1)}, bf16[2,1,384,384]{3,2,1,0:T(8,128)(2,1)}, u32[]{:S(2)}, u32[]{:S(2)}) collective-permute-start(bf16[2,1,384,384]{3,2,1,0:T(8,128)(2,1)} %get-tuple-element.22), channel_id=1, source_target_pairs={{4,0},{8,4},{12,8},{5,1},{9,5},{13,9},{6,2},{10,6},{14,10},{7,3},{... | collective-permute-start | bytes 1769480 | tf_op jit(solution)/shard_map/ppermute | solution.py:21
  70.7 14.8 %collective-permute-start.8 = (f32[1,768,64]{1,2,0:T(8,128)}, f32[1,768,64]{1,2,0:T(8,128)}, u32[]{:S(2)}, u32[]{:S(2)}) collective-permute-start(f32[1,768,64]{1,2,0:T(8,128)} %fusion.16), channel_id=1, source_target_pairs={{0,2},{2,0},{1,3},{3,1},{4,6},{6,4},{5,7},{7,5},{8,10},{10,8},{9,1... | collective-permute-start | bytes 589832 | tf_op jit(solution)/shard_map/ppermute | solution.py:31
  72.3 1.2 %copy-start.6 = (bf16[1,768,384]{2,1,0:T(8,128)(2,1)S(1)}, bf16[1,768,384]{2,1,0:T(8,128)(2,1)}, u32[]{:S(2)}) copy-start(bf16[1,768,384]{2,1,0:T(8,128)(2,1)} %get-tuple-element.23) | copy-start | bytes 1769476
  73.8 8.6 %copy-start.8 = (bf16[1,768,384]{2,1,0:T(8,128)(2,1)S(1)}, bf16[1,768,384]{2,1,0:T(8,128)(2,1)}, u32[]{:S(2)}) copy-start(bf16[1,768,384]{2,1,0:T(8,128)(2,1)} %get-tuple-element.20) | copy-start | bytes 1769476
  73.8 8.6 %copy-start.9 = (bf16[1,768,384]{2,1,0:T(8,128)(2,1)S(1)}, bf16[1,768,384]{2,1,0:T(8,128)(2,1)}, u32[]{:S(2)}) copy-start(bf16[1,768,384]{2,1,0:T(8,128)(2,1)} %get-tuple-element.24) | copy-start | bytes 1769476
  83.6 3.4 %copy-start.1 = (bf16[1,768,768]{2,1,0:T(8,128)(2,1)}, bf16[1,768,768]{2,1,0:T(8,128)(2,1)S(1)}, u32[]{:S(2)}) copy-start(bf16[1,768,768]{2,1,0:T(8,128)(2,1)S(1)} %pad_maximum_fusion.2) | copy-start | bytes 3538948
  84.0 5.7 %collective-permute-start.9 = (f32[1,768,64]{1,2,0:T(8,128)S(1)}, f32[1,768,64]{1,2,0:T(8,128)S(1)}, u32[]{:S(2)}, u32[]{:S(2)}) collective-permute-start(f32[1,768,64]{1,2,0:T(8,128)S(1)} %fusion.19), channel_id=1, source_target_pairs={{0,2},{2,0},{1,3},{3,1},{4,6},{6,4},{5,7},{7,5},{8,10},{10,8},{9,1... | collective-permute-start | bytes 589832 | tf_op jit(solution)/shard_map/ppermute | solution.py:31
  90.1 14.7 %copy-start.10 = (bf16[1,768,384]{2,1,0:T(8,128)(2,1)S(1)}, bf16[1,768,384]{2,1,0:T(8,128)(2,1)}, u32[]{:S(2)}) copy-start(bf16[1,768,384]{2,1,0:T(8,128)(2,1)} %get-tuple-element.15) | copy-start | bytes 1769476
  90.1 1.6 %collective-permute-start.10 = (f32[49152]{0:T(1024)S(1)}, f32[49152]{0:T(1024)}, u32[]{:S(2)}, u32[]{:S(2)}) collective-permute-start(f32[49152]{0:T(1024)S(1)} %select_n.63), channel_id=1, source_target_pairs={{0,1},{1,0},{2,3},{3,2},{4,5},{5,4},{6,7},{7,6},{8,9},{9,8},{10,11... | collective-permute-start | bytes 589832 | tf_op jit(solution)/shard_map/ppermute | solution.py:45
  90.2 14.6 %copy-start.11 = (bf16[1,768,384]{2,1,0:T(8,128)(2,1)S(1)}, bf16[1,768,384]{2,1,0:T(8,128)(2,1)}, u32[]{:S(2)}) copy-start(bf16[1,768,384]{2,1,0:T(8,128)(2,1)} %get-tuple-element.16) | copy-start | bytes 1769476
  92.7 4.9 %collective-permute-start.11 = (f32[24576]{0:T(1024)S(1)}, f32[24576]{0:T(1024)S(1)}, u32[]{:S(2)}, u32[]{:S(2)}) collective-permute-start(f32[24576]{0:T(1024)S(1)} %slice_select_fusion), channel_id=1, source_target_pairs={{0,4},{4,0},{8,12},{12,8},{1,5},{5,1},{9,13},{13,9},{2,6},{6,2},{1... | collective-permute-start | bytes 294920 | tf_op jit(solution)/shard_map/ppermute | solution.py:45
  97.7 7.1 %collective-permute-start.12 = (f32[24576]{0:T(1024)S(1)}, f32[24576]{0:T(1024)S(1)}, u32[]{:S(2)}, u32[]{:S(2)}) collective-permute-start(f32[24576]{0:T(1024)S(1)} %select_add_fusion), channel_id=1, source_target_pairs={{0,8},{4,12},{8,0},{12,4},{1,9},{5,13},{9,1},{13,5},{2,10},{6,14},... | collective-permute-start | bytes 294920 | tf_op jit(solution)/shard_map/ppermute | solution.py:78
  104.8 4.7 %collective-permute-start.13 = (f32[24576]{0:T(1024)S(1)}, f32[24576]{0:T(1024)S(1)}, u32[]{:S(2)}, u32[]{:S(2)}) collective-permute-start(f32[24576]{0:T(1024)S(1)} %add.46), channel_id=1, source_target_pairs={{0,4},{4,0},{8,12},{12,8},{1,5},{5,1},{9,13},{13,9},{2,6},{6,2},{1... | collective-permute-start | bytes 294920 | tf_op jit(solution)/shard_map/ppermute | solution.py:53
  109.5 1.5 %collective-permute-start.14 = (f32[49152]{0:T(1024)S(1)}, f32[49152]{0:T(1024)S(1)}, u32[]{:S(2)}, u32[]{:S(2)}) collective-permute-start(f32[49152]{0:T(1024)S(1)} %maximum_select_fusion.1), channel_id=1, source_target_pairs={{0,1},{1,0},{2,3},{3,2},{4,5},{5,4},{6,7},{7,6},{8,9},{9,8},{10,11... | collective-permute-start | bytes 589832 | tf_op jit(solution)/shard_map/ppermute | solution.py:53
  (6 other events, 4.9 us)

commit v13 on v12

--- a/solution.py
+++ b/solution.py
@@ -240,9 +240,8 @@
     gradient_up_local = adapter_scale * jnp.einsum(
         "igb,igu->bu", lowered_rows, value_gradient, preferred_element_type=jnp.float32
     )
-    both = jnp.stack((gradient_down_local.T, gradient_up_local), 0)
-    both = all_sum(both, ("rep", "seq"))
-    down_projection_grad, up_projection_grad = both[0].T, both[1]
+    up_projection_grad = all_sum(gradient_up_local, ("rep", "seq"))
+    down_projection_grad = all_sum(gradient_down_local.T, ("rep", "seq")).T
     return (query_grad, key_grad, value_gradient, down_projection_grad, up_projection_grad)
 
 

time: 112 us -> 121 us (1.080)
  starting transfers between devices: 28.9 us -> 32.3 us
  other arithmetic: 10.7 us -> 14 us
  waiting for transfers between devices: 32.4 us -> 30.9 us
  local copies, waits for them, and re-layouts: 7.82 us -> 9.31 us
  matrix products: 4.26 us -> 5.57 us
    ppermute x2 -> x4, waiting for transfers between devices: 5.66 us -> 1.79 us  [scatter_sum(): lax.ppermute(send, axis, [(i, i ^ step) for i in range(peers)])]
    ppermute x2 -> x4, waiting for transfers between devices: 3.72 us -> 6.07 us  [gather_back(): other = lax.ppermute(flat, axis, [(i, i ^ step) for i in range(peers)])]
    ppermute x2 -> x4, starting transfers between devices: 0.14 us -> 2.12 us  [gather_back(): other = lax.ppermute(flat, axis, [(i, i ^ step) for i in range(peers)])]
    ppermute x2, waiting for transfers between devices: 2.82 us -> 4.45 us  [butterfly_sum(): other = lax.ppermute(tree, axis, pairs)]
    ppermute x1 -> x2, waiting for transfers between devices: 6.53 us -> 4.97 us  [all_sum(): lax.ppermute(flat, axis, [(i, i ^ step) for i in range(lax.axis_size(axis...]
    select_n x1 -> x2, local copies, waits for them, and re-layouts: 0.01 us -> 1.55 us  [scatter_sum(): send = jnp.where(upper, flat[:half], flat[half:])]
    select_n x1 -> x2, local copies, waits for them, and re-layouts: 0.01 us -> 1.55 us  [scatter_sum(): keep = jnp.where(upper, flat[half:], flat[:half])]
    concatenate x3, other arithmetic: 2.31 us -> 3.55 us  [on_device(): jnp.concatenate([o[i] for o in outs], 2)]
  transfers between devices with their start and end apart: 15 -> 20, of which waited for: 10 -> 11; matrix products, arithmetic and copies ran while one was open for 12% -> 14% of each run, Pallas kernels for 24% -> 22%
where the time goes in v13:
time: 121 us; the launch traced here: 120 us
  starting transfers between devices  32.3 us (27%)
  waiting for transfers between devices  30.9 us (26%)
  Pallas kernels  26.9 us (22%)
  other arithmetic  14 us (12%)
  local copies, waits for them, and re-layouts  9.31 us (8%)
  matrix products  5.57 us (5%)
    pallas_call x2, Pallas kernels, attention_backward(): pl.pallas_call(attention_kernel, grid=(clip_count, heads), in_specs=[pl.B...  26.9 us
    ppermute x8, starting transfers between devices, shifted(): return lax.ppermute(shard, axis, pairs)  24.4 us
    ppermute x8, waiting for transfers between devices, shifted(): return lax.ppermute(shard, axis, pairs)  13.6 us
    ppermute x4, waiting for transfers between devices, gather_back(): other = lax.ppermute(flat, axis, [(i, i ^ step) for i in range(peers)])  6.07 us
    ppermute x2, waiting for transfers between devices, all_sum(): lax.ppermute(flat, axis, [(i, i ^ step) for i in range(lax.axis_size(axis...  4.97 us
    ppermute x2, waiting for transfers between devices, butterfly_sum(): other = lax.ppermute(tree, axis, pairs)  4.45 us
    unnamed x24, local copies, waits for them, and re-layouts  4.04 us
    concatenate x3, other arithmetic, on_device(): jnp.concatenate([o[i] for o in outs], 2)  3.55 us
  transfers between devices with their start and end apart: 20, of which 11 were waited for; matrix products, arithmetic and copies ran while one was open for 14% of the time, Pallas kernels for 22%

profile of v13, /device:TPU:0, one launch (start us, length us, event | category | flops | bytes accessed | tf_op | source)
XLA Modules:
  0.0 119.9 jit_solution(7291110173446669493)
XLA Ops:
  0.6 1.9 %slice_bitcast_fusion.8 = (bf16[1,1,384,384]{3,2,1,0:T(8,128)(2,1)S(1)}, bf16[1,1,384,384]{3,2,1,0:T(8,128)(2,1)S(1)}, bf16[1,1,384,384]{3,2,1,0:T(8,128)(2,1)S(...) fusion(bf16[1,768,768]{2,1,0:T(8,128)(2,1)} %v_ref.3, ...), kind=kLoop, calls=%fused_computation.37 | loop fusion | bytes 4718592 | tf_op jit(solution)/shard_map/stack | solution.py:218
  3.5 5.0 %collective-permute-start = (bf16[2,1,384,384]{3,2,1,0:T(8,128)(2,1)}, bf16[2,1,384,384]{3,2,1,0:T(8,128)(2,1)S(1)}, u32[]{:S(2)}, u32[]{:S(2)}) collective-permute-start(bf16[2,1,384,384]{3,2,1,0:T(8,128)(2,1)} %pad_maximum_fusion.3), channel_id=1, source_target_pairs={{0,4},{4,8},{8,12},{1,5},{5,9},{9,13},{2,6},{6,10},{10,14},{3,7},{... | collective-permute-start | bytes 1769480 | tf_op jit(solution)/shard_map/ppermute | solution.py:21
  13.7 5.2 %collective-permute-start.2 = (bf16[2,1,384,384]{3,2,1,0:T(8,128)(2,1)}, bf16[2,1,384,384]{3,2,1,0:T(8,128)(2,1)S(1)}, u32[]{:S(2)}, u32[]{:S(2)}) collective-permute-start(bf16[2,1,384,384]{3,2,1,0:T(8,128)(2,1)} %pad_maximum_fusion.5), channel_id=1, source_target_pairs={{0,4},{4,8},{8,12},{1,5},{5,9},{9,13},{2,6},{6,10},{10,14},{3,7},{... | collective-permute-start | bytes 1769480 | tf_op jit(solution)/shard_map/ppermute | solution.py:21
  22.4 5.2 %collective-permute-done.1.right_ref = bf16[2,1,384,384]{3,2,1,0:T(8,128)(2,1)S(1)} collective-permute-done((bf16[2,1,384,384]{3,2,1,0:T(8,128)(2,1)}, bf16[2,1,384,384]{3,2,1,0:T(8,128)(2,1)S(1)}, u32[]{:S(2)}, u32[]{:S(2)}) %collective-permute-start.1) | collective-permute-done | bytes 589856 | tf_op jit(solution)/shard_map/ppermute | solution.py:21
  28.5 13.4 %shard_map.128 = (bf16[1,768,384]{2,1,0:T(8,128)(2,1)}, bf16[1,768,384]{2,1,0:T(8,128)(2,1)}, bf16[1,768,384]{2,1,0:T(8,128)(2,1)}, bf16[2,1,384,384]{3,2,1,0:T(8,128)(2,1)}, bf16[2,1,384,384]{3,2,1,0:T(8,128)(2,1)}) custom-call(f32[6]{0:T(128)} %and_select_fusion.bias_ref, bf16[1,768,768]{2,1,0:T(8,128)(2,1)} %q_ref.3, bf16[1,768,768]{2,1,0:T(8,128)(2,1)} %g_ref.3, ...), custom_call_target="tpu_custom_call" | custom-call | tf_op jit(solution)/shard_map/pallas_call | solution.py:168
  41.9 3.5 %collective-permute-start.4 = (bf16[2,1,384,384]{3,2,1,0:T(8,128)(2,1)}, bf16[2,1,384,384]{3,2,1,0:T(8,128)(2,1)S(1)}, u32[]{:S(2)}, u32[]{:S(2)}) collective-permute-start(bf16[2,1,384,384]{3,2,1,0:T(8,128)(2,1)} %get-tuple-element.18), channel_id=1, source_target_pairs={{0,4},{4,8},{8,12},{1,5},{5,9},{9,13},{2,6},{6,10},{10,14},{3,7},{... | collective-permute-start | bytes 1769480 | tf_op jit(solution)/shard_map/ppermute | solution.py:21
  48.3 13.4 %shard_map.129 = (bf16[1,768,384]{2,1,0:T(8,128)(2,1)}, bf16[1,768,384]{2,1,0:T(8,128)(2,1)}, bf16[1,768,384]{2,1,0:T(8,128)(2,1)}, bf16[2,1,384,384]{3,2,1,0:T(8,128)(2,1)}, bf16[2,1,384,384]{3,2,1,0:T(8,128)(2,1)}) custom-call(f32[6]{0:T(128)} %and_select_fusion.bias_ref, bf16[1,768,768]{2,1,0:T(8,128)(2,1)} %q_ref.3, bf16[1,768,768]{2,1,0:T(8,128)(2,1)} %g_ref.3, ...), custom_call_target="tpu_custom_call" | custom-call | tf_op jit(solution)/shard_map/pallas_call | solution.py:168
  61.8 5.4 %collective-permute-start.6 = (bf16[2,1,384,384]{3,2,1,0:T(8,128)(2,1)}, bf16[2,1,384,384]{3,2,1,0:T(8,128)(2,1)}, u32[]{:S(2)}, u32[]{:S(2)}) collective-permute-start(bf16[2,1,384,384]{3,2,1,0:T(8,128)(2,1)} %get-tuple-element.21), channel_id=1, source_target_pairs={{0,4},{4,8},{8,12},{1,5},{5,9},{9,13},{2,6},{6,10},{10,14},{3,7},{... | collective-permute-start | bytes 1769480 | tf_op jit(solution)/shard_map/ppermute | solution.py:21
  67.2 1.5 %collective-permute-start.7 = (bf16[2,1,384,384]{3,2,1,0:T(8,128)(2,1)}, bf16[2,1,384,384]{3,2,1,0:T(8,128)(2,1)}, u32[]{:S(2)}, u32[]{:S(2)}) collective-permute-start(bf16[2,1,384,384]{3,2,1,0:T(8,128)(2,1)} %get-tuple-element.22), channel_id=1, source_target_pairs={{4,0},{8,4},{12,8},{5,1},{9,5},{13,9},{6,2},{10,6},{14,10},{7,3},{... | collective-permute-start | bytes 1769480 | tf_op jit(solution)/shard_map/ppermute | solution.py:21
  68.7 2.1 %fusion.19 = f32[1,768,64]{1,2,0:T(8,128)} fusion(bf16[768,64]{0,1:T(8,128)(2,1)} %param.14, bf16[1,768,768]{2,1,0:T(8,128)(2,1)S(1)} %copy-done), kind=kOutput, calls=%fused_computation.26 | convolution fusion | flops 75497472 | bytes 1474560 | tf_op jit(solution)/shard_map/pqg,gv->pqv/dot_general | solution.py:192
  70.7 1.5 %collective-permute-start.14 = (f32[1,768,64]{1,2,0:T(8,128)}, f32[1,768,64]{1,2,0:T(8,128)}, u32[]{:S(2)}, u32[]{:S(2)}) collective-permute-start(f32[1,768,64]{1,2,0:T(8,128)} %fusion.19), channel_id=1, source_target_pairs={{0,2},{2,0},{1,3},{3,1},{4,6},{6,4},{5,7},{7,5},{8,10},{10,8},{9,1... | collective-permute-start | bytes 589832 | tf_op jit(solution)/shard_map/ppermute | solution.py:31
  73.8 2.2 %collective-permute-done.6 = bf16[2,1,384,384]{3,2,1,0:T(8,128)(2,1)} collective-permute-done((bf16[2,1,384,384]{3,2,1,0:T(8,128)(2,1)}, bf16[2,1,384,384]{3,2,1,0:T(8,128)(2,1)}, u32[]{:S(2)}, u32[]{:S(2)}) %collective-permute-start.6) | collective-permute-done | bytes 589856 | tf_op jit(solution)/shard_map/ppermute | solution.py:21
  76.0 4.9 %collective-permute-done.7 = bf16[2,1,384,384]{3,2,1,0:T(8,128)(2,1)} collective-permute-done((bf16[2,1,384,384]{3,2,1,0:T(8,128)(2,1)}, bf16[2,1,384,384]{3,2,1,0:T(8,128)(2,1)}, u32[]{:S(2)}, u32[]{:S(2)}) %collective-permute-start.7) | collective-permute-done | bytes 589856 | tf_op jit(solution)/shard_map/ppermute | solution.py:21
  80.9 1.4 %maximum_convert_fusion.1 = f32[2,1,768,384]{3,2,1,0:T(8,128)S(1)} fusion(bf16[2,1,384,384]{3,2,1,0:T(8,128)(2,1)} %collective-permute-done.7, bf16[2,1,384,384]{3,2,1,0:T(8,128)(2,1)} %collective-permute-done.6), kind=kLoop, calls=%fused_computation.14 | loop fusion | flops 2359296 | bytes 3538944 | tf_op jit(solution)/shard_map/convert_element_type | solution.py:225
  82.8 1.8 %fusion.22 = f32[64,768]{1,0:T(8,128)S(1)} fusion(bf16[1,768,768]{2,1,0:T(8,128)(2,1)S(1)} %pad_maximum_fusion.2, f32[1,768,64]{1,2,0:T(8,128)} %fusion.19, f32[1,768,64]{1,2,0:T(8,128)} %collective-permute-done.14), kind=kOutput, calls=%fused_computation.27 | convolution fusion | flops 75644928 | bytes 1769472 | tf_op jit(solution)/shard_map/igb,igu->bu/dot_general | solution.py:240
  85.2 1.5 %select_n.106 = f32[24576]{0:T(1024)} reshape(f32[32,768]{1,0:T(8,128)} %get-tuple-element.37) | data formatting | bytes 196608 | tf_op jit(solution)/shard_map/jit(_where)/select_n | solution.py:44
  86.8 2.3 %pad_maximum_fusion = bf16[1,768,768]{2,1,0:T(8,128)(2,1)} fusion(bf16[1,768,384]{2,1,0:T(8,128)(2,1)} %get-tuple-element.16, bf16[1,768,384]{2,1,0:T(8,128)(2,1)} %get-tuple-element.15), kind=kLoop, calls=%fused_computation.12 | loop fusion | flops 2359296 | bytes 2359296 | tf_op jit(solution)/shard_map/concatenate | solution.py:230
  89.1 1.5 %select_n.104 = f32[24576]{0:T(1024)} reshape(f32[32,768]{1,0:T(8,128)} %get-tuple-element.38) | data formatting | bytes 196608 | tf_op jit(solution)/shard_map/jit(_where)/select_n | solution.py:43
  92.4 1.4 %fusion.16 = f32[1,768,64]{1,2,0:T(8,128)S(1)} fusion(bf16[64,768]{1,0:T(8,128)(2,1)} %param.15, bf16[1,768,768]{2,1,0:T(8,128)(2,1)S(1)} %pad_maximum_fusion.2), kind=kOutput, calls=%fused_computation.25 | convolution fusion | flops 75497472 | bytes 1474560 | tf_op jit(solution)/shard_map/dsi,ji->dsj/dot_general | solution.py:233
  93.8 1.5 %collective-permute-start.8 = (f32[1,768,64]{1,2,0:T(8,128)S(1)}, f32[1,768,64]{1,2,0:T(8,128)S(1)}, u32[]{:S(2)}, u32[]{:S(2)}) collective-permute-start(f32[1,768,64]{1,2,0:T(8,128)S(1)} %fusion.16), channel_id=1, source_target_pairs={{0,2},{2,0},{1,3},{3,1},{4,6},{6,4},{5,7},{7,5},{8,10},{10,8},{9,1... | collective-permute-start | bytes 589832 | tf_op jit(solution)/shard_map/ppermute | solution.py:31
  96.4 4.4 %collective-permute-done.8 = f32[1,768,64]{1,2,0:T(8,128)S(1)} collective-permute-done((f32[1,768,64]{1,2,0:T(8,128)S(1)}, f32[1,768,64]{1,2,0:T(8,128)S(1)}, u32[]{:S(2)}, u32[]{:S(2)}) %collective-permute-start.8) | collective-permute-done | bytes 196640 | tf_op jit(solution)/shard_map/ppermute | solution.py:31
  104.7 2.0 %collective-permute-done.18 = f32[12288]{0:T(1024)S(1)} collective-permute-done((f32[12288]{0:T(1024)S(1)}, f32[12288]{0:T(1024)S(1)}, u32[]{:S(2)}, u32[]{:S(2)}) %collective-permute-start.18) | collective-permute-done | bytes 49184 | tf_op jit(solution)/shard_map/ppermute | solution.py:53
  108.7 5.0 %collective-permute-done.11 = f32[12288]{0:T(1024)S(1)} collective-permute-done((f32[12288]{0:T(1024)S(1)}, f32[12288]{0:T(1024)S(1)}, u32[]{:S(2)}, u32[]{:S(2)}) %collective-permute-start.11) | collective-permute-done | bytes 49184 | tf_op jit(solution)/shard_map/ppermute | solution.py:78
  115.0 2.8 %collective-permute-done.12 = f32[12288]{0:T(1024)S(1)} collective-permute-done((f32[12288]{0:T(1024)S(1)}, f32[12288]{0:T(1024)S(1)}, u32[]{:S(2)}, u32[]{:S(2)}) %collective-permute-start.12) | collective-permute-done | bytes 49184 | tf_op jit(solution)/shard_map/ppermute | solution.py:53
  (92 shorter events, 27.9 us)
Async XLA Ops:
  0.6 68.0 %copy-start = (bf16[1,768,768]{2,1,0:T(8,128)(2,1)S(1)}, bf16[1,768,768]{2,1,0:T(8,128)(2,1)}, u32[]{:S(2)}) copy-start(bf16[1,768,768]{2,1,0:T(8,128)(2,1)} %param.13) | copy-start | bytes 3538948
  3.5 19.0 %collective-permute-start = (bf16[2,1,384,384]{3,2,1,0:T(8,128)(2,1)}, bf16[2,1,384,384]{3,2,1,0:T(8,128)(2,1)S(1)}, u32[]{:S(2)}, u32[]{:S(2)}) collective-permute-start(bf16[2,1,384,384]{3,2,1,0:T(8,128)(2,1)} %pad_maximum_fusion.3), channel_id=1, source_target_pairs={{0,4},{4,8},{8,12},{1,5},{5,9},{9,13},{2,6},{6,10},{10,14},{3,7},{... | collective-permute-start | bytes 1769480 | tf_op jit(solution)/shard_map/ppermute | solution.py:21
  9.3 18.3 %collective-permute-start.1 = (bf16[2,1,384,384]{3,2,1,0:T(8,128)(2,1)}, bf16[2,1,384,384]{3,2,1,0:T(8,128)(2,1)S(1)}, u32[]{:S(2)}, u32[]{:S(2)}) collective-permute-start(bf16[2,1,384,384]{3,2,1,0:T(8,128)(2,1)} %pad_maximum_fusion.4), channel_id=1, source_target_pairs={{4,0},{8,4},{12,8},{5,1},{9,5},{13,9},{6,2},{10,6},{14,10},{7,3},{... | collective-permute-start | bytes 1769480 | tf_op jit(solution)/shard_map/ppermute | solution.py:21
  10.6 9.0 %copy-start.10 = (s32[8,3]{0,1:T(4,128)S(1)}, s32[8,3]{0,1:T(4,128)}, u32[]{:S(2)}) copy-start(s32[8,3]{0,1:T(4,128)} %param.16) | copy-start | bytes 292
  11.5 35.2 %collective-permute-start.3 = (bf16[2,1,384,384]{3,2,1,0:T(8,128)(2,1)}, bf16[2,1,384,384]{3,2,1,0:T(8,128)(2,1)S(1)}, u32[]{:S(2)}, u32[]{:S(2)}) collective-permute-start(bf16[2,1,384,384]{3,2,1,0:T(8,128)(2,1)} %pad_maximum_fusion.6), channel_id=1, source_target_pairs={{4,0},{8,4},{12,8},{5,1},{9,5},{13,9},{6,2},{10,6},{14,10},{7,3},{... | collective-permute-start | bytes 1769480 | tf_op jit(solution)/shard_map/ppermute | solution.py:21
  13.7 33.1 %collective-permute-start.2 = (bf16[2,1,384,384]{3,2,1,0:T(8,128)(2,1)}, bf16[2,1,384,384]{3,2,1,0:T(8,128)(2,1)S(1)}, u32[]{:S(2)}, u32[]{:S(2)}) collective-permute-start(bf16[2,1,384,384]{3,2,1,0:T(8,128)(2,1)} %pad_maximum_fusion.5), channel_id=1, source_target_pairs={{0,4},{4,8},{8,12},{1,5},{5,9},{9,13},{2,6},{6,10},{10,14},{3,7},{... | collective-permute-start | bytes 1769480 | tf_op jit(solution)/shard_map/ppermute | solution.py:21
  41.9 30.3 %collective-permute-start.4 = (bf16[2,1,384,384]{3,2,1,0:T(8,128)(2,1)}, bf16[2,1,384,384]{3,2,1,0:T(8,128)(2,1)S(1)}, u32[]{:S(2)}, u32[]{:S(2)}) collective-permute-start(bf16[2,1,384,384]{3,2,1,0:T(8,128)(2,1)} %get-tuple-element.18), channel_id=1, source_target_pairs={{0,4},{4,8},{8,12},{1,5},{5,9},{9,13},{2,6},{6,10},{10,14},{3,7},{... | collective-permute-start | bytes 1769480 | tf_op jit(solution)/shard_map/ppermute | solution.py:21
  45.4 26.8 %collective-permute-start.5 = (bf16[2,1,384,384]{3,2,1,0:T(8,128)(2,1)}, bf16[2,1,384,384]{3,2,1,0:T(8,128)(2,1)S(1)}, u32[]{:S(2)}, u32[]{:S(2)}) collective-permute-start(bf16[2,1,384,384]{3,2,1,0:T(8,128)(2,1)} %get-tuple-element.19), channel_id=1, source_target_pairs={{4,0},{8,4},{12,8},{5,1},{9,5},{13,9},{6,2},{10,6},{14,10},{7,3},{... | collective-permute-start | bytes 1769480 | tf_op jit(solution)/shard_map/ppermute | solution.py:21
  61.8 14.2 %collective-permute-start.6 = (bf16[2,1,384,384]{3,2,1,0:T(8,128)(2,1)}, bf16[2,1,384,384]{3,2,1,0:T(8,128)(2,1)}, u32[]{:S(2)}, u32[]{:S(2)}) collective-permute-start(bf16[2,1,384,384]{3,2,1,0:T(8,128)(2,1)} %get-tuple-element.21), channel_id=1, source_target_pairs={{0,4},{4,8},{8,12},{1,5},{5,9},{9,13},{2,6},{6,10},{10,14},{3,7},{... | collective-permute-start | bytes 1769480 | tf_op jit(solution)/shard_map/ppermute | solution.py:21
  67.2 13.8 %collective-permute-start.7 = (bf16[2,1,384,384]{3,2,1,0:T(8,128)(2,1)}, bf16[2,1,384,384]{3,2,1,0:T(8,128)(2,1)}, u32[]{:S(2)}, u32[]{:S(2)}) collective-permute-start(bf16[2,1,384,384]{3,2,1,0:T(8,128)(2,1)} %get-tuple-element.22), channel_id=1, source_target_pairs={{4,0},{8,4},{12,8},{5,1},{9,5},{13,9},{6,2},{10,6},{14,10},{7,3},{... | collective-permute-start | bytes 1769480 | tf_op jit(solution)/shard_map/ppermute | solution.py:21
  70.7 12.0 %collective-permute-start.14 = (f32[1,768,64]{1,2,0:T(8,128)}, f32[1,768,64]{1,2,0:T(8,128)}, u32[]{:S(2)}, u32[]{:S(2)}) collective-permute-start(f32[1,768,64]{1,2,0:T(8,128)} %fusion.19), channel_id=1, source_target_pairs={{0,2},{2,0},{1,3},{3,1},{4,6},{6,4},{5,7},{7,5},{8,10},{10,8},{9,1... | collective-permute-start | bytes 589832 | tf_op jit(solution)/shard_map/ppermute | solution.py:31
  73.7 8.6 %copy-start.7 = (bf16[1,768,384]{2,1,0:T(8,128)(2,1)S(1)}, bf16[1,768,384]{2,1,0:T(8,128)(2,1)}, u32[]{:S(2)}) copy-start(bf16[1,768,384]{2,1,0:T(8,128)(2,1)} %get-tuple-element.20) | copy-start | bytes 1769476
  82.7 9.7 %copy-start.1 = (bf16[1,768,768]{2,1,0:T(8,128)(2,1)}, bf16[1,768,768]{2,1,0:T(8,128)(2,1)S(1)}, u32[]{:S(2)}) copy-start(bf16[1,768,768]{2,1,0:T(8,128)(2,1)S(1)} %pad_maximum_fusion.2) | copy-start | bytes 3538948
  86.8 3.9 %collective-permute-start.15 = (f32[24576]{0:T(1024)}, f32[24576]{0:T(1024)}, u32[]{:S(2)}, u32[]{:S(2)}) collective-permute-start(f32[24576]{0:T(1024)} %select_n.106), channel_id=1, source_target_pairs={{0,1},{1,0},{2,3},{3,2},{4,5},{5,4},{6,7},{7,6},{8,9},{9,8},{10,11... | collective-permute-start | bytes 294920 | tf_op jit(solution)/shard_map/ppermute | solution.py:45
  91.6 4.2 %collective-permute-start.16 = (f32[12288]{0:T(1024)S(1)}, f32[12288]{0:T(1024)S(1)}, u32[]{:S(2)}, u32[]{:S(2)}) collective-permute-start(f32[12288]{0:T(1024)S(1)} %slice_select_fusion.4), channel_id=1, source_target_pairs={{0,4},{4,0},{8,12},{12,8},{1,5},{5,1},{9,13},{13,9},{2,6},{6,2},{1... | collective-permute-start | bytes 147464 | tf_op jit(solution)/shard_map/ppermute | solution.py:45
  93.8 7.1 %collective-permute-start.8 = (f32[1,768,64]{1,2,0:T(8,128)S(1)}, f32[1,768,64]{1,2,0:T(8,128)S(1)}, u32[]{:S(2)}, u32[]{:S(2)}) collective-permute-start(f32[1,768,64]{1,2,0:T(8,128)S(1)} %fusion.16), channel_id=1, source_target_pairs={{0,2},{2,0},{1,3},{3,1},{4,6},{6,4},{5,7},{7,5},{8,10},{10,8},{9,1... | collective-permute-start | bytes 589832 | tf_op jit(solution)/shard_map/ppermute | solution.py:31
  95.9 6.6 %collective-permute-start.17 = (f32[12288]{0:T(1024)S(1)}, f32[12288]{0:T(1024)S(1)}, u32[]{:S(2)}, u32[]{:S(2)}) collective-permute-start(f32[12288]{0:T(1024)S(1)} %select_add_fusion), channel_id=1, source_target_pairs={{0,8},{4,12},{8,0},{12,4},{1,9},{5,13},{9,1},{13,5},{2,10},{6,14},... | collective-permute-start | bytes 147464 | tf_op jit(solution)/shard_map/ppermute | solution.py:78
  101.3 2.6 %collective-permute-start.9 = (f32[24576]{0:T(1024)S(1)}, f32[24576]{0:T(1024)S(1)}, u32[]{:S(2)}, u32[]{:S(2)}) collective-permute-start(f32[24576]{0:T(1024)S(1)} %select_n.96), channel_id=1, source_target_pairs={{0,1},{1,0},{2,3},{3,2},{4,5},{5,4},{6,7},{7,6},{8,9},{9,8},{10,11... | collective-permute-start | bytes 294920 | tf_op jit(solution)/shard_map/ppermute | solution.py:45
  102.5 4.2 %collective-permute-start.18 = (f32[12288]{0:T(1024)S(1)}, f32[12288]{0:T(1024)S(1)}, u32[]{:S(2)}, u32[]{:S(2)}) collective-permute-start(f32[12288]{0:T(1024)S(1)} %add.58), channel_id=1, source_target_pairs={{0,4},{4,0},{8,12},{12,8},{1,5},{5,1},{9,13},{13,9},{2,6},{6,2},{1... | collective-permute-start | bytes 147464 | tf_op jit(solution)/shard_map/ppermute | solution.py:53
  103.9 4.2 %collective-permute-start.10 = (f32[12288]{0:T(1024)S(1)}, f32[12288]{0:T(1024)S(1)}, u32[]{:S(2)}, u32[]{:S(2)}) collective-permute-start(f32[12288]{0:T(1024)S(1)} %slice_select_fusion.5), channel_id=1, source_target_pairs={{0,4},{4,0},{8,12},{12,8},{1,5},{5,1},{9,13},{13,9},{2,6},{6,2},{1... | collective-permute-start | bytes 147464 | tf_op jit(solution)/shard_map/ppermute | solution.py:45
  106.7 2.0 %collective-permute-start.19 = (f32[24576]{0:T(1024)S(1)}, f32[24576]{0:T(1024)S(1)}, u32[]{:S(2)}, u32[]{:S(2)}) collective-permute-start(f32[24576]{0:T(1024)S(1)} %maximum_select_fusion.4), channel_id=1, source_target_pairs={{0,1},{1,0},{2,3},{3,2},{4,5},{5,4},{6,7},{7,6},{8,9},{9,8},{10,11... | collective-permute-start | bytes 294920 | tf_op jit(solution)/shard_map/ppermute | solution.py:53
  108.1 5.6 %collective-permute-start.11 = (f32[12288]{0:T(1024)S(1)}, f32[12288]{0:T(1024)S(1)}, u32[]{:S(2)}, u32[]{:S(2)}) collective-permute-start(f32[12288]{0:T(1024)S(1)} %select_add_fusion.1), channel_id=1, source_target_pairs={{0,8},{4,12},{8,0},{12,4},{1,9},{5,13},{9,1},{13,5},{2,10},{6,14},... | collective-permute-start | bytes 147464 | tf_op jit(solution)/shard_map/ppermute | solution.py:78
  113.7 4.2 %collective-permute-start.12 = (f32[12288]{0:T(1024)S(1)}, f32[12288]{0:T(1024)S(1)}, u32[]{:S(2)}, u32[]{:S(2)}) collective-permute-start(f32[12288]{0:T(1024)S(1)} %add.54), channel_id=1, source_target_pairs={{0,4},{4,0},{8,12},{12,8},{1,5},{5,1},{9,13},{13,9},{2,6},{6,2},{1... | collective-permute-start | bytes 147464 | tf_op jit(solution)/shard_map/ppermute | solution.py:53
  117.8 1.4 %collective-permute-start.13 = (f32[24576]{0:T(1024)S(1)}, f32[24576]{0:T(1024)S(1)}, u32[]{:S(2)}, u32[]{:S(2)}) collective-permute-start(f32[24576]{0:T(1024)S(1)} %maximum_select_fusion.2), channel_id=1, source_target_pairs={{0,1},{1,0},{2,3},{3,2},{4,5},{5,4},{6,7},{7,6},{8,9},{9,8},{10,11... | collective-permute-start | bytes 294920 | tf_op jit(solution)/shard_map/ppermute | solution.py:53
  (8 other events, 19.2 us)

commit v14 on v12

--- a/solution.py
+++ b/solution.py
@@ -209,11 +209,12 @@
     outs = []
     for chunk in range(chunks):
         cols = slice(chunk * per_chunk * HEAD_SIZE, (chunk + 1) * per_chunk * HEAD_SIZE)
-        left_kv = shifted(
-            jnp.stack((key_matrix[:, block_len - TILE:, cols], values[:, block_len - TILE:, cols])),
-            "seq",
-            1,
+        last_tile = jnp.stack(
+            (key_matrix[:, block_len - TILE:, cols], values[:, block_len - TILE:, cols])
         )
+        if chunk == 0:
+            last_tile, lowered_rows = lax.optimization_barrier((last_tile, lowered_rows))
+        left_kv = shifted(last_tile, "seq", 1)
         right_kv = shifted(
             jnp.stack((key_matrix[:, :TILE, cols], values[:, :TILE, cols]), 0), "seq", -1
         )

time: 112 us -> 114 us (1.018)
  starting transfers between devices: 28.9 us -> 33.1 us
  matrix products: 4.26 us -> 2.53 us
  local copies, waits for them, and re-layouts: 7.82 us -> 6.32 us
    ppermute x1, starting transfers between devices: 0.55 us -> 2.64 us  [all_sum(): lax.ppermute(flat, axis, [(i, i ^ step) for i in range(lax.axis_size(axis...]
    ppermute x1, waiting for transfers between devices: 6.53 us -> 4.44 us  [all_sum(): lax.ppermute(flat, axis, [(i, i ^ step) for i in range(lax.axis_size(axis...]
    ppermute x2, waiting for transfers between devices: 2.82 us -> 4.64 us  [butterfly_sum(): other = lax.ppermute(tree, axis, pairs)]
    convert_element_type x2, other arithmetic: 1.55 us -> 2.71 us  [on_device(): arrived = jnp.concatenate((from_left, from_right), 2).astype(jnp.float32)]
    unnamed x30 -> x32, local copies, waits for them, and re-layouts: 4.85 us -> 3.77 us
  transfers between devices with their start and end apart: 15 -> 15, of which waited for: 10 -> 10; matrix products, arithmetic and copies ran while one was open for 12% -> 10% of each run, Pallas kernels for 24% -> 24%
where the time goes in v14:
time: 114 us; the launch traced here: 113 us
  starting transfers between devices  33.1 us (29%)
  waiting for transfers between devices  31.5 us (28%)
  Pallas kernels  26.9 us (24%)
  other arithmetic  11.8 us (10%)
  local copies, waits for them, and re-layouts  6.32 us (6%)
  matrix products  2.53 us (2%)
    pallas_call x2, Pallas kernels, attention_backward(): pl.pallas_call(attention_kernel, grid=(clip_count, heads), in_specs=[pl.B...  26.9 us
    ppermute x8, starting transfers between devices, shifted(): return lax.ppermute(shard, axis, pairs)  25.1 us
    ppermute x8, waiting for transfers between devices, shifted(): return lax.ppermute(shard, axis, pairs)  13.8 us
    ppermute x2, waiting for transfers between devices, scatter_sum(): lax.ppermute(send, axis, [(i, i ^ step) for i in range(peers)])  4.95 us
    ppermute x2, waiting for transfers between devices, butterfly_sum(): other = lax.ppermute(tree, axis, pairs)  4.64 us
    ppermute x1, waiting for transfers between devices, all_sum(): lax.ppermute(flat, axis, [(i, i ^ step) for i in range(lax.axis_size(axis...  4.44 us
    unnamed x32, local copies, waits for them, and re-layouts  3.77 us
    ppermute x2, waiting for transfers between devices, gather_back(): other = lax.ppermute(flat, axis, [(i, i ^ step) for i in range(peers)])  3.72 us
  transfers between devices with their start and end apart: 15, of which 10 were waited for; matrix products, arithmetic and copies ran while one was open for 10% of the time, Pallas kernels for 24%

profile of v14, /device:TPU:0, one launch (start us, length us, event | category | flops | bytes accessed | tf_op | source)
XLA Modules:
  0.0 113.2 jit_solution(18250489788586003540)
XLA Ops:
  1.9 1.4 %fusion.16 = f32[1,768,64]{1,2,0:T(8,128)S(1)} fusion(bf16[768,64]{0,1:T(8,128)(2,1)} %param.14, bf16[1,768,768]{2,1,0:T(8,128)(2,1)S(1)} %copy-done), kind=kOutput, calls=%fused_computation.25 | convolution fusion | flops 75497472 | bytes 1474560 | tf_op jit(solution)/shard_map/pqg,gv->pqv/dot_general | solution.py:192
  3.3 3.0 %collective-permute-start = (f32[1,768,64]{1,2,0:T(8,128)S(1)}, f32[1,768,64]{1,2,0:T(8,128)S(1)}, u32[]{:S(2)}, u32[]{:S(2)}) collective-permute-start(f32[1,768,64]{1,2,0:T(8,128)S(1)} %fusion.16), channel_id=1, source_target_pairs={{0,2},{2,0},{1,3},{3,1},{4,6},{6,4},{5,7},{7,5},{8,10},{10,8},{9,1... | collective-permute-start | bytes 589832 | tf_op jit(solution)/shard_map/ppermute | solution.py:31
  6.3 1.5 %slice_bitcast_fusion.8 = (bf16[1,1,384,384]{3,2,1,0:T(8,128)(2,1)S(1)}, bf16[1,1,384,384]{3,2,1,0:T(8,128)(2,1)S(1)}, bf16[1,1,384,384]{3,2,1,0:T(8,128)(2,1)S(...) fusion(bf16[1,768,768]{2,1,0:T(8,128)(2,1)} %v_ref.3, ...), kind=kLoop, calls=%fused_computation.38 | loop fusion | bytes 4718592 | tf_op jit(solution)/shard_map/stack | solution.py:219
  10.9 5.4 %collective-permute-start.3 = (bf16[2,1,384,384]{3,2,1,0:T(8,128)(2,1)}, bf16[2,1,384,384]{3,2,1,0:T(8,128)(2,1)}, u32[]{:S(2)}, u32[]{:S(2)}) collective-permute-start(bf16[2,1,384,384]{3,2,1,0:T(8,128)(2,1)} %pad_maximum_fusion.5), channel_id=1, source_target_pairs={{0,4},{4,8},{8,12},{1,5},{5,9},{9,13},{2,6},{6,10},{10,14},{3,7},{... | collective-permute-start | bytes 1769480 | tf_op jit(solution)/shard_map/ppermute | solution.py:21
  20.6 4.6 %collective-permute-start.1 = (bf16[2,1,384,384]{3,2,1,0:T(8,128)(2,1)}, bf16[2,1,384,384]{3,2,1,0:T(8,128)(2,1)S(1)}, u32[]{:S(2)}, u32[]{:S(2)}) collective-permute-start(bf16[2,1,384,384]{3,2,1,0:T(8,128)(2,1)} %pad_maximum_fusion.3), channel_id=1, source_target_pairs={{0,4},{4,8},{8,12},{1,5},{5,9},{9,13},{2,6},{6,10},{10,14},{3,7},{... | collective-permute-start | bytes 1769480 | tf_op jit(solution)/shard_map/ppermute | solution.py:21
  25.7 1.3 %collective-permute-done.4.right_ref = bf16[2,1,384,384]{3,2,1,0:T(8,128)(2,1)S(1)} collective-permute-done((bf16[2,1,384,384]{3,2,1,0:T(8,128)(2,1)}, bf16[2,1,384,384]{3,2,1,0:T(8,128)(2,1)S(1)}, u32[]{:S(2)}, u32[]{:S(2)}) %collective-permute-start.4) | collective-permute-done | bytes 589856 | tf_op jit(solution)/shard_map/ppermute | solution.py:21
  27.0 2.5 %collective-permute-done.3.left_ref = bf16[2,1,384,384]{3,2,1,0:T(8,128)(2,1)} collective-permute-done((bf16[2,1,384,384]{3,2,1,0:T(8,128)(2,1)}, bf16[2,1,384,384]{3,2,1,0:T(8,128)(2,1)}, u32[]{:S(2)}, u32[]{:S(2)}) %collective-permute-start.3) | collective-permute-done | bytes 589856 | tf_op jit(solution)/shard_map/ppermute | solution.py:21
  29.5 13.4 %shard_map.129 = (bf16[1,768,384]{2,1,0:T(8,128)(2,1)}, bf16[1,768,384]{2,1,0:T(8,128)(2,1)}, bf16[1,768,384]{2,1,0:T(8,128)(2,1)}, bf16[2,1,384,384]{3,2,1,0:T(8,128)(2,1)}, bf16[2,1,384,384]{3,2,1,0:T(8,128)(2,1)}) custom-call(f32[6]{0:T(128)} %and_select_fusion.bias_ref, bf16[1,768,768]{2,1,0:T(8,128)(2,1)} %q_ref.3, bf16[1,768,768]{2,1,0:T(8,128)(2,1)} %g_ref.3, ...), custom_call_target="tpu_custom_call" | custom-call | tf_op jit(solution)/shard_map/pallas_call | solution.py:168
  42.9 4.4 %collective-permute-start.7 = (bf16[2,1,384,384]{3,2,1,0:T(8,128)(2,1)}, bf16[2,1,384,384]{3,2,1,0:T(8,128)(2,1)S(1)}, u32[]{:S(2)}, u32[]{:S(2)}) collective-permute-start(bf16[2,1,384,384]{3,2,1,0:T(8,128)(2,1)} %get-tuple-element.24), channel_id=1, source_target_pairs={{0,4},{4,8},{8,12},{1,5},{5,9},{9,13},{2,6},{6,10},{10,14},{3,7},{... | collective-permute-start | bytes 1769480 | tf_op jit(solution)/shard_map/ppermute | solution.py:21
  47.4 1.3 %collective-permute-start.8 = (bf16[2,1,384,384]{3,2,1,0:T(8,128)(2,1)}, bf16[2,1,384,384]{3,2,1,0:T(8,128)(2,1)}, u32[]{:S(2)}, u32[]{:S(2)}) collective-permute-start(bf16[2,1,384,384]{3,2,1,0:T(8,128)(2,1)} %get-tuple-element.25), channel_id=1, source_target_pairs={{4,0},{8,4},{12,8},{5,1},{9,5},{13,9},{6,2},{10,6},{14,10},{7,3},{... | collective-permute-start | bytes 1769480 | tf_op jit(solution)/shard_map/ppermute | solution.py:21
  50.3 13.4 %shard_map.128 = (bf16[1,768,384]{2,1,0:T(8,128)(2,1)}, bf16[1,768,384]{2,1,0:T(8,128)(2,1)}, bf16[1,768,384]{2,1,0:T(8,128)(2,1)}, bf16[2,1,384,384]{3,2,1,0:T(8,128)(2,1)}, bf16[2,1,384,384]{3,2,1,0:T(8,128)(2,1)}) custom-call(f32[6]{0:T(128)} %and_select_fusion.bias_ref, bf16[1,768,768]{2,1,0:T(8,128)(2,1)} %q_ref.3, bf16[1,768,768]{2,1,0:T(8,128)(2,1)} %g_ref.3, ...), custom_call_target="tpu_custom_call" | custom-call | tf_op jit(solution)/shard_map/pallas_call | solution.py:168
  63.8 5.4 %collective-permute-start.5 = (bf16[2,1,384,384]{3,2,1,0:T(8,128)(2,1)}, bf16[2,1,384,384]{3,2,1,0:T(8,128)(2,1)}, u32[]{:S(2)}, u32[]{:S(2)}) collective-permute-start(bf16[2,1,384,384]{3,2,1,0:T(8,128)(2,1)} %get-tuple-element.21), channel_id=1, source_target_pairs={{0,4},{4,8},{8,12},{1,5},{5,9},{9,13},{2,6},{6,10},{10,14},{3,7},{... | collective-permute-start | bytes 1769480 | tf_op jit(solution)/shard_map/ppermute | solution.py:21
  69.2 1.5 %collective-permute-start.6 = (bf16[2,1,384,384]{3,2,1,0:T(8,128)(2,1)}, bf16[2,1,384,384]{3,2,1,0:T(8,128)(2,1)}, u32[]{:S(2)}, u32[]{:S(2)}) collective-permute-start(bf16[2,1,384,384]{3,2,1,0:T(8,128)(2,1)} %get-tuple-element.22), channel_id=1, source_target_pairs={{4,0},{8,4},{12,8},{5,1},{9,5},{13,9},{6,2},{10,6},{14,10},{7,3},{... | collective-permute-start | bytes 1769480 | tf_op jit(solution)/shard_map/ppermute | solution.py:21
  70.7 1.3 %maximum_convert_fusion.1 = f32[2,1,768,384]{3,2,1,0:T(8,128)S(1)} fusion(bf16[2,1,384,384]{3,2,1,0:T(8,128)(2,1)} %collective-permute-done.8, bf16[2,1,384,384]{3,2,1,0:T(8,128)(2,1)S(1)} %collective-permute-done.7), kind=kLoop, calls=%fused_computation.14 | loop fusion | flops 2359296 | bytes 3538944 | tf_op jit(solution)/shard_map/convert_element_type | solution.py:226
  72.3 5.0 %collective-permute-done.5 = bf16[2,1,384,384]{3,2,1,0:T(8,128)(2,1)} collective-permute-done((bf16[2,1,384,384]{3,2,1,0:T(8,128)(2,1)}, bf16[2,1,384,384]{3,2,1,0:T(8,128)(2,1)}, u32[]{:S(2)}, u32[]{:S(2)}) %collective-permute-start.5) | collective-permute-done | bytes 589856 | tf_op jit(solution)/shard_map/ppermute | solution.py:21
  77.4 4.9 %collective-permute-done.6 = bf16[2,1,384,384]{3,2,1,0:T(8,128)(2,1)} collective-permute-done((bf16[2,1,384,384]{3,2,1,0:T(8,128)(2,1)}, bf16[2,1,384,384]{3,2,1,0:T(8,128)(2,1)}, u32[]{:S(2)}, u32[]{:S(2)}) %collective-permute-start.6) | collective-permute-done | bytes 589856 | tf_op jit(solution)/shard_map/ppermute | solution.py:21
  82.3 1.4 %maximum_convert_fusion = f32[2,1,768,384]{3,2,1,0:T(8,128)S(1)} fusion(bf16[2,1,384,384]{3,2,1,0:T(8,128)(2,1)} %collective-permute-done.6, bf16[2,1,384,384]{3,2,1,0:T(8,128)(2,1)} %collective-permute-done.5), kind=kLoop, calls=%fused_computation.13 | loop fusion | flops 2359296 | bytes 3538944 | tf_op jit(solution)/shard_map/convert_element_type | solution.py:226
  86.5 4.6 %collective-permute-done.9 = f32[1,768,64]{1,2,0:T(8,128)S(1)} collective-permute-done((f32[1,768,64]{1,2,0:T(8,128)S(1)}, f32[1,768,64]{1,2,0:T(8,128)S(1)}, u32[]{:S(2)}, u32[]{:S(2)}) %collective-permute-start.9) | collective-permute-done | bytes 196640 | tf_op jit(solution)/shard_map/ppermute | solution.py:31
  91.6 1.5 %collective-permute-done.10 = f32[49152]{0:T(1024)} collective-permute-done((f32[49152]{0:T(1024)S(1)}, f32[49152]{0:T(1024)}, u32[]{:S(2)}, u32[]{:S(2)}) %collective-permute-start.10) | collective-permute-done | bytes 196640 | tf_op jit(solution)/shard_map/ppermute | solution.py:45
  94.1 1.5 %collective-permute-start.11 = (f32[24576]{0:T(1024)S(1)}, f32[24576]{0:T(1024)S(1)}, u32[]{:S(2)}, u32[]{:S(2)}) collective-permute-start(f32[24576]{0:T(1024)S(1)} %slice_select_fusion), channel_id=1, source_target_pairs={{0,4},{4,0},{8,12},{12,8},{1,5},{5,1},{9,13},{13,9},{2,6},{6,2},{1... | collective-permute-start | bytes 294920 | tf_op jit(solution)/shard_map/ppermute | solution.py:45
  95.6 3.4 %collective-permute-done.11 = f32[24576]{0:T(1024)S(1)} collective-permute-done((f32[24576]{0:T(1024)S(1)}, f32[24576]{0:T(1024)S(1)}, u32[]{:S(2)}, u32[]{:S(2)}) %collective-permute-start.11) | collective-permute-done | bytes 98336 | tf_op jit(solution)/shard_map/ppermute | solution.py:45
  99.0 2.6 %collective-permute-start.12 = (f32[24576]{0:T(1024)S(1)}, f32[24576]{0:T(1024)S(1)}, u32[]{:S(2)}, u32[]{:S(2)}) collective-permute-start(f32[24576]{0:T(1024)S(1)} %select_add_fusion), channel_id=1, source_target_pairs={{0,8},{4,12},{8,0},{12,4},{1,9},{5,13},{9,1},{13,5},{2,10},{6,14},... | collective-permute-start | bytes 294920 | tf_op jit(solution)/shard_map/ppermute | solution.py:78
  101.7 4.4 %collective-permute-done.12 = f32[24576]{0:T(1024)S(1)} collective-permute-done((f32[24576]{0:T(1024)S(1)}, f32[24576]{0:T(1024)S(1)}, u32[]{:S(2)}, u32[]{:S(2)}) %collective-permute-start.12) | collective-permute-done | bytes 98336 | tf_op jit(solution)/shard_map/ppermute | solution.py:78
  107.3 3.5 %collective-permute-done.13 = f32[24576]{0:T(1024)S(1)} collective-permute-done((f32[24576]{0:T(1024)S(1)}, f32[24576]{0:T(1024)S(1)}, u32[]{:S(2)}, u32[]{:S(2)}) %collective-permute-start.13) | collective-permute-done | bytes 98336 | tf_op jit(solution)/shard_map/ppermute | solution.py:53
  (78 shorter events, 18.8 us)
Async XLA Ops:
  0.6 5.6 %copy-start.2 = (bf16[1,768,768]{2,1,0:T(8,128)(2,1)S(1)}, bf16[1,768,768]{2,1,0:T(8,128)(2,1)}, u32[]{:S(2)}) copy-start(bf16[1,768,768]{2,1,0:T(8,128)(2,1)} %k_ref.3) | copy-start | bytes 3538948
  3.3 16.6 %collective-permute-start = (f32[1,768,64]{1,2,0:T(8,128)S(1)}, f32[1,768,64]{1,2,0:T(8,128)S(1)}, u32[]{:S(2)}, u32[]{:S(2)}) collective-permute-start(f32[1,768,64]{1,2,0:T(8,128)S(1)} %fusion.16), channel_id=1, source_target_pairs={{0,2},{2,0},{1,3},{3,1},{4,6},{6,4},{5,7},{7,5},{8,10},{10,8},{9,1... | collective-permute-start | bytes 589832 | tf_op jit(solution)/shard_map/ppermute | solution.py:31
  8.7 18.3 %collective-permute-start.4 = (bf16[2,1,384,384]{3,2,1,0:T(8,128)(2,1)}, bf16[2,1,384,384]{3,2,1,0:T(8,128)(2,1)S(1)}, u32[]{:S(2)}, u32[]{:S(2)}) collective-permute-start(bf16[2,1,384,384]{3,2,1,0:T(8,128)(2,1)} %pad_maximum_fusion.6), channel_id=1, source_target_pairs={{4,0},{8,4},{12,8},{5,1},{9,5},{13,9},{6,2},{10,6},{14,10},{7,3},{... | collective-permute-start | bytes 1769480 | tf_op jit(solution)/shard_map/ppermute | solution.py:21
  10.0 8.6 %copy-start.15 = (s32[8]{0:T(128)S(1)}, s32[8]{0:T(128)}, u32[]{:S(2)}) copy-start(s32[8]{0:T(128)} %param.17) | copy-start | bytes 100
  10.0 8.9 %copy-start.14 = (s32[8,3]{0,1:T(4,128)S(1)}, s32[8,3]{0,1:T(4,128)}, u32[]{:S(2)}) copy-start(s32[8,3]{0,1:T(4,128)} %param.16) | copy-start | bytes 292
  10.9 18.6 %collective-permute-start.3 = (bf16[2,1,384,384]{3,2,1,0:T(8,128)(2,1)}, bf16[2,1,384,384]{3,2,1,0:T(8,128)(2,1)}, u32[]{:S(2)}, u32[]{:S(2)}) collective-permute-start(bf16[2,1,384,384]{3,2,1,0:T(8,128)(2,1)} %pad_maximum_fusion.5), channel_id=1, source_target_pairs={{0,4},{4,8},{8,12},{1,5},{5,9},{9,13},{2,6},{6,10},{10,14},{3,7},{... | collective-permute-start | bytes 1769480 | tf_op jit(solution)/shard_map/ppermute | solution.py:21
  17.1 31.6 %collective-permute-start.2 = (bf16[2,1,384,384]{3,2,1,0:T(8,128)(2,1)}, bf16[2,1,384,384]{3,2,1,0:T(8,128)(2,1)S(1)}, u32[]{:S(2)}, u32[]{:S(2)}) collective-permute-start(bf16[2,1,384,384]{3,2,1,0:T(8,128)(2,1)} %pad_maximum_fusion.4), channel_id=1, source_target_pairs={{4,0},{8,4},{12,8},{5,1},{9,5},{13,9},{6,2},{10,6},{14,10},{7,3},{... | collective-permute-start | bytes 1769480 | tf_op jit(solution)/shard_map/ppermute | solution.py:21
  20.6 28.1 %collective-permute-start.1 = (bf16[2,1,384,384]{3,2,1,0:T(8,128)(2,1)}, bf16[2,1,384,384]{3,2,1,0:T(8,128)(2,1)S(1)}, u32[]{:S(2)}, u32[]{:S(2)}) collective-permute-start(bf16[2,1,384,384]{3,2,1,0:T(8,128)(2,1)} %pad_maximum_fusion.3), channel_id=1, source_target_pairs={{0,4},{4,8},{8,12},{1,5},{5,9},{9,13},{2,6},{6,10},{10,14},{3,7},{... | collective-permute-start | bytes 1769480 | tf_op jit(solution)/shard_map/ppermute | solution.py:21
  27.0 2.5 %copy-start.4 = (bf16[2,1,384,384]{3,2,1,0:T(8,128)(2,1)}, bf16[2,1,384,384]{3,2,1,0:T(8,128)(2,1)S(1)}, u32[]{:S(2)}) copy-start(bf16[2,1,384,384]{3,2,1,0:T(8,128)(2,1)S(1)} %collective-permute-done.4.right_ref) | copy-start | bytes 1769476
  42.9 27.7 %collective-permute-start.7 = (bf16[2,1,384,384]{3,2,1,0:T(8,128)(2,1)}, bf16[2,1,384,384]{3,2,1,0:T(8,128)(2,1)S(1)}, u32[]{:S(2)}, u32[]{:S(2)}) collective-permute-start(bf16[2,1,384,384]{3,2,1,0:T(8,128)(2,1)} %get-tuple-element.24), channel_id=1, source_target_pairs={{0,4},{4,8},{8,12},{1,5},{5,9},{9,13},{2,6},{6,10},{10,14},{3,7},{... | collective-permute-start | bytes 1769480 | tf_op jit(solution)/shard_map/ppermute | solution.py:21
  47.4 23.3 %collective-permute-start.8 = (bf16[2,1,384,384]{3,2,1,0:T(8,128)(2,1)}, bf16[2,1,384,384]{3,2,1,0:T(8,128)(2,1)}, u32[]{:S(2)}, u32[]{:S(2)}) collective-permute-start(bf16[2,1,384,384]{3,2,1,0:T(8,128)(2,1)} %get-tuple-element.25), channel_id=1, source_target_pairs={{4,0},{8,4},{12,8},{5,1},{9,5},{13,9},{6,2},{10,6},{14,10},{7,3},{... | collective-permute-start | bytes 1769480 | tf_op jit(solution)/shard_map/ppermute | solution.py:21
  63.8 13.6 %collective-permute-start.5 = (bf16[2,1,384,384]{3,2,1,0:T(8,128)(2,1)}, bf16[2,1,384,384]{3,2,1,0:T(8,128)(2,1)}, u32[]{:S(2)}, u32[]{:S(2)}) collective-permute-start(bf16[2,1,384,384]{3,2,1,0:T(8,128)(2,1)} %get-tuple-element.21), channel_id=1, source_target_pairs={{0,4},{4,8},{8,12},{1,5},{5,9},{9,13},{2,6},{6,10},{10,14},{3,7},{... | collective-permute-start | bytes 1769480 | tf_op jit(solution)/shard_map/ppermute | solution.py:21
  69.2 13.2 %collective-permute-start.6 = (bf16[2,1,384,384]{3,2,1,0:T(8,128)(2,1)}, bf16[2,1,384,384]{3,2,1,0:T(8,128)(2,1)}, u32[]{:S(2)}, u32[]{:S(2)}) collective-permute-start(bf16[2,1,384,384]{3,2,1,0:T(8,128)(2,1)} %get-tuple-element.22), channel_id=1, source_target_pairs={{4,0},{8,4},{12,8},{5,1},{9,5},{13,9},{6,2},{10,6},{14,10},{7,3},{... | collective-permute-start | bytes 1769480 | tf_op jit(solution)/shard_map/ppermute | solution.py:21
  72.3 11.4 %copy-start.7 = (bf16[1,768,384]{2,1,0:T(8,128)(2,1)S(1)}, bf16[1,768,384]{2,1,0:T(8,128)(2,1)}, u32[]{:S(2)}) copy-start(bf16[1,768,384]{2,1,0:T(8,128)(2,1)} %get-tuple-element.20) | copy-start | bytes 1769476
  72.3 11.4 %copy-start.8 = (bf16[1,768,384]{2,1,0:T(8,128)(2,1)S(1)}, bf16[1,768,384]{2,1,0:T(8,128)(2,1)}, u32[]{:S(2)}) copy-start(bf16[1,768,384]{2,1,0:T(8,128)(2,1)} %get-tuple-element.26) | copy-start | bytes 1769476
  84.9 1.5 %copy-start.1 = (bf16[1,768,768]{2,1,0:T(8,128)(2,1)}, bf16[1,768,768]{2,1,0:T(8,128)(2,1)S(1)}, u32[]{:S(2)}) copy-start(bf16[1,768,768]{2,1,0:T(8,128)(2,1)S(1)} %pad_maximum_fusion.2) | copy-start | bytes 3538948
  85.4 5.7 %collective-permute-start.9 = (f32[1,768,64]{1,2,0:T(8,128)S(1)}, f32[1,768,64]{1,2,0:T(8,128)S(1)}, u32[]{:S(2)}, u32[]{:S(2)}) collective-permute-start(f32[1,768,64]{1,2,0:T(8,128)S(1)} %fusion.19), channel_id=1, source_target_pairs={{0,2},{2,0},{1,3},{3,1},{4,6},{6,4},{5,7},{7,5},{8,10},{10,8},{9,1... | collective-permute-start | bytes 589832 | tf_op jit(solution)/shard_map/ppermute | solution.py:31
  91.4 14.7 %copy-start.10 = (bf16[1,768,384]{2,1,0:T(8,128)(2,1)S(1)}, bf16[1,768,384]{2,1,0:T(8,128)(2,1)}, u32[]{:S(2)}) copy-start(bf16[1,768,384]{2,1,0:T(8,128)(2,1)} %get-tuple-element.19) | copy-start | bytes 1769476
  91.5 1.6 %collective-permute-start.10 = (f32[49152]{0:T(1024)S(1)}, f32[49152]{0:T(1024)}, u32[]{:S(2)}, u32[]{:S(2)}) collective-permute-start(f32[49152]{0:T(1024)S(1)} %select_n.63), channel_id=1, source_target_pairs={{0,1},{1,0},{2,3},{3,2},{4,5},{5,4},{6,7},{7,6},{8,9},{9,8},{10,11... | collective-permute-start | bytes 589832 | tf_op jit(solution)/shard_map/ppermute | solution.py:45
  91.6 14.6 %copy-start.11 = (bf16[1,768,384]{2,1,0:T(8,128)(2,1)S(1)}, bf16[1,768,384]{2,1,0:T(8,128)(2,1)}, u32[]{:S(2)}) copy-start(bf16[1,768,384]{2,1,0:T(8,128)(2,1)} %get-tuple-element.18) | copy-start | bytes 1769476
  94.1 4.9 %collective-permute-start.11 = (f32[24576]{0:T(1024)S(1)}, f32[24576]{0:T(1024)S(1)}, u32[]{:S(2)}, u32[]{:S(2)}) collective-permute-start(f32[24576]{0:T(1024)S(1)} %slice_select_fusion), channel_id=1, source_target_pairs={{0,4},{4,0},{8,12},{12,8},{1,5},{5,1},{9,13},{13,9},{2,6},{6,2},{1... | collective-permute-start | bytes 294920 | tf_op jit(solution)/shard_map/ppermute | solution.py:45
  99.0 7.1 %collective-permute-start.12 = (f32[24576]{0:T(1024)S(1)}, f32[24576]{0:T(1024)S(1)}, u32[]{:S(2)}, u32[]{:S(2)}) collective-permute-start(f32[24576]{0:T(1024)S(1)} %select_add_fusion), channel_id=1, source_target_pairs={{0,8},{4,12},{8,0},{12,4},{1,9},{5,13},{9,1},{13,5},{2,10},{6,14},... | collective-permute-start | bytes 294920 | tf_op jit(solution)/shard_map/ppermute | solution.py:78
  106.1 4.7 %collective-permute-start.13 = (f32[24576]{0:T(1024)S(1)}, f32[24576]{0:T(1024)S(1)}, u32[]{:S(2)}, u32[]{:S(2)}) collective-permute-start(f32[24576]{0:T(1024)S(1)} %add.46), channel_id=1, source_target_pairs={{0,4},{4,0},{8,12},{12,8},{1,5},{5,1},{9,13},{13,9},{2,6},{6,2},{1... | collective-permute-start | bytes 294920 | tf_op jit(solution)/shard_map/ppermute | solution.py:53
  110.8 1.5 %collective-permute-start.14 = (f32[49152]{0:T(1024)S(1)}, f32[49152]{0:T(1024)S(1)}, u32[]{:S(2)}, u32[]{:S(2)}) collective-permute-start(f32[49152]{0:T(1024)S(1)} %maximum_select_fusion.1), channel_id=1, source_target_pairs={{0,1},{1,0},{2,3},{3,2},{4,5},{5,4},{6,7},{7,6},{8,9},{9,8},{10,11... | collective-permute-start | bytes 589832 | tf_op jit(solution)/shard_map/ppermute | solution.py:53
  (7 other events, 7.8 us)

commit v15 on v12

--- a/solution.py
+++ b/solution.py
@@ -204,7 +204,7 @@
     bias = jnp.where(allowed, 0.0, masked_score).astype(jnp.float32)
 
     local_heads = queries.shape[2] // HEAD_SIZE
-    chunks = 2 if local_heads % 2 == 0 else 1
+    chunks = 3 if local_heads % 3 == 0 else (2 if local_heads % 2 == 0 else 1)
     per_chunk = local_heads // chunks
     outs = []
     for chunk in range(chunks):

time: 112 us -> 118 us (1.054)
  starting transfers between devices: 28.9 us -> 41.4 us
  waiting for transfers between devices: 32.4 us -> 24.7 us
  local copies, waits for them, and re-layouts: 7.82 us -> 5.33 us
  Pallas kernels: 26.8 us -> 28.9 us
  other arithmetic: 10.7 us -> 12.2 us
    ppermute x8 -> x12, starting transfers between devices: 24.3 us -> 35.8 us  [shifted(): return lax.ppermute(shard, axis, pairs)]
    ppermute x8 -> x12, waiting for transfers between devices: 13.6 us -> 6.77 us  [shifted(): return lax.ppermute(shard, axis, pairs)]
    unnamed x30 -> x40, local copies, waits for them, and re-layouts: 4.85 us -> 1.63 us
    pallas_call x2 -> x3, Pallas kernels: 26.8 us -> 28.9 us  [attention_backward(): pl.pallas_call(attention_kernel, grid=(clip_count, heads), in_specs=[pl.B...]
    another operation x2 -> x3, other arithmetic: 1.77 us -> 2.36 us  [on_device(): jnp.stack((key_matrix[:, block_len - TILE:, cols], values[:, block_len -...]
  transfers between devices with their start and end apart: 15 -> 19, of which waited for: 10 -> 8; matrix products, arithmetic and copies ran while one was open for 12% -> 12% of each run, Pallas kernels for 24% -> 24%
where the time goes in v15:
time: 118 us
  starting transfers between devices  41.4 us (35%)
  Pallas kernels  28.9 us (24%)
  waiting for transfers between devices  24.7 us (21%)
  other arithmetic  12.2 us (10%)
  local copies, waits for them, and re-layouts  5.33 us (5%)
  matrix products  4.25 us (4%)
    ppermute x12, starting transfers between devices, shifted(): return lax.ppermute(shard, axis, pairs)  35.8 us
    pallas_call x3, Pallas kernels, attention_backward(): pl.pallas_call(attention_kernel, grid=(clip_count, heads), in_specs=[pl.B...  28.9 us
    ppermute x12, waiting for transfers between devices, shifted(): return lax.ppermute(shard, axis, pairs)  6.77 us
    ppermute x1, waiting for transfers between devices, all_sum(): lax.ppermute(flat, axis, [(i, i ^ step) for i in range(lax.axis_size(axis...  5.54 us
    ppermute x2, waiting for transfers between devices, scatter_sum(): lax.ppermute(send, axis, [(i, i ^ step) for i in range(peers)])  5.12 us
    ppermute x2, waiting for transfers between devices, gather_back(): other = lax.ppermute(flat, axis, [(i, i ^ step) for i in range(peers)])  3.7 us
    ppermute x2, waiting for transfers between devices, butterfly_sum(): other = lax.ppermute(tree, axis, pairs)  3.53 us
    another operation x3, other arithmetic, on_device(): jnp.stack((key_matrix[:, block_len - TILE:, cols], values[:, block_len -...  2.36 us
  transfers between devices with their start and end apart: 19, of which 8 were waited for; matrix products, arithmetic and copies ran while one was open for 12% of the time, Pallas kernels for 24%

profile of v15, /device:TPU:0, one launch (start us, length us, event | category | flops | bytes accessed | tf_op | source)
XLA Modules:
  0.0 117.8 jit_solution(4237280769742766732)
XLA Ops:
  0.6 2.0 %slice_bitcast_fusion.15 = (bf16[1,1,384,256]{3,2,1,0:T(8,128)(2,1)S(1)}, bf16[1,1,384,256]{3,2,1,0:T(8,128)(2,1)S(1)}, bf16[1,1,384,256]{3,2,1,0:T(8,128)(2,1)S...) fusion(bf16[1,768,768]{2,1,0:T(8,128)(2,1)} %v_ref.5, ...), kind=kLoop, calls=%fused_computation.56 | loop fusion | bytes 4718592 | tf_op jit(solution)/shard_map/stack | solution.py:218
  3.4 4.9 %collective-permute-start = (bf16[2,1,384,256]{3,2,1,0:T(8,128)(2,1)}, bf16[2,1,384,256]{3,2,1,0:T(8,128)(2,1)S(1)}, u32[]{:S(2)}, u32[]{:S(2)}) collective-permute-start(bf16[2,1,384,256]{3,2,1,0:T(8,128)(2,1)} %pad_maximum_fusion.3), channel_id=1, source_target_pairs={{0,4},{4,8},{8,12},{1,5},{5,9},{9,13},{2,6},{6,10},{10,14},{3,7},{... | collective-permute-start | bytes 1179656 | tf_op jit(solution)/shard_map/ppermute | solution.py:21
  11.3 4.6 %collective-permute-start.2 = (bf16[2,1,384,256]{3,2,1,0:T(8,128)(2,1)}, bf16[2,1,384,256]{3,2,1,0:T(8,128)(2,1)S(1)}, u32[]{:S(2)}, u32[]{:S(2)}) collective-permute-start(bf16[2,1,384,256]{3,2,1,0:T(8,128)(2,1)} %pad_maximum_fusion.5), channel_id=1, source_target_pairs={{0,4},{4,8},{8,12},{1,5},{5,9},{9,13},{2,6},{6,10},{10,14},{3,7},{... | collective-permute-start | bytes 1179656 | tf_op jit(solution)/shard_map/ppermute | solution.py:21
  23.1 5.2 %collective-permute-start.4 = (bf16[2,1,384,256]{3,2,1,0:T(8,128)(2,1)}, bf16[2,1,384,256]{3,2,1,0:T(8,128)(2,1)S(1)}, u32[]{:S(2)}, u32[]{:S(2)}) collective-permute-start(bf16[2,1,384,256]{3,2,1,0:T(8,128)(2,1)} %pad_maximum_fusion.7), channel_id=1, source_target_pairs={{0,4},{4,8},{8,12},{1,5},{5,9},{9,13},{2,6},{6,10},{10,14},{3,7},{... | collective-permute-start | bytes 1179656 | tf_op jit(solution)/shard_map/ppermute | solution.py:21
  29.0 9.6 %shard_map.128 = (bf16[1,768,256]{2,1,0:T(8,128)(2,1)}, bf16[1,768,256]{2,1,0:T(8,128)(2,1)}, bf16[1,768,256]{2,1,0:T(8,128)(2,1)}, bf16[2,1,384,256]{3,2,1,0:T(8,128)(2,1)}, bf16[2,1,384,256]{3,2,1,0:T(8,128)(2,1)}) custom-call(f32[6]{0:T(128)} %and_select_fusion.bias_ref, bf16[1,768,768]{2,1,0:T(8,128)(2,1)} %q_ref.5, bf16[1,768,768]{2,1,0:T(8,128)(2,1)} %g_ref.5, ...), custom_call_target="tpu_custom_call" | custom-call | tf_op jit(solution)/shard_map/pallas_call | solution.py:168
  38.7 3.9 %collective-permute-start.6 = (bf16[2,1,384,256]{3,2,1,0:T(8,128)(2,1)}, bf16[2,1,384,256]{3,2,1,0:T(8,128)(2,1)S(1)}, u32[]{:S(2)}, u32[]{:S(2)}) collective-permute-start(bf16[2,1,384,256]{3,2,1,0:T(8,128)(2,1)} %get-tuple-element.24), channel_id=1, source_target_pairs={{0,4},{4,8},{8,12},{1,5},{5,9},{9,13},{2,6},{6,10},{10,14},{3,7},{... | collective-permute-start | bytes 1179656 | tf_op jit(solution)/shard_map/ppermute | solution.py:21
  43.9 2.1 %fusion.8 = f32[1,768,64]{1,2,0:T(8,128)} fusion(bf16[768,64]{0,1:T(8,128)(2,1)} %param.14, bf16[1,768,768]{2,1,0:T(8,128)(2,1)S(1)} %copy-done), kind=kOutput, calls=%fused_computation.11 | convolution fusion | flops 75497472 | bytes 1474560 | tf_op jit(solution)/shard_map/pqg,gv->pqv/dot_general | solution.py:192
  46.0 1.5 %collective-permute-start.12 = (f32[1,768,64]{1,2,0:T(8,128)}, f32[1,768,64]{1,2,0:T(8,128)}, u32[]{:S(2)}, u32[]{:S(2)}) collective-permute-start(f32[1,768,64]{1,2,0:T(8,128)} %fusion.8), channel_id=1, source_target_pairs={{0,2},{2,0},{1,3},{3,1},{4,6},{6,4},{5,7},{7,5},{8,10},{10,8},{9,1... | collective-permute-start | bytes 589832 | tf_op jit(solution)/shard_map/ppermute | solution.py:31
  47.5 9.6 %shard_map.129 = (bf16[1,768,256]{2,1,0:T(8,128)(2,1)}, bf16[1,768,256]{2,1,0:T(8,128)(2,1)}, bf16[1,768,256]{2,1,0:T(8,128)(2,1)}, bf16[2,1,384,256]{3,2,1,0:T(8,128)(2,1)}, bf16[2,1,384,256]{3,2,1,0:T(8,128)(2,1)}) custom-call(f32[6]{0:T(128)} %and_select_fusion.bias_ref, bf16[1,768,768]{2,1,0:T(8,128)(2,1)} %q_ref.5, bf16[1,768,768]{2,1,0:T(8,128)(2,1)} %g_ref.5, ...), custom_call_target="tpu_custom_call" | custom-call | tf_op jit(solution)/shard_map/pallas_call | solution.py:168
  57.1 4.6 %collective-permute-start.8 = (bf16[2,1,384,256]{3,2,1,0:T(8,128)(2,1)}, bf16[2,1,384,256]{3,2,1,0:T(8,128)(2,1)S(1)}, u32[]{:S(2)}, u32[]{:S(2)}) collective-permute-start(bf16[2,1,384,256]{3,2,1,0:T(8,128)(2,1)} %get-tuple-element.27), channel_id=1, source_target_pairs={{0,4},{4,8},{8,12},{1,5},{5,9},{9,13},{2,6},{6,10},{10,14},{3,7},{... | collective-permute-start | bytes 1179656 | tf_op jit(solution)/shard_map/ppermute | solution.py:21
  61.7 1.5 %collective-permute-start.9 = (bf16[2,1,384,256]{3,2,1,0:T(8,128)(2,1)}, bf16[2,1,384,256]{3,2,1,0:T(8,128)(2,1)}, u32[]{:S(2)}, u32[]{:S(2)}) collective-permute-start(bf16[2,1,384,256]{3,2,1,0:T(8,128)(2,1)} %get-tuple-element.28), channel_id=1, source_target_pairs={{4,0},{8,4},{12,8},{5,1},{9,5},{13,9},{6,2},{10,6},{14,10},{7,3},{... | collective-permute-start | bytes 1179656 | tf_op jit(solution)/shard_map/ppermute | solution.py:21
  63.2 9.6 %shard_map.130 = (bf16[1,768,256]{2,1,0:T(8,128)(2,1)}, bf16[1,768,256]{2,1,0:T(8,128)(2,1)}, bf16[1,768,256]{2,1,0:T(8,128)(2,1)}, bf16[2,1,384,256]{3,2,1,0:T(8,128)(2,1)}, bf16[2,1,384,256]{3,2,1,0:T(8,128)(2,1)}) custom-call(f32[6]{0:T(128)} %and_select_fusion.bias_ref, bf16[1,768,768]{2,1,0:T(8,128)(2,1)} %q_ref.5, bf16[1,768,768]{2,1,0:T(8,128)(2,1)} %g_ref.5, ...), custom_call_target="tpu_custom_call" | custom-call | tf_op jit(solution)/shard_map/pallas_call | solution.py:168
  72.9 4.6 %collective-permute-start.10 = (bf16[2,1,384,256]{3,2,1,0:T(8,128)(2,1)}, bf16[2,1,384,256]{3,2,1,0:T(8,128)(2,1)S(1)}, u32[]{:S(2)}, u32[]{:S(2)}) collective-permute-start(bf16[2,1,384,256]{3,2,1,0:T(8,128)(2,1)} %get-tuple-element.30), channel_id=1, source_target_pairs={{0,4},{4,8},{8,12},{1,5},{5,9},{9,13},{2,6},{6,10},{10,14},{3,7},{... | collective-permute-start | bytes 1179656 | tf_op jit(solution)/shard_map/ppermute | solution.py:21
  77.5 1.4 %collective-permute-start.11 = (bf16[2,1,384,256]{3,2,1,0:T(8,128)(2,1)}, bf16[2,1,384,256]{3,2,1,0:T(8,128)(2,1)S(1)}, u32[]{:S(2)}, u32[]{:S(2)}) collective-permute-start(bf16[2,1,384,256]{3,2,1,0:T(8,128)(2,1)} %get-tuple-element.31), channel_id=1, source_target_pairs={{4,0},{8,4},{12,8},{5,1},{9,5},{13,9},{6,2},{10,6},{14,10},{7,3},{... | collective-permute-start | bytes 1179656 | tf_op jit(solution)/shard_map/ppermute | solution.py:21
  80.8 2.3 %collective-permute-done.10 = bf16[2,1,384,256]{3,2,1,0:T(8,128)(2,1)S(1)} collective-permute-done((bf16[2,1,384,256]{3,2,1,0:T(8,128)(2,1)}, bf16[2,1,384,256]{3,2,1,0:T(8,128)(2,1)S(1)}, u32[]{:S(2)}, u32[]{:S(2)}) %collective-permute-start.10) | collective-permute-done | bytes 393248 | tf_op jit(solution)/shard_map/ppermute | solution.py:21
  83.0 4.5 %collective-permute-done.11 = bf16[2,1,384,256]{3,2,1,0:T(8,128)(2,1)S(1)} collective-permute-done((bf16[2,1,384,256]{3,2,1,0:T(8,128)(2,1)}, bf16[2,1,384,256]{3,2,1,0:T(8,128)(2,1)S(1)}, u32[]{:S(2)}, u32[]{:S(2)}) %collective-permute-start.11) | collective-permute-done | bytes 393248 | tf_op jit(solution)/shard_map/ppermute | solution.py:21
  90.0 1.4 %fusion.17 = f32[64,768]{1,0:T(8,128)S(1)} fusion(bf16[1,768,768]{2,1,0:T(8,128)(2,1)S(1)} %pad_maximum_fusion.2, f32[1,768,64]{1,2,0:T(8,128)} %fusion.8, f32[1,768,64]{1,2,0:T(8,128)} %collective-permute-done.12), kind=kOutput, calls=%fused_computation.14 | convolution fusion | flops 75644928 | bytes 1769472 | tf_op jit(solution)/shard_map/igb,igu->bu/dot_general | solution.py:240
  91.4 3.5 %collective-permute-done.13 = f32[1,768,64]{1,2,0:T(8,128)S(1)} collective-permute-done((f32[1,768,64]{1,2,0:T(8,128)S(1)}, f32[1,768,64]{1,2,0:T(8,128)S(1)}, u32[]{:S(2)}, u32[]{:S(2)}) %collective-permute-start.13) | collective-permute-done | bytes 196640 | tf_op jit(solution)/shard_map/ppermute | solution.py:31
  96.0 1.8 %collective-permute-done.14 = f32[49152]{0:T(1024)} collective-permute-done((f32[49152]{0:T(1024)}, f32[49152]{0:T(1024)}, u32[]{:S(2)}, u32[]{:S(2)}) %collective-permute-start.14) | collective-permute-done | bytes 196640 | tf_op jit(solution)/shard_map/ppermute | solution.py:45
  98.7 1.5 %collective-permute-start.15 = (f32[24576]{0:T(1024)S(1)}, f32[24576]{0:T(1024)S(1)}, u32[]{:S(2)}, u32[]{:S(2)}) collective-permute-start(f32[24576]{0:T(1024)S(1)} %slice_select_fusion), channel_id=1, source_target_pairs={{0,4},{4,0},{8,12},{12,8},{1,5},{5,1},{9,13},{13,9},{2,6},{6,2},{1... | collective-permute-start | bytes 294920 | tf_op jit(solution)/shard_map/ppermute | solution.py:45
  100.3 3.4 %collective-permute-done.15 = f32[24576]{0:T(1024)S(1)} collective-permute-done((f32[24576]{0:T(1024)S(1)}, f32[24576]{0:T(1024)S(1)}, u32[]{:S(2)}, u32[]{:S(2)}) %collective-permute-start.15) | collective-permute-done | bytes 98336 | tf_op jit(solution)/shard_map/ppermute | solution.py:45
  103.7 1.5 %collective-permute-start.16 = (f32[24576]{0:T(1024)S(1)}, f32[24576]{0:T(1024)S(1)}, u32[]{:S(2)}, u32[]{:S(2)}) collective-permute-start(f32[24576]{0:T(1024)S(1)} %select_add_fusion), channel_id=1, source_target_pairs={{0,8},{4,12},{8,0},{12,4},{1,9},{5,13},{9,1},{13,5},{2,10},{6,14},... | collective-permute-start | bytes 294920 | tf_op jit(solution)/shard_map/ppermute | solution.py:78
  105.2 5.5 %collective-permute-done.16 = f32[24576]{0:T(1024)S(1)} collective-permute-done((f32[24576]{0:T(1024)S(1)}, f32[24576]{0:T(1024)S(1)}, u32[]{:S(2)}, u32[]{:S(2)}) %collective-permute-start.16) | collective-permute-done | bytes 98336 | tf_op jit(solution)/shard_map/ppermute | solution.py:78
  112.0 3.4 %collective-permute-done.17 = f32[24576]{0:T(1024)S(1)} collective-permute-done((f32[24576]{0:T(1024)S(1)}, f32[24576]{0:T(1024)S(1)}, u32[]{:S(2)}, u32[]{:S(2)}) %collective-permute-start.17) | collective-permute-done | bytes 98336 | tf_op jit(solution)/shard_map/ppermute | solution.py:53
  (98 shorter events, 22.8 us)
Async XLA Ops:
  0.6 43.3 %copy-start = (bf16[1,768,768]{2,1,0:T(8,128)(2,1)S(1)}, bf16[1,768,768]{2,1,0:T(8,128)(2,1)}, u32[]{:S(2)}) copy-start(bf16[1,768,768]{2,1,0:T(8,128)(2,1)} %param.13) | copy-start | bytes 3538948
  3.4 19.6 %collective-permute-start = (bf16[2,1,384,256]{3,2,1,0:T(8,128)(2,1)}, bf16[2,1,384,256]{3,2,1,0:T(8,128)(2,1)S(1)}, u32[]{:S(2)}, u32[]{:S(2)}) collective-permute-start(bf16[2,1,384,256]{3,2,1,0:T(8,128)(2,1)} %pad_maximum_fusion.3), channel_id=1, source_target_pairs={{0,4},{4,8},{8,12},{1,5},{5,9},{9,13},{2,6},{6,10},{10,14},{3,7},{... | collective-permute-start | bytes 1179656 | tf_op jit(solution)/shard_map/ppermute | solution.py:21
  9.2 19.1 %collective-permute-start.1 = (bf16[2,1,384,256]{3,2,1,0:T(8,128)(2,1)}, bf16[2,1,384,256]{3,2,1,0:T(8,128)(2,1)S(1)}, u32[]{:S(2)}, u32[]{:S(2)}) collective-permute-start(bf16[2,1,384,256]{3,2,1,0:T(8,128)(2,1)} %pad_maximum_fusion.4), channel_id=1, source_target_pairs={{4,0},{8,4},{12,8},{5,1},{9,5},{13,9},{6,2},{10,6},{14,10},{7,3},{... | collective-permute-start | bytes 1179656 | tf_op jit(solution)/shard_map/ppermute | solution.py:21
  10.5 10.5 %copy-start.18 = (s32[8,3]{0,1:T(4,128)S(1)}, s32[8,3]{0,1:T(4,128)}, u32[]{:S(2)}) copy-start(s32[8,3]{0,1:T(4,128)} %param.16) | copy-start | bytes 292
  11.3 31.3 %collective-permute-start.2 = (bf16[2,1,384,256]{3,2,1,0:T(8,128)(2,1)}, bf16[2,1,384,256]{3,2,1,0:T(8,128)(2,1)S(1)}, u32[]{:S(2)}, u32[]{:S(2)}) collective-permute-start(bf16[2,1,384,256]{3,2,1,0:T(8,128)(2,1)} %pad_maximum_fusion.5), channel_id=1, source_target_pairs={{0,4},{4,8},{8,12},{1,5},{5,9},{9,13},{2,6},{6,10},{10,14},{3,7},{... | collective-permute-start | bytes 1179656 | tf_op jit(solution)/shard_map/ppermute | solution.py:21
  16.6 29.4 %collective-permute-start.3 = (bf16[2,1,384,256]{3,2,1,0:T(8,128)(2,1)}, bf16[2,1,384,256]{3,2,1,0:T(8,128)(2,1)S(1)}, u32[]{:S(2)}, u32[]{:S(2)}) collective-permute-start(bf16[2,1,384,256]{3,2,1,0:T(8,128)(2,1)} %pad_maximum_fusion.6), channel_id=1, source_target_pairs={{4,0},{8,4},{12,8},{5,1},{9,5},{13,9},{6,2},{10,6},{14,10},{7,3},{... | collective-permute-start | bytes 1179656 | tf_op jit(solution)/shard_map/ppermute | solution.py:21
  18.7 38.4 %collective-permute-start.5 = (bf16[2,1,384,256]{3,2,1,0:T(8,128)(2,1)}, bf16[2,1,384,256]{3,2,1,0:T(8,128)(2,1)S(1)}, u32[]{:S(2)}, u32[]{:S(2)}) collective-permute-start(bf16[2,1,384,256]{3,2,1,0:T(8,128)(2,1)} %pad_maximum_fusion.8), channel_id=1, source_target_pairs={{4,0},{8,4},{12,8},{5,1},{9,5},{13,9},{6,2},{10,6},{14,10},{7,3},{... | collective-permute-start | bytes 1179656 | tf_op jit(solution)/shard_map/ppermute | solution.py:21
  23.1 38.6 %collective-permute-start.4 = (bf16[2,1,384,256]{3,2,1,0:T(8,128)(2,1)}, bf16[2,1,384,256]{3,2,1,0:T(8,128)(2,1)S(1)}, u32[]{:S(2)}, u32[]{:S(2)}) collective-permute-start(bf16[2,1,384,256]{3,2,1,0:T(8,128)(2,1)} %pad_maximum_fusion.7), channel_id=1, source_target_pairs={{0,4},{4,8},{8,12},{1,5},{5,9},{9,13},{2,6},{6,10},{10,14},{3,7},{... | collective-permute-start | bytes 1179656 | tf_op jit(solution)/shard_map/ppermute | solution.py:21
  38.7 34.2 %collective-permute-start.6 = (bf16[2,1,384,256]{3,2,1,0:T(8,128)(2,1)}, bf16[2,1,384,256]{3,2,1,0:T(8,128)(2,1)S(1)}, u32[]{:S(2)}, u32[]{:S(2)}) collective-permute-start(bf16[2,1,384,256]{3,2,1,0:T(8,128)(2,1)} %get-tuple-element.24), channel_id=1, source_target_pairs={{0,4},{4,8},{8,12},{1,5},{5,9},{9,13},{2,6},{6,10},{10,14},{3,7},{... | collective-permute-start | bytes 1179656 | tf_op jit(solution)/shard_map/ppermute | solution.py:21
  42.6 34.9 %collective-permute-start.7 = (bf16[2,1,384,256]{3,2,1,0:T(8,128)(2,1)}, bf16[2,1,384,256]{3,2,1,0:T(8,128)(2,1)S(1)}, u32[]{:S(2)}, u32[]{:S(2)}) collective-permute-start(bf16[2,1,384,256]{3,2,1,0:T(8,128)(2,1)} %get-tuple-element.25), channel_id=1, source_target_pairs={{4,0},{8,4},{12,8},{5,1},{9,5},{13,9},{6,2},{10,6},{14,10},{7,3},{... | collective-permute-start | bytes 1179656 | tf_op jit(solution)/shard_map/ppermute | solution.py:21
  46.0 44.0 %collective-permute-start.12 = (f32[1,768,64]{1,2,0:T(8,128)}, f32[1,768,64]{1,2,0:T(8,128)}, u32[]{:S(2)}, u32[]{:S(2)}) collective-permute-start(f32[1,768,64]{1,2,0:T(8,128)} %fusion.8), channel_id=1, source_target_pairs={{0,2},{2,0},{1,3},{3,1},{4,6},{6,4},{5,7},{7,5},{8,10},{10,8},{9,1... | collective-permute-start | bytes 589832 | tf_op jit(solution)/shard_map/ppermute | solution.py:31
  57.1 22.2 %collective-permute-start.8 = (bf16[2,1,384,256]{3,2,1,0:T(8,128)(2,1)}, bf16[2,1,384,256]{3,2,1,0:T(8,128)(2,1)S(1)}, u32[]{:S(2)}, u32[]{:S(2)}) collective-permute-start(bf16[2,1,384,256]{3,2,1,0:T(8,128)(2,1)} %get-tuple-element.27), channel_id=1, source_target_pairs={{0,4},{4,8},{8,12},{1,5},{5,9},{9,13},{2,6},{6,10},{10,14},{3,7},{... | collective-permute-start | bytes 1179656 | tf_op jit(solution)/shard_map/ppermute | solution.py:21
  61.7 17.6 %collective-permute-start.9 = (bf16[2,1,384,256]{3,2,1,0:T(8,128)(2,1)}, bf16[2,1,384,256]{3,2,1,0:T(8,128)(2,1)}, u32[]{:S(2)}, u32[]{:S(2)}) collective-permute-start(bf16[2,1,384,256]{3,2,1,0:T(8,128)(2,1)} %get-tuple-element.28), channel_id=1, source_target_pairs={{4,0},{8,4},{12,8},{5,1},{9,5},{13,9},{6,2},{10,6},{14,10},{7,3},{... | collective-permute-start | bytes 1179656 | tf_op jit(solution)/shard_map/ppermute | solution.py:21
  72.9 10.2 %collective-permute-start.10 = (bf16[2,1,384,256]{3,2,1,0:T(8,128)(2,1)}, bf16[2,1,384,256]{3,2,1,0:T(8,128)(2,1)S(1)}, u32[]{:S(2)}, u32[]{:S(2)}) collective-permute-start(bf16[2,1,384,256]{3,2,1,0:T(8,128)(2,1)} %get-tuple-element.30), channel_id=1, source_target_pairs={{0,4},{4,8},{8,12},{1,5},{5,9},{9,13},{2,6},{6,10},{10,14},{3,7},{... | collective-permute-start | bytes 1179656 | tf_op jit(solution)/shard_map/ppermute | solution.py:21
  77.5 10.0 %collective-permute-start.11 = (bf16[2,1,384,256]{3,2,1,0:T(8,128)(2,1)}, bf16[2,1,384,256]{3,2,1,0:T(8,128)(2,1)S(1)}, u32[]{:S(2)}, u32[]{:S(2)}) collective-permute-start(bf16[2,1,384,256]{3,2,1,0:T(8,128)(2,1)} %get-tuple-element.31), channel_id=1, source_target_pairs={{4,0},{8,4},{12,8},{5,1},{9,5},{13,9},{6,2},{10,6},{14,10},{7,3},{... | collective-permute-start | bytes 1179656 | tf_op jit(solution)/shard_map/ppermute | solution.py:21
  89.2 5.7 %collective-permute-start.13 = (f32[1,768,64]{1,2,0:T(8,128)S(1)}, f32[1,768,64]{1,2,0:T(8,128)S(1)}, u32[]{:S(2)}, u32[]{:S(2)}) collective-permute-start(f32[1,768,64]{1,2,0:T(8,128)S(1)} %fusion.11), channel_id=1, source_target_pairs={{0,2},{2,0},{1,3},{3,1},{4,6},{6,4},{5,7},{7,5},{8,10},{10,8},{9,1... | collective-permute-start | bytes 589832 | tf_op jit(solution)/shard_map/ppermute | solution.py:31
  95.3 15.6 %copy-start.2 = (bf16[1,768,256]{2,1,0:T(8,128)(2,1)S(1)}, bf16[1,768,256]{2,1,0:T(8,128)(2,1)}, u32[]{:S(2)}) copy-start(bf16[1,768,256]{2,1,0:T(8,128)(2,1)} %get-tuple-element.20) | copy-start | bytes 1179652
  95.3 15.6 %copy-start.3 = (bf16[1,768,256]{2,1,0:T(8,128)(2,1)S(1)}, bf16[1,768,256]{2,1,0:T(8,128)(2,1)}, u32[]{:S(2)}) copy-start(bf16[1,768,256]{2,1,0:T(8,128)(2,1)} %get-tuple-element.21) | copy-start | bytes 1179652
  96.0 1.8 %collective-permute-start.14 = (f32[49152]{0:T(1024)}, f32[49152]{0:T(1024)}, u32[]{:S(2)}, u32[]{:S(2)}) collective-permute-start(f32[49152]{0:T(1024)} %select_n.63), channel_id=1, source_target_pairs={{0,1},{1,0},{2,3},{3,2},{4,5},{5,4},{6,7},{7,6},{8,9},{9,8},{10,11... | collective-permute-start | bytes 589832 | tf_op jit(solution)/shard_map/ppermute | solution.py:45
  96.0 14.9 %copy-start.4 = (bf16[1,768,256]{2,1,0:T(8,128)(2,1)S(1)}, bf16[1,768,256]{2,1,0:T(8,128)(2,1)}, u32[]{:S(2)}) copy-start(bf16[1,768,256]{2,1,0:T(8,128)(2,1)} %get-tuple-element.22) | copy-start | bytes 1179652
  98.7 4.9 %collective-permute-start.15 = (f32[24576]{0:T(1024)S(1)}, f32[24576]{0:T(1024)S(1)}, u32[]{:S(2)}, u32[]{:S(2)}) collective-permute-start(f32[24576]{0:T(1024)S(1)} %slice_select_fusion), channel_id=1, source_target_pairs={{0,4},{4,0},{8,12},{12,8},{1,5},{5,1},{9,13},{13,9},{2,6},{6,2},{1... | collective-permute-start | bytes 294920 | tf_op jit(solution)/shard_map/ppermute | solution.py:45
  103.7 7.1 %collective-permute-start.16 = (f32[24576]{0:T(1024)S(1)}, f32[24576]{0:T(1024)S(1)}, u32[]{:S(2)}, u32[]{:S(2)}) collective-permute-start(f32[24576]{0:T(1024)S(1)} %select_add_fusion), channel_id=1, source_target_pairs={{0,8},{4,12},{8,0},{12,4},{1,9},{5,13},{9,1},{13,5},{2,10},{6,14},... | collective-permute-start | bytes 294920 | tf_op jit(solution)/shard_map/ppermute | solution.py:78
  110.8 4.7 %collective-permute-start.17 = (f32[24576]{0:T(1024)S(1)}, f32[24576]{0:T(1024)S(1)}, u32[]{:S(2)}, u32[]{:S(2)}) collective-permute-start(f32[24576]{0:T(1024)S(1)} %add.54), channel_id=1, source_target_pairs={{0,4},{4,0},{8,12},{12,8},{1,5},{5,1},{9,13},{13,9},{2,6},{6,2},{1... | collective-permute-start | bytes 294920 | tf_op jit(solution)/shard_map/ppermute | solution.py:53
  115.5 1.5 %collective-permute-start.18 = (f32[49152]{0:T(1024)S(1)}, f32[49152]{0:T(1024)S(1)}, u32[]{:S(2)}, u32[]{:S(2)}) collective-permute-start(f32[49152]{0:T(1024)S(1)} %maximum_select_fusion.1), channel_id=1, source_target_pairs={{0,1},{1,0},{2,3},{3,2},{4,5},{5,4},{6,7},{7,6},{8,9},{9,8},{10,11... | collective-permute-start | bytes 589832 | tf_op jit(solution)/shard_map/ppermute | solution.py:53
  (15 other events, 52.6 us)

commit v16 on v12

--- a/solution.py
+++ b/solution.py
@@ -206,7 +206,10 @@
     local_heads = queries.shape[2] // HEAD_SIZE
     chunks = 2 if local_heads % 2 == 0 else 1
     per_chunk = local_heads // chunks
-    outs = []
+    def project(term, up_cols):
+        return jnp.einsum("dsi,ji->dsj", term, up_cols, preferred_element_type=jnp.float32)
+
+    outs, pieces = [], []
     for chunk in range(chunks):
         cols = slice(chunk * per_chunk * HEAD_SIZE, (chunk + 1) * per_chunk * HEAD_SIZE)
         left_kv = shifted(
@@ -225,15 +228,26 @@
         arrived = jnp.concatenate((from_left, from_right), 2).astype(jnp.float32)
         dk = (dk_own.astype(jnp.float32) + arrived[0]).astype(jnp.bfloat16)
         dv = (dv_own.astype(jnp.float32) + arrived[1]).astype(jnp.bfloat16)
+        up_cols = adapter_up_weight[:, cols]
+        if chunk < chunks - 1:
+            pieces.append(project(dv, up_cols))
+        else:
+            pieces.append(project(dv_own, up_cols))
+            sent = butterfly_sum(
+                jnp.stack((project(to_left[1], up_cols), project(to_right[1], up_cols))), "head"
+            )
+            late = jnp.concatenate(
+                (shifted(sent[1], "seq", 1), shifted(sent[0], "seq", -1)), 1
+            )
         outs.append((dq, dk, dv))
     query_grad, key_grad, value_gradient = (
         jnp.concatenate([o[i] for o in outs], 2) for i in range(3)
     )
 
-    backward_piece = jnp.einsum(
-        "dsi,ji->dsj", value_gradient, adapter_up_weight, preferred_element_type=jnp.float32
-    )
-    backward_rows = butterfly_sum(backward_piece, "head").astype(jnp.bfloat16)
+    backward_piece = pieces[0]
+    for piece in pieces[1:]:
+        backward_piece = backward_piece + piece
+    backward_rows = (butterfly_sum(backward_piece, "head") + late).astype(jnp.bfloat16)
     gradient_down_local = adapter_scale * jnp.einsum(
         "yhm,yhz->mz", normed, backward_rows, preferred_element_type=jnp.float32
     )

time: 112 us -> 113 us (level)
  starting transfers between devices: 28.9 us -> 40.1 us
  waiting for transfers between devices: 32.4 us -> 25.9 us
  local copies, waits for them, and re-layouts: 7.82 us -> 4.67 us
    ppermute x8 -> x10, starting transfers between devices: 24.3 us -> 29.8 us  [shifted(): return lax.ppermute(shard, axis, pairs)]
    ppermute x8 -> x10, waiting for transfers between devices: 13.6 us -> 8.29 us  [shifted(): return lax.ppermute(shard, axis, pairs)]
    unnamed x30 -> x32, local copies, waits for them, and re-layouts: 4.85 us -> 1.69 us
    dot_general x1 -> x4, matrix products: 0.48 us -> 3.01 us  [project(): jnp.einsum('dsi,ji->dsj', term, up_cols, preferred_element_type=jnp.float32)]
    ppermute x1, starting transfers between devices: 0.55 us -> 2.73 us  [all_sum(): lax.ppermute(flat, axis, [(i, i ^ step) for i in range(lax.axis_size(axis...]
    ppermute x2, starting transfers between devices: 0.84 us -> 2.78 us  [scatter_sum(): lax.ppermute(send, axis, [(i, i ^ step) for i in range(peers)])]
    ppermute x1, waiting for transfers between devices: 6.53 us -> 4.67 us  [all_sum(): lax.ppermute(flat, axis, [(i, i ^ step) for i in range(lax.axis_size(axis...]
    ppermute x2 -> x3, waiting for transfers between devices: 2.82 us -> 4.57 us  [butterfly_sum(): other = lax.ppermute(tree, axis, pairs)]
  transfers between devices with their start and end apart: 15 -> 18, of which waited for: 10 -> 11; matrix products, arithmetic and copies ran while one was open for 12% -> 11% of each run, Pallas kernels for 24% -> 24%
where the time goes in v16:
time: 113 us
  starting transfers between devices  40.1 us (35%)
  Pallas kernels  26.9 us (24%)
  waiting for transfers between devices  25.9 us (23%)
  other arithmetic  9.82 us (9%)
  local copies, waits for them, and re-layouts  4.67 us (4%)
  matrix products  4.16 us (4%)
    ppermute x10, starting transfers between devices, shifted(): return lax.ppermute(shard, axis, pairs)  29.8 us
    pallas_call x2, Pallas kernels, attention_backward(): pl.pallas_call(attention_kernel, grid=(clip_count, heads), in_specs=[pl.B...  26.9 us
    ppermute x10, waiting for transfers between devices, shifted(): return lax.ppermute(shard, axis, pairs)  8.29 us
    ppermute x1, waiting for transfers between devices, all_sum(): lax.ppermute(flat, axis, [(i, i ^ step) for i in range(lax.axis_size(axis...  4.67 us
    ppermute x2, waiting for transfers between devices, scatter_sum(): lax.ppermute(send, axis, [(i, i ^ step) for i in range(peers)])  4.62 us
    ppermute x3, starting transfers between devices, butterfly_sum(): other = lax.ppermute(tree, axis, pairs)  4.6 us
    ppermute x3, waiting for transfers between devices, butterfly_sum(): other = lax.ppermute(tree, axis, pairs)  4.57 us
    ppermute x2, waiting for transfers between devices, gather_back(): other = lax.ppermute(flat, axis, [(i, i ^ step) for i in range(peers)])  3.72 us
  transfers between devices with their start and end apart: 18, of which 11 were waited for; matrix products, arithmetic and copies ran while one was open for 11% of the time, Pallas kernels for 24%

profile of v16, /device:TPU:0, one launch (start us, length us, event | category | flops | bytes accessed | tf_op | source)
XLA Modules:
  0.0 112.6 jit_solution(15159103926634328714)
XLA Ops:
  0.6 1.9 %slice_bitcast_fusion.8 = (bf16[1,1,384,384]{3,2,1,0:T(8,128)(2,1)S(1)}, bf16[1,1,384,384]{3,2,1,0:T(8,128)(2,1)S(1)}, bf16[1,1,384,384]{3,2,1,0:T(8,128)(2,1)S(...) fusion(bf16[1,768,768]{2,1,0:T(8,128)(2,1)} %v_ref.3, ...), kind=kLoop, calls=%fused_computation.47 | loop fusion | bytes 4718592 | tf_op jit(solution)/shard_map/stack | solution.py:221
  3.5 5.0 %collective-permute-start = (bf16[2,1,384,384]{3,2,1,0:T(8,128)(2,1)}, bf16[2,1,384,384]{3,2,1,0:T(8,128)(2,1)S(1)}, u32[]{:S(2)}, u32[]{:S(2)}) collective-permute-start(bf16[2,1,384,384]{3,2,1,0:T(8,128)(2,1)} %pad_maximum_fusion.3), channel_id=1, source_target_pairs={{0,4},{4,8},{8,12},{1,5},{5,9},{9,13},{2,6},{6,10},{10,14},{3,7},{... | collective-permute-start | bytes 1769480 | tf_op jit(solution)/shard_map/ppermute | solution.py:21
  9.3 1.3 %collective-permute-start.1 = (bf16[2,1,384,384]{3,2,1,0:T(8,128)(2,1)}, bf16[2,1,384,384]{3,2,1,0:T(8,128)(2,1)}, u32[]{:S(2)}, u32[]{:S(2)}) collective-permute-start(bf16[2,1,384,384]{3,2,1,0:T(8,128)(2,1)} %pad_maximum_fusion.4), channel_id=1, source_target_pairs={{4,0},{8,4},{12,8},{5,1},{9,5},{13,9},{6,2},{10,6},{14,10},{7,3},{... | collective-permute-start | bytes 1769480 | tf_op jit(solution)/shard_map/ppermute | solution.py:21
  13.7 5.2 %collective-permute-start.2 = (bf16[2,1,384,384]{3,2,1,0:T(8,128)(2,1)}, bf16[2,1,384,384]{3,2,1,0:T(8,128)(2,1)S(1)}, u32[]{:S(2)}, u32[]{:S(2)}) collective-permute-start(bf16[2,1,384,384]{3,2,1,0:T(8,128)(2,1)} %pad_maximum_fusion.5), channel_id=1, source_target_pairs={{0,4},{4,8},{8,12},{1,5},{5,9},{9,13},{2,6},{6,10},{10,14},{3,7},{... | collective-permute-start | bytes 1769480 | tf_op jit(solution)/shard_map/ppermute | solution.py:21
  19.4 1.5 %collective-permute-start.8 = (f32[1,768,64]{1,2,0:T(8,128)S(1)}, f32[1,768,64]{1,2,0:T(8,128)S(1)}, u32[]{:S(2)}, u32[]{:S(2)}) collective-permute-start(f32[1,768,64]{1,2,0:T(8,128)S(1)} %fusion.14), channel_id=1, source_target_pairs={{0,2},{2,0},{1,3},{3,1},{4,6},{6,4},{5,7},{7,5},{8,10},{10,8},{9,1... | collective-permute-start | bytes 589832 | tf_op jit(solution)/shard_map/ppermute | solution.py:31
  22.4 5.3 %collective-permute-done.1.right_ref = bf16[2,1,384,384]{3,2,1,0:T(8,128)(2,1)} collective-permute-done((bf16[2,1,384,384]{3,2,1,0:T(8,128)(2,1)}, bf16[2,1,384,384]{3,2,1,0:T(8,128)(2,1)}, u32[]{:S(2)}, u32[]{:S(2)}) %collective-permute-start.1) | collective-permute-done | bytes 589856 | tf_op jit(solution)/shard_map/ppermute | solution.py:21
  27.8 13.4 %shard_map.128 = (bf16[1,768,384]{2,1,0:T(8,128)(2,1)}, bf16[1,768,384]{2,1,0:T(8,128)(2,1)}, bf16[1,768,384]{2,1,0:T(8,128)(2,1)}, bf16[2,1,384,384]{3,2,1,0:T(8,128)(2,1)}, bf16[2,1,384,384]{3,2,1,0:T(8,128)(2,1)}) custom-call(f32[6]{0:T(128)} %and_select_fusion.bias_ref, bf16[1,768,768]{2,1,0:T(8,128)(2,1)} %q_ref.3, bf16[1,768,768]{2,1,0:T(8,128)(2,1)} %g_ref.3, ...), custom_call_target="tpu_custom_call" | custom-call | tf_op jit(solution)/shard_map/pallas_call | solution.py:168
  41.2 3.5 %collective-permute-start.4 = (bf16[2,1,384,384]{3,2,1,0:T(8,128)(2,1)}, bf16[2,1,384,384]{3,2,1,0:T(8,128)(2,1)S(1)}, u32[]{:S(2)}, u32[]{:S(2)}) collective-permute-start(bf16[2,1,384,384]{3,2,1,0:T(8,128)(2,1)} %get-tuple-element.18), channel_id=1, source_target_pairs={{0,4},{4,8},{8,12},{1,5},{5,9},{9,13},{2,6},{6,10},{10,14},{3,7},{... | collective-permute-start | bytes 1769480 | tf_op jit(solution)/shard_map/ppermute | solution.py:21
  44.7 1.4 %collective-permute-start.5 = (bf16[2,1,384,384]{3,2,1,0:T(8,128)(2,1)}, bf16[2,1,384,384]{3,2,1,0:T(8,128)(2,1)}, u32[]{:S(2)}, u32[]{:S(2)}) collective-permute-start(bf16[2,1,384,384]{3,2,1,0:T(8,128)(2,1)} %get-tuple-element.19), channel_id=1, source_target_pairs={{4,0},{8,4},{12,8},{5,1},{9,5},{13,9},{6,2},{10,6},{14,10},{7,3},{... | collective-permute-start | bytes 1769480 | tf_op jit(solution)/shard_map/ppermute | solution.py:21
  47.8 13.4 %shard_map.129 = (bf16[1,768,384]{2,1,0:T(8,128)(2,1)}, bf16[1,768,384]{2,1,0:T(8,128)(2,1)}, bf16[1,768,384]{2,1,0:T(8,128)(2,1)}, bf16[2,1,384,384]{3,2,1,0:T(8,128)(2,1)}, bf16[2,1,384,384]{3,2,1,0:T(8,128)(2,1)}) custom-call(f32[6]{0:T(128)} %and_select_fusion.bias_ref, bf16[1,768,768]{2,1,0:T(8,128)(2,1)} %q_ref.3, bf16[1,768,768]{2,1,0:T(8,128)(2,1)} %g_ref.3, ...), custom_call_target="tpu_custom_call" | custom-call | tf_op jit(solution)/shard_map/pallas_call | solution.py:168
  61.2 4.7 %collective-permute-start.6 = (bf16[2,1,384,384]{3,2,1,0:T(8,128)(2,1)}, bf16[2,1,384,384]{3,2,1,0:T(8,128)(2,1)S(1)}, u32[]{:S(2)}, u32[]{:S(2)}) collective-permute-start(bf16[2,1,384,384]{3,2,1,0:T(8,128)(2,1)} %get-tuple-element.21), channel_id=1, source_target_pairs={{0,4},{4,8},{8,12},{1,5},{5,9},{9,13},{2,6},{6,10},{10,14},{3,7},{... | collective-permute-start | bytes 1769480 | tf_op jit(solution)/shard_map/ppermute | solution.py:21
  68.4 1.5 %collective-permute-start.10 = (f32[2,1,384,64]{2,3,1,0:T(8,128)S(1)}, f32[2,1,384,64]{2,3,1,0:T(8,128)S(1)}, u32[]{:S(2)}, u32[]{:S(2)}) collective-permute-start(f32[2,1,384,64]{2,3,1,0:T(8,128)S(1)} %pad_maximum_fusion.7), channel_id=1, source_target_pairs={{0,2},{2,0},{1,3},{3,1},{4,6},{6,4},{5,7},{7,5},{8,10},{10,8},{9,1... | collective-permute-start | bytes 589832 | tf_op jit(solution)/shard_map/ppermute | solution.py:31
  70.2 3.9 %collective-permute-done.10 = f32[2,1,384,64]{2,3,1,0:T(8,128)S(1)} collective-permute-done((f32[2,1,384,64]{2,3,1,0:T(8,128)S(1)}, f32[2,1,384,64]{2,3,1,0:T(8,128)S(1)}, u32[]{:S(2)}, u32[]{:S(2)}) %collective-permute-start.10) | collective-permute-done | bytes 196640 | tf_op jit(solution)/shard_map/ppermute | solution.py:31
  74.1 1.3 %collective-permute-start.7 = (bf16[2,1,384,384]{3,2,1,0:T(8,128)(2,1)S(1)}, bf16[2,1,384,384]{3,2,1,0:T(8,128)(2,1)S(1)}, u32[]{:S(2)}, u32[]{:S(2)}) collective-permute-start(bf16[2,1,384,384]{3,2,1,0:T(8,128)(2,1)S(1)} %copy-done.12), channel_id=1, source_target_pairs={{4,0},{8,4},{12,8},{5,1},{9,5},{13,9},{6,2},{10,6},{14,10},{7,3},{... | collective-permute-start | bytes 1769480 | tf_op jit(solution)/shard_map/ppermute | solution.py:21
  75.5 4.6 %collective-permute-start.11 = (f32[1,384,64]{1,2,0:T(8,128)S(1)}, f32[1,384,64]{1,2,0:T(8,128)S(1)}, u32[]{:S(2)}, u32[]{:S(2)}) collective-permute-start(f32[1,384,64]{1,2,0:T(8,128)S(1)} %get-tuple-element.41), channel_id=1, source_target_pairs={{0,4},{4,8},{8,12},{1,5},{5,9},{9,13},{2,6},{6,10},{10,14},{3,7},{... | collective-permute-start | bytes 294920 | tf_op jit(solution)/shard_map/ppermute | solution.py:21
  80.0 1.6 %collective-permute-start.12 = (f32[1,384,64]{1,2,0:T(8,128)S(1)}, f32[1,384,64]{1,2,0:T(8,128)S(1)}, u32[]{:S(2)}, u32[]{:S(2)}) collective-permute-start(f32[1,384,64]{1,2,0:T(8,128)S(1)} %get-tuple-element.42), channel_id=1, source_target_pairs={{4,0},{8,4},{12,8},{5,1},{9,5},{13,9},{6,2},{10,6},{14,10},{7,3},{... | collective-permute-start | bytes 294920 | tf_op jit(solution)/shard_map/ppermute | solution.py:21
  83.5 1.5 %collective-permute-start.9 = (f32[1,768,64]{1,2,0:T(8,128)S(1)}, f32[1,768,64]{1,2,0:T(8,128)S(1)}, u32[]{:S(2)}, u32[]{:S(2)}) collective-permute-start(f32[1,768,64]{1,2,0:T(8,128)S(1)} %fusion.30), channel_id=1, source_target_pairs={{0,2},{2,0},{1,3},{3,1},{4,6},{6,4},{5,7},{7,5},{8,10},{10,8},{9,1... | collective-permute-start | bytes 589832 | tf_op jit(solution)/shard_map/ppermute | solution.py:31
  85.1 2.5 %collective-permute-done.7 = bf16[2,1,384,384]{3,2,1,0:T(8,128)(2,1)S(1)} collective-permute-done((bf16[2,1,384,384]{3,2,1,0:T(8,128)(2,1)S(1)}, bf16[2,1,384,384]{3,2,1,0:T(8,128)(2,1)S(1)}, u32[]{:S(2)}, u32[]{:S(2)}) %collective-permute-start.7) | collective-permute-done | bytes 589856 | tf_op jit(solution)/shard_map/ppermute | solution.py:21
  89.8 1.5 %collective-permute-done.13 = f32[49152]{0:T(1024)} collective-permute-done((f32[49152]{0:T(1024)S(1)}, f32[49152]{0:T(1024)}, u32[]{:S(2)}, u32[]{:S(2)}) %collective-permute-start.13) | collective-permute-done | bytes 196640 | tf_op jit(solution)/shard_map/ppermute | solution.py:45
  92.3 2.7 %collective-permute-start.14 = (f32[24576]{0:T(1024)S(1)}, f32[24576]{0:T(1024)S(1)}, u32[]{:S(2)}, u32[]{:S(2)}) collective-permute-start(f32[24576]{0:T(1024)S(1)} %slice_select_fusion), channel_id=1, source_target_pairs={{0,4},{4,0},{8,12},{12,8},{1,5},{5,1},{9,13},{13,9},{2,6},{6,2},{1... | collective-permute-start | bytes 294920 | tf_op jit(solution)/shard_map/ppermute | solution.py:45
  95.0 3.1 %collective-permute-done.14 = f32[24576]{0:T(1024)S(1)} collective-permute-done((f32[24576]{0:T(1024)S(1)}, f32[24576]{0:T(1024)S(1)}, u32[]{:S(2)}, u32[]{:S(2)}) %collective-permute-start.14) | collective-permute-done | bytes 98336 | tf_op jit(solution)/shard_map/ppermute | solution.py:45
  98.1 2.7 %collective-permute-start.15 = (f32[24576]{0:T(1024)S(1)}, f32[24576]{0:T(1024)S(1)}, u32[]{:S(2)}, u32[]{:S(2)}) collective-permute-start(f32[24576]{0:T(1024)S(1)} %select_add_fusion), channel_id=1, source_target_pairs={{0,8},{4,12},{8,0},{12,4},{1,9},{5,13},{9,1},{13,5},{2,10},{6,14},... | collective-permute-start | bytes 294920 | tf_op jit(solution)/shard_map/ppermute | solution.py:78
  100.8 4.7 %collective-permute-done.15 = f32[24576]{0:T(1024)S(1)} collective-permute-done((f32[24576]{0:T(1024)S(1)}, f32[24576]{0:T(1024)S(1)}, u32[]{:S(2)}, u32[]{:S(2)}) %collective-permute-start.15) | collective-permute-done | bytes 98336 | tf_op jit(solution)/shard_map/ppermute | solution.py:78
  106.7 3.5 %collective-permute-done.16 = f32[24576]{0:T(1024)S(1)} collective-permute-done((f32[24576]{0:T(1024)S(1)}, f32[24576]{0:T(1024)S(1)}, u32[]{:S(2)}, u32[]{:S(2)}) %collective-permute-start.16) | collective-permute-done | bytes 98336 | tf_op jit(solution)/shard_map/ppermute | solution.py:53
  (89 shorter events, 19.7 us)
Async XLA Ops:
  0.6 18.3 %copy-start = (bf16[1,768,768]{2,1,0:T(8,128)(2,1)S(1)}, bf16[1,768,768]{2,1,0:T(8,128)(2,1)}, u32[]{:S(2)}) copy-start(bf16[1,768,768]{2,1,0:T(8,128)(2,1)} %param.13) | copy-start | bytes 3538948
  3.5 19.0 %collective-permute-start = (bf16[2,1,384,384]{3,2,1,0:T(8,128)(2,1)}, bf16[2,1,384,384]{3,2,1,0:T(8,128)(2,1)S(1)}, u32[]{:S(2)}, u32[]{:S(2)}) collective-permute-start(bf16[2,1,384,384]{3,2,1,0:T(8,128)(2,1)} %pad_maximum_fusion.3), channel_id=1, source_target_pairs={{0,4},{4,8},{8,12},{1,5},{5,9},{9,13},{2,6},{6,10},{10,14},{3,7},{... | collective-permute-start | bytes 1769480 | tf_op jit(solution)/shard_map/ppermute | solution.py:21
  9.3 18.5 %collective-permute-start.1 = (bf16[2,1,384,384]{3,2,1,0:T(8,128)(2,1)}, bf16[2,1,384,384]{3,2,1,0:T(8,128)(2,1)}, u32[]{:S(2)}, u32[]{:S(2)}) collective-permute-start(bf16[2,1,384,384]{3,2,1,0:T(8,128)(2,1)} %pad_maximum_fusion.4), channel_id=1, source_target_pairs={{4,0},{8,4},{12,8},{5,1},{9,5},{13,9},{6,2},{10,6},{14,10},{7,3},{... | collective-permute-start | bytes 1769480 | tf_op jit(solution)/shard_map/ppermute | solution.py:21
  11.5 34.7 %collective-permute-start.3 = (bf16[2,1,384,384]{3,2,1,0:T(8,128)(2,1)}, bf16[2,1,384,384]{3,2,1,0:T(8,128)(2,1)S(1)}, u32[]{:S(2)}, u32[]{:S(2)}) collective-permute-start(bf16[2,1,384,384]{3,2,1,0:T(8,128)(2,1)} %pad_maximum_fusion.6), channel_id=1, source_target_pairs={{4,0},{8,4},{12,8},{5,1},{9,5},{13,9},{6,2},{10,6},{14,10},{7,3},{... | collective-permute-start | bytes 1769480 | tf_op jit(solution)/shard_map/ppermute | solution.py:21
  13.7 32.5 %collective-permute-start.2 = (bf16[2,1,384,384]{3,2,1,0:T(8,128)(2,1)}, bf16[2,1,384,384]{3,2,1,0:T(8,128)(2,1)S(1)}, u32[]{:S(2)}, u32[]{:S(2)}) collective-permute-start(bf16[2,1,384,384]{3,2,1,0:T(8,128)(2,1)} %pad_maximum_fusion.5), channel_id=1, source_target_pairs={{0,4},{4,8},{8,12},{1,5},{5,9},{9,13},{2,6},{6,10},{10,14},{3,7},{... | collective-permute-start | bytes 1769480 | tf_op jit(solution)/shard_map/ppermute | solution.py:21
  19.4 68.7 %collective-permute-start.8 = (f32[1,768,64]{1,2,0:T(8,128)S(1)}, f32[1,768,64]{1,2,0:T(8,128)S(1)}, u32[]{:S(2)}, u32[]{:S(2)}) collective-permute-start(f32[1,768,64]{1,2,0:T(8,128)S(1)} %fusion.14), channel_id=1, source_target_pairs={{0,2},{2,0},{1,3},{3,1},{4,6},{6,4},{5,7},{7,5},{8,10},{10,8},{9,1... | collective-permute-start | bytes 589832 | tf_op jit(solution)/shard_map/ppermute | solution.py:31
  41.2 34.3 %collective-permute-start.4 = (bf16[2,1,384,384]{3,2,1,0:T(8,128)(2,1)}, bf16[2,1,384,384]{3,2,1,0:T(8,128)(2,1)S(1)}, u32[]{:S(2)}, u32[]{:S(2)}) collective-permute-start(bf16[2,1,384,384]{3,2,1,0:T(8,128)(2,1)} %get-tuple-element.18), channel_id=1, source_target_pairs={{0,4},{4,8},{8,12},{1,5},{5,9},{9,13},{2,6},{6,10},{10,14},{3,7},{... | collective-permute-start | bytes 1769480 | tf_op jit(solution)/shard_map/ppermute | solution.py:21
  44.7 21.3 %copy-start.11 = (bf16[64,768]{1,0:T(8,128)(2,1)S(1)}, bf16[64,768]{1,0:T(8,128)(2,1)}, u32[]{:S(2)}) copy-start(bf16[64,768]{1,0:T(8,128)(2,1)} %param.15) | copy-start | bytes 294916
  44.7 35.3 %collective-permute-start.5 = (bf16[2,1,384,384]{3,2,1,0:T(8,128)(2,1)}, bf16[2,1,384,384]{3,2,1,0:T(8,128)(2,1)}, u32[]{:S(2)}, u32[]{:S(2)}) collective-permute-start(bf16[2,1,384,384]{3,2,1,0:T(8,128)(2,1)} %get-tuple-element.19), channel_id=1, source_target_pairs={{4,0},{8,4},{12,8},{5,1},{9,5},{13,9},{6,2},{10,6},{14,10},{7,3},{... | collective-permute-start | bytes 1769480 | tf_op jit(solution)/shard_map/ppermute | solution.py:21
  61.2 8.7 %copy-start.2 = (bf16[1,768,384]{2,1,0:T(8,128)(2,1)S(1)}, bf16[1,768,384]{2,1,0:T(8,128)(2,1)}, u32[]{:S(2)}) copy-start(bf16[1,768,384]{2,1,0:T(8,128)(2,1)} %get-tuple-element.24) | copy-start | bytes 1769476
  61.2 12.9 %copy-start.12 = (bf16[2,1,384,384]{3,2,1,0:T(8,128)(2,1)S(1)}, bf16[2,1,384,384]{3,2,1,0:T(8,128)(2,1)}, u32[]{:S(2)}) copy-start(bf16[2,1,384,384]{3,2,1,0:T(8,128)(2,1)} %get-tuple-element.22) | copy-start | bytes 1769476
  61.2 22.3 %collective-permute-start.6 = (bf16[2,1,384,384]{3,2,1,0:T(8,128)(2,1)}, bf16[2,1,384,384]{3,2,1,0:T(8,128)(2,1)S(1)}, u32[]{:S(2)}, u32[]{:S(2)}) collective-permute-start(bf16[2,1,384,384]{3,2,1,0:T(8,128)(2,1)} %get-tuple-element.21), channel_id=1, source_target_pairs={{0,4},{4,8},{8,12},{1,5},{5,9},{9,13},{2,6},{6,10},{10,14},{3,7},{... | collective-permute-start | bytes 1769480 | tf_op jit(solution)/shard_map/ppermute | solution.py:21
  68.4 5.7 %collective-permute-start.10 = (f32[2,1,384,64]{2,3,1,0:T(8,128)S(1)}, f32[2,1,384,64]{2,3,1,0:T(8,128)S(1)}, u32[]{:S(2)}, u32[]{:S(2)}) collective-permute-start(f32[2,1,384,64]{2,3,1,0:T(8,128)S(1)} %pad_maximum_fusion.7), channel_id=1, source_target_pairs={{0,2},{2,0},{1,3},{3,1},{4,6},{6,4},{5,7},{7,5},{8,10},{10,8},{9,1... | collective-permute-start | bytes 589832 | tf_op jit(solution)/shard_map/ppermute | solution.py:31
  74.1 13.4 %collective-permute-start.7 = (bf16[2,1,384,384]{3,2,1,0:T(8,128)(2,1)S(1)}, bf16[2,1,384,384]{3,2,1,0:T(8,128)(2,1)S(1)}, u32[]{:S(2)}, u32[]{:S(2)}) collective-permute-start(bf16[2,1,384,384]{3,2,1,0:T(8,128)(2,1)S(1)} %copy-done.12), channel_id=1, source_target_pairs={{4,0},{8,4},{12,8},{5,1},{9,5},{13,9},{6,2},{10,6},{14,10},{7,3},{... | collective-permute-start | bytes 1769480 | tf_op jit(solution)/shard_map/ppermute | solution.py:21
  75.5 13.0 %collective-permute-start.11 = (f32[1,384,64]{1,2,0:T(8,128)S(1)}, f32[1,384,64]{1,2,0:T(8,128)S(1)}, u32[]{:S(2)}, u32[]{:S(2)}) collective-permute-start(f32[1,384,64]{1,2,0:T(8,128)S(1)} %get-tuple-element.41), channel_id=1, source_target_pairs={{0,4},{4,8},{8,12},{1,5},{5,9},{9,13},{2,6},{6,10},{10,14},{3,7},{... | collective-permute-start | bytes 294920 | tf_op jit(solution)/shard_map/ppermute | solution.py:21
  80.0 8.5 %collective-permute-start.12 = (f32[1,384,64]{1,2,0:T(8,128)S(1)}, f32[1,384,64]{1,2,0:T(8,128)S(1)}, u32[]{:S(2)}, u32[]{:S(2)}) collective-permute-start(f32[1,384,64]{1,2,0:T(8,128)S(1)} %get-tuple-element.42), channel_id=1, source_target_pairs={{4,0},{8,4},{12,8},{5,1},{9,5},{13,9},{6,2},{10,6},{14,10},{7,3},{... | collective-permute-start | bytes 294920 | tf_op jit(solution)/shard_map/ppermute | solution.py:21
  83.5 5.7 %collective-permute-start.9 = (f32[1,768,64]{1,2,0:T(8,128)S(1)}, f32[1,768,64]{1,2,0:T(8,128)S(1)}, u32[]{:S(2)}, u32[]{:S(2)}) collective-permute-start(f32[1,768,64]{1,2,0:T(8,128)S(1)} %fusion.30), channel_id=1, source_target_pairs={{0,2},{2,0},{1,3},{3,1},{4,6},{6,4},{5,7},{7,5},{8,10},{10,8},{9,1... | collective-permute-start | bytes 589832 | tf_op jit(solution)/shard_map/ppermute | solution.py:31
  89.6 16.0 %copy-start.9 = (bf16[1,768,384]{2,1,0:T(8,128)(2,1)S(1)}, bf16[1,768,384]{2,1,0:T(8,128)(2,1)}, u32[]{:S(2)}) copy-start(bf16[1,768,384]{2,1,0:T(8,128)(2,1)} %get-tuple-element.15) | copy-start | bytes 1769476
  89.6 1.6 %collective-permute-start.13 = (f32[49152]{0:T(1024)S(1)}, f32[49152]{0:T(1024)}, u32[]{:S(2)}, u32[]{:S(2)}) collective-permute-start(f32[49152]{0:T(1024)S(1)} %select_n.63), channel_id=1, source_target_pairs={{0,1},{1,0},{2,3},{3,2},{4,5},{5,4},{6,7},{7,6},{8,9},{9,8},{10,11... | collective-permute-start | bytes 589832 | tf_op jit(solution)/shard_map/ppermute | solution.py:45
  89.7 15.8 %copy-start.10 = (bf16[1,768,384]{2,1,0:T(8,128)(2,1)S(1)}, bf16[1,768,384]{2,1,0:T(8,128)(2,1)}, u32[]{:S(2)}) copy-start(bf16[1,768,384]{2,1,0:T(8,128)(2,1)} %get-tuple-element.16) | copy-start | bytes 1769476
  92.3 5.8 %collective-permute-start.14 = (f32[24576]{0:T(1024)S(1)}, f32[24576]{0:T(1024)S(1)}, u32[]{:S(2)}, u32[]{:S(2)}) collective-permute-start(f32[24576]{0:T(1024)S(1)} %slice_select_fusion), channel_id=1, source_target_pairs={{0,4},{4,0},{8,12},{12,8},{1,5},{5,1},{9,13},{13,9},{2,6},{6,2},{1... | collective-permute-start | bytes 294920 | tf_op jit(solution)/shard_map/ppermute | solution.py:45
  98.1 7.4 %collective-permute-start.15 = (f32[24576]{0:T(1024)S(1)}, f32[24576]{0:T(1024)S(1)}, u32[]{:S(2)}, u32[]{:S(2)}) collective-permute-start(f32[24576]{0:T(1024)S(1)} %select_add_fusion), channel_id=1, source_target_pairs={{0,8},{4,12},{8,0},{12,4},{1,9},{5,13},{9,1},{13,5},{2,10},{6,14},... | collective-permute-start | bytes 294920 | tf_op jit(solution)/shard_map/ppermute | solution.py:78
  105.5 4.7 %collective-permute-start.16 = (f32[24576]{0:T(1024)S(1)}, f32[24576]{0:T(1024)S(1)}, u32[]{:S(2)}, u32[]{:S(2)}) collective-permute-start(f32[24576]{0:T(1024)S(1)} %add.62), channel_id=1, source_target_pairs={{0,4},{4,0},{8,12},{12,8},{1,5},{5,1},{9,13},{13,9},{2,6},{6,2},{1... | collective-permute-start | bytes 294920 | tf_op jit(solution)/shard_map/ppermute | solution.py:53
  110.2 1.5 %collective-permute-start.17 = (f32[49152]{0:T(1024)S(1)}, f32[49152]{0:T(1024)S(1)}, u32[]{:S(2)}, u32[]{:S(2)}) collective-permute-start(f32[49152]{0:T(1024)S(1)} %maximum_select_fusion.1), channel_id=1, source_target_pairs={{0,1},{1,0},{2,3},{3,2},{4,5},{5,4},{6,7},{7,6},{8,9},{9,8},{10,11... | collective-permute-start | bytes 589832 | tf_op jit(solution)/shard_map/ppermute | solution.py:53
  (10 other events, 43.6 us)

commit v17 on v12

--- a/solution.py
+++ b/solution.py
@@ -233,7 +233,14 @@
     backward_piece = jnp.einsum(
         "dsi,ji->dsj", value_gradient, adapter_up_weight, preferred_element_type=jnp.float32
     )
-    backward_rows = butterfly_sum(backward_piece, "head").astype(jnp.bfloat16)
+    head_peers = lax.axis_size("head")
+    step = 1
+    while step < head_peers:
+        sent = backward_piece.astype(jnp.bfloat16)
+        other = lax.ppermute(sent, "head", [(i, i ^ step) for i in range(head_peers)])
+        backward_piece = sent.astype(jnp.float32) + other.astype(jnp.float32)
+        step *= 2
+    backward_rows = backward_piece.astype(jnp.bfloat16)
     gradient_down_local = adapter_scale * jnp.einsum(
         "yhm,yhz->mz", normed, backward_rows, preferred_element_type=jnp.float32
     )

time: 112 us -> 111 us (level)
    ppermute x2 -> x1, waiting for transfers between devices: 2.82 us -> 0.01 us  [butterfly_sum(): other = lax.ppermute(tree, axis, pairs)]
    ppermute x0 -> x1, waiting for transfers between devices: none -> 1.77 us  [on_device(): lax.ppermute(sent, 'head', [(i, i ^ step) for i in range(head_peers)])]
    ppermute x0 -> x1, starting transfers between devices: none -> 1.53 us  [on_device(): lax.ppermute(sent, 'head', [(i, i ^ step) for i in range(head_peers)])]
    ppermute x2 -> x1, starting transfers between devices: 3 us -> 1.51 us  [butterfly_sum(): other = lax.ppermute(tree, axis, pairs)]
where the time goes in v17:
time: 111 us
  waiting for transfers between devices  31.3 us (28%)
  starting transfers between devices  28.9 us (26%)
  Pallas kernels  26.8 us (24%)
  other arithmetic  10.7 us (10%)
  local copies, waits for them, and re-layouts  7.82 us (7%)
  matrix products  4.25 us (4%)
    pallas_call x2, Pallas kernels, attention_backward(): pl.pallas_call(attention_kernel, grid=(clip_count, heads), in_specs=[pl.B...  26.8 us
    ppermute x8, starting transfers between devices, shifted(): return lax.ppermute(shard, axis, pairs)  24.3 us
    ppermute x8, waiting for transfers between devices, shifted(): return lax.ppermute(shard, axis, pairs)  13.6 us
    ppermute x1, waiting for transfers between devices, all_sum(): lax.ppermute(flat, axis, [(i, i ^ step) for i in range(lax.axis_size(axis...  6.53 us
    ppermute x2, waiting for transfers between devices, scatter_sum(): lax.ppermute(send, axis, [(i, i ^ step) for i in range(peers)])  5.66 us
    unnamed x30, local copies, waits for them, and re-layouts  4.85 us
    ppermute x2, waiting for transfers between devices, gather_back(): other = lax.ppermute(flat, axis, [(i, i ^ step) for i in range(peers)])  3.72 us
    concatenate x3, other arithmetic, on_device(): jnp.concatenate([o[i] for o in outs], 2)  2.31 us
  transfers between devices with their start and end apart: 15, of which 10 were waited for; matrix products, arithmetic and copies ran while one was open for 12% of the time, Pallas kernels for 24%

profile of v17, /device:TPU:0, one launch (start us, length us, event | category | flops | bytes accessed | tf_op | source)
XLA Modules:
  0.0 110.8 jit_solution(13711190721961272897)
XLA Ops:
  0.6 1.9 %slice_bitcast_fusion.8 = (bf16[1,1,384,384]{3,2,1,0:T(8,128)(2,1)S(1)}, bf16[1,1,384,384]{3,2,1,0:T(8,128)(2,1)S(1)}, bf16[1,1,384,384]{3,2,1,0:T(8,128)(2,1)S(...) fusion(bf16[1,768,768]{2,1,0:T(8,128)(2,1)} %v_ref.3, ...), kind=kLoop, calls=%fused_computation.39 | loop fusion | bytes 4718592 | tf_op jit(solution)/shard_map/stack | solution.py:218
  3.5 5.0 %collective-permute-start = (bf16[2,1,384,384]{3,2,1,0:T(8,128)(2,1)}, bf16[2,1,384,384]{3,2,1,0:T(8,128)(2,1)S(1)}, u32[]{:S(2)}, u32[]{:S(2)}) collective-permute-start(bf16[2,1,384,384]{3,2,1,0:T(8,128)(2,1)} %pad_maximum_fusion.3), channel_id=1, source_target_pairs={{0,4},{4,8},{8,12},{1,5},{5,9},{9,13},{2,6},{6,10},{10,14},{3,7},{... | collective-permute-start | bytes 1769480 | tf_op jit(solution)/shard_map/ppermute | solution.py:21
  9.3 1.3 %collective-permute-start.1 = (bf16[2,1,384,384]{3,2,1,0:T(8,128)(2,1)}, bf16[2,1,384,384]{3,2,1,0:T(8,128)(2,1)S(1)}, u32[]{:S(2)}, u32[]{:S(2)}) collective-permute-start(bf16[2,1,384,384]{3,2,1,0:T(8,128)(2,1)} %pad_maximum_fusion.4), channel_id=1, source_target_pairs={{4,0},{8,4},{12,8},{5,1},{9,5},{13,9},{6,2},{10,6},{14,10},{7,3},{... | collective-permute-start | bytes 1769480 | tf_op jit(solution)/shard_map/ppermute | solution.py:21
  11.5 1.3 %collective-permute-start.3 = (bf16[2,1,384,384]{3,2,1,0:T(8,128)(2,1)}, bf16[2,1,384,384]{3,2,1,0:T(8,128)(2,1)S(1)}, u32[]{:S(2)}, u32[]{:S(2)}) collective-permute-start(bf16[2,1,384,384]{3,2,1,0:T(8,128)(2,1)} %pad_maximum_fusion.6), channel_id=1, source_target_pairs={{4,0},{8,4},{12,8},{5,1},{9,5},{13,9},{6,2},{10,6},{14,10},{7,3},{... | collective-permute-start | bytes 1769480 | tf_op jit(solution)/shard_map/ppermute | solution.py:21
  13.7 5.2 %collective-permute-start.2 = (bf16[2,1,384,384]{3,2,1,0:T(8,128)(2,1)}, bf16[2,1,384,384]{3,2,1,0:T(8,128)(2,1)S(1)}, u32[]{:S(2)}, u32[]{:S(2)}) collective-permute-start(bf16[2,1,384,384]{3,2,1,0:T(8,128)(2,1)} %pad_maximum_fusion.5), channel_id=1, source_target_pairs={{0,4},{4,8},{8,12},{1,5},{5,9},{9,13},{2,6},{6,10},{10,14},{3,7},{... | collective-permute-start | bytes 1769480 | tf_op jit(solution)/shard_map/ppermute | solution.py:21
  22.4 5.3 %collective-permute-done.1.right_ref = bf16[2,1,384,384]{3,2,1,0:T(8,128)(2,1)S(1)} collective-permute-done((bf16[2,1,384,384]{3,2,1,0:T(8,128)(2,1)}, bf16[2,1,384,384]{3,2,1,0:T(8,128)(2,1)S(1)}, u32[]{:S(2)}, u32[]{:S(2)}) %collective-permute-start.1) | collective-permute-done | bytes 589856 | tf_op jit(solution)/shard_map/ppermute | solution.py:21
  28.5 13.4 %shard_map.128 = (bf16[1,768,384]{2,1,0:T(8,128)(2,1)}, bf16[1,768,384]{2,1,0:T(8,128)(2,1)}, bf16[1,768,384]{2,1,0:T(8,128)(2,1)}, bf16[2,1,384,384]{3,2,1,0:T(8,128)(2,1)}, bf16[2,1,384,384]{3,2,1,0:T(8,128)(2,1)}) custom-call(f32[6]{0:T(128)} %and_select_fusion.bias_ref, bf16[1,768,768]{2,1,0:T(8,128)(2,1)} %q_ref.3, bf16[1,768,768]{2,1,0:T(8,128)(2,1)} %g_ref.3, ...), custom_call_target="tpu_custom_call" | custom-call | tf_op jit(solution)/shard_map/pallas_call | solution.py:168
  41.9 3.5 %collective-permute-start.4 = (bf16[2,1,384,384]{3,2,1,0:T(8,128)(2,1)}, bf16[2,1,384,384]{3,2,1,0:T(8,128)(2,1)S(1)}, u32[]{:S(2)}, u32[]{:S(2)}) collective-permute-start(bf16[2,1,384,384]{3,2,1,0:T(8,128)(2,1)} %get-tuple-element.18), channel_id=1, source_target_pairs={{0,4},{4,8},{8,12},{1,5},{5,9},{9,13},{2,6},{6,10},{10,14},{3,7},{... | collective-permute-start | bytes 1769480 | tf_op jit(solution)/shard_map/ppermute | solution.py:21
  45.4 1.3 %collective-permute-start.5 = (bf16[2,1,384,384]{3,2,1,0:T(8,128)(2,1)}, bf16[2,1,384,384]{3,2,1,0:T(8,128)(2,1)S(1)}, u32[]{:S(2)}, u32[]{:S(2)}) collective-permute-start(bf16[2,1,384,384]{3,2,1,0:T(8,128)(2,1)} %get-tuple-element.19), channel_id=1, source_target_pairs={{4,0},{8,4},{12,8},{5,1},{9,5},{13,9},{6,2},{10,6},{14,10},{7,3},{... | collective-permute-start | bytes 1769480 | tf_op jit(solution)/shard_map/ppermute | solution.py:21
  48.4 13.4 %shard_map.129 = (bf16[1,768,384]{2,1,0:T(8,128)(2,1)}, bf16[1,768,384]{2,1,0:T(8,128)(2,1)}, bf16[1,768,384]{2,1,0:T(8,128)(2,1)}, bf16[2,1,384,384]{3,2,1,0:T(8,128)(2,1)}, bf16[2,1,384,384]{3,2,1,0:T(8,128)(2,1)}) custom-call(f32[6]{0:T(128)} %and_select_fusion.bias_ref, bf16[1,768,768]{2,1,0:T(8,128)(2,1)} %q_ref.3, bf16[1,768,768]{2,1,0:T(8,128)(2,1)} %g_ref.3, ...), custom_call_target="tpu_custom_call" | custom-call | tf_op jit(solution)/shard_map/pallas_call | solution.py:168
  61.8 5.4 %collective-permute-start.6 = (bf16[2,1,384,384]{3,2,1,0:T(8,128)(2,1)}, bf16[2,1,384,384]{3,2,1,0:T(8,128)(2,1)}, u32[]{:S(2)}, u32[]{:S(2)}) collective-permute-start(bf16[2,1,384,384]{3,2,1,0:T(8,128)(2,1)} %get-tuple-element.21), channel_id=1, source_target_pairs={{0,4},{4,8},{8,12},{1,5},{5,9},{9,13},{2,6},{6,10},{10,14},{3,7},{... | collective-permute-start | bytes 1769480 | tf_op jit(solution)/shard_map/ppermute | solution.py:21
  67.2 1.5 %collective-permute-start.7 = (bf16[2,1,384,384]{3,2,1,0:T(8,128)(2,1)}, bf16[2,1,384,384]{3,2,1,0:T(8,128)(2,1)}, u32[]{:S(2)}, u32[]{:S(2)}) collective-permute-start(bf16[2,1,384,384]{3,2,1,0:T(8,128)(2,1)} %get-tuple-element.22), channel_id=1, source_target_pairs={{4,0},{8,4},{12,8},{5,1},{9,5},{13,9},{6,2},{10,6},{14,10},{7,3},{... | collective-permute-start | bytes 1769480 | tf_op jit(solution)/shard_map/ppermute | solution.py:21
  68.7 2.1 %fusion.16 = f32[1,768,64]{1,2,0:T(8,128)} fusion(bf16[768,64]{0,1:T(8,128)(2,1)} %param.14, bf16[1,768,768]{2,1,0:T(8,128)(2,1)S(1)} %copy-done), kind=kOutput, calls=%fused_computation.25 | convolution fusion | flops 75497472 | bytes 1474560 | tf_op jit(solution)/shard_map/pqg,gv->pqv/dot_general | solution.py:192
  70.7 1.5 %collective-permute-start.8 = (f32[1,768,64]{1,2,0:T(8,128)}, f32[1,768,64]{1,2,0:T(8,128)}, u32[]{:S(2)}, u32[]{:S(2)}) collective-permute-start(f32[1,768,64]{1,2,0:T(8,128)} %fusion.16), channel_id=1, source_target_pairs={{0,2},{2,0},{1,3},{3,1},{4,6},{6,4},{5,7},{7,5},{8,10},{10,8},{9,1... | collective-permute-start | bytes 589832 | tf_op jit(solution)/shard_map/ppermute | solution.py:31
  73.8 2.2 %collective-permute-done.6 = bf16[2,1,384,384]{3,2,1,0:T(8,128)(2,1)} collective-permute-done((bf16[2,1,384,384]{3,2,1,0:T(8,128)(2,1)}, bf16[2,1,384,384]{3,2,1,0:T(8,128)(2,1)}, u32[]{:S(2)}, u32[]{:S(2)}) %collective-permute-start.6) | collective-permute-done | bytes 589856 | tf_op jit(solution)/shard_map/ppermute | solution.py:21
  76.0 4.9 %collective-permute-done.7 = bf16[2,1,384,384]{3,2,1,0:T(8,128)(2,1)} collective-permute-done((bf16[2,1,384,384]{3,2,1,0:T(8,128)(2,1)}, bf16[2,1,384,384]{3,2,1,0:T(8,128)(2,1)}, u32[]{:S(2)}, u32[]{:S(2)}) %collective-permute-start.7) | collective-permute-done | bytes 589856 | tf_op jit(solution)/shard_map/ppermute | solution.py:21
  81.0 1.4 %maximum_convert_fusion.1 = f32[2,1,768,384]{3,2,1,0:T(8,128)S(1)} fusion(bf16[2,1,384,384]{3,2,1,0:T(8,128)(2,1)} %collective-permute-done.7, bf16[2,1,384,384]{3,2,1,0:T(8,128)(2,1)} %collective-permute-done.6), kind=kLoop, calls=%fused_computation.14 | loop fusion | flops 2359296 | bytes 3538944 | tf_op jit(solution)/shard_map/convert_element_type | solution.py:225
  84.1 1.5 %collective-permute-start.9 = (bf16[1,768,64]{1,2,0:T(8,128)(2,1)S(1)}, bf16[1,768,64]{1,2,0:T(8,128)(2,1)S(1)}, u32[]{:S(2)}, u32[]{:S(2)}) collective-permute-start(bf16[1,768,64]{1,2,0:T(8,128)(2,1)S(1)} %fusion.28), channel_id=1, source_target_pairs={{0,2},{2,0},{1,3},{3,1},{4,6},{6,4},{5,7},{7,5},{8,10},{10,8},{9,1... | collective-permute-start | bytes 294920 | tf_op jit(solution)/shard_map/ppermute | solution.py:240
  85.6 1.4 %fusion.22 = f32[64,768]{1,0:T(8,128)S(1)} fusion(bf16[1,768,768]{2,1,0:T(8,128)(2,1)S(1)} %pad_maximum_fusion.2, f32[1,768,64]{1,2,0:T(8,128)} %fusion.16, f32[1,768,64]{1,2,0:T(8,128)} %collective-permute-done.8), kind=kOutput, calls=%fused_computation.27 | convolution fusion | flops 75644928 | bytes 1769472 | tf_op jit(solution)/shard_map/igb,igu->bu/dot_general | solution.py:247
  87.0 1.8 %collective-permute-done.9 = bf16[1,768,64]{1,2,0:T(8,128)(2,1)S(1)} collective-permute-done((bf16[1,768,64]{1,2,0:T(8,128)(2,1)S(1)}, bf16[1,768,64]{1,2,0:T(8,128)(2,1)S(1)}, u32[]{:S(2)}, u32[]{:S(2)}) %collective-permute-start.9) | collective-permute-done | bytes 98336 | tf_op jit(solution)/shard_map/ppermute | solution.py:240
  89.2 1.5 %collective-permute-done.10 = f32[49152]{0:T(1024)} collective-permute-done((f32[49152]{0:T(1024)S(1)}, f32[49152]{0:T(1024)}, u32[]{:S(2)}, u32[]{:S(2)}) %collective-permute-start.10) | collective-permute-done | bytes 196640 | tf_op jit(solution)/shard_map/ppermute | solution.py:45
  92.5 4.1 %collective-permute-done.11 = f32[24576]{0:T(1024)S(1)} collective-permute-done((f32[24576]{0:T(1024)S(1)}, f32[24576]{0:T(1024)S(1)}, u32[]{:S(2)}, u32[]{:S(2)}) %collective-permute-start.11) | collective-permute-done | bytes 98336 | tf_op jit(solution)/shard_map/ppermute | solution.py:45
  97.2 6.5 %collective-permute-done.12 = f32[24576]{0:T(1024)S(1)} collective-permute-done((f32[24576]{0:T(1024)S(1)}, f32[24576]{0:T(1024)S(1)}, u32[]{:S(2)}, u32[]{:S(2)}) %collective-permute-start.12) | collective-permute-done | bytes 98336 | tf_op jit(solution)/shard_map/ppermute | solution.py:78
  104.9 3.5 %collective-permute-done.13 = f32[24576]{0:T(1024)S(1)} collective-permute-done((f32[24576]{0:T(1024)S(1)}, f32[24576]{0:T(1024)S(1)}, u32[]{:S(2)}, u32[]{:S(2)}) %collective-permute-start.13) | collective-permute-done | bytes 98336 | tf_op jit(solution)/shard_map/ppermute | solution.py:53
  (75 shorter events, 19.0 us)
Async XLA Ops:
  0.6 68.0 %copy-start = (bf16[1,768,768]{2,1,0:T(8,128)(2,1)S(1)}, bf16[1,768,768]{2,1,0:T(8,128)(2,1)}, u32[]{:S(2)}) copy-start(bf16[1,768,768]{2,1,0:T(8,128)(2,1)} %param.13) | copy-start | bytes 3538948
  3.5 19.0 %collective-permute-start = (bf16[2,1,384,384]{3,2,1,0:T(8,128)(2,1)}, bf16[2,1,384,384]{3,2,1,0:T(8,128)(2,1)S(1)}, u32[]{:S(2)}, u32[]{:S(2)}) collective-permute-start(bf16[2,1,384,384]{3,2,1,0:T(8,128)(2,1)} %pad_maximum_fusion.3), channel_id=1, source_target_pairs={{0,4},{4,8},{8,12},{1,5},{5,9},{9,13},{2,6},{6,10},{10,14},{3,7},{... | collective-permute-start | bytes 1769480 | tf_op jit(solution)/shard_map/ppermute | solution.py:21
  9.3 18.3 %collective-permute-start.1 = (bf16[2,1,384,384]{3,2,1,0:T(8,128)(2,1)}, bf16[2,1,384,384]{3,2,1,0:T(8,128)(2,1)S(1)}, u32[]{:S(2)}, u32[]{:S(2)}) collective-permute-start(bf16[2,1,384,384]{3,2,1,0:T(8,128)(2,1)} %pad_maximum_fusion.4), channel_id=1, source_target_pairs={{4,0},{8,4},{12,8},{5,1},{9,5},{13,9},{6,2},{10,6},{14,10},{7,3},{... | collective-permute-start | bytes 1769480 | tf_op jit(solution)/shard_map/ppermute | solution.py:21
  10.6 9.0 %copy-start.13 = (s32[8,3]{0,1:T(4,128)S(1)}, s32[8,3]{0,1:T(4,128)}, u32[]{:S(2)}) copy-start(s32[8,3]{0,1:T(4,128)} %param.16) | copy-start | bytes 292
  11.5 35.2 %collective-permute-start.3 = (bf16[2,1,384,384]{3,2,1,0:T(8,128)(2,1)}, bf16[2,1,384,384]{3,2,1,0:T(8,128)(2,1)S(1)}, u32[]{:S(2)}, u32[]{:S(2)}) collective-permute-start(bf16[2,1,384,384]{3,2,1,0:T(8,128)(2,1)} %pad_maximum_fusion.6), channel_id=1, source_target_pairs={{4,0},{8,4},{12,8},{5,1},{9,5},{13,9},{6,2},{10,6},{14,10},{7,3},{... | collective-permute-start | bytes 1769480 | tf_op jit(solution)/shard_map/ppermute | solution.py:21
  13.7 33.1 %collective-permute-start.2 = (bf16[2,1,384,384]{3,2,1,0:T(8,128)(2,1)}, bf16[2,1,384,384]{3,2,1,0:T(8,128)(2,1)S(1)}, u32[]{:S(2)}, u32[]{:S(2)}) collective-permute-start(bf16[2,1,384,384]{3,2,1,0:T(8,128)(2,1)} %pad_maximum_fusion.5), channel_id=1, source_target_pairs={{0,4},{4,8},{8,12},{1,5},{5,9},{9,13},{2,6},{6,10},{10,14},{3,7},{... | collective-permute-start | bytes 1769480 | tf_op jit(solution)/shard_map/ppermute | solution.py:21
  22.4 5.3 %copy-start.4 = (bf16[2,1,384,384]{3,2,1,0:T(8,128)(2,1)}, bf16[2,1,384,384]{3,2,1,0:T(8,128)(2,1)S(1)}, u32[]{:S(2)}) copy-start(bf16[2,1,384,384]{3,2,1,0:T(8,128)(2,1)S(1)} %collective-permute-done.left_ref) | copy-start | bytes 1769476
  41.9 30.3 %collective-permute-start.4 = (bf16[2,1,384,384]{3,2,1,0:T(8,128)(2,1)}, bf16[2,1,384,384]{3,2,1,0:T(8,128)(2,1)S(1)}, u32[]{:S(2)}, u32[]{:S(2)}) collective-permute-start(bf16[2,1,384,384]{3,2,1,0:T(8,128)(2,1)} %get-tuple-element.18), channel_id=1, source_target_pairs={{0,4},{4,8},{8,12},{1,5},{5,9},{9,13},{2,6},{6,10},{10,14},{3,7},{... | collective-permute-start | bytes 1769480 | tf_op jit(solution)/shard_map/ppermute | solution.py:21
  45.4 26.8 %collective-permute-start.5 = (bf16[2,1,384,384]{3,2,1,0:T(8,128)(2,1)}, bf16[2,1,384,384]{3,2,1,0:T(8,128)(2,1)S(1)}, u32[]{:S(2)}, u32[]{:S(2)}) collective-permute-start(bf16[2,1,384,384]{3,2,1,0:T(8,128)(2,1)} %get-tuple-element.19), channel_id=1, source_target_pairs={{4,0},{8,4},{12,8},{5,1},{9,5},{13,9},{6,2},{10,6},{14,10},{7,3},{... | collective-permute-start | bytes 1769480 | tf_op jit(solution)/shard_map/ppermute | solution.py:21
  61.8 14.2 %collective-permute-start.6 = (bf16[2,1,384,384]{3,2,1,0:T(8,128)(2,1)}, bf16[2,1,384,384]{3,2,1,0:T(8,128)(2,1)}, u32[]{:S(2)}, u32[]{:S(2)}) collective-permute-start(bf16[2,1,384,384]{3,2,1,0:T(8,128)(2,1)} %get-tuple-element.21), channel_id=1, source_target_pairs={{0,4},{4,8},{8,12},{1,5},{5,9},{9,13},{2,6},{6,10},{10,14},{3,7},{... | collective-permute-start | bytes 1769480 | tf_op jit(solution)/shard_map/ppermute | solution.py:21
  67.2 13.8 %collective-permute-start.7 = (bf16[2,1,384,384]{3,2,1,0:T(8,128)(2,1)}, bf16[2,1,384,384]{3,2,1,0:T(8,128)(2,1)}, u32[]{:S(2)}, u32[]{:S(2)}) collective-permute-start(bf16[2,1,384,384]{3,2,1,0:T(8,128)(2,1)} %get-tuple-element.22), channel_id=1, source_target_pairs={{4,0},{8,4},{12,8},{5,1},{9,5},{13,9},{6,2},{10,6},{14,10},{7,3},{... | collective-permute-start | bytes 1769480 | tf_op jit(solution)/shard_map/ppermute | solution.py:21
  70.7 14.8 %collective-permute-start.8 = (f32[1,768,64]{1,2,0:T(8,128)}, f32[1,768,64]{1,2,0:T(8,128)}, u32[]{:S(2)}, u32[]{:S(2)}) collective-permute-start(f32[1,768,64]{1,2,0:T(8,128)} %fusion.16), channel_id=1, source_target_pairs={{0,2},{2,0},{1,3},{3,1},{4,6},{6,4},{5,7},{7,5},{8,10},{10,8},{9,1... | collective-permute-start | bytes 589832 | tf_op jit(solution)/shard_map/ppermute | solution.py:31
  72.3 1.2 %copy-start.6 = (bf16[1,768,384]{2,1,0:T(8,128)(2,1)S(1)}, bf16[1,768,384]{2,1,0:T(8,128)(2,1)}, u32[]{:S(2)}) copy-start(bf16[1,768,384]{2,1,0:T(8,128)(2,1)} %get-tuple-element.23) | copy-start | bytes 1769476
  73.8 8.6 %copy-start.8 = (bf16[1,768,384]{2,1,0:T(8,128)(2,1)S(1)}, bf16[1,768,384]{2,1,0:T(8,128)(2,1)}, u32[]{:S(2)}) copy-start(bf16[1,768,384]{2,1,0:T(8,128)(2,1)} %get-tuple-element.20) | copy-start | bytes 1769476
  73.8 8.6 %copy-start.9 = (bf16[1,768,384]{2,1,0:T(8,128)(2,1)S(1)}, bf16[1,768,384]{2,1,0:T(8,128)(2,1)}, u32[]{:S(2)}) copy-start(bf16[1,768,384]{2,1,0:T(8,128)(2,1)} %get-tuple-element.24) | copy-start | bytes 1769476
  83.6 3.4 %copy-start.1 = (bf16[1,768,768]{2,1,0:T(8,128)(2,1)}, bf16[1,768,768]{2,1,0:T(8,128)(2,1)S(1)}, u32[]{:S(2)}) copy-start(bf16[1,768,768]{2,1,0:T(8,128)(2,1)S(1)} %pad_maximum_fusion.2) | copy-start | bytes 3538948
  84.1 4.7 %collective-permute-start.9 = (bf16[1,768,64]{1,2,0:T(8,128)(2,1)S(1)}, bf16[1,768,64]{1,2,0:T(8,128)(2,1)S(1)}, u32[]{:S(2)}, u32[]{:S(2)}) collective-permute-start(bf16[1,768,64]{1,2,0:T(8,128)(2,1)S(1)} %fusion.28), channel_id=1, source_target_pairs={{0,2},{2,0},{1,3},{3,1},{4,6},{6,4},{5,7},{7,5},{8,10},{10,8},{9,1... | collective-permute-start | bytes 294920 | tf_op jit(solution)/shard_map/ppermute | solution.py:240
  89.1 14.7 %copy-start.10 = (bf16[1,768,384]{2,1,0:T(8,128)(2,1)S(1)}, bf16[1,768,384]{2,1,0:T(8,128)(2,1)}, u32[]{:S(2)}) copy-start(bf16[1,768,384]{2,1,0:T(8,128)(2,1)} %get-tuple-element.15) | copy-start | bytes 1769476
  89.1 1.6 %collective-permute-start.10 = (f32[49152]{0:T(1024)S(1)}, f32[49152]{0:T(1024)}, u32[]{:S(2)}, u32[]{:S(2)}) collective-permute-start(f32[49152]{0:T(1024)S(1)} %select_n.63), channel_id=1, source_target_pairs={{0,1},{1,0},{2,3},{3,2},{4,5},{5,4},{6,7},{7,6},{8,9},{9,8},{10,11... | collective-permute-start | bytes 589832 | tf_op jit(solution)/shard_map/ppermute | solution.py:45
  89.2 14.6 %copy-start.11 = (bf16[1,768,384]{2,1,0:T(8,128)(2,1)S(1)}, bf16[1,768,384]{2,1,0:T(8,128)(2,1)}, u32[]{:S(2)}) copy-start(bf16[1,768,384]{2,1,0:T(8,128)(2,1)} %get-tuple-element.16) | copy-start | bytes 1769476
  91.7 4.9 %collective-permute-start.11 = (f32[24576]{0:T(1024)S(1)}, f32[24576]{0:T(1024)S(1)}, u32[]{:S(2)}, u32[]{:S(2)}) collective-permute-start(f32[24576]{0:T(1024)S(1)} %slice_select_fusion), channel_id=1, source_target_pairs={{0,4},{4,0},{8,12},{12,8},{1,5},{5,1},{9,13},{13,9},{2,6},{6,2},{1... | collective-permute-start | bytes 294920 | tf_op jit(solution)/shard_map/ppermute | solution.py:45
  96.6 7.1 %collective-permute-start.12 = (f32[24576]{0:T(1024)S(1)}, f32[24576]{0:T(1024)S(1)}, u32[]{:S(2)}, u32[]{:S(2)}) collective-permute-start(f32[24576]{0:T(1024)S(1)} %select_add_fusion), channel_id=1, source_target_pairs={{0,8},{4,12},{8,0},{12,4},{1,9},{5,13},{9,1},{13,5},{2,10},{6,14},... | collective-permute-start | bytes 294920 | tf_op jit(solution)/shard_map/ppermute | solution.py:78
  103.7 4.7 %collective-permute-start.13 = (f32[24576]{0:T(1024)S(1)}, f32[24576]{0:T(1024)S(1)}, u32[]{:S(2)}, u32[]{:S(2)}) collective-permute-start(f32[24576]{0:T(1024)S(1)} %add.46), channel_id=1, source_target_pairs={{0,4},{4,0},{8,12},{12,8},{1,5},{5,1},{9,13},{13,9},{2,6},{6,2},{1... | collective-permute-start | bytes 294920 | tf_op jit(solution)/shard_map/ppermute | solution.py:53
  108.4 1.5 %collective-permute-start.14 = (f32[49152]{0:T(1024)S(1)}, f32[49152]{0:T(1024)S(1)}, u32[]{:S(2)}, u32[]{:S(2)}) collective-permute-start(f32[49152]{0:T(1024)S(1)} %maximum_select_fusion.1), channel_id=1, source_target_pairs={{0,1},{1,0},{2,3},{3,2},{4,5},{5,4},{6,7},{7,6},{8,9},{9,8},{10,11... | collective-permute-start | bytes 589832 | tf_op jit(solution)/shard_map/ppermute | solution.py:53
  (6 other events, 4.9 us)
